TPU v7x, 32 devices: a whole 2x2x4 slice. The times are simulated.
32 devices in a mesh: seq: 4 (over y, x), tp: 8 (over z, core).
Axes of the slice: x: 2, y: 2, z: 4, core: 2. Of those that a mesh axis runs over, the one named last changes fastest.
Arguments:
- hidden: bfloat16 [512, 28672], P('seq', 'tp'), may hold values from -6 to 6
- down_weight: bfloat16 [28672, 8192], P('tp', 'seq'), may hold values from -0.03125 to 0.03125
- channel_scale: float32 [8192], P('seq'), may hold values from 0.25 to 1.75
Outputs:
- mixed: bfloat16 [512, 8192], P('tp', 'seq')
All inputs are finite; a program needn't handle non-finite values.
Results may differ from a plain program's by a relative error of at most 0.0049.
Values may be sent and summed in bfloat16 or wider, within the bound.
No kernel may reach another device: no remote copies, remote signals or barrier semaphores. Data moves between devices by JAX's collectives and lax.ppermute only.
A program may use at most 128 MiB of HBM per device.

v0:
```python
import math

import jax
import jax.numpy as jnp
import numpy as np
from jax import lax
from jax.sharding import PartitionSpec as P

PALEY = 28


def paley_table():
    residues = set((value * value % 13 for value in range(1, 13)))
    conference = np.zeros((14, 14))
    conference[0, 1:] = 1.0
    conference[1:, 0] = 1.0
    for first in range(13):
        for second in range(13):
            gap = (second - first) % 13
            if gap != 0:
                conference[1 + first, 1 + second] = 1.0 if gap in residues else -1.0
    upper = np.array([[1.0, 1.0], [1.0, -1.0]])
    lower = np.array([[1.0, -1.0], [-1.0, -1.0]])
    return np.kron(conference, upper) + np.kron(np.eye(14), lower)


def walsh_table(order):
    index_rows = np.arange(order)[:, None]
    index_cols = np.arange(order)[None, :]
    signs = np.ones((order, order))
    bit_value = 1
    while bit_value < order:
        both_set = index_rows // bit_value % 2 * (index_cols // bit_value % 2)
        signs = signs * (1 - 2 * both_set)
        bit_value = bit_value * 2
    return signs


def shards(hidden, down_weight, channel_scale):
    tp_count = lax.axis_size("tp")
    units = hidden.shape[1]
    total_units = units * tp_count
    local_table = jnp.asarray(np.kron(walsh_table(units // PALEY), paley_table()), jnp.bfloat16)
    factor = 1.0 / math.sqrt(total_units)
    spread = lax.all_to_all(hidden, "tp", split_axis=0, concat_axis=1, tiled=True)
    few_rows = spread.shape[0]
    blocks = spread.reshape(few_rows, tp_count, units)
    inner = jnp.einsum("rtl,lm->rtm", blocks, local_table, preferred_element_type=jnp.float32)
    cross_table = jnp.asarray(walsh_table(tp_count), jnp.float32)
    outer = jnp.einsum("rtm,tu->rum", inner, cross_table, precision=lax.Precision.HIGHEST)
    turned = (outer * factor).astype(jnp.bfloat16).reshape(few_rows, total_units)
    rotated = lax.all_to_all(turned, "tp", split_axis=1, concat_axis=0, tiled=True)
    partial_terms = jnp.dot(
        lax.all_gather(rotated, "seq", axis=0, tiled=True),
        down_weight,
        preferred_element_type=jnp.float32,
    )
    summed = lax.psum_scatter(partial_terms, "tp", scatter_dimension=0, tiled=True)
    return (summed * channel_scale[None, :]).astype(jnp.bfloat16)


def solution(mesh):
    placed = (P("seq", "tp"), P("tp", "seq"), P("seq"))
    return jax.shard_map(
        shards, mesh=mesh, in_specs=placed, out_specs=P("tp", "seq"), check_vma=False
    )
```

profile of v0, /device:TPU:0, one launch (start us, length us, event | category | flops | bytes accessed | tf_op | source)
XLA Modules:
  0.0 195.8 jit_solution(9701736656185318527)
XLA Ops:
  6.5 0.0 all-gather.2.cloned.1.call-start
  6.5 30.1 %all_to_all.32 = bf16[8,16,3584]{2,1,0:T(8,128)(2,1)S(1)} all-to-all(bf16[8,16,3584]{2,1,0:T(8,128)(2,1)} %bitcast.19), channel_id=1, replica_groups=mesh['seq'=4,'tp'=8] {'tp'}, dimensions={0} | all-to-all | bytes 1835008 | tf_op jit(solution)/shard_map/all_to_all | solution.py:45
  36.6 0.0 copy-start.1
  36.6 10.7 %convolution_bitcast_fusion = f32[16,8,3584]{2,1,0:T(8,128)S(1)} fusion(bf16[3584,3584,1]{1,0,2:T(8,128)(2,1)} %constant.8, bf16[8,16,3584]{2,1,0:T(8,128)(2,1)S(1)} %all_to_all.32), kind=kOutput, calls=%fused_computation.1 | convolution fusion | flops 3288334336 | bytes 28442624 | tf_op jit(solution)/shard_map/rtl,lm->rtm/dot_general | solution.py:48
  47.3 0.0 copy-done.1
  47.3 1.7 fusion.1
  49.0 0.3 copy.11
  49.3 26.9 %all_to_all.33 = bf16[16,8,3584]{2,0,1:T(8,128)(2,1)} all-to-all(bf16[16,8,3584]{2,0,1:T(8,128)(2,1)S(1)} %copy.11), channel_id=1, replica_groups=mesh['seq'=4,'tp'=8] {'tp'}, dimensions={1} | all-to-all | bytes 1835008 | tf_op jit(solution)/shard_map/all_to_all | solution.py:52
  76.2 0.0 all-gather.2.cloned.1.call-update
  76.2 0.0 reduce-scatter.2.cloned.1.call-start
  76.2 47.4 %all-gather.2.cloned.1.call-done = bf16[512,3584]{1,0:T(8,128)(2,1)} async-done(((bf16[128,3584]{1,0:T(8,128)(2,1)}), bf16[512,3584]{1,0:T(8,128)(2,1)}) %all-gather.2.cloned.1.call-update) | async-done | bytes 3670032 | tf_op jit(solution)/shard_map/all_gather | solution.py:54
  123.6 13.4 %fusion.2 = f32[512,2048]{1,0:T(8,128)} fusion(bf16[512,3584]{1,0:T(8,128)(2,1)} %all-gather.2.cloned.1.call-done, bf16[3584,2048]{1,0:T(8,128)(2,1)} %param.6), kind=kOutput, calls=%fused_computation.6 | convolution fusion | flops 7516192768 | bytes 22544384 | tf_op jit(solution)/shard_map/dot_general | solution.py:53
  137.0 0.0 copy-start
  137.0 0.0 reduce-scatter.2.cloned.1.call-update
  137.0 50.2 %reduce-scatter.2.cloned.1.call-done = f32[64,2048]{1,0:T(8,128)} async-done(((f32[512,2048]{1,0:T(8,128)}), f32[64,2048]{1,0:T(8,128)}) %reduce-scatter.2.cloned.1.call-update) | async-done | bytes 524304 | tf_op jit(solution)/shard_map/reduce_scatter | solution.py:58
  187.2 0.0 copy-done
  187.2 1.8 multiply_convert_fusion
Async XLA Ops:
  6.5 117.1 %all-gather.2.cloned.1.call-start = ((), (), s32[]{:S(2)}) async-start(), calls=%async_computation.3 | async-start | bytes 4587520 | tf_op jit(solution)/shard_map/all_gather | solution.py:54
  36.6 10.7 %copy-start.1 = (f32[8,8,1]{0,1,2:T(8,128)S(1)}, f32[8,8,1]{0,1,2:T(8,128)}, u32[]{:S(2)}) copy-start(f32[8,8,1]{0,1,2:T(8,128)} %constant.9) | copy-start | bytes 772
  76.2 111.0 %reduce-scatter.2.cloned.1.call-start = ((), (), s32[]{:S(2)}) async-start(), calls=%async_computation.4 | async-start | bytes 4718592 | tf_op jit(solution)/shard_map/reduce_scatter | solution.py:58
  137.0 50.2 %copy-start = (f32[2048]{0:T(1024)S(1)}, f32[2048]{0:T(1024)}, u32[]{:S(2)}) copy-start(f32[2048]{0:T(1024)} %param.7) | copy-start | bytes 24580
Sparse Core Ops, SparseCore 0:
  76.3 47.2 all-gather.1
  137.1 49.9 reduce-scatter.1
where the time goes:
time: 196 us
  waiting for transfers between devices  97.6 us (50%)
  blocking collectives  57 us (29%)
  matrix products  25.7 us (13%)
  between operations  13.4 us (7%)
    reduce_scatter x1, waiting for transfers between devices, shards(): lax.psum_scatter(partial_terms, 'tp', scatter_dimension=0, tiled=True)  50.2 us
    all_gather x1, waiting for transfers between devices, shards(): lax.all_gather(rotated, 'seq', axis=0, tiled=True)  47.4 us
    all_to_all x1, blocking collectives, shards(): lax.all_to_all(hidden, 'tp', split_axis=0, concat_axis=1, tiled=True)  30.1 us
    all_to_all x1, blocking collectives, shards(): lax.all_to_all(turned, 'tp', split_axis=1, concat_axis=0, tiled=True)  26.9 us
    dot_general x1, matrix products, shards(): jnp.dot(lax.all_gather(rotated, 'seq', axis=0, tiled=True), down_weight,...  13.4 us
    dot_general x1, matrix products, shards(): jnp.einsum('rtl,lm->rtm', blocks, local_table, preferred_element_type=jnp...  10.7 us
  transfers between devices with their start and end apart: 2, of which 2 were waited for; matrix products, arithmetic and copies ran while one was open for 0% of the time, Pallas kernels for 0%

commit v1 on v0

--- a/solution.py
+++ b/solution.py
@@ -7,6 +7,7 @@
 from jax.sharding import PartitionSpec as P
 
 PALEY = 28
+INNER = 32
 
 
 def paley_table():
@@ -36,27 +37,33 @@
     return signs
 
 
+def rotate(spread):
+    rows, total_units = spread.shape
+    walsh = total_units // PALEY
+    outer_order = walsh // INNER
+    width = INNER * PALEY
+    inner_table = jnp.asarray(np.kron(walsh_table(INNER), paley_table()), jnp.bfloat16)
+    outer_table = jnp.asarray(walsh_table(outer_order), jnp.float32)
+    blocks = spread.reshape(rows, outer_order, width)
+    inner = jnp.einsum("rbl,lm->rbm", blocks, inner_table, preferred_element_type=jnp.float32)
+    outer = jnp.einsum("rbm,bc->rcm", inner, outer_table, precision=lax.Precision.HIGHEST)
+    factor = 1.0 / math.sqrt(total_units)
+    return (outer * factor).astype(jnp.bfloat16).reshape(rows, total_units)
+
+
 def shards(hidden, down_weight, channel_scale):
-    tp_count = lax.axis_size("tp")
-    units = hidden.shape[1]
-    total_units = units * tp_count
-    local_table = jnp.asarray(np.kron(walsh_table(units // PALEY), paley_table()), jnp.bfloat16)
-    factor = 1.0 / math.sqrt(total_units)
     spread = lax.all_to_all(hidden, "tp", split_axis=0, concat_axis=1, tiled=True)
-    few_rows = spread.shape[0]
-    blocks = spread.reshape(few_rows, tp_count, units)
-    inner = jnp.einsum("rtl,lm->rtm", blocks, local_table, preferred_element_type=jnp.float32)
-    cross_table = jnp.asarray(walsh_table(tp_count), jnp.float32)
-    outer = jnp.einsum("rtm,tu->rum", inner, cross_table, precision=lax.Precision.HIGHEST)
-    turned = (outer * factor).astype(jnp.bfloat16).reshape(few_rows, total_units)
+    turned = rotate(spread)
     rotated = lax.all_to_all(turned, "tp", split_axis=1, concat_axis=0, tiled=True)
     partial_terms = jnp.dot(
         lax.all_gather(rotated, "seq", axis=0, tiled=True),
         down_weight,
         preferred_element_type=jnp.float32,
     )
-    summed = lax.psum_scatter(partial_terms, "tp", scatter_dimension=0, tiled=True)
-    return (summed * channel_scale[None, :]).astype(jnp.bfloat16)
+    summed = lax.psum_scatter(
+        partial_terms.astype(jnp.bfloat16), "tp", scatter_dimension=0, tiled=True
+    )
+    return (summed.astype(jnp.float32) * channel_scale[None, :]).astype(jnp.bfloat16)
 
 
 def solution(mesh):

time: 196 us -> 174 us (0.89)
  waiting for transfers between devices: 97.6 us -> 83.3 us
  matrix products: 25.7 us -> 16 us
    reduce_scatter x1, waiting for transfers between devices: 50.2 us -> 36 us  [shards(): lax.psum_scatter(partial_terms.astype(jnp.bfloat16), 'tp', scatter_dimens...]
    dot_general x2, matrix products: 12.3 us -> 2.94 us  [the longest x1 1.72 us: rotate(): jnp.einsum('rbm,bc->rcm', inner, outer_table, precision=lax.Precision.HIG...]
where the time goes in v1:
time: 174 us
  waiting for transfers between devices  83.3 us (48%)
  blocking collectives  57 us (33%)
  matrix products  16 us (9%)
  between operations  13.5 us (8%)
  local copies, waits for them, and re-layouts  2.23 us (1%)
    all_gather x1, waiting for transfers between devices, shards(): lax.all_gather(rotated, 'seq', axis=0, tiled=True)  47.3 us
    reduce_scatter x1, waiting for transfers between devices, shards(): lax.psum_scatter(partial_terms.astype(jnp.bfloat16), 'tp', scatter_dimens...  36 us
    all_to_all x1, blocking collectives, shards(): lax.all_to_all(hidden, 'tp', split_axis=0, concat_axis=1, tiled=True)  30.1 us
    all_to_all x1, blocking collectives, shards(): lax.all_to_all(turned, 'tp', split_axis=1, concat_axis=0, tiled=True)  26.9 us
    dot_general x1, matrix products, shards(): jnp.dot(lax.all_gather(rotated, 'seq', axis=0, tiled=True), down_weight,...  13.1 us
  transfers between devices with their start and end apart: 2, of which 2 were waited for; matrix products, arithmetic and copies ran while one was open for 0% of the time, Pallas kernels for 0%

profile of v1, /device:TPU:0, one launch (start us, length us, event | category | flops | bytes accessed | tf_op | source)
XLA Modules:
  0.0 173.8 jit_solution(6805328041319989861)
XLA Ops:
  6.5 0.0 all-gather.2.cloned.1.call-start
  6.5 30.1 %all_to_all.35 = bf16[8,16,3584]{2,1,0:T(8,128)(2,1)S(1)} all-to-all(bf16[8,16,3584]{2,1,0:T(8,128)(2,1)} %bitcast.23), channel_id=1, replica_groups=mesh['seq'=4,'tp'=8] {'tp'}, dimensions={0} | all-to-all | bytes 1835008 | tf_op jit(solution)/shard_map/all_to_all | solution.py:55
  36.6 0.0 copy-start.2
  36.6 0.5 copy.8
  37.2 0.5 reshape.13
  37.7 0.4 copy-done.2
  38.1 0.0 copy-start
  38.1 1.2 fusion.7
  39.3 0.0 copy-done
  39.3 1.7 fusion.4
  41.0 0.5 all_to_all.29
  41.6 0.3 copy.9
  41.9 26.9 %all_to_all.36 = bf16[16,8,3584]{2,0,1:T(8,128)(2,1)} all-to-all(bf16[16,8,3584]{2,0,1:T(8,128)(2,1)S(1)} %copy.9), channel_id=1, replica_groups=mesh['seq'=4,'tp'=8] {'tp'}, dimensions={1} | all-to-all | bytes 1835008 | tf_op jit(solution)/shard_map/all_to_all | solution.py:57
  68.8 0.0 all-gather.2.cloned.1.call-update
  68.8 0.0 reduce-scatter.2.cloned.1.call-start
  68.8 47.3 %all-gather.2.cloned.1.call-done = bf16[512,3584]{1,0:T(8,128)(2,1)} async-done(((bf16[128,3584]{1,0:T(8,128)(2,1)}), bf16[512,3584]{1,0:T(8,128)(2,1)}) %all-gather.2.cloned.1.call-update) | async-done | bytes 3670032 | tf_op jit(solution)/shard_map/all_gather | solution.py:59
  116.2 13.1 %convolution_convert_fusion = bf16[512,2048]{1,0:T(8,128)(2,1)} fusion(bf16[512,3584]{1,0:T(8,128)(2,1)} %all-gather.2.cloned.1.call-done, bf16[3584,2048]{1,0:T(8,128)(2,1)} %param.6), kind=kOutput, calls=%fused_computation | convolution fusion | flops 7517241344 | bytes 20447232 | tf_op jit(solution)/shard_map/dot_general | solution.py:58
  129.2 0.0 copy-start.1
  129.2 0.0 reduce-scatter.2.cloned.1.call-update
  129.3 36.0 %reduce-scatter.2.cloned.1.call-done = bf16[64,2048]{1,0:T(8,128)(2,1)} async-done(((bf16[512,2048]{1,0:T(8,128)(2,1)}), bf16[64,2048]{1,0:T(8,128)(2,1)}) %reduce-scatter.2.cloned.1.call-update) | async-done | bytes 262160 | tf_op jit(solution)/shard_map/reduce_scatter | solution.py:63
  165.2 0.0 copy-done.1
  165.2 1.7 multiply_convert_fusion.1
Async XLA Ops:
  6.5 109.6 %all-gather.2.cloned.1.call-start = ((), (), s32[]{:S(2)}) async-start(), calls=%async_computation.3 | async-start | bytes 4587520 | tf_op jit(solution)/shard_map/all_gather | solution.py:59
  36.6 1.4 copy-start.2
  38.1 1.2 copy-start
  68.8 96.4 %reduce-scatter.2.cloned.1.call-start = ((), (), s32[]{:S(2)}) async-start(), calls=%async_computation.4 | async-start | bytes 2359296 | tf_op jit(solution)/shard_map/reduce_scatter | solution.py:63
  129.2 36.0 %copy-start.1 = (f32[2048]{0:T(1024)S(1)}, f32[2048]{0:T(1024)}, u32[]{:S(2)}) copy-start(f32[2048]{0:T(1024)} %param.7) | copy-start | bytes 24580
Sparse Core Ops, SparseCore 0:
  68.9 47.2 all-gather.1
  129.4 35.7 reduce-scatter.1

commit v2 on v1

--- a/solution.py
+++ b/solution.py
@@ -8,6 +8,7 @@
 
 PALEY = 28
 INNER = 32
+CHUNKS = 2
 
 
 def paley_table():
@@ -52,18 +53,27 @@
 
 
 def shards(hidden, down_weight, channel_scale):
-    spread = lax.all_to_all(hidden, "tp", split_axis=0, concat_axis=1, tiled=True)
-    turned = rotate(spread)
-    rotated = lax.all_to_all(turned, "tp", split_axis=1, concat_axis=0, tiled=True)
-    partial_terms = jnp.dot(
-        lax.all_gather(rotated, "seq", axis=0, tiled=True),
-        down_weight,
-        preferred_element_type=jnp.float32,
-    )
-    summed = lax.psum_scatter(
-        partial_terms.astype(jnp.bfloat16), "tp", scatter_dimension=0, tiled=True
-    )
-    return (summed.astype(jnp.float32) * channel_scale[None, :]).astype(jnp.bfloat16)
+    seq_count = lax.axis_size("seq")
+    tp_count = lax.axis_size("tp")
+    tokens, units = hidden.shape
+    groups = tp_count // seq_count
+    owned = tokens // groups
+    piece = owned // CHUNKS
+    grouped = hidden.reshape(groups, CHUNKS, piece, units)
+    outputs = []
+    for chunk in range(CHUNKS):
+        part = grouped[:, chunk].reshape(groups * piece, units)
+        spread = lax.all_to_all(part, "tp", split_axis=0, concat_axis=1, tiled=True)
+        turned = rotate(spread)
+        rotated = lax.all_to_all(turned, "tp", split_axis=1, concat_axis=0, tiled=True)
+        partial_terms = jnp.dot(
+            lax.all_gather(rotated, "seq", axis=0, tiled=True),
+            down_weight,
+            preferred_element_type=jnp.float32,
+        )
+        outputs.append(lax.psum_scatter(partial_terms, "tp", scatter_dimension=0, tiled=True))
+    summed = jnp.concatenate(outputs, axis=0)
+    return (summed * channel_scale[None, :]).astype(jnp.bfloat16)
 
 
 def solution(mesh):

time: 174 us -> 199 us (1.14)
  blocking collectives: 57 us -> 70.6 us
  matrix products: 16 us -> 25.3 us
    reduce_scatter x1 -> x2, waiting for transfers between devices: 36 us -> 63.8 us  [shards(): lax.psum_scatter(partial_terms, 'tp', scatter_dimension=0, tiled=True)]
    all_gather x1 -> x2, waiting for transfers between devices: 47.3 us -> 20.8 us  [shards(): lax.all_gather(rotated, 'seq', axis=0, tiled=True)]
    dot_general x1 -> x2, matrix products: 13.1 us -> 22.1 us  [shards(): jnp.dot(lax.all_gather(rotated, 'seq', axis=0, tiled=True), down_weight,...]
    all_to_all x1 -> x2, blocking collectives: 26.9 us -> 34.1 us  [shards(): lax.all_to_all(turned, 'tp', split_axis=1, concat_axis=0, tiled=True)]
    all_to_all x1 -> x2, blocking collectives: 30.1 us -> 36.6 us  [shards(): spread = lax.all_to_all(part, 'tp', split_axis=0, concat_axis=1, tiled=True)]
  transfers between devices with their start and end apart: 2 -> 4, of which waited for: 2 -> 3; matrix products, arithmetic and copies ran while one was open for 0% -> 12% of each run, Pallas kernels for 0% -> 0%
where the time goes in v2:
time: 199 us
  waiting for transfers between devices  84.7 us (43%)
  blocking collectives  70.6 us (35%)
  matrix products  25.3 us (13%)
  between operations  13.2 us (7%)
  local copies, waits for them, and re-layouts  2.92 us (1%)
    reduce_scatter x2, waiting for transfers between devices, shards(): lax.psum_scatter(partial_terms, 'tp', scatter_dimension=0, tiled=True)  63.8 us
    all_to_all x2, blocking collectives, shards(): spread = lax.all_to_all(part, 'tp', split_axis=0, concat_axis=1, tiled=True)  36.6 us
    all_to_all x2, blocking collectives, shards(): lax.all_to_all(turned, 'tp', split_axis=1, concat_axis=0, tiled=True)  34.1 us
    dot_general x2, matrix products, shards(): jnp.dot(lax.all_gather(rotated, 'seq', axis=0, tiled=True), down_weight,...  22.1 us
    all_gather x2, waiting for transfers between devices, shards(): lax.all_gather(rotated, 'seq', axis=0, tiled=True)  20.8 us
  transfers between devices with their start and end apart: 4, of which 3 were waited for; matrix products, arithmetic and copies ran while one was open for 12% of the time, Pallas kernels for 0%

profile of v2, /device:TPU:0, one launch (start us, length us, event | category | flops | bytes accessed | tf_op | source)
XLA Modules:
  0.0 198.8 jit_solution(16339326473404441674)
XLA Ops:
  6.5 1.2 fusion.5
  7.8 20.2 %all_to_all.70 = bf16[8,8,3584]{2,1,0:T(8,128)(2,1)S(1)} all-to-all(bf16[8,8,3584]{2,1,0:T(8,128)(2,1)S(1)} %bitcast.34), channel_id=1, replica_groups=mesh['seq'=4,'tp'=8] {'tp'}, dimensions={0} | all-to-all | bytes 917504 | tf_op jit(solution)/shard_map/all_to_all | solution.py:66
  28.0 0.1 copy.14
  28.1 0.3 reshape.31
  28.4 0.7 convolution_bitcast_fusion.1
  29.1 0.0 copy-done
  29.1 0.9 fusion.3
  30.1 0.3 all_to_all.55
  30.3 0.1 copy.15
  30.5 17.0 %all_to_all.71 = bf16[8,8,3584]{2,0,1:T(8,128)(2,1)} all-to-all(bf16[8,8,3584]{2,0,1:T(8,128)(2,1)S(1)} %copy.15), channel_id=1, replica_groups=mesh['seq'=4,'tp'=8] {'tp'}, dimensions={1} | all-to-all | bytes 917504 | tf_op jit(solution)/shard_map/all_to_all | solution.py:68
  47.5 0.0 all-gather.3.cloned.1.call-update
  47.6 0.0 all-gather.5.cloned.1.call-start
  47.6 16.4 %all_to_all.72 = bf16[8,8,3584]{2,1,0:T(8,128)(2,1)S(1)} all-to-all(bf16[8,8,3584]{2,1,0:T(8,128)(2,1)S(1)} %bitcast.33), channel_id=1, replica_groups=mesh['seq'=4,'tp'=8] {'tp'}, dimensions={0} | all-to-all | bytes 917504 | tf_op jit(solution)/shard_map/all_to_all | solution.py:66
  64.0 0.1 copy.16
  64.1 0.3 reshape.32
  64.4 0.7 convolution_bitcast_fusion
  65.1 0.9 fusion.2
  66.0 0.3 all_to_all.62
  66.3 0.1 copy.17
  66.4 17.0 %all_to_all.73 = bf16[8,8,3584]{2,0,1:T(8,128)(2,1)} all-to-all(bf16[8,8,3584]{2,0,1:T(8,128)(2,1)S(1)} %copy.17), channel_id=1, replica_groups=mesh['seq'=4,'tp'=8] {'tp'}, dimensions={1} | all-to-all | bytes 917504 | tf_op jit(solution)/shard_map/all_to_all | solution.py:68
  83.5 0.0 all-gather.5.cloned.1.call-update
  83.5 0.0 reduce-scatter.3.cloned.1.call-start
  83.5 0.0 all-gather.3.cloned.1.call-done
  83.6 11.1 %fusion.6 = f32[256,2048]{1,0:T(8,128)} fusion(bf16[256,3584]{1,0:T(8,128)(2,1)} %all-gather.3.cloned.1.call-done, bf16[3584,2048]{1,0:T(8,128)(2,1)} %param.8), kind=kOutput, calls=%fused_computation.11 | convolution fusion | flops 3758096384 | bytes 18612224 | tf_op jit(solution)/shard_map/dot_general | solution.py:69
  94.6 0.0 reduce-scatter.3.cloned.1.call-update
  94.7 0.2 reduce-scatter.5.cloned.1.call-start
  94.9 20.8 %all-gather.5.cloned.1.call-done = bf16[256,3584]{1,0:T(8,128)(2,1)} async-done(((bf16[64,3584]{1,0:T(8,128)(2,1)}), bf16[256,3584]{1,0:T(8,128)(2,1)}) %all-gather.5.cloned.1.call-update) | async-done | bytes 1835024 | tf_op jit(solution)/shard_map/all_gather | solution.py:70
  115.7 11.0 %fusion.7 = f32[256,2048]{1,0:T(8,128)} fusion(bf16[256,3584]{1,0:T(8,128)(2,1)} %all-gather.5.cloned.1.call-done, bf16[3584,2048]{1,0:T(8,128)(2,1)} %param.8), kind=kOutput, calls=%fused_computation.12 | convolution fusion | flops 3758096384 | bytes 18612224 | tf_op jit(solution)/shard_map/dot_general | solution.py:69
  126.7 0.0 reduce-scatter.5.cloned.1.call-update
  126.7 27.1 %reduce-scatter.3.cloned.1.call-done = f32[32,2048]{1,0:T(8,128)} async-done(((f32[256,2048]{1,0:T(8,128)}), f32[32,2048]{1,0:T(8,128)}) %reduce-scatter.3.cloned.1.call-update) | async-done | bytes 262160 | tf_op jit(solution)/shard_map/reduce_scatter | solution.py:74
  153.8 36.7 %reduce-scatter.5.cloned.1.call-done = f32[32,2048]{1,0:T(8,128)} async-done(((f32[256,2048]{1,0:T(8,128)}), f32[32,2048]{1,0:T(8,128)}) %reduce-scatter.5.cloned.1.call-update) | async-done | bytes 262160 | tf_op jit(solution)/shard_map/reduce_scatter | solution.py:74
  190.5 1.8 fusion.4
  (6 shorter events, 0.0 us)
Async XLA Ops:
  6.5 77.0 %all-gather.3.cloned.1.call-start = ((), (), s32[]{:S(2)}) async-start(), calls=%async_computation.6 | async-start | bytes 2293760 | tf_op jit(solution)/shard_map/all_gather | solution.py:70
  7.8 20.7 %copy-start.2 = (bf16[896,896,1]{1,0,2:T(8,128)(2,1)S(1)}, bf16[896,896,1]{1,0,2:T(8,128)(2,1)}, u32[]{:S(2)}) copy-start(bf16[896,896,1]{1,0,2:T(8,128)(2,1)} %constant.8) | copy-start | bytes 4816900
  28.4 0.7 copy-start
  47.6 68.1 %all-gather.5.cloned.1.call-start = ((), (), s32[]{:S(2)}) async-start(), calls=%async_computation.8 | async-start | bytes 2293760 | tf_op jit(solution)/shard_map/all_gather | solution.py:70
  83.5 70.3 %reduce-scatter.3.cloned.1.call-start = ((), (), s32[]{:S(2)}) async-start(), calls=%async_computation.7 | async-start | bytes 2359296 | tf_op jit(solution)/shard_map/reduce_scatter | solution.py:74
  94.7 95.9 %reduce-scatter.5.cloned.1.call-start = ((), (), s32[]{:S(2)}) async-start(), calls=%async_computation.9 | async-start | bytes 2359296 | tf_op jit(solution)/shard_map/reduce_scatter | solution.py:74
  126.7 63.8 %copy-start.1 = (f32[2048]{0:T(1024)S(1)}, f32[2048]{0:T(1024)}, u32[]{:S(2)}) copy-start(f32[2048]{0:T(1024)} %param.9) | copy-start | bytes 24580
Sparse Core Ops, SparseCore 0:
  47.7 32.0 all-gather.2
  83.6 32.0 all-gather.4
  118.0 35.7 reduce-scatter.2
  156.0 34.5 reduce-scatter.4

commit v3 on v2

--- a/solution.py
+++ b/solution.py
@@ -8,7 +8,7 @@
 
 PALEY = 28
 INNER = 32
-CHUNKS = 2
+CHUNKS = 1
 
 
 def paley_table():
@@ -52,6 +52,25 @@
     return (outer * factor).astype(jnp.bfloat16).reshape(rows, total_units)
 
 
+def gather_seq(block):
+    seq_count = lax.axis_size("seq")
+    if seq_count != 4:
+        return lax.all_gather(block, "seq", axis=0, tiled=True)
+    rows = block.shape[0]
+    half = rows // 2
+    across_x = lax.ppermute(block, "seq", [(s, s ^ 1) for s in range(4)])
+    across_y = lax.ppermute(block, "seq", [(s, s ^ 2) for s in range(4)])
+    first = lax.ppermute(across_y[:half], "seq", [(s, s ^ 1) for s in range(4)])
+    second = lax.ppermute(across_x[half:], "seq", [(s, s ^ 2) for s in range(4)])
+    diagonal = jnp.concatenate([first, second], axis=0)
+    stacked = jnp.stack([block, across_x, across_y, diagonal])
+    me = lax.axis_index("seq")
+    return jnp.concatenate(
+        [lax.dynamic_index_in_dim(stacked, me ^ other, 0, keepdims=False) for other in range(4)],
+        axis=0,
+    )
+
+
 def shards(hidden, down_weight, channel_scale):
     seq_count = lax.axis_size("seq")
     tp_count = lax.axis_size("tp")
@@ -67,9 +86,7 @@
         turned = rotate(spread)
         rotated = lax.all_to_all(turned, "tp", split_axis=1, concat_axis=0, tiled=True)
         partial_terms = jnp.dot(
-            lax.all_gather(rotated, "seq", axis=0, tiled=True),
-            down_weight,
-            preferred_element_type=jnp.float32,
+            gather_seq(rotated), down_weight, preferred_element_type=jnp.float32
         )
         outputs.append(lax.psum_scatter(partial_terms, "tp", scatter_dimension=0, tiled=True))
     summed = jnp.concatenate(outputs, axis=0)

time: 199 us -> 177 us (0.89)
  blocking collectives: 70.6 us -> 56.4 us
  matrix products: 25.3 us -> 15.7 us
  waiting for transfers between devices: 84.7 us -> 77.6 us
  starting transfers between devices: 0.31 us -> 6.02 us
    ppermute x0 -> x4, waiting for transfers between devices: none -> 28.6 us  [the longest x1 18.9 us: gather_seq(): across_y = lax.ppermute(block, 'seq', [(s, s ^ 2) for s in range(4)])]
    all_gather x2 -> x0, waiting for transfers between devices: 20.8 us -> none  [shards(): lax.all_gather(rotated, 'seq', axis=0, tiled=True)]
    reduce_scatter x2 -> x1, waiting for transfers between devices: 63.8 us -> 49 us  [shards(): lax.psum_scatter(partial_terms, 'tp', scatter_dimension=0, tiled=True)]
    dot_general x2 -> x1, matrix products: 22.1 us -> 12.7 us  [shards(): jnp.dot(gather_seq(rotated), down_weight, preferred_element_type=jnp.floa...]
    all_to_all x2 -> x1, blocking collectives: 34.1 us -> 26.2 us  [shards(): lax.all_to_all(turned, 'tp', split_axis=1, concat_axis=0, tiled=True)]
    all_to_all x2 -> x1, blocking collectives: 36.6 us -> 30.2 us  [shards(): spread = lax.all_to_all(part, 'tp', split_axis=0, concat_axis=1, tiled=True)]
    ppermute x0 -> x4, starting transfers between devices: none -> 6.02 us  [the longest x1 1.52 us: gather_seq(): across_y = lax.ppermute(block, 'seq', [(s, s ^ 2) for s in range(4)])]
  transfers between devices with their start and end apart: 4 -> 5, of which waited for: 3 -> 4; matrix products, arithmetic and copies ran while one was open for 12% -> 1% of each run, Pallas kernels for 0% -> 0%
where the time goes in v3:
time: 177 us; the launch traced here: 176 us
  waiting for transfers between devices  77.6 us (44%)
  blocking collectives  56.4 us (32%)
  matrix products  15.7 us (9%)
  between operations  13.5 us (8%)
  starting transfers between devices  6.02 us (3%)
  local copies, waits for them, and re-layouts  3.76 us (2%)
  other arithmetic  3.37 us (2%)
    reduce_scatter x1, waiting for transfers between devices, shards(): lax.psum_scatter(partial_terms, 'tp', scatter_dimension=0, tiled=True)  49 us
    all_to_all x1, blocking collectives, shards(): spread = lax.all_to_all(part, 'tp', split_axis=0, concat_axis=1, tiled=True)  30.2 us
    all_to_all x1, blocking collectives, shards(): lax.all_to_all(turned, 'tp', split_axis=1, concat_axis=0, tiled=True)  26.2 us
    ppermute x1, waiting for transfers between devices, gather_seq(): across_y = lax.ppermute(block, 'seq', [(s, s ^ 2) for s in range(4)])  18.9 us
    dot_general x1, matrix products, shards(): jnp.dot(gather_seq(rotated), down_weight, preferred_element_type=jnp.floa...  12.7 us
    ppermute x1, waiting for transfers between devices, gather_seq(): first = lax.ppermute(across_y[:half], 'seq', [(s, s ^ 1) for s in range(4)])  7.56 us
  transfers between devices with their start and end apart: 5, of which 4 were waited for; matrix products, arithmetic and copies ran while one was open for 1% of the time, Pallas kernels for 0%

profile of v3, /device:TPU:0, one launch (start us, length us, event | category | flops | bytes accessed | tf_op | source)
XLA Modules:
  0.0 176.3 jit_solution(6206235974202936580)
XLA Ops:
  6.5 0.0 copy-start.2
  6.5 0.0 reduce-scatter.2.cloned.1.call-start
  6.5 30.2 %all_to_all.35 = bf16[8,16,3584]{2,1,0:T(8,128)(2,1)S(1)} all-to-all(bf16[8,16,3584]{2,1,0:T(8,128)(2,1)} %bitcast.40), channel_id=1, replica_groups=mesh['seq'=4,'tp'=8] {'tp'}, dimensions={0} | all-to-all | bytes 1835008 | tf_op jit(solution)/shard_map/all_to_all | solution.py:85
  36.8 0.5 copy.8
  37.3 0.5 reshape.14
  37.8 0.0 copy-done.2
  37.9 0.0 copy-start
  37.9 1.2 fusion.16
  39.1 0.0 copy-done
  39.1 1.7 fusion.12
  40.8 0.5 all_to_all.29
  41.4 0.3 copy.9
  41.7 26.2 %all_to_all.36 = bf16[16,8,3584]{2,0,1:T(8,128)(2,1)S(1)} all-to-all(bf16[16,8,3584]{2,0,1:T(8,128)(2,1)S(1)} %copy.9), channel_id=1, replica_groups=mesh['seq'=4,'tp'=8] {'tp'}, dimensions={1} | all-to-all | bytes 1835008 | tf_op jit(solution)/shard_map/all_to_all | solution.py:87
  67.8 1.5 collective-permute-start.1
  69.4 1.5 collective-permute-start
  70.9 18.9 %collective-permute-done.1 = bf16[128,3584]{1,0:T(8,128)(2,1)S(1)} collective-permute-done((bf16[128,3584]{1,0:T(8,128)(2,1)S(1)}, bf16[128,3584]{1,0:T(8,128)(2,1)S(1)}, u32[]{:S(2)}, u32[]{:S(2)}) %collective-permute-start.1) | collective-permute-done | bytes 917536 | tf_op jit(solution)/shard_map/ppermute | solution.py:62
  89.8 0.8 slice.8
  90.6 1.5 collective-permute-start.2
  92.1 0.0 collective-permute-done
  92.1 0.8 slice.9
  92.9 1.5 collective-permute-start.3
  94.4 7.6 %collective-permute-done.2 = bf16[64,3584]{1,0:T(8,128)(2,1)S(1)} collective-permute-done((bf16[64,3584]{1,0:T(8,128)(2,1)}, bf16[64,3584]{1,0:T(8,128)(2,1)S(1)}, u32[]{:S(2)}, u32[]{:S(2)}) %collective-permute-start.2) | collective-permute-done | bytes 458784 | tf_op jit(solution)/shard_map/ppermute | solution.py:63
  102.0 2.1 %collective-permute-done.3 = bf16[64,3584]{1,0:T(8,128)(2,1)} collective-permute-done((bf16[64,3584]{1,0:T(8,128)(2,1)}, bf16[64,3584]{1,0:T(8,128)(2,1)}, u32[]{:S(2)}, u32[]{:S(2)}) %collective-permute-start.3) | collective-permute-done | bytes 458784 | tf_op jit(solution)/shard_map/ppermute | solution.py:64
  104.1 1.1 maximum_bitcast_fusion
  105.2 0.5 pad_maximum_fusion
  105.7 0.2 dynamic-slice_bitcast_fusion.3
  105.9 12.7 %fusion = f32[512,2048]{1,0:T(8,128)} fusion(bf16[3584,2048]{1,0:T(8,128)(2,1)} %param.6, bf16[128,3584]{1,0:T(8,128)(2,1)S(1)} %get-tuple-element.6, bf16[128,3584]{1,0:T(8,128)(2,1)S(1)} %get-tuple-element.7, bf16[128,3584]{1,0:T(8,128)(2,1)S(1)} %get-tuple-element.8, bf16[128,3584]{1,0:T(8,128)(2,1)S(1)} %get-tuple-element.5), kind=kOutput, calls=%fused_computation.1 | convolution fusion | flops 7530872832 | bytes 22544384 | tf_op jit(solution)/shard_map/dot_general | solution.py:88
  118.6 0.0 copy-start.1
  118.6 0.0 reduce-scatter.2.cloned.1.call-update
  118.7 49.0 %reduce-scatter.2.cloned.1.call-done = f32[64,2048]{1,0:T(8,128)} async-done(((f32[512,2048]{1,0:T(8,128)}), f32[64,2048]{1,0:T(8,128)}) %reduce-scatter.2.cloned.1.call-update) | async-done | bytes 524304 | tf_op jit(solution)/shard_map/reduce_scatter | solution.py:91
  167.7 0.0 copy-done.1
  167.7 1.8 %multiply_convert_fusion.1 = bf16[64,2048]{1,0:T(8,128)(2,1)} fusion(f32[64,2048]{1,0:T(8,128)} %reduce-scatter.2.cloned.1.call-done, f32[2048]{0:T(1024)S(1)} %copy-done.1), kind=kLoop, calls=%fused_computation.18 | loop fusion | flops 262144 | bytes 794624 | tf_op jit(solution)/shard_map/convert_element_type | solution.py:93
Async XLA Ops:
  6.5 31.3 %copy-start.2 = (bf16[896,896,1]{1,0,2:T(8,128)(2,1)S(1)}, bf16[896,896,1]{1,0,2:T(8,128)(2,1)}, u32[]{:S(2)}) copy-start(bf16[896,896,1]{1,0,2:T(8,128)(2,1)} %constant.31) | copy-start | bytes 4816900
  6.5 161.2 %reduce-scatter.2.cloned.1.call-start = ((), (), s32[]{:S(2)}) async-start(), calls=%async_computation.3 | async-start | bytes 4718592 | tf_op jit(solution)/shard_map/reduce_scatter | solution.py:91
  37.9 1.2 copy-start
  67.8 21.9 %collective-permute-start.1 = (bf16[128,3584]{1,0:T(8,128)(2,1)S(1)}, bf16[128,3584]{1,0:T(8,128)(2,1)S(1)}, u32[]{:S(2)}, u32[]{:S(2)}) collective-permute-start(bf16[128,3584]{1,0:T(8,128)(2,1)S(1)} %bitcast.34), channel_id=1, source_target_pairs={{0,16},{8,24},{16,0},{24,8},{1,17},{9,25},{17,1},{25,9},{2,18},{10... | collective-permute-start | bytes 2752520 | tf_op jit(solution)/shard_map/ppermute | solution.py:62
  69.4 22.7 %collective-permute-start = (bf16[128,3584]{1,0:T(8,128)(2,1)S(1)}, bf16[128,3584]{1,0:T(8,128)(2,1)S(1)}, u32[]{:S(2)}, u32[]{:S(2)}) collective-permute-start(bf16[128,3584]{1,0:T(8,128)(2,1)S(1)} %bitcast.35), channel_id=1, source_target_pairs={{0,8},{8,0},{16,24},{24,16},{1,9},{9,1},{17,25},{25,17},{2,10},{10... | collective-permute-start | bytes 2752520 | tf_op jit(solution)/shard_map/ppermute | solution.py:61
  90.6 11.4 %collective-permute-start.2 = (bf16[64,3584]{1,0:T(8,128)(2,1)}, bf16[64,3584]{1,0:T(8,128)(2,1)S(1)}, u32[]{:S(2)}, u32[]{:S(2)}) collective-permute-start(bf16[64,3584]{1,0:T(8,128)(2,1)} %slice.8), channel_id=1, source_target_pairs={{0,8},{8,0},{16,24},{24,16},{1,9},{9,1},{17,25},{25,17},{2,10},{10... | collective-permute-start | bytes 1376264 | tf_op jit(solution)/shard_map/ppermute | solution.py:63
  92.9 11.2 %collective-permute-start.3 = (bf16[64,3584]{1,0:T(8,128)(2,1)}, bf16[64,3584]{1,0:T(8,128)(2,1)}, u32[]{:S(2)}, u32[]{:S(2)}) collective-permute-start(bf16[64,3584]{1,0:T(8,128)(2,1)} %slice.9), channel_id=1, source_target_pairs={{0,16},{8,24},{16,0},{24,8},{1,17},{9,25},{17,1},{25,9},{2,18},{10... | collective-permute-start | bytes 1376264 | tf_op jit(solution)/shard_map/ppermute | solution.py:64
  118.6 49.0 %copy-start.1 = (f32[2048]{0:T(1024)S(1)}, f32[2048]{0:T(1024)}, u32[]{:S(2)}) copy-start(f32[2048]{0:T(1024)} %param.7) | copy-start | bytes 24580
Sparse Core Ops, SparseCore 0:
  118.8 48.8 reduce-scatter.1

commit v4 on v3

--- a/solution.py
+++ b/solution.py
@@ -52,10 +52,11 @@
     return (outer * factor).astype(jnp.bfloat16).reshape(rows, total_units)
 
 
-def gather_seq(block):
+def gathered_product(block, down_weight):
     seq_count = lax.axis_size("seq")
     if seq_count != 4:
-        return lax.all_gather(block, "seq", axis=0, tiled=True)
+        gathered = lax.all_gather(block, "seq", axis=0, tiled=True)
+        return jnp.dot(gathered, down_weight, preferred_element_type=jnp.float32)
     rows = block.shape[0]
     half = rows // 2
     across_x = lax.ppermute(block, "seq", [(s, s ^ 1) for s in range(4)])
@@ -63,12 +64,13 @@
     first = lax.ppermute(across_y[:half], "seq", [(s, s ^ 1) for s in range(4)])
     second = lax.ppermute(across_x[half:], "seq", [(s, s ^ 2) for s in range(4)])
     diagonal = jnp.concatenate([first, second], axis=0)
-    stacked = jnp.stack([block, across_x, across_y, diagonal])
     me = lax.axis_index("seq")
-    return jnp.concatenate(
-        [lax.dynamic_index_in_dim(stacked, me ^ other, 0, keepdims=False) for other in range(4)],
-        axis=0,
-    )
+    columns = down_weight.shape[1]
+    result = jnp.zeros((4 * rows, columns), jnp.float32)
+    for other, piece in enumerate((block, across_x, across_y, diagonal)):
+        product = jnp.dot(piece, down_weight, preferred_element_type=jnp.float32)
+        result = lax.dynamic_update_slice_in_dim(result, product, (me ^ other) * rows, 0)
+    return result
 
 
 def shards(hidden, down_weight, channel_scale):
@@ -85,9 +87,7 @@
         spread = lax.all_to_all(part, "tp", split_axis=0, concat_axis=1, tiled=True)
         turned = rotate(spread)
         rotated = lax.all_to_all(turned, "tp", split_axis=1, concat_axis=0, tiled=True)
-        partial_terms = jnp.dot(
-            gather_seq(rotated), down_weight, preferred_element_type=jnp.float32
-        )
+        partial_terms = gathered_product(rotated, down_weight)
         outputs.append(lax.psum_scatter(partial_terms, "tp", scatter_dimension=0, tiled=True))
     summed = jnp.concatenate(outputs, axis=0)
     return (summed * channel_scale[None, :]).astype(jnp.bfloat16)

time: 177 us -> 163 us (0.921)
  waiting for transfers between devices: 77.6 us -> 59.6 us
  matrix products: 15.7 us -> 21.2 us
    ppermute x4, waiting for transfers between devices: 28.6 us -> 10.5 us  [the longest x1 7.87 us: gathered_product(): across_y = lax.ppermute(block, 'seq', [(s, s ^ 2) for s in range(4)])]
    dot_general x1 -> x4, matrix products: 12.7 us -> 18.3 us  [gathered_product(): product = jnp.dot(piece, down_weight, preferred_element_type=jnp.float32)]
    broadcast_in_dim x0 -> x1, local copies, waits for them, and re-layouts: none -> 2.65 us  [gathered_product(): result = jnp.zeros((4 * rows, columns), jnp.float32)]
  transfers between devices with their start and end apart: 5 -> 5, of which waited for: 4 -> 4; matrix products, arithmetic and copies ran while one was open for 1% -> 11% of each run, Pallas kernels for 0% -> 0%
where the time goes in v4:
time: 163 us
  waiting for transfers between devices  59.6 us (37%)
  blocking collectives  56.4 us (35%)
  matrix products  21.2 us (13%)
  between operations  13.5 us (8%)
  starting transfers between devices  6.15 us (4%)
  local copies, waits for them, and re-layouts  4.61 us (3%)
  other arithmetic  1.78 us (1%)
    reduce_scatter x1, waiting for transfers between devices, shards(): lax.psum_scatter(partial_terms, 'tp', scatter_dimension=0, tiled=True)  49 us
    all_to_all x1, blocking collectives, shards(): spread = lax.all_to_all(part, 'tp', split_axis=0, concat_axis=1, tiled=True)  30.2 us
    all_to_all x1, blocking collectives, shards(): lax.all_to_all(turned, 'tp', split_axis=1, concat_axis=0, tiled=True)  26.2 us
    dot_general x4, matrix products, gathered_product(): product = jnp.dot(piece, down_weight, preferred_element_type=jnp.float32)  18.3 us
    ppermute x1, waiting for transfers between devices, gathered_product(): across_y = lax.ppermute(block, 'seq', [(s, s ^ 2) for s in range(4)])  7.87 us
  transfers between devices with their start and end apart: 5, of which 4 were waited for; matrix products, arithmetic and copies ran while one was open for 11% of the time, Pallas kernels for 0%

profile of v4, /device:TPU:0, one launch (start us, length us, event | category | flops | bytes accessed | tf_op | source)
XLA Modules:
  0.0 163.2 jit_solution(8616967100131408873)
XLA Ops:
  6.5 0.0 reduce-scatter.2.cloned.1.call-start
  6.5 30.2 %all_to_all.35 = bf16[8,16,3584]{2,1,0:T(8,128)(2,1)S(1)} all-to-all(bf16[8,16,3584]{2,1,0:T(8,128)(2,1)} %bitcast.32), channel_id=1, replica_groups=mesh['seq'=4,'tp'=8] {'tp'}, dimensions={0} | all-to-all | bytes 1835008 | tf_op jit(solution)/shard_map/all_to_all | solution.py:87
  36.8 0.5 copy.8
  37.3 0.5 reshape.13
  37.8 0.0 copy-done.2
  37.9 0.0 copy-start
  37.9 1.2 fusion.11
  39.1 0.0 copy-done
  39.1 1.7 %fusion.4 = bf16[16,32,896]{2,1,0:T(8,128)(2,1)S(1)} fusion(f32[32,32,1]{0,1,2:T(8,128)S(1)} %copy-done, f32[896,16,32]{0,2,1:T(8,128)S(1)} %fusion.11), kind=kOutput, calls=%fused_computation.7 | convolution fusion | flops 177078272 | bytes 2756608 | tf_op jit(solution)/shard_map/rbm,bc->rcm/dot_general | solution.py:50
  40.8 0.5 all_to_all.29
  41.4 0.3 copy.9
  41.7 26.2 %all_to_all.36 = bf16[16,8,3584]{2,0,1:T(8,128)(2,1)S(1)} all-to-all(bf16[16,8,3584]{2,0,1:T(8,128)(2,1)S(1)} %copy.9), channel_id=1, replica_groups=mesh['seq'=4,'tp'=8] {'tp'}, dimensions={1} | all-to-all | bytes 1835008 | tf_op jit(solution)/shard_map/all_to_all | solution.py:89
  67.9 1.5 collective-permute-start.1
  69.4 1.5 collective-permute-start
  70.9 2.6 %broadcast_in_dim.4 = f32[512,2048]{1,0:T(8,128)} broadcast(f32[]{:T(128)} %constant.11.clone.1), dimensions={} | broadcast | bytes 4194308 | tf_op jit(solution)/shard_map/broadcast_in_dim | solution.py:69
  73.5 8.4 %convolution_dynamic-update-slice_fusion.3 = f32[512,2048]{1,0:T(8,128)} fusion(f32[512,2048]{1,0:T(8,128)} %broadcast_in_dim.4, s32[]{:T(128)S(6)} %select_n.12, bf16[128,3584]{1,0:T(8,128)(2,1)S(1)} %bitcast.30, bf16[3584,2048]{1,0:T(8,128)(2,1)} %param.6), kind=kOutput, calls=%fused_computation.3 | convolution fusion | flops 1879048192 | bytes 16646148 | tf_op jit(solution)/shard_map/dot_general | solution.py:71
  81.9 7.9 %collective-permute-done.1 = bf16[128,3584]{1,0:T(8,128)(2,1)S(1)} collective-permute-done((bf16[128,3584]{1,0:T(8,128)(2,1)S(1)}, bf16[128,3584]{1,0:T(8,128)(2,1)S(1)}, u32[]{:S(2)}, u32[]{:S(2)}) %collective-permute-start.1) | collective-permute-done | bytes 917536 | tf_op jit(solution)/shard_map/ppermute | solution.py:63
  89.8 1.6 collective-permute-start.2
  91.3 0.0 collective-permute-done
  91.4 1.6 collective-permute-start.3
  93.0 0.0 slice-done
  93.0 0.0 slice-done.1
  93.0 0.0 slice-done.2
  93.0 3.4 %convolution_dynamic-update-slice_fusion.2 = f32[512,2048]{1,0:T(8,128)} fusion(f32[512,2048]{1,0:T(8,128)} %convolution_dynamic-update-slice_fusion.3, s32[]{:T(128)S(6)} %select_n.13, bf16[128,3584]{1,0:T(8,128)(2,1)S(1)} %collective-permute-done, bf16[3584,2048]{1,0:T(8,128)(2,1)S(1)} %bitcast.27), kind=kOutput, calls=%fused_computation.2 | convolution fusion | flops 1879048192 | bytes 16646148 | tf_op jit(solution)/shard_map/dot_general | solution.py:71
  96.3 3.3 %convolution_dynamic-update-slice_fusion.1 = f32[512,2048]{1,0:T(8,128)} fusion(f32[512,2048]{1,0:T(8,128)} %convolution_dynamic-update-slice_fusion.2, s32[]{:T(128)S(6)} %select_n.14, bf16[128,3584]{1,0:T(8,128)(2,1)S(1)} %collective-permute-done.1, bf16[3584,2048]{1,0:T(8,128)(2,1)S(1)} %bitcast.27), kind=kOutput, calls=%fused_computation.1 | convolution fusion | flops 1879048192 | bytes 16646148 | tf_op jit(solution)/shard_map/dot_general | solution.py:71
  99.7 1.3 collective-permute-done.2
  101.0 1.3 collective-permute-done.3
  102.3 3.2 %convolution_dynamic-update-slice_fusion = f32[512,2048]{1,0:T(8,128)} fusion(f32[512,2048]{1,0:T(8,128)} %convolution_dynamic-update-slice_fusion.1, s32[]{:T(128)S(6)} %select_n.15, bf16[3584,2048]{1,0:T(8,128)(2,1)S(1)} %bitcast.27, bf16[64,3584]{1,0:T(8,128)(2,1)S(1)} %collective-permute-done.3, bf16[64,3584]{1,0:T(8,128)(2,1)S(1)} %collective-permute-done.2), kind=kOutput, calls=%fused_computation | convolution fusion | flops 1880883200 | bytes 16646148 | tf_op jit(solution)/shard_map/dot_general | solution.py:71
  105.5 0.0 reduce-scatter.2.cloned.1.call-update
  105.6 49.0 %reduce-scatter.2.cloned.1.call-done = f32[64,2048]{1,0:T(8,128)} async-done(((f32[512,2048]{1,0:T(8,128)}), f32[64,2048]{1,0:T(8,128)}) %reduce-scatter.2.cloned.1.call-update) | async-done | bytes 524304 | tf_op jit(solution)/shard_map/reduce_scatter | solution.py:91
  154.6 0.0 copy-done.1
  154.6 1.8 %multiply_convert_fusion.1 = bf16[64,2048]{1,0:T(8,128)(2,1)} fusion(f32[64,2048]{1,0:T(8,128)} %reduce-scatter.2.cloned.1.call-done, f32[2048]{0:T(1024)S(1)} %copy-done.1), kind=kLoop, calls=%fused_computation.11 | loop fusion | flops 262144 | bytes 794624 | tf_op jit(solution)/shard_map/convert_element_type | solution.py:93
  (10 shorter events, 0.1 us)
Async XLA Ops:
  6.5 31.3 %copy-start.2 = (bf16[896,896,1]{1,0,2:T(8,128)(2,1)S(1)}, bf16[896,896,1]{1,0,2:T(8,128)(2,1)}, u32[]{:S(2)}) copy-start(bf16[896,896,1]{1,0,2:T(8,128)(2,1)} %constant.27) | copy-start | bytes 4816900
  6.5 148.0 %reduce-scatter.2.cloned.1.call-start = ((), (), s32[]{:S(2)}) async-start(), calls=%async_computation.3 | async-start | bytes 4718592 | tf_op jit(solution)/shard_map/reduce_scatter | solution.py:91
  37.9 1.2 copy-start
  67.9 21.9 %collective-permute-start.1 = (bf16[128,3584]{1,0:T(8,128)(2,1)S(1)}, bf16[128,3584]{1,0:T(8,128)(2,1)S(1)}, u32[]{:S(2)}, u32[]{:S(2)}) collective-permute-start(bf16[128,3584]{1,0:T(8,128)(2,1)S(1)} %bitcast.28), channel_id=1, source_target_pairs={{0,16},{8,24},{16,0},{24,8},{1,17},{9,25},{17,1},{25,9},{2,18},{10... | collective-permute-start | bytes 2752520 | tf_op jit(solution)/shard_map/ppermute | solution.py:63
  69.4 22.0 %collective-permute-start = (bf16[128,3584]{1,0:T(8,128)(2,1)S(1)}, bf16[128,3584]{1,0:T(8,128)(2,1)S(1)}, u32[]{:S(2)}, u32[]{:S(2)}) collective-permute-start(bf16[128,3584]{1,0:T(8,128)(2,1)S(1)} %bitcast.29), channel_id=1, source_target_pairs={{0,8},{8,0},{16,24},{24,16},{1,9},{9,1},{17,25},{25,17},{2,10},{10... | collective-permute-start | bytes 2752520 | tf_op jit(solution)/shard_map/ppermute | solution.py:62
  70.9 22.1 %slice-start = ((s8[14680064]{0:T(1024)(128)(4,1)}), s8[4194304]{0:T(1024)(128)(4,1)S(1)}, s32[]{:S(2)}) async-start(s8[14680064]{0:T(1024)(128)(4,1)} %bitcast.26), calls=%async_computation.4 | async-start | bytes 8388608
  73.5 19.5 %slice-start.1 = ((s8[14680064]{0:T(1024)(128)(4,1)}), s8[4194304]{0:T(1024)(128)(4,1)S(1)}, s32[]{:S(2)}) async-start(s8[14680064]{0:T(1024)(128)(4,1)} %bitcast.26), calls=%async_computation.5 | async-start | bytes 8388608
  73.5 19.5 %slice-start.2 = ((s8[14680064]{0:T(1024)(128)(4,1)}), s8[4194304]{0:T(1024)(128)(4,1)S(1)}, s32[]{:S(2)}) async-start(s8[14680064]{0:T(1024)(128)(4,1)} %bitcast.26), calls=%async_computation.6 | async-start | bytes 8388608
  73.5 19.5 %slice-start.3 = ((s8[14680064]{0:T(1024)(128)(4,1)}), s8[2097152]{0:T(1024)(128)(4,1)S(1)}, s32[]{:S(2)}) async-start(s8[14680064]{0:T(1024)(128)(4,1)} %bitcast.26), calls=%async_computation.7 | async-start | bytes 4194304
  89.8 11.2 %collective-permute-start.2 = (bf16[64,3584]{1,0:T(8,128)(2,1)S(1)}, bf16[64,3584]{1,0:T(8,128)(2,1)S(1)}, u32[]{:S(2)}, u32[]{:S(2)}) collective-permute-start(bf16[64,3584]{1,0:T(8,128)(2,1)S(1)} %slice.8), channel_id=1, source_target_pairs={{0,8},{8,0},{16,24},{24,16},{1,9},{9,1},{17,25},{25,17},{2,10},{10... | collective-permute-start | bytes 1376264 | tf_op jit(solution)/shard_map/ppermute | solution.py:64
  91.4 11.0 %collective-permute-start.3 = (bf16[64,3584]{1,0:T(8,128)(2,1)S(1)}, bf16[64,3584]{1,0:T(8,128)(2,1)S(1)}, u32[]{:S(2)}, u32[]{:S(2)}) collective-permute-start(bf16[64,3584]{1,0:T(8,128)(2,1)S(1)} %slice.9), channel_id=1, source_target_pairs={{0,16},{8,24},{16,0},{24,8},{1,17},{9,25},{17,1},{25,9},{2,18},{10... | collective-permute-start | bytes 1376264 | tf_op jit(solution)/shard_map/ppermute | solution.py:65
  105.5 49.0 %copy-start.1 = (f32[2048]{0:T(1024)S(1)}, f32[2048]{0:T(1024)}, u32[]{:S(2)}) copy-start(f32[2048]{0:T(1024)} %param.7) | copy-start | bytes 24580
Sparse Core Ops, SparseCore 0:
  105.7 48.8 reduce-scatter.1

commit v5 on v4

--- a/solution.py
+++ b/solution.py
@@ -26,6 +26,13 @@
     return np.kron(conference, upper) + np.kron(np.eye(14), lower)
 
 
+def inner_kron():
+    walsh = jnp.asarray(walsh_table(INNER), jnp.bfloat16)
+    paley = jnp.asarray(paley_table(), jnp.bfloat16)
+    width = INNER * PALEY
+    return (walsh[:, None, :, None] * paley[None, :, None, :]).reshape(width, width)
+
+
 def walsh_table(order):
     index_rows = np.arange(order)[:, None]
     index_cols = np.arange(order)[None, :]
@@ -43,7 +50,7 @@
     walsh = total_units // PALEY
     outer_order = walsh // INNER
     width = INNER * PALEY
-    inner_table = jnp.asarray(np.kron(walsh_table(INNER), paley_table()), jnp.bfloat16)
+    inner_table = inner_kron()
     outer_table = jnp.asarray(walsh_table(outer_order), jnp.float32)
     blocks = spread.reshape(rows, outer_order, width)
     inner = jnp.einsum("rbl,lm->rbm", blocks, inner_table, preferred_element_type=jnp.float32)
@@ -73,6 +80,45 @@
     return result
 
 
+def spread_rotate_return(part):
+    tp_count = lax.axis_size("tp")
+    rows, units = part.shape
+    share = rows // tp_count
+    width = INNER * PALEY
+    sub = units // width
+    me = lax.axis_index("tp")
+    pairs = lambda distance: [(k, k ^ distance) for k in range(tp_count)]
+    inner_table = inner_kron()
+    landed = []
+    for distance in range(tp_count):
+        send = lax.dynamic_slice_in_dim(part, (me ^ distance) * share, share, 0)
+        if distance:
+            send = lax.ppermute(send, "tp", pairs(distance))
+        landed.append(
+            jnp.einsum(
+                "rbl,lm->rbm",
+                send.reshape(share, sub, width),
+                inner_table,
+                preferred_element_type=jnp.float32,
+            )
+        )
+    inner = jnp.stack(landed, axis=1).reshape(share, tp_count * sub, width)
+    order = jnp.arange(tp_count, dtype=jnp.int32)
+    source = me ^ order
+    signs = 1 - 2 * (lax.population_count(source[:, None] & source[None, :]) % 2)
+    mixing = jnp.kron(signs.astype(jnp.float32), jnp.asarray(walsh_table(sub), jnp.float32))
+    outer = jnp.einsum("rbm,bc->rcm", inner, mixing, precision=lax.Precision.HIGHEST)
+    factor = 1.0 / math.sqrt(units * tp_count)
+    turned = (outer * factor).astype(jnp.bfloat16).reshape(share, tp_count, units)
+    result = jnp.zeros((rows, units), jnp.bfloat16)
+    for distance in range(tp_count):
+        block = turned[:, distance]
+        if distance:
+            block = lax.ppermute(block, "tp", pairs(distance))
+        result = lax.dynamic_update_slice_in_dim(result, block, (me ^ distance) * share, 0)
+    return result
+
+
 def shards(hidden, down_weight, channel_scale):
     seq_count = lax.axis_size("seq")
     tp_count = lax.axis_size("tp")
@@ -84,9 +130,12 @@
     outputs = []
     for chunk in range(CHUNKS):
         part = grouped[:, chunk].reshape(groups * piece, units)
-        spread = lax.all_to_all(part, "tp", split_axis=0, concat_axis=1, tiled=True)
-        turned = rotate(spread)
-        rotated = lax.all_to_all(turned, "tp", split_axis=1, concat_axis=0, tiled=True)
+        if tp_count == 8:
+            rotated = spread_rotate_return(part)
+        else:
+            spread = lax.all_to_all(part, "tp", split_axis=0, concat_axis=1, tiled=True)
+            turned = rotate(spread)
+            rotated = lax.all_to_all(turned, "tp", split_axis=1, concat_axis=0, tiled=True)
         partial_terms = gathered_product(rotated, down_weight)
         outputs.append(lax.psum_scatter(partial_terms, "tp", scatter_dimension=0, tiled=True))
     summed = jnp.concatenate(outputs, axis=0)

time: 163 us -> 177 us (1.086)
  blocking collectives: 56.4 us -> 0 us
  local copies, waits for them, and re-layouts: 4.61 us -> 24.3 us
  starting transfers between devices: 6.15 us -> 24.9 us
  waiting for transfers between devices: 59.6 us -> 78.1 us
  matrix products: 21.2 us -> 29.3 us
  other arithmetic: 1.78 us -> 6.06 us
    all_to_all x2 -> x0, blocking collectives: 56.4 us -> none  [the longest x1 30.2 us: shards(): spread = lax.all_to_all(part, 'tp', split_axis=0, concat_axis=1, tiled=True)]
    ppermute x0 -> x14, starting transfers between devices: none -> 18.7 us  [the longest x7 9.62 us: spread_rotate_return(): send = lax.ppermute(send, 'tp', pairs(distance))]
    mul x0 -> x2, local copies, waits for them, and re-layouts: none -> 15.3 us  [the longest x1 13.7 us: inner_kron(): walsh[:, None, :, None] * paley[None, :, None, :]]
    ppermute x0 -> x14, waiting for transfers between devices: none -> 13.4 us  [the longest x7 11.9 us: spread_rotate_return(): block = lax.ppermute(block, 'tp', pairs(distance))]
    dot_general x2 -> x9, matrix products: 2.95 us -> 11 us  [the longest x8 7.47 us: spread_rotate_return(): jnp.einsum('rbl,lm->rbm', send.reshape(share, sub, width), inner_table, p...]
    mul x0 -> x2, other arithmetic: none -> 4.2 us  [the longest x1 3.46 us: inner_kron(): walsh[:, None, :, None] * paley[None, :, None, :]]
    reduce_scatter x1, waiting for transfers between devices: 49 us -> 52.4 us  [shards(): lax.psum_scatter(partial_terms, 'tp', scatter_dimension=0, tiled=True)]
    dynamic_slice x0 -> x1, local copies, waits for them, and re-layouts: none -> 2.21 us  [spread_rotate_return(): send = lax.dynamic_slice_in_dim(part, (me ^ distance) * share, share, 0)]
  transfers between devices with their start and end apart: 5 -> 19, of which waited for: 4 -> 7; matrix products, arithmetic and copies ran while one was open for 11% -> 25% of each run, Pallas kernels for 0% -> 0%
where the time goes in v5:
time: 177 us; the launch traced here: 176 us
  waiting for transfers between devices  78.1 us (44%)
  matrix products  29.3 us (17%)
  starting transfers between devices  24.9 us (14%)
  local copies, waits for them, and re-layouts  24.3 us (14%)
  between operations  13.7 us (8%)
  other arithmetic  6.06 us (3%)
    reduce_scatter x1, waiting for transfers between devices, shards(): lax.psum_scatter(partial_terms, 'tp', scatter_dimension=0, tiled=True)  52.4 us
    dot_general x4, matrix products, gathered_product(): product = jnp.dot(piece, down_weight, preferred_element_type=jnp.float32)  18.3 us
    mul x1, local copies, waits for them, and re-layouts, inner_kron(): walsh[:, None, :, None] * paley[None, :, None, :]  13.7 us
    ppermute x7, waiting for transfers between devices, spread_rotate_return(): block = lax.ppermute(block, 'tp', pairs(distance))  11.9 us
    ppermute x7, starting transfers between devices, spread_rotate_return(): send = lax.ppermute(send, 'tp', pairs(distance))  9.62 us
    ppermute x7, starting transfers between devices, spread_rotate_return(): block = lax.ppermute(block, 'tp', pairs(distance))  9.1 us
    ppermute x1, waiting for transfers between devices, gathered_product(): across_y = lax.ppermute(block, 'seq', [(s, s ^ 2) for s in range(4)])  8.79 us
    dot_general x8, matrix products, spread_rotate_return(): jnp.einsum('rbl,lm->rbm', send.reshape(share, sub, width), inner_table, p...  7.47 us
  transfers between devices with their start and end apart: 19, of which 7 were waited for; matrix products, arithmetic and copies ran while one was open for 25% of the time, Pallas kernels for 0%

profile of v5, /device:TPU:0, one launch (start us, length us, event | category | flops | bytes accessed | tf_op | source)
XLA Modules:
  0.0 176.4 jit_solution(15096345071937771328)
XLA Ops:
  6.5 2.2 %constant_dynamic-slice_fusion = (bf16[16,3584]{1,0:T(8,128)(2,1)}, bf16[16,3584]{1,0:T(8,128)(2,1)}, bf16[16,3584]{1,0:T(8,128)(2,1)}, bf16[16,3584]{1,0:T(8,12...) fusion(bf16[128,3584]{1,0:T(8,128)(2,1)} %param.6, ...), kind=kLoop, calls=%fused_computation.66 | loop fusion | bytes 1835040 | tf_op jit(solution)/shard_map/dynamic_slice | solution.py:94
  9.2 2.6 %collective-permute-start.1 = (bf16[16,3584]{1,0:T(8,128)(2,1)}, bf16[16,3584]{1,0:T(8,128)(2,1)}, u32[]{:S(2)}, u32[]{:S(2)}) collective-permute-start(bf16[16,3584]{1,0:T(8,128)(2,1)} %get-tuple-element.17), channel_id=1, source_target_pairs={{0,2},{1,3},{2,0},{3,1},{4,6},{5,7},{6,4},{7,5},{8,10},{9,11},{10,... | collective-permute-start | bytes 344072 | tf_op jit(solution)/shard_map/ppermute | solution.py:96
  11.9 2.7 %collective-permute-start.3 = (bf16[16,3584]{1,0:T(8,128)(2,1)}, bf16[16,3584]{1,0:T(8,128)(2,1)}, u32[]{:S(2)}, u32[]{:S(2)}) collective-permute-start(bf16[16,3584]{1,0:T(8,128)(2,1)} %get-tuple-element.15), channel_id=1, source_target_pairs={{0,4},{1,5},{2,6},{3,7},{4,0},{5,1},{6,2},{7,3},{8,12},{9,13},{10,... | collective-permute-start | bytes 344072 | tf_op jit(solution)/shard_map/ppermute | solution.py:96
  14.7 3.5 %broadcast_multiply_fusion = bf16[32,28,32,28]{3,2,1,0:T(8,128)(2,1)} fusion(bf16[28,28]{1,0:T(8,128)(2,1)S(1)} %copy-done.5, bf16[32,32]{1,0:T(8,128)(2,1)S(1)} %copy-done.4), kind=kLoop, calls=%fused_computation | loop fusion | flops 802816 | bytes 1609248 | tf_op jit(solution)/shard_map/mul | solution.py:33
  18.2 13.7 %reshape.148 = bf16[896,896,1]{1,0,2:T(8,128)(2,1)S(1)} reshape(bf16[32,28,32,28]{3,2,1,0:T(8,128)(2,1)} %broadcast_multiply_fusion) | data formatting | bytes 3211264 | tf_op jit(solution)/shard_map/mul | solution.py:33
  33.3 1.6 mul.152
  34.9 3.6 %collective-permute-start.5 = (bf16[16,3584]{1,0:T(8,128)(2,1)}, bf16[16,3584]{1,0:T(8,128)(2,1)S(1)}, u32[]{:S(2)}, u32[]{:S(2)}) collective-permute-start(bf16[16,3584]{1,0:T(8,128)(2,1)} %get-tuple-element.20), channel_id=1, source_target_pairs={{0,6},{1,7},{2,4},{3,5},{4,2},{5,3},{6,0},{7,1},{8,14},{9,15},{10,... | collective-permute-start | bytes 344072 | tf_op jit(solution)/shard_map/ppermute | solution.py:96
  41.2 1.3 fusion.11
  42.5 1.3 fusion.10
  45.5 1.5 collective-permute-done.6
  48.6 3.5 %fusion.4 = bf16[16,32,896]{2,1,0:T(8,128)(2,1)S(1)} fusion(f32[16,32,896]{2,0,1:T(8,128)} %bitcast.116, f32[32,32]{1,0:T(8,128)S(1)} %copy-done.2), kind=kOutput, calls=%fused_computation.8 | convolution fusion | flops 177078272 | bytes 2756608 | tf_op jit(solution)/shard_map/rbm,bc->rcm/dot_general | solution.py:110
  52.7 1.7 fusion.41
  54.6 2.4 %collective-permute-start.8 = (bf16[16,3584]{1,0:T(8,128)(2,1)S(1)}, bf16[16,3584]{1,0:T(8,128)(2,1)S(1)}, u32[]{:S(2)}, u32[]{:S(2)}) collective-permute-start(bf16[16,3584]{1,0:T(8,128)(2,1)S(1)} %bitcast.123), channel_id=1, source_target_pairs={{0,2},{1,3},{2,0},{3,1},{4,6},{5,7},{6,4},{7,5},{8,10},{9,11},{10,... | collective-permute-start | bytes 344072 | tf_op jit(solution)/shard_map/ppermute | solution.py:117
  57.1 2.7 %collective-permute-start.10 = (bf16[16,3584]{1,0:T(8,128)(2,1)S(1)}, bf16[16,3584]{1,0:T(8,128)(2,1)S(1)}, u32[]{:S(2)}, u32[]{:S(2)}) collective-permute-start(bf16[16,3584]{1,0:T(8,128)(2,1)S(1)} %bitcast.120), channel_id=1, source_target_pairs={{0,4},{1,5},{2,6},{3,7},{4,0},{5,1},{6,2},{7,3},{8,12},{9,13},{10,... | collective-permute-start | bytes 344072 | tf_op jit(solution)/shard_map/ppermute | solution.py:117
  60.2 2.1 %collective-permute-start.12 = (bf16[16,3584]{1,0:T(8,128)(2,1)S(1)}, bf16[16,3584]{1,0:T(8,128)(2,1)S(1)}, u32[]{:S(2)}, u32[]{:S(2)}) collective-permute-start(bf16[16,3584]{1,0:T(8,128)(2,1)S(1)} %bitcast.122), channel_id=1, source_target_pairs={{0,6},{1,7},{2,4},{3,5},{4,2},{5,3},{6,0},{7,1},{8,14},{9,15},{10,... | collective-permute-start | bytes 344072 | tf_op jit(solution)/shard_map/ppermute | solution.py:117
  62.3 1.4 collective-permute-start.13
  63.8 2.8 %collective-permute-done.9 = bf16[16,3584]{1,0:T(8,128)(2,1)S(1)} collective-permute-done((bf16[16,3584]{1,0:T(8,128)(2,1)S(1)}, bf16[16,3584]{1,0:T(8,128)(2,1)S(1)}, u32[]{:S(2)}, u32[]{:S(2)}) %collective-permute-start.9) | collective-permute-done | bytes 114720 | tf_op jit(solution)/shard_map/ppermute | solution.py:117
  66.6 9.0 %collective-permute-done.11 = bf16[16,3584]{1,0:T(8,128)(2,1)S(1)} collective-permute-done((bf16[16,3584]{1,0:T(8,128)(2,1)S(1)}, bf16[16,3584]{1,0:T(8,128)(2,1)S(1)}, u32[]{:S(2)}, u32[]{:S(2)}) %collective-permute-start.11) | collective-permute-done | bytes 114720 | tf_op jit(solution)/shard_map/ppermute | solution.py:117
  75.8 1.5 collective-permute-start.15
  77.3 1.5 collective-permute-start.14
  78.8 2.6 %broadcast_in_dim.6 = f32[512,2048]{1,0:T(8,128)} broadcast(f32[]{:T(128)} %constant.19.clone.1), dimensions={} | broadcast | bytes 4194308 | tf_op jit(solution)/shard_map/broadcast_in_dim | solution.py:76
  81.4 8.4 %convolution_dynamic-update-slice_fusion.3 = f32[512,2048]{1,0:T(8,128)} fusion(f32[512,2048]{1,0:T(8,128)} %broadcast_in_dim.6, s32[]{:T(128)S(6)} %select_n.64, bf16[128,3584]{1,0:T(8,128)(2,1)S(1)} %constant_dynamic-update-slice_fusion, bf16[3584,2048]{1,0:T(8,128)(2,1)} %param.7), kind=kOutput, calls=%fused_computation.4 | convolution fusion | flops 1879048192 | bytes 16646148 | tf_op jit(solution)/shard_map/dot_general | solution.py:78
  89.8 8.8 %collective-permute-done.15 = bf16[128,3584]{1,0:T(8,128)(2,1)S(1)} collective-permute-done((bf16[128,3584]{1,0:T(8,128)(2,1)S(1)}, bf16[128,3584]{1,0:T(8,128)(2,1)S(1)}, u32[]{:S(2)}, u32[]{:S(2)}) %collective-permute-start.15) | collective-permute-done | bytes 917536 | tf_op jit(solution)/shard_map/ppermute | solution.py:70
  98.6 1.6 collective-permute-start.16
  100.2 1.6 collective-permute-start.17
  101.8 3.6 %convolution_dynamic-update-slice_fusion.2 = f32[512,2048]{1,0:T(8,128)} fusion(f32[512,2048]{1,0:T(8,128)} %convolution_dynamic-update-slice_fusion.3, s32[]{:T(128)S(6)} %select_n.65, bf16[128,3584]{1,0:T(8,128)(2,1)S(1)} %collective-permute-done.14, bf16[3584,2048]{1,0:T(8,128)(2,1)S(1)} %bitcast.115), kind=kOutput, calls=%fused_computation.3 | convolution fusion | flops 1879048192 | bytes 16646148 | tf_op jit(solution)/shard_map/dot_general | solution.py:78
  105.4 3.3 %convolution_dynamic-update-slice_fusion.1 = f32[512,2048]{1,0:T(8,128)} fusion(f32[512,2048]{1,0:T(8,128)} %convolution_dynamic-update-slice_fusion.2, s32[]{:T(128)S(6)} %select_n.66, bf16[128,3584]{1,0:T(8,128)(2,1)S(1)} %collective-permute-done.15, bf16[3584,2048]{1,0:T(8,128)(2,1)S(1)} %bitcast.115), kind=kOutput, calls=%fused_computation.2 | convolution fusion | flops 1879048192 | bytes 16646148 | tf_op jit(solution)/shard_map/dot_general | solution.py:78
  108.7 2.1 %collective-permute-done.16 = bf16[64,3584]{1,0:T(8,128)(2,1)S(1)} collective-permute-done((bf16[64,3584]{1,0:T(8,128)(2,1)S(1)}, bf16[64,3584]{1,0:T(8,128)(2,1)S(1)}, u32[]{:S(2)}, u32[]{:S(2)}) %collective-permute-start.16) | collective-permute-done | bytes 458784 | tf_op jit(solution)/shard_map/ppermute | solution.py:71
  110.9 1.4 collective-permute-done.17
  112.2 3.0 %convolution_dynamic-update-slice_fusion = f32[512,2048]{1,0:T(8,128)} fusion(f32[512,2048]{1,0:T(8,128)} %convolution_dynamic-update-slice_fusion.1, s32[]{:T(128)S(6)} %select_n.67, bf16[3584,2048]{1,0:T(8,128)(2,1)S(1)} %bitcast.115, bf16[64,3584]{1,0:T(8,128)(2,1)S(1)} %collective-permute-done.17, bf16[64,3584]{1,0:T(8,128)(2,1)S(1)} %collective-permute-done.16), kind=kOutput, calls=%fused_computation.1 | convolution fusion | flops 1880883200 | bytes 16646148 | tf_op jit(solution)/shard_map/dot_general | solution.py:78
  115.3 52.4 %reduce-scatter.2.cloned.1.call-done = f32[64,2048]{1,0:T(8,128)} async-done(((f32[512,2048]{1,0:T(8,128)}), f32[64,2048]{1,0:T(8,128)}) %reduce-scatter.2.cloned.1.call-update) | async-done | bytes 524304 | tf_op jit(solution)/shard_map/reduce_scatter | solution.py:140
  167.7 1.8 %multiply_convert_fusion.1 = bf16[64,2048]{1,0:T(8,128)(2,1)} fusion(f32[64,2048]{1,0:T(8,128)} %reduce-scatter.2.cloned.1.call-done, f32[2048]{0:T(1024)S(1)} %copy-done.3), kind=kLoop, calls=%fused_computation.28 | loop fusion | flops 262144 | bytes 794624 | tf_op jit(solution)/shard_map/convert_element_type | solution.py:142
  (72 shorter events, 9.3 us)
Async XLA Ops:
  6.5 8.1 %copy-start.4 = (bf16[32,32]{1,0:T(8,128)(2,1)S(1)}, bf16[32,32]{1,0:T(8,128)(2,1)}, u32[]{:S(2)}) copy-start(bf16[32,32]{1,0:T(8,128)(2,1)} %constant.55.clone) | copy-start | bytes 6148
  6.5 8.1 %copy-start.5 = (bf16[28,28]{1,0:T(8,128)(2,1)S(1)}, bf16[28,28]{1,0:T(8,128)(2,1)}, u32[]{:S(2)}) copy-start(bf16[28,28]{1,0:T(8,128)(2,1)} %constant.56.clone) | copy-start | bytes 4708
  6.5 161.2 %reduce-scatter.2.cloned.1.call-start = ((), (), s32[]{:S(2)}) async-start(), calls=%async_computation.1 | async-start | bytes 4718592 | tf_op jit(solution)/shard_map/reduce_scatter | solution.py:140
  8.8 26.2 %collective-permute-start = (bf16[16,3584]{1,0:T(8,128)(2,1)}, bf16[16,3584]{1,0:T(8,128)(2,1)}, u32[]{:S(2)}, u32[]{:S(2)}) collective-permute-start(bf16[16,3584]{1,0:T(8,128)(2,1)} %get-tuple-element.18), channel_id=1, source_target_pairs={{0,1},{1,0},{2,3},{3,2},{4,5},{5,4},{6,7},{7,6},{8,9},{9,8},{10,11... | collective-permute-start | bytes 344072 | tf_op jit(solution)/shard_map/ppermute | solution.py:96
  9.2 30.6 %collective-permute-start.1 = (bf16[16,3584]{1,0:T(8,128)(2,1)}, bf16[16,3584]{1,0:T(8,128)(2,1)}, u32[]{:S(2)}, u32[]{:S(2)}) collective-permute-start(bf16[16,3584]{1,0:T(8,128)(2,1)} %get-tuple-element.17), channel_id=1, source_target_pairs={{0,2},{1,3},{2,0},{3,1},{4,6},{5,7},{6,4},{7,5},{8,10},{9,11},{10,... | collective-permute-start | bytes 344072 | tf_op jit(solution)/shard_map/ppermute | solution.py:96
  11.8 29.4 %collective-permute-start.2 = (bf16[16,3584]{1,0:T(8,128)(2,1)}, bf16[16,3584]{1,0:T(8,128)(2,1)}, u32[]{:S(2)}, u32[]{:S(2)}) collective-permute-start(bf16[16,3584]{1,0:T(8,128)(2,1)} %get-tuple-element.16), channel_id=1, source_target_pairs={{0,3},{1,2},{2,1},{3,0},{4,7},{5,6},{6,5},{7,4},{8,11},{9,10},{10,... | collective-permute-start | bytes 344072 | tf_op jit(solution)/shard_map/ppermute | solution.py:96
  11.9 30.6 %collective-permute-start.3 = (bf16[16,3584]{1,0:T(8,128)(2,1)}, bf16[16,3584]{1,0:T(8,128)(2,1)}, u32[]{:S(2)}, u32[]{:S(2)}) collective-permute-start(bf16[16,3584]{1,0:T(8,128)(2,1)} %get-tuple-element.15), channel_id=1, source_target_pairs={{0,4},{1,5},{2,6},{3,7},{4,0},{5,1},{6,2},{7,3},{8,12},{9,13},{10,... | collective-permute-start | bytes 344072 | tf_op jit(solution)/shard_map/ppermute | solution.py:96
  14.7 29.1 %collective-permute-start.4 = (bf16[16,3584]{1,0:T(8,128)(2,1)}, bf16[16,3584]{1,0:T(8,128)(2,1)}, u32[]{:S(2)}, u32[]{:S(2)}) collective-permute-start(bf16[16,3584]{1,0:T(8,128)(2,1)} %get-tuple-element.14), channel_id=1, source_target_pairs={{0,5},{1,4},{2,7},{3,6},{4,1},{5,0},{6,3},{7,2},{8,13},{9,12},{10,... | collective-permute-start | bytes 344072 | tf_op jit(solution)/shard_map/ppermute | solution.py:96
  31.9 0.7 copy-start.6
  32.6 7.2 %copy-start.1 = (bf16[16,3584]{1,0:T(8,128)(2,1)S(1)}, bf16[16,3584]{1,0:T(8,128)(2,1)}, u32[]{:S(2)}) copy-start(bf16[16,3584]{1,0:T(8,128)(2,1)} %get-tuple-element.13) | copy-start | bytes 344068
  34.9 10.1 %collective-permute-start.5 = (bf16[16,3584]{1,0:T(8,128)(2,1)}, bf16[16,3584]{1,0:T(8,128)(2,1)S(1)}, u32[]{:S(2)}, u32[]{:S(2)}) collective-permute-start(bf16[16,3584]{1,0:T(8,128)(2,1)} %get-tuple-element.20), channel_id=1, source_target_pairs={{0,6},{1,7},{2,4},{3,5},{4,2},{5,3},{6,0},{7,1},{8,14},{9,15},{10,... | collective-permute-start | bytes 344072 | tf_op jit(solution)/shard_map/ppermute | solution.py:96
  39.8 7.2 %collective-permute-start.6 = (bf16[16,3584]{1,0:T(8,128)(2,1)S(1)}, bf16[16,3584]{1,0:T(8,128)(2,1)S(1)}, u32[]{:S(2)}, u32[]{:S(2)}) collective-permute-start(bf16[16,3584]{1,0:T(8,128)(2,1)S(1)} %copy-done.1), channel_id=1, source_target_pairs={{0,7},{1,6},{2,5},{3,4},{4,3},{5,2},{6,1},{7,0},{8,15},{9,14},{10,... | collective-permute-start | bytes 344072 | tf_op jit(solution)/shard_map/ppermute | solution.py:96
  45.1 3.5 %copy-start.2 = (f32[32,32]{1,0:T(8,128)S(1)}, f32[32,32]{1,0:T(8,128)}, u32[]{:S(2)}) copy-start(f32[32,32]{1,0:T(8,128)} %mul.152) | copy-start | bytes 12292
  47.3 1.3 copy-start
  54.4 5.8 %collective-permute-start.7 = (bf16[16,3584]{1,0:T(8,128)(2,1)S(1)}, bf16[16,3584]{1,0:T(8,128)(2,1)S(1)}, u32[]{:S(2)}, u32[]{:S(2)}) collective-permute-start(bf16[16,3584]{1,0:T(8,128)(2,1)S(1)} %bitcast.124), channel_id=1, source_target_pairs={{0,1},{1,0},{2,3},{3,2},{4,5},{5,4},{6,7},{7,6},{8,9},{9,8},{10,11... | collective-permute-start | bytes 344072 | tf_op jit(solution)/shard_map/ppermute | solution.py:117
  54.6 7.8 %collective-permute-start.8 = (bf16[16,3584]{1,0:T(8,128)(2,1)S(1)}, bf16[16,3584]{1,0:T(8,128)(2,1)S(1)}, u32[]{:S(2)}, u32[]{:S(2)}) collective-permute-start(bf16[16,3584]{1,0:T(8,128)(2,1)S(1)} %bitcast.123), channel_id=1, source_target_pairs={{0,2},{1,3},{2,0},{3,1},{4,6},{5,7},{6,4},{7,5},{8,10},{9,11},{10,... | collective-permute-start | bytes 344072 | tf_op jit(solution)/shard_map/ppermute | solution.py:117
  57.0 9.6 %collective-permute-start.9 = (bf16[16,3584]{1,0:T(8,128)(2,1)S(1)}, bf16[16,3584]{1,0:T(8,128)(2,1)S(1)}, u32[]{:S(2)}, u32[]{:S(2)}) collective-permute-start(bf16[16,3584]{1,0:T(8,128)(2,1)S(1)} %bitcast.121), channel_id=1, source_target_pairs={{0,3},{1,2},{2,1},{3,0},{4,7},{5,6},{6,5},{7,4},{8,11},{9,10},{10,... | collective-permute-start | bytes 344072 | tf_op jit(solution)/shard_map/ppermute | solution.py:117
  57.1 9.5 %collective-permute-start.10 = (bf16[16,3584]{1,0:T(8,128)(2,1)S(1)}, bf16[16,3584]{1,0:T(8,128)(2,1)S(1)}, u32[]{:S(2)}, u32[]{:S(2)}) collective-permute-start(bf16[16,3584]{1,0:T(8,128)(2,1)S(1)} %bitcast.120), channel_id=1, source_target_pairs={{0,4},{1,5},{2,6},{3,7},{4,0},{5,1},{6,2},{7,3},{8,12},{9,13},{10,... | collective-permute-start | bytes 344072 | tf_op jit(solution)/shard_map/ppermute | solution.py:117
  59.8 15.9 %collective-permute-start.11 = (bf16[16,3584]{1,0:T(8,128)(2,1)S(1)}, bf16[16,3584]{1,0:T(8,128)(2,1)S(1)}, u32[]{:S(2)}, u32[]{:S(2)}) collective-permute-start(bf16[16,3584]{1,0:T(8,128)(2,1)S(1)} %bitcast.119), channel_id=1, source_target_pairs={{0,5},{1,4},{2,7},{3,6},{4,1},{5,0},{6,3},{7,2},{8,13},{9,12},{10,... | collective-permute-start | bytes 344072 | tf_op jit(solution)/shard_map/ppermute | solution.py:117
  60.2 15.5 %collective-permute-start.12 = (bf16[16,3584]{1,0:T(8,128)(2,1)S(1)}, bf16[16,3584]{1,0:T(8,128)(2,1)S(1)}, u32[]{:S(2)}, u32[]{:S(2)}) collective-permute-start(bf16[16,3584]{1,0:T(8,128)(2,1)S(1)} %bitcast.122), channel_id=1, source_target_pairs={{0,6},{1,7},{2,4},{3,5},{4,2},{5,3},{6,0},{7,1},{8,14},{9,15},{10,... | collective-permute-start | bytes 344072 | tf_op jit(solution)/shard_map/ppermute | solution.py:117
  62.3 13.4 %collective-permute-start.13 = (bf16[16,3584]{1,0:T(8,128)(2,1)S(1)}, bf16[16,3584]{1,0:T(8,128)(2,1)S(1)}, u32[]{:S(2)}, u32[]{:S(2)}) collective-permute-start(bf16[16,3584]{1,0:T(8,128)(2,1)S(1)} %bitcast.118), channel_id=1, source_target_pairs={{0,7},{1,6},{2,5},{3,4},{4,3},{5,2},{6,1},{7,0},{8,15},{9,14},{10,... | collective-permute-start | bytes 344072 | tf_op jit(solution)/shard_map/ppermute | solution.py:117
  75.8 22.8 %collective-permute-start.15 = (bf16[128,3584]{1,0:T(8,128)(2,1)S(1)}, bf16[128,3584]{1,0:T(8,128)(2,1)S(1)}, u32[]{:S(2)}, u32[]{:S(2)}) collective-permute-start(bf16[128,3584]{1,0:T(8,128)(2,1)S(1)} %constant_dynamic-update-slice_fusion), channel_id=1, source_target_pairs={{0,16},{8,24},{16,0},{24,8},{1,17},{9,25},{17,1},{25,9},{2,18},{10... | collective-permute-start | bytes 2752520 | tf_op jit(solution)/shard_map/ppermute | solution.py:70
  77.3 22.9 %collective-permute-start.14 = (bf16[128,3584]{1,0:T(8,128)(2,1)S(1)}, bf16[128,3584]{1,0:T(8,128)(2,1)S(1)}, u32[]{:S(2)}, u32[]{:S(2)}) collective-permute-start(bf16[128,3584]{1,0:T(8,128)(2,1)S(1)} %constant_dynamic-update-slice_fusion), channel_id=1, source_target_pairs={{0,8},{8,0},{16,24},{24,16},{1,9},{9,1},{17,25},{25,17},{2,10},{10... | collective-permute-start | bytes 2752520 | tf_op jit(solution)/shard_map/ppermute | solution.py:69
  78.8 23.0 %slice-start = ((s8[14680064]{0:T(1024)(128)(4,1)}), s8[4194304]{0:T(1024)(128)(4,1)S(1)}, s32[]{:S(2)}) async-start(s8[14680064]{0:T(1024)(128)(4,1)} %bitcast.114), calls=%async_computation.2 | async-start | bytes 8388608
  81.4 20.4 %slice-start.1 = ((s8[14680064]{0:T(1024)(128)(4,1)}), s8[4194304]{0:T(1024)(128)(4,1)S(1)}, s32[]{:S(2)}) async-start(s8[14680064]{0:T(1024)(128)(4,1)} %bitcast.114), calls=%async_computation.3 | async-start | bytes 8388608
  81.4 20.4 %slice-start.2 = ((s8[14680064]{0:T(1024)(128)(4,1)}), s8[4194304]{0:T(1024)(128)(4,1)S(1)}, s32[]{:S(2)}) async-start(s8[14680064]{0:T(1024)(128)(4,1)} %bitcast.114), calls=%async_computation.4 | async-start | bytes 8388608
  81.4 20.4 %slice-start.3 = ((s8[14680064]{0:T(1024)(128)(4,1)}), s8[2097152]{0:T(1024)(128)(4,1)S(1)}, s32[]{:S(2)}) async-start(s8[14680064]{0:T(1024)(128)(4,1)} %bitcast.114), calls=%async_computation.5 | async-start | bytes 4194304
  98.6 12.2 %collective-permute-start.16 = (bf16[64,3584]{1,0:T(8,128)(2,1)S(1)}, bf16[64,3584]{1,0:T(8,128)(2,1)S(1)}, u32[]{:S(2)}, u32[]{:S(2)}) collective-permute-start(bf16[64,3584]{1,0:T(8,128)(2,1)S(1)} %slice.48), channel_id=1, source_target_pairs={{0,8},{8,0},{16,24},{24,16},{1,9},{9,1},{17,25},{25,17},{2,10},{10... | collective-permute-start | bytes 1376264 | tf_op jit(solution)/shard_map/ppermute | solution.py:71
  100.2 12.0 %collective-permute-start.17 = (bf16[64,3584]{1,0:T(8,128)(2,1)S(1)}, bf16[64,3584]{1,0:T(8,128)(2,1)S(1)}, u32[]{:S(2)}, u32[]{:S(2)}) collective-permute-start(bf16[64,3584]{1,0:T(8,128)(2,1)S(1)} %slice.49), channel_id=1, source_target_pairs={{0,16},{8,24},{16,0},{24,8},{1,17},{9,25},{17,1},{25,9},{2,18},{10... | collective-permute-start | bytes 1376264 | tf_op jit(solution)/shard_map/ppermute | solution.py:72
  115.3 52.5 %copy-start.3 = (f32[2048]{0:T(1024)S(1)}, f32[2048]{0:T(1024)}, u32[]{:S(2)}) copy-start(f32[2048]{0:T(1024)} %param.8) | copy-start | bytes 24580
Sparse Core Ops, SparseCore 0:
  115.4 52.2 reduce-scatter.1

commit v6 on v5

--- a/solution.py
+++ b/solution.py
@@ -26,13 +26,6 @@
     return np.kron(conference, upper) + np.kron(np.eye(14), lower)
 
 
-def inner_kron():
-    walsh = jnp.asarray(walsh_table(INNER), jnp.bfloat16)
-    paley = jnp.asarray(paley_table(), jnp.bfloat16)
-    width = INNER * PALEY
-    return (walsh[:, None, :, None] * paley[None, :, None, :]).reshape(width, width)
-
-
 def walsh_table(order):
     index_rows = np.arange(order)[:, None]
     index_cols = np.arange(order)[None, :]
@@ -50,7 +43,7 @@
     walsh = total_units // PALEY
     outer_order = walsh // INNER
     width = INNER * PALEY
-    inner_table = inner_kron()
+    inner_table = jnp.asarray(np.kron(walsh_table(INNER), paley_table()), jnp.bfloat16)
     outer_table = jnp.asarray(walsh_table(outer_order), jnp.float32)
     blocks = spread.reshape(rows, outer_order, width)
     inner = jnp.einsum("rbl,lm->rbm", blocks, inner_table, preferred_element_type=jnp.float32)
@@ -88,7 +81,7 @@
     sub = units // width
     me = lax.axis_index("tp")
     pairs = lambda distance: [(k, k ^ distance) for k in range(tp_count)]
-    inner_table = inner_kron()
+    inner_table = jnp.asarray(np.kron(walsh_table(INNER), paley_table()), jnp.bfloat16)
     landed = []
     for distance in range(tp_count):
         send = lax.dynamic_slice_in_dim(part, (me ^ distance) * share, share, 0)

time: 177 us -> 165 us (0.932)
  local copies, waits for them, and re-layouts: 24.3 us -> 10.3 us
  other arithmetic: 6.06 us -> 2.6 us
  waiting for transfers between devices: 78.1 us -> 81.4 us
  starting transfers between devices: 24.9 us -> 27.1 us
    mul x1 -> x0, local copies, waits for them, and re-layouts: 13.7 us -> none  [inner_kron(): walsh[:, None, :, None] * paley[None, :, None, :]]
    mul x1 -> x0, other arithmetic: 3.46 us -> none  [inner_kron(): walsh[:, None, :, None] * paley[None, :, None, :]]
    ppermute x7, waiting for transfers between devices: 1.5 us -> 4.56 us  [spread_rotate_return(): send = lax.ppermute(send, 'tp', pairs(distance))]
    ppermute x7, starting transfers between devices: 9.1 us -> 11.2 us  [spread_rotate_return(): block = lax.ppermute(block, 'tp', pairs(distance))]
  transfers between devices with their start and end apart: 19 -> 19, of which waited for: 7 -> 7; matrix products, arithmetic and copies ran while one was open for 25% -> 17% of each run, Pallas kernels for 0% -> 0%
where the time goes in v6:
time: 165 us; the launch traced here: 164 us
  waiting for transfers between devices  81.4 us (49%)
  matrix products  29.3 us (18%)
  starting transfers between devices  27.1 us (16%)
  between operations  13.7 us (8%)
  local copies, waits for them, and re-layouts  10.3 us (6%)
  other arithmetic  2.6 us (2%)
    reduce_scatter x1, waiting for transfers between devices, shards(): lax.psum_scatter(partial_terms, 'tp', scatter_dimension=0, tiled=True)  52.1 us
    dot_general x4, matrix products, gathered_product(): product = jnp.dot(piece, down_weight, preferred_element_type=jnp.float32)  18.2 us
    ppermute x7, waiting for transfers between devices, spread_rotate_return(): block = lax.ppermute(block, 'tp', pairs(distance))  11.7 us
    ppermute x7, starting transfers between devices, spread_rotate_return(): block = lax.ppermute(block, 'tp', pairs(distance))  11.2 us
    ppermute x7, starting transfers between devices, spread_rotate_return(): send = lax.ppermute(send, 'tp', pairs(distance))  9.66 us
    ppermute x1, waiting for transfers between devices, gathered_product(): across_y = lax.ppermute(block, 'seq', [(s, s ^ 2) for s in range(4)])  9.17 us
    dot_general x8, matrix products, spread_rotate_return(): jnp.einsum('rbl,lm->rbm', send.reshape(share, sub, width), inner_table, p...  7.46 us
    ppermute x7, waiting for transfers between devices, spread_rotate_return(): send = lax.ppermute(send, 'tp', pairs(distance))  4.56 us
  transfers between devices with their start and end apart: 19, of which 7 were waited for; matrix products, arithmetic and copies ran while one was open for 17% of the time, Pallas kernels for 0%

profile of v6, /device:TPU:0, one launch (start us, length us, event | category | flops | bytes accessed | tf_op | source)
XLA Modules:
  0.0 164.4 jit_solution(6885766820267327839)
XLA Ops:
  6.5 2.2 %constant_dynamic-slice_fusion = (bf16[16,3584]{1,0:T(8,128)(2,1)S(1)}, bf16[16,3584]{1,0:T(8,128)(2,1)}, bf16[16,3584]{1,0:T(8,128)(2,1)}, bf16[16,3584]{1,0:T(...) fusion(bf16[128,3584]{1,0:T(8,128)(2,1)} %param.5, ...), kind=kLoop, calls=%fused_computation.57 | loop fusion | bytes 1835040 | tf_op jit(solution)/shard_map/dynamic_slice | solution.py:87
  9.2 2.6 %collective-permute-start.1 = (bf16[16,3584]{1,0:T(8,128)(2,1)}, bf16[16,3584]{1,0:T(8,128)(2,1)}, u32[]{:S(2)}, u32[]{:S(2)}) collective-permute-start(bf16[16,3584]{1,0:T(8,128)(2,1)} %get-tuple-element.17), channel_id=1, source_target_pairs={{0,2},{1,3},{2,0},{3,1},{4,6},{5,7},{6,4},{7,5},{8,10},{9,11},{10,... | collective-permute-start | bytes 344072 | tf_op jit(solution)/shard_map/ppermute | solution.py:89
  12.0 2.7 %collective-permute-start.3 = (bf16[16,3584]{1,0:T(8,128)(2,1)}, bf16[16,3584]{1,0:T(8,128)(2,1)}, u32[]{:S(2)}, u32[]{:S(2)}) collective-permute-start(bf16[16,3584]{1,0:T(8,128)(2,1)} %get-tuple-element.15), channel_id=1, source_target_pairs={{0,4},{1,5},{2,6},{3,7},{4,0},{5,1},{6,2},{7,3},{8,12},{9,13},{10,... | collective-permute-start | bytes 344072 | tf_op jit(solution)/shard_map/ppermute | solution.py:89
  15.9 1.6 mul.101
  17.5 3.6 %collective-permute-start.5 = (bf16[16,3584]{1,0:T(8,128)(2,1)}, bf16[16,3584]{1,0:T(8,128)(2,1)S(1)}, u32[]{:S(2)}, u32[]{:S(2)}) collective-permute-start(bf16[16,3584]{1,0:T(8,128)(2,1)} %get-tuple-element.20), channel_id=1, source_target_pairs={{0,6},{1,7},{2,4},{3,5},{4,2},{5,3},{6,0},{7,1},{8,14},{9,15},{10,... | collective-permute-start | bytes 344072 | tf_op jit(solution)/shard_map/ppermute | solution.py:89
  21.1 1.3 fusion.13
  22.5 1.3 fusion.12
  23.8 1.3 fusion.11
  25.1 1.3 fusion.10
  26.4 4.5 %collective-permute-done.4 = bf16[16,3584]{1,0:T(8,128)(2,1)} collective-permute-done((bf16[16,3584]{1,0:T(8,128)(2,1)}, bf16[16,3584]{1,0:T(8,128)(2,1)}, u32[]{:S(2)}, u32[]{:S(2)}) %collective-permute-start.4) | collective-permute-done | bytes 114720 | tf_op jit(solution)/shard_map/ppermute | solution.py:89
  30.9 1.3 fusion.9
  34.3 3.5 %fusion.4 = bf16[16,32,896]{2,1,0:T(8,128)(2,1)S(1)} fusion(f32[16,32,896]{2,0,1:T(8,128)} %bitcast.115, f32[32,32]{1,0:T(8,128)S(1)} %copy-done.2), kind=kOutput, calls=%fused_computation.7 | convolution fusion | flops 177078272 | bytes 2756608 | tf_op jit(solution)/shard_map/rbm,bc->rcm/dot_general | solution.py:103
  38.4 1.7 %fusion.25 = (bf16[16,1,3584]{2,1,0:T(2,128)(2,1)S(1)}, bf16[16,1,3584]{2,1,0:T(2,128)(2,1)S(1)}, bf16[16,1,3584]{2,1,0:T(2,128)(2,1)S(1)}, bf16[16,1,3584]{2,1,...) fusion(bf16[16,8,3584]{2,1,0:T(8,128)(2,1)S(1)} %reshape.104), kind=kLoop, calls=%fused_computation.71 | loop fusion | bytes 1835008 | tf_op jit(solution)/shard_map/slice | solution.py:108
  40.4 3.8 %collective-permute-start.8 = (bf16[16,3584]{1,0:T(8,128)(2,1)S(1)}, bf16[16,3584]{1,0:T(8,128)(2,1)S(1)}, u32[]{:S(2)}, u32[]{:S(2)}) collective-permute-start(bf16[16,3584]{1,0:T(8,128)(2,1)S(1)} %bitcast.122), channel_id=1, source_target_pairs={{0,2},{1,3},{2,0},{3,1},{4,6},{5,7},{6,4},{7,5},{8,10},{9,11},{10,... | collective-permute-start | bytes 344072 | tf_op jit(solution)/shard_map/ppermute | solution.py:110
  44.4 3.1 %collective-permute-start.10 = (bf16[16,3584]{1,0:T(8,128)(2,1)S(1)}, bf16[16,3584]{1,0:T(8,128)(2,1)S(1)}, u32[]{:S(2)}, u32[]{:S(2)}) collective-permute-start(bf16[16,3584]{1,0:T(8,128)(2,1)S(1)} %bitcast.119), channel_id=1, source_target_pairs={{0,4},{1,5},{2,6},{3,7},{4,0},{5,1},{6,2},{7,3},{8,12},{9,13},{10,... | collective-permute-start | bytes 344072 | tf_op jit(solution)/shard_map/ppermute | solution.py:110
  48.1 2.1 %collective-permute-start.12 = (bf16[16,3584]{1,0:T(8,128)(2,1)S(1)}, bf16[16,3584]{1,0:T(8,128)(2,1)S(1)}, u32[]{:S(2)}, u32[]{:S(2)}) collective-permute-start(bf16[16,3584]{1,0:T(8,128)(2,1)S(1)} %bitcast.121), channel_id=1, source_target_pairs={{0,6},{1,7},{2,4},{3,5},{4,2},{5,3},{6,0},{7,1},{8,14},{9,15},{10,... | collective-permute-start | bytes 344072 | tf_op jit(solution)/shard_map/ppermute | solution.py:110
  51.5 2.7 %collective-permute-done.9 = bf16[16,3584]{1,0:T(8,128)(2,1)S(1)} collective-permute-done((bf16[16,3584]{1,0:T(8,128)(2,1)S(1)}, bf16[16,3584]{1,0:T(8,128)(2,1)S(1)}, u32[]{:S(2)}, u32[]{:S(2)}) %collective-permute-start.9) | collective-permute-done | bytes 114720 | tf_op jit(solution)/shard_map/ppermute | solution.py:110
  54.3 9.0 %collective-permute-done.11 = bf16[16,3584]{1,0:T(8,128)(2,1)S(1)} collective-permute-done((bf16[16,3584]{1,0:T(8,128)(2,1)S(1)}, bf16[16,3584]{1,0:T(8,128)(2,1)S(1)}, u32[]{:S(2)}, u32[]{:S(2)}) %collective-permute-start.11) | collective-permute-done | bytes 114720 | tf_op jit(solution)/shard_map/ppermute | solution.py:110
  63.4 1.6 collective-permute-start.15
  64.9 1.5 collective-permute-start.14
  66.4 2.6 %broadcast_in_dim.8 = f32[512,2048]{1,0:T(8,128)} broadcast(f32[]{:T(128)} %constant.18.clone.1), dimensions={} | broadcast | bytes 4194308 | tf_op jit(solution)/shard_map/broadcast_in_dim | solution.py:69
  69.1 8.4 %convolution_dynamic-update-slice_fusion.3 = f32[512,2048]{1,0:T(8,128)} fusion(f32[512,2048]{1,0:T(8,128)} %broadcast_in_dim.8, s32[]{:T(128)S(6)} %select_n.64, bf16[128,3584]{1,0:T(8,128)(2,1)S(1)} %constant_dynamic-update-slice_fusion, bf16[3584,2048]{1,0:T(8,128)(2,1)} %param.6), kind=kOutput, calls=%fused_computation.3 | convolution fusion | flops 1879048192 | bytes 16646148 | tf_op jit(solution)/shard_map/dot_general | solution.py:71
  77.5 9.2 %collective-permute-done.15 = bf16[128,3584]{1,0:T(8,128)(2,1)S(1)} collective-permute-done((bf16[128,3584]{1,0:T(8,128)(2,1)S(1)}, bf16[128,3584]{1,0:T(8,128)(2,1)S(1)}, u32[]{:S(2)}, u32[]{:S(2)}) %collective-permute-start.15) | collective-permute-done | bytes 917536 | tf_op jit(solution)/shard_map/ppermute | solution.py:63
  86.7 1.6 collective-permute-start.16
  88.3 1.6 collective-permute-start.17
  89.9 3.5 %convolution_dynamic-update-slice_fusion.2 = f32[512,2048]{1,0:T(8,128)} fusion(f32[512,2048]{1,0:T(8,128)} %convolution_dynamic-update-slice_fusion.3, s32[]{:T(128)S(6)} %select_n.65, bf16[128,3584]{1,0:T(8,128)(2,1)S(1)} %collective-permute-done.14, bf16[3584,2048]{1,0:T(8,128)(2,1)S(1)} %bitcast.114), kind=kOutput, calls=%fused_computation.2 | convolution fusion | flops 1879048192 | bytes 16646148 | tf_op jit(solution)/shard_map/dot_general | solution.py:71
  93.4 3.3 %convolution_dynamic-update-slice_fusion.1 = f32[512,2048]{1,0:T(8,128)} fusion(f32[512,2048]{1,0:T(8,128)} %convolution_dynamic-update-slice_fusion.2, s32[]{:T(128)S(6)} %select_n.66, bf16[128,3584]{1,0:T(8,128)(2,1)S(1)} %collective-permute-done.15, bf16[3584,2048]{1,0:T(8,128)(2,1)S(1)} %bitcast.114), kind=kOutput, calls=%fused_computation.1 | convolution fusion | flops 1879048192 | bytes 16646148 | tf_op jit(solution)/shard_map/dot_general | solution.py:71
  96.7 2.6 %collective-permute-done.16 = bf16[64,3584]{1,0:T(8,128)(2,1)S(1)} collective-permute-done((bf16[64,3584]{1,0:T(8,128)(2,1)S(1)}, bf16[64,3584]{1,0:T(8,128)(2,1)S(1)}, u32[]{:S(2)}, u32[]{:S(2)}) %collective-permute-start.16) | collective-permute-done | bytes 458784 | tf_op jit(solution)/shard_map/ppermute | solution.py:64
  99.3 1.3 collective-permute-done.17
  100.6 3.0 %convolution_dynamic-update-slice_fusion = f32[512,2048]{1,0:T(8,128)} fusion(f32[512,2048]{1,0:T(8,128)} %convolution_dynamic-update-slice_fusion.1, s32[]{:T(128)S(6)} %select_n.67, bf16[3584,2048]{1,0:T(8,128)(2,1)S(1)} %bitcast.114, bf16[64,3584]{1,0:T(8,128)(2,1)S(1)} %collective-permute-done.17, bf16[64,3584]{1,0:T(8,128)(2,1)S(1)} %collective-permute-done.16), kind=kOutput, calls=%fused_computation | convolution fusion | flops 1880883200 | bytes 16646148 | tf_op jit(solution)/shard_map/dot_general | solution.py:71
  103.7 52.1 %reduce-scatter.2.cloned.1.call-done = f32[64,2048]{1,0:T(8,128)} async-done(((f32[512,2048]{1,0:T(8,128)}), f32[64,2048]{1,0:T(8,128)}) %reduce-scatter.2.cloned.1.call-update) | async-done | bytes 524304 | tf_op jit(solution)/shard_map/reduce_scatter | solution.py:133
  155.7 1.8 %multiply_convert_fusion.1 = bf16[64,2048]{1,0:T(8,128)(2,1)} fusion(f32[64,2048]{1,0:T(8,128)} %reduce-scatter.2.cloned.1.call-done, f32[2048]{0:T(1024)S(1)} %copy-done.3), kind=kLoop, calls=%fused_computation.27 | loop fusion | flops 262144 | bytes 794624 | tf_op jit(solution)/shard_map/convert_element_type | solution.py:135
  (66 shorter events, 7.1 us)
Async XLA Ops:
  6.5 8.2 %copy-start = (bf16[896,896,1]{1,0,2:T(8,128)(2,1)S(1)}, bf16[896,896,1]{1,0,2:T(8,128)(2,1)}, u32[]{:S(2)}) copy-start(bf16[896,896,1]{1,0,2:T(8,128)(2,1)} %constant.55) | copy-start | bytes 4816900
  6.5 149.2 %reduce-scatter.2.cloned.1.call-start = ((), (), s32[]{:S(2)}) async-start(), calls=%async_computation.1 | async-start | bytes 4718592 | tf_op jit(solution)/shard_map/reduce_scatter | solution.py:133
  6.5 8.6 %copy-start.4 = (f32[4,4]{1,0:T(4,128)S(1)}, f32[4,4]{1,0:T(4,128)}, u32[]{:S(2)}) copy-start(f32[4,4]{1,0:T(4,128)} %constant.54.clone) | copy-start | bytes 196
  8.8 8.7 %collective-permute-start = (bf16[16,3584]{1,0:T(8,128)(2,1)}, bf16[16,3584]{1,0:T(8,128)(2,1)}, u32[]{:S(2)}, u32[]{:S(2)}) collective-permute-start(bf16[16,3584]{1,0:T(8,128)(2,1)} %get-tuple-element.18), channel_id=1, source_target_pairs={{0,1},{1,0},{2,3},{3,2},{4,5},{5,4},{6,7},{7,6},{8,9},{9,8},{10,11... | collective-permute-start | bytes 344072 | tf_op jit(solution)/shard_map/ppermute | solution.py:89
  9.2 13.1 %collective-permute-start.1 = (bf16[16,3584]{1,0:T(8,128)(2,1)}, bf16[16,3584]{1,0:T(8,128)(2,1)}, u32[]{:S(2)}, u32[]{:S(2)}) collective-permute-start(bf16[16,3584]{1,0:T(8,128)(2,1)} %get-tuple-element.17), channel_id=1, source_target_pairs={{0,2},{1,3},{2,0},{3,1},{4,6},{5,7},{6,4},{7,5},{8,10},{9,11},{10,... | collective-permute-start | bytes 344072 | tf_op jit(solution)/shard_map/ppermute | solution.py:89
  11.9 12.0 %collective-permute-start.2 = (bf16[16,3584]{1,0:T(8,128)(2,1)}, bf16[16,3584]{1,0:T(8,128)(2,1)}, u32[]{:S(2)}, u32[]{:S(2)}) collective-permute-start(bf16[16,3584]{1,0:T(8,128)(2,1)} %get-tuple-element.16), channel_id=1, source_target_pairs={{0,3},{1,2},{2,1},{3,0},{4,7},{5,6},{6,5},{7,4},{8,11},{9,10},{10,... | collective-permute-start | bytes 344072 | tf_op jit(solution)/shard_map/ppermute | solution.py:89
  12.0 13.2 %collective-permute-start.3 = (bf16[16,3584]{1,0:T(8,128)(2,1)}, bf16[16,3584]{1,0:T(8,128)(2,1)}, u32[]{:S(2)}, u32[]{:S(2)}) collective-permute-start(bf16[16,3584]{1,0:T(8,128)(2,1)} %get-tuple-element.15), channel_id=1, source_target_pairs={{0,4},{1,5},{2,6},{3,7},{4,0},{5,1},{6,2},{7,3},{8,12},{9,13},{10,... | collective-permute-start | bytes 344072 | tf_op jit(solution)/shard_map/ppermute | solution.py:89
  14.7 16.3 %collective-permute-start.4 = (bf16[16,3584]{1,0:T(8,128)(2,1)}, bf16[16,3584]{1,0:T(8,128)(2,1)}, u32[]{:S(2)}, u32[]{:S(2)}) collective-permute-start(bf16[16,3584]{1,0:T(8,128)(2,1)} %get-tuple-element.14), channel_id=1, source_target_pairs={{0,5},{1,4},{2,7},{3,6},{4,1},{5,0},{6,3},{7,2},{8,13},{9,12},{10,... | collective-permute-start | bytes 344072 | tf_op jit(solution)/shard_map/ppermute | solution.py:89
  17.5 14.7 %collective-permute-start.5 = (bf16[16,3584]{1,0:T(8,128)(2,1)}, bf16[16,3584]{1,0:T(8,128)(2,1)S(1)}, u32[]{:S(2)}, u32[]{:S(2)}) collective-permute-start(bf16[16,3584]{1,0:T(8,128)(2,1)} %get-tuple-element.20), channel_id=1, source_target_pairs={{0,6},{1,7},{2,4},{3,5},{4,2},{5,3},{6,0},{7,1},{8,14},{9,15},{10,... | collective-permute-start | bytes 344072 | tf_op jit(solution)/shard_map/ppermute | solution.py:89
  22.4 10.2 %collective-permute-start.6 = (bf16[16,3584]{1,0:T(8,128)(2,1)S(1)}, bf16[16,3584]{1,0:T(8,128)(2,1)S(1)}, u32[]{:S(2)}, u32[]{:S(2)}) collective-permute-start(bf16[16,3584]{1,0:T(8,128)(2,1)S(1)} %get-tuple-element.13), channel_id=1, source_target_pairs={{0,7},{1,6},{2,5},{3,4},{4,3},{5,2},{6,1},{7,0},{8,15},{9,14},{10,... | collective-permute-start | bytes 344072 | tf_op jit(solution)/shard_map/ppermute | solution.py:89
  32.2 2.1 %copy-start.2 = (f32[32,32]{1,0:T(8,128)S(1)}, f32[32,32]{1,0:T(8,128)}, u32[]{:S(2)}) copy-start(f32[32,32]{1,0:T(8,128)} %mul.101) | copy-start | bytes 12292
  33.0 1.3 copy-start.1
  40.1 8.0 %collective-permute-start.7 = (bf16[16,3584]{1,0:T(8,128)(2,1)S(1)}, bf16[16,3584]{1,0:T(8,128)(2,1)S(1)}, u32[]{:S(2)}, u32[]{:S(2)}) collective-permute-start(bf16[16,3584]{1,0:T(8,128)(2,1)S(1)} %bitcast.123), channel_id=1, source_target_pairs={{0,1},{1,0},{2,3},{3,2},{4,5},{5,4},{6,7},{7,6},{8,9},{9,8},{10,11... | collective-permute-start | bytes 344072 | tf_op jit(solution)/shard_map/ppermute | solution.py:110
  40.4 9.8 %collective-permute-start.8 = (bf16[16,3584]{1,0:T(8,128)(2,1)S(1)}, bf16[16,3584]{1,0:T(8,128)(2,1)S(1)}, u32[]{:S(2)}, u32[]{:S(2)}) collective-permute-start(bf16[16,3584]{1,0:T(8,128)(2,1)S(1)} %bitcast.122), channel_id=1, source_target_pairs={{0,2},{1,3},{2,0},{3,1},{4,6},{5,7},{6,4},{7,5},{8,10},{9,11},{10,... | collective-permute-start | bytes 344072 | tf_op jit(solution)/shard_map/ppermute | solution.py:110
  44.2 10.0 %collective-permute-start.9 = (bf16[16,3584]{1,0:T(8,128)(2,1)S(1)}, bf16[16,3584]{1,0:T(8,128)(2,1)S(1)}, u32[]{:S(2)}, u32[]{:S(2)}) collective-permute-start(bf16[16,3584]{1,0:T(8,128)(2,1)S(1)} %bitcast.120), channel_id=1, source_target_pairs={{0,3},{1,2},{2,1},{3,0},{4,7},{5,6},{6,5},{7,4},{8,11},{9,10},{10,... | collective-permute-start | bytes 344072 | tf_op jit(solution)/shard_map/ppermute | solution.py:110
  44.4 9.8 %collective-permute-start.10 = (bf16[16,3584]{1,0:T(8,128)(2,1)S(1)}, bf16[16,3584]{1,0:T(8,128)(2,1)S(1)}, u32[]{:S(2)}, u32[]{:S(2)}) collective-permute-start(bf16[16,3584]{1,0:T(8,128)(2,1)S(1)} %bitcast.119), channel_id=1, source_target_pairs={{0,4},{1,5},{2,6},{3,7},{4,0},{5,1},{6,2},{7,3},{8,12},{9,13},{10,... | collective-permute-start | bytes 344072 | tf_op jit(solution)/shard_map/ppermute | solution.py:110
  47.5 15.7 %collective-permute-start.11 = (bf16[16,3584]{1,0:T(8,128)(2,1)S(1)}, bf16[16,3584]{1,0:T(8,128)(2,1)S(1)}, u32[]{:S(2)}, u32[]{:S(2)}) collective-permute-start(bf16[16,3584]{1,0:T(8,128)(2,1)S(1)} %bitcast.118), channel_id=1, source_target_pairs={{0,5},{1,4},{2,7},{3,6},{4,1},{5,0},{6,3},{7,2},{8,13},{9,12},{10,... | collective-permute-start | bytes 344072 | tf_op jit(solution)/shard_map/ppermute | solution.py:110
  48.1 15.2 %collective-permute-start.12 = (bf16[16,3584]{1,0:T(8,128)(2,1)S(1)}, bf16[16,3584]{1,0:T(8,128)(2,1)S(1)}, u32[]{:S(2)}, u32[]{:S(2)}) collective-permute-start(bf16[16,3584]{1,0:T(8,128)(2,1)S(1)} %bitcast.121), channel_id=1, source_target_pairs={{0,6},{1,7},{2,4},{3,5},{4,2},{5,3},{6,0},{7,1},{8,14},{9,15},{10,... | collective-permute-start | bytes 344072 | tf_op jit(solution)/shard_map/ppermute | solution.py:110
  50.3 13.0 %collective-permute-start.13 = (bf16[16,3584]{1,0:T(8,128)(2,1)S(1)}, bf16[16,3584]{1,0:T(8,128)(2,1)S(1)}, u32[]{:S(2)}, u32[]{:S(2)}) collective-permute-start(bf16[16,3584]{1,0:T(8,128)(2,1)S(1)} %bitcast.117), channel_id=1, source_target_pairs={{0,7},{1,6},{2,5},{3,4},{4,3},{5,2},{6,1},{7,0},{8,15},{9,14},{10,... | collective-permute-start | bytes 344072 | tf_op jit(solution)/shard_map/ppermute | solution.py:110
  63.4 23.3 %collective-permute-start.15 = (bf16[128,3584]{1,0:T(8,128)(2,1)S(1)}, bf16[128,3584]{1,0:T(8,128)(2,1)S(1)}, u32[]{:S(2)}, u32[]{:S(2)}) collective-permute-start(bf16[128,3584]{1,0:T(8,128)(2,1)S(1)} %constant_dynamic-update-slice_fusion), channel_id=1, source_target_pairs={{0,16},{8,24},{16,0},{24,8},{1,17},{9,25},{17,1},{25,9},{2,18},{10... | collective-permute-start | bytes 2752520 | tf_op jit(solution)/shard_map/ppermute | solution.py:63
  64.9 23.3 %collective-permute-start.14 = (bf16[128,3584]{1,0:T(8,128)(2,1)S(1)}, bf16[128,3584]{1,0:T(8,128)(2,1)S(1)}, u32[]{:S(2)}, u32[]{:S(2)}) collective-permute-start(bf16[128,3584]{1,0:T(8,128)(2,1)S(1)} %constant_dynamic-update-slice_fusion), channel_id=1, source_target_pairs={{0,8},{8,0},{16,24},{24,16},{1,9},{9,1},{17,25},{25,17},{2,10},{10... | collective-permute-start | bytes 2752520 | tf_op jit(solution)/shard_map/ppermute | solution.py:62
  66.4 23.4 %slice-start = ((s8[14680064]{0:T(1024)(128)(4,1)}), s8[4194304]{0:T(1024)(128)(4,1)S(1)}, s32[]{:S(2)}) async-start(s8[14680064]{0:T(1024)(128)(4,1)} %bitcast.113), calls=%async_computation.2 | async-start | bytes 8388608
  69.1 20.8 %slice-start.1 = ((s8[14680064]{0:T(1024)(128)(4,1)}), s8[4194304]{0:T(1024)(128)(4,1)S(1)}, s32[]{:S(2)}) async-start(s8[14680064]{0:T(1024)(128)(4,1)} %bitcast.113), calls=%async_computation.3 | async-start | bytes 8388608
  69.1 20.8 %slice-start.2 = ((s8[14680064]{0:T(1024)(128)(4,1)}), s8[4194304]{0:T(1024)(128)(4,1)S(1)}, s32[]{:S(2)}) async-start(s8[14680064]{0:T(1024)(128)(4,1)} %bitcast.113), calls=%async_computation.4 | async-start | bytes 8388608
  69.1 20.8 %slice-start.3 = ((s8[14680064]{0:T(1024)(128)(4,1)}), s8[2097152]{0:T(1024)(128)(4,1)S(1)}, s32[]{:S(2)}) async-start(s8[14680064]{0:T(1024)(128)(4,1)} %bitcast.113), calls=%async_computation.5 | async-start | bytes 4194304
  86.7 12.6 %collective-permute-start.16 = (bf16[64,3584]{1,0:T(8,128)(2,1)S(1)}, bf16[64,3584]{1,0:T(8,128)(2,1)S(1)}, u32[]{:S(2)}, u32[]{:S(2)}) collective-permute-start(bf16[64,3584]{1,0:T(8,128)(2,1)S(1)} %slice.48), channel_id=1, source_target_pairs={{0,8},{8,0},{16,24},{24,16},{1,9},{9,1},{17,25},{25,17},{2,10},{10... | collective-permute-start | bytes 1376264 | tf_op jit(solution)/shard_map/ppermute | solution.py:64
  88.3 12.3 %collective-permute-start.17 = (bf16[64,3584]{1,0:T(8,128)(2,1)S(1)}, bf16[64,3584]{1,0:T(8,128)(2,1)S(1)}, u32[]{:S(2)}, u32[]{:S(2)}) collective-permute-start(bf16[64,3584]{1,0:T(8,128)(2,1)S(1)} %slice.49), channel_id=1, source_target_pairs={{0,16},{8,24},{16,0},{24,8},{1,17},{9,25},{17,1},{25,9},{2,18},{10... | collective-permute-start | bytes 1376264 | tf_op jit(solution)/shard_map/ppermute | solution.py:65
  103.6 52.1 %copy-start.3 = (f32[2048]{0:T(1024)S(1)}, f32[2048]{0:T(1024)}, u32[]{:S(2)}) copy-start(f32[2048]{0:T(1024)} %param.7) | copy-start | bytes 24580
Sparse Core Ops, SparseCore 0:
  103.8 51.9 reduce-scatter.1

commit v7 on v4

--- a/solution.py
+++ b/solution.py
@@ -73,6 +73,29 @@
     return result
 
 
+def scatter_sum_tp(partial_terms):
+    tp_count = lax.axis_size("tp")
+    if tp_count != 8:
+        return lax.psum_scatter(partial_terms, "tp", scatter_dimension=0, tiled=True)
+    rows, columns = partial_terms.shape
+    share = rows // tp_count
+    me = lax.axis_index("tp")
+    pairs = lambda distance: [(k, k ^ distance) for k in range(tp_count)]
+    blocks = partial_terms.reshape(2, 2, 2, share, columns)
+    low = me % 2
+    keep = lax.dynamic_index_in_dim(blocks, low, 2, keepdims=False)
+    send = lax.dynamic_index_in_dim(blocks, 1 - low, 2, keepdims=False)
+    summed = keep + lax.ppermute(send, "tp", pairs(1))
+    middle = me // 2 % 2
+    keep = lax.dynamic_index_in_dim(summed, middle, 1, keepdims=False)
+    send = lax.dynamic_index_in_dim(summed, 1 - middle, 1, keepdims=False)
+    summed = keep + lax.ppermute(send, "tp", pairs(2))
+    high = me // 4 % 2
+    keep = lax.dynamic_index_in_dim(summed, high, 0, keepdims=False)
+    send = lax.dynamic_index_in_dim(summed, 1 - high, 0, keepdims=False)
+    return keep + lax.ppermute(send, "tp", pairs(4))
+
+
 def shards(hidden, down_weight, channel_scale):
     seq_count = lax.axis_size("seq")
     tp_count = lax.axis_size("tp")
@@ -88,7 +111,7 @@
         turned = rotate(spread)
         rotated = lax.all_to_all(turned, "tp", split_axis=1, concat_axis=0, tiled=True)
         partial_terms = gathered_product(rotated, down_weight)
-        outputs.append(lax.psum_scatter(partial_terms, "tp", scatter_dimension=0, tiled=True))
+        outputs.append(scatter_sum_tp(partial_terms))
     summed = jnp.concatenate(outputs, axis=0)
     return (summed * channel_scale[None, :]).astype(jnp.bfloat16)
 

time: 163 us -> 160 us (0.982)
  between operations: 13.5 us -> 0.25 us
  waiting for transfers between devices: 59.6 us -> 68.9 us
  matrix products: 21.2 us -> 17.2 us
  other arithmetic: 1.78 us -> 4.57 us
    ppermute x0 -> x3, waiting for transfers between devices: none -> 53.4 us  [the longest x1 25.1 us: scatter_sum_tp(): summed = keep + lax.ppermute(send, 'tp', pairs(2))]
    reduce_scatter x1 -> x0, waiting for transfers between devices: 49 us -> none  [shards(): lax.psum_scatter(partial_terms, 'tp', scatter_dimension=0, tiled=True)]
    ppermute x1, waiting for transfers between devices: 0.01 us -> 10.8 us  [gathered_product(): across_x = lax.ppermute(block, 'seq', [(s, s ^ 1) for s in range(4)])]
    ppermute x1, waiting for transfers between devices: 7.87 us -> 0.01 us  [gathered_product(): across_y = lax.ppermute(block, 'seq', [(s, s ^ 2) for s in range(4)])]
    dot_general x4, matrix products: 18.3 us -> 14.3 us  [gathered_product(): product = jnp.dot(piece, down_weight, preferred_element_type=jnp.float32)]
    add x0 -> x2, other arithmetic: none -> 3.81 us  [the longest x1 2.47 us: scatter_sum_tp(): summed = keep + lax.ppermute(send, 'tp', pairs(1))]
    broadcast_in_dim x1, local copies, waits for them, and re-layouts: 2.65 us -> 0.49 us  [gathered_product(): result = jnp.zeros((4 * rows, columns), jnp.float32)]
    ppermute x1, waiting for transfers between devices: 1.31 us -> 3.31 us  [gathered_product(): lax.ppermute(across_x[half:], 'seq', [(s, s ^ 2) for s in range(4)])]
  transfers between devices with their start and end apart: 5 -> 7, of which waited for: 4 -> 6; matrix products, arithmetic and copies ran while one was open for 11% -> 8% of each run, Pallas kernels for 0% -> 0%
where the time goes in v7:
time: 160 us
  waiting for transfers between devices  68.9 us (43%)
  blocking collectives  56.4 us (35%)
  matrix products  17.2 us (11%)
  starting transfers between devices  7.53 us (5%)
  local copies, waits for them, and re-layouts  4.69 us (3%)
  other arithmetic  4.57 us (3%)
    all_to_all x1, blocking collectives, shards(): spread = lax.all_to_all(part, 'tp', split_axis=0, concat_axis=1, tiled=True)  30.2 us
    all_to_all x1, blocking collectives, shards(): lax.all_to_all(turned, 'tp', split_axis=1, concat_axis=0, tiled=True)  26.2 us
    ppermute x1, waiting for transfers between devices, scatter_sum_tp(): summed = keep + lax.ppermute(send, 'tp', pairs(2))  25.1 us
    ppermute x1, waiting for transfers between devices, scatter_sum_tp(): return keep + lax.ppermute(send, 'tp', pairs(4))  24.1 us
    dot_general x4, matrix products, gathered_product(): product = jnp.dot(piece, down_weight, preferred_element_type=jnp.float32)  14.3 us
    ppermute x1, waiting for transfers between devices, gathered_product(): across_x = lax.ppermute(block, 'seq', [(s, s ^ 1) for s in range(4)])  10.8 us
    ppermute x1, waiting for transfers between devices, scatter_sum_tp(): summed = keep + lax.ppermute(send, 'tp', pairs(1))  4.23 us
    ppermute x1, waiting for transfers between devices, gathered_product(): lax.ppermute(across_x[half:], 'seq', [(s, s ^ 2) for s in range(4)])  3.31 us
  transfers between devices with their start and end apart: 7, of which 6 were waited for; matrix products, arithmetic and copies ran while one was open for 8% of the time, Pallas kernels for 0%

profile of v7, /device:TPU:0, one launch (start us, length us, event | category | flops | bytes accessed | tf_op | source)
XLA Modules:
  0.0 159.6 jit_solution(2442247375005910968)
XLA Ops:
  0.0 30.2 %all_to_all.35 = bf16[8,16,3584]{2,1,0:T(8,128)(2,1)S(1)} all-to-all(bf16[8,16,3584]{2,1,0:T(8,128)(2,1)} %bitcast.51), channel_id=1, replica_groups=mesh['seq'=4,'tp'=8] {'tp'}, dimensions={0} | all-to-all | bytes 1835008 | tf_op jit(solution)/shard_map/all_to_all | solution.py:110
  30.2 0.5 copy.10
  30.8 0.5 reshape.16
  31.3 1.2 fusion.13
  32.6 1.7 %fusion.4 = bf16[16,32,896]{2,1,0:T(8,128)(2,1)S(1)} fusion(f32[32,32,1]{0,1,2:T(8,128)S(1)} %copy-done.1, f32[896,16,32]{0,2,1:T(8,128)S(1)} %fusion.13), kind=kOutput, calls=%fused_computation.9 | convolution fusion | flops 177078272 | bytes 2756608 | tf_op jit(solution)/shard_map/rbm,bc->rcm/dot_general | solution.py:50
  34.3 0.5 all_to_all.29
  34.9 0.3 copy.11
  35.1 26.2 %all_to_all.36 = bf16[16,8,3584]{2,0,1:T(8,128)(2,1)S(1)} all-to-all(bf16[16,8,3584]{2,0,1:T(8,128)(2,1)S(1)} %copy.11), channel_id=1, replica_groups=mesh['seq'=4,'tp'=8] {'tp'}, dimensions={1} | all-to-all | bytes 1835008 | tf_op jit(solution)/shard_map/all_to_all | solution.py:112
  61.3 1.5 collective-permute-start
  62.8 1.5 collective-permute-start.1
  64.3 0.5 broadcast_in_dim.4
  64.9 7.5 %convolution_dynamic-update-slice_fusion.3 = f32[512,2048]{1,0:T(8,128)S(1)} fusion(f32[512,2048]{1,0:T(8,128)S(1)} %broadcast_in_dim.4, s32[]{:T(128)S(6)} %select_n.55, bf16[128,3584]{1,0:T(8,128)(2,1)S(1)} %bitcast.49, bf16[3584,2048]{1,0:T(8,128)(2,1)} %param.6), kind=kOutput, calls=%fused_computation.3 | convolution fusion | flops 1879048192 | bytes 16646148 | tf_op jit(solution)/shard_map/dot_general | solution.py:71
  72.4 10.8 %collective-permute-done = bf16[128,3584]{1,0:T(8,128)(2,1)S(1)} collective-permute-done((bf16[128,3584]{1,0:T(8,128)(2,1)S(1)}, bf16[128,3584]{1,0:T(8,128)(2,1)S(1)}, u32[]{:S(2)}, u32[]{:S(2)}) %collective-permute-start) | collective-permute-done | bytes 917536 | tf_op jit(solution)/shard_map/ppermute | solution.py:62
  83.2 1.6 collective-permute-start.3
  84.9 1.6 collective-permute-start.2
  86.5 2.3 %convolution_dynamic-update-slice_fusion.2 = f32[512,2048]{1,0:T(8,128)S(1)} fusion(f32[512,2048]{1,0:T(8,128)S(1)} %convolution_dynamic-update-slice_fusion.3, s32[]{:T(128)S(6)} %select_n.56, bf16[128,3584]{1,0:T(8,128)(2,1)S(1)} %collective-permute-done, bf16[3584,2048]{1,0:T(8,128)(2,1)S(1)} %bitcast.44), kind=kOutput, calls=%fused_computation.2 | convolution fusion | flops 1879048192 | bytes 16646148 | tf_op jit(solution)/shard_map/dot_general | solution.py:71
  88.8 2.4 %convolution_dynamic-update-slice_fusion.1 = f32[512,2048]{1,0:T(8,128)S(1)} fusion(f32[512,2048]{1,0:T(8,128)S(1)} %convolution_dynamic-update-slice_fusion.2, s32[]{:T(128)S(6)} %select_n.57, bf16[128,3584]{1,0:T(8,128)(2,1)S(1)} %collective-permute-done.1, bf16[3584,2048]{1,0:T(8,128)(2,1)S(1)} %bitcast.44), kind=kOutput, calls=%fused_computation.1 | convolution fusion | flops 1879048192 | bytes 16646148 | tf_op jit(solution)/shard_map/dot_general | solution.py:71
  91.2 3.3 %collective-permute-done.3 = bf16[64,3584]{1,0:T(8,128)(2,1)S(1)} collective-permute-done((bf16[64,3584]{1,0:T(8,128)(2,1)S(1)}, bf16[64,3584]{1,0:T(8,128)(2,1)S(1)}, u32[]{:S(2)}, u32[]{:S(2)}) %collective-permute-start.3) | collective-permute-done | bytes 458784 | tf_op jit(solution)/shard_map/ppermute | solution.py:65
  94.5 1.3 collective-permute-done.2
  95.8 2.1 %convolution_dynamic-update-slice_fusion = f32[512,2048]{1,0:T(8,128)S(1)} fusion(f32[512,2048]{1,0:T(8,128)S(1)} %convolution_dynamic-update-slice_fusion.1, s32[]{:T(128)S(6)} %select_n.58, bf16[3584,2048]{1,0:T(8,128)(2,1)S(1)} %bitcast.44, bf16[64,3584]{1,0:T(8,128)(2,1)S(1)} %collective-permute-done.3, bf16[64,3584]{1,0:T(8,128)(2,1)S(1)} %collective-permute-done.2), kind=kOutput, calls=%fused_computation | convolution fusion | flops 1880883200 | bytes 16646148 | tf_op jit(solution)/shard_map/dot_general | solution.py:71
  97.9 1.9 %copy-done = f32[512,2048]{1,0:T(8,128)} copy-done((f32[512,2048]{1,0:T(8,128)}, f32[512,2048]{1,0:T(8,128)S(1)}, u32[]{:S(2)}) %copy-start) | copy-done | bytes 4194328
  99.9 0.1 dynamic-slice_bitcast_fusion
  100.0 0.1 collective-permute-start.4
  100.1 4.2 %collective-permute-done.4 = f32[2,2,64,2048]{3,2,1,0:T(8,128)} collective-permute-done((f32[2,2,64,2048]{3,2,1,0:T(8,128)S(1)}, f32[2,2,64,2048]{3,2,1,0:T(8,128)}, u32[]{:S(2)}, u32[]{:S(2)}) %collective-permute-start.4) | collective-permute-done | bytes 2097184 | tf_op jit(solution)/shard_map/ppermute | solution.py:88
  104.4 2.5 %bitcast_add_fusion = f32[2,2,64,2048]{3,2,1,0:T(8,128)S(1)} fusion(f32[2,2,64,2048]{3,2,1,0:T(8,128)} %collective-permute-done.4, f32[2,2,2,64,2048]{4,3,2,1,0:T(8,128)} %bitcast.46, s32[]{:T(128)S(6)} %select_n.60), kind=kLoop, calls=%fused_computation.4 | loop fusion | flops 524288 | bytes 6291460 | tf_op jit(solution)/shard_map/add | solution.py:88
  106.8 0.1 dynamic-slice_bitcast_fusion.1
  106.9 0.3 collective-permute-start.5
  107.2 25.1 %collective-permute-done.5 = f32[2,64,2048]{2,1,0:T(8,128)} collective-permute-done((f32[2,64,2048]{2,1,0:T(8,128)S(1)}, f32[2,64,2048]{2,1,0:T(8,128)}, u32[]{:S(2)}, u32[]{:S(2)}) %collective-permute-start.5) | collective-permute-done | bytes 1048608 | tf_op jit(solution)/shard_map/ppermute | solution.py:92
  132.3 1.3 bitcast_add_fusion.1
  133.7 1.0 collective-permute-start.6
  134.8 24.1 %collective-permute-done.6 = f32[64,2048]{1,0:T(8,128)S(1)} collective-permute-done((f32[64,2048]{1,0:T(8,128)S(1)}, f32[64,2048]{1,0:T(8,128)S(1)}, u32[]{:S(2)}, u32[]{:S(2)}) %collective-permute-start.6) | collective-permute-done | bytes 524320 | tf_op jit(solution)/shard_map/ppermute | solution.py:96
  158.9 0.8 fusion.11
  (20 shorter events, 0.1 us)
Async XLA Ops:
  0.0 31.3 %copy-start.3 = (bf16[896,896,1]{1,0,2:T(8,128)(2,1)S(1)}, bf16[896,896,1]{1,0,2:T(8,128)(2,1)}, u32[]{:S(2)}) copy-start(bf16[896,896,1]{1,0,2:T(8,128)(2,1)} %constant.88) | copy-start | bytes 4816900
  31.3 1.2 copy-start.1
  61.3 21.9 %collective-permute-start = (bf16[128,3584]{1,0:T(8,128)(2,1)S(1)}, bf16[128,3584]{1,0:T(8,128)(2,1)S(1)}, u32[]{:S(2)}, u32[]{:S(2)}) collective-permute-start(bf16[128,3584]{1,0:T(8,128)(2,1)S(1)} %bitcast.47), channel_id=1, source_target_pairs={{0,8},{8,0},{16,24},{24,16},{1,9},{9,1},{17,25},{25,17},{2,10},{10... | collective-permute-start | bytes 2752520 | tf_op jit(solution)/shard_map/ppermute | solution.py:62
  62.8 22.0 %collective-permute-start.1 = (bf16[128,3584]{1,0:T(8,128)(2,1)S(1)}, bf16[128,3584]{1,0:T(8,128)(2,1)S(1)}, u32[]{:S(2)}, u32[]{:S(2)}) collective-permute-start(bf16[128,3584]{1,0:T(8,128)(2,1)S(1)} %bitcast.48), channel_id=1, source_target_pairs={{0,16},{8,24},{16,0},{24,8},{1,17},{9,25},{17,1},{25,9},{2,18},{10... | collective-permute-start | bytes 2752520 | tf_op jit(solution)/shard_map/ppermute | solution.py:63
  64.3 22.1 %slice-start = ((s8[14680064]{0:T(1024)(128)(4,1)}), s8[4194304]{0:T(1024)(128)(4,1)S(1)}, s32[]{:S(2)}) async-start(s8[14680064]{0:T(1024)(128)(4,1)} %bitcast.43), calls=%async_computation.2 | async-start | bytes 8388608
  64.8 21.6 %slice-start.1 = ((s8[14680064]{0:T(1024)(128)(4,1)}), s8[4194304]{0:T(1024)(128)(4,1)S(1)}, s32[]{:S(2)}) async-start(s8[14680064]{0:T(1024)(128)(4,1)} %bitcast.43), calls=%async_computation.3 | async-start | bytes 8388608
  64.8 21.6 %slice-start.2 = ((s8[14680064]{0:T(1024)(128)(4,1)}), s8[4194304]{0:T(1024)(128)(4,1)S(1)}, s32[]{:S(2)}) async-start(s8[14680064]{0:T(1024)(128)(4,1)} %bitcast.43), calls=%async_computation.4 | async-start | bytes 8388608
  64.9 21.6 %slice-start.3 = ((s8[14680064]{0:T(1024)(128)(4,1)}), s8[2097152]{0:T(1024)(128)(4,1)S(1)}, s32[]{:S(2)}) async-start(s8[14680064]{0:T(1024)(128)(4,1)} %bitcast.43), calls=%async_computation.5 | async-start | bytes 4194304
  83.2 11.2 %collective-permute-start.3 = (bf16[64,3584]{1,0:T(8,128)(2,1)S(1)}, bf16[64,3584]{1,0:T(8,128)(2,1)S(1)}, u32[]{:S(2)}, u32[]{:S(2)}) collective-permute-start(bf16[64,3584]{1,0:T(8,128)(2,1)S(1)} %slice.9), channel_id=1, source_target_pairs={{0,16},{8,24},{16,0},{24,8},{1,17},{9,25},{17,1},{25,9},{2,18},{10... | collective-permute-start | bytes 1376264 | tf_op jit(solution)/shard_map/ppermute | solution.py:65
  84.9 11.0 %collective-permute-start.2 = (bf16[64,3584]{1,0:T(8,128)(2,1)S(1)}, bf16[64,3584]{1,0:T(8,128)(2,1)S(1)}, u32[]{:S(2)}, u32[]{:S(2)}) collective-permute-start(bf16[64,3584]{1,0:T(8,128)(2,1)S(1)} %slice.8), channel_id=1, source_target_pairs={{0,8},{8,0},{16,24},{24,16},{1,9},{9,1},{17,25},{25,17},{2,10},{10... | collective-permute-start | bytes 1376264 | tf_op jit(solution)/shard_map/ppermute | solution.py:64
  97.9 2.0 %copy-start = (f32[512,2048]{1,0:T(8,128)}, f32[512,2048]{1,0:T(8,128)S(1)}, u32[]{:S(2)}) copy-start(f32[512,2048]{1,0:T(8,128)S(1)} %convolution_dynamic-update-slice_fusion) | copy-start | bytes 12582916
  100.0 4.4 %collective-permute-start.4 = (f32[2,2,64,2048]{3,2,1,0:T(8,128)S(1)}, f32[2,2,64,2048]{3,2,1,0:T(8,128)}, u32[]{:S(2)}, u32[]{:S(2)}) collective-permute-start(f32[2,2,64,2048]{3,2,1,0:T(8,128)S(1)} %dynamic-slice_bitcast_fusion), channel_id=1, source_target_pairs={{0,1},{1,0},{2,3},{3,2},{4,5},{5,4},{6,7},{7,6},{8,9},{9,8},{10,11... | collective-permute-start | bytes 6291464 | tf_op jit(solution)/shard_map/ppermute | solution.py:88
  106.8 52.0 %copy-start.2 = (f32[2048]{0:T(1024)S(1)}, f32[2048]{0:T(1024)}, u32[]{:S(2)}) copy-start(f32[2048]{0:T(1024)} %param.7) | copy-start | bytes 24580
  106.9 25.4 %collective-permute-start.5 = (f32[2,64,2048]{2,1,0:T(8,128)S(1)}, f32[2,64,2048]{2,1,0:T(8,128)}, u32[]{:S(2)}, u32[]{:S(2)}) collective-permute-start(f32[2,64,2048]{2,1,0:T(8,128)S(1)} %dynamic-slice_bitcast_fusion.1), channel_id=1, source_target_pairs={{0,2},{1,3},{2,0},{3,1},{4,6},{5,7},{6,4},{7,5},{8,10},{9,11},{10,... | collective-permute-start | bytes 3145736 | tf_op jit(solution)/shard_map/ppermute | solution.py:92
  133.7 25.2 %collective-permute-start.6 = (f32[64,2048]{1,0:T(8,128)S(1)}, f32[64,2048]{1,0:T(8,128)S(1)}, u32[]{:S(2)}, u32[]{:S(2)}) collective-permute-start(f32[64,2048]{1,0:T(8,128)S(1)} %dynamic-slice_bitcast_fusion.2), channel_id=1, source_target_pairs={{0,4},{1,5},{2,6},{3,7},{4,0},{5,1},{6,2},{7,3},{8,12},{9,13},{10,... | collective-permute-start | bytes 1572872 | tf_op jit(solution)/shard_map/ppermute | solution.py:96

commit v8 on v7

--- a/solution.py
+++ b/solution.py
@@ -96,6 +96,42 @@
     return keep + lax.ppermute(send, "tp", pairs(4))
 
 
+def product_and_reduce(block, down_weight):
+    rows = block.shape[0]
+    half = rows // 2
+    seq_pairs = lambda distance: [(s, s ^ distance) for s in range(4)]
+    tp_pairs = lambda distance: [(k, k ^ distance) for k in range(8)]
+    here = lax.axis_index("seq")
+    me = lax.axis_index("tp")
+    low, middle, high = me % 2, me // 2 % 2, me // 4 % 2
+    across_x = lax.ppermute(block, "seq", seq_pairs(1))
+    across_y = lax.ppermute(block, "seq", seq_pairs(2))
+    first = lax.ppermute(across_y[:half], "seq", seq_pairs(1))
+    second = lax.ppermute(across_x[half:], "seq", seq_pairs(2))
+    diagonal = jnp.concatenate([first, second], axis=0)
+
+    def halve_pair(pieces):
+        products = jnp.stack(
+            [jnp.dot(piece, down_weight, preferred_element_type=jnp.float32) for piece in pieces]
+        )
+        split = products.reshape(2, 2, half, products.shape[-1])
+        keep = lax.dynamic_index_in_dim(split, low, 1, keepdims=False)
+        send = lax.dynamic_index_in_dim(split, 1 - low, 1, keepdims=False)
+        summed = keep + lax.ppermute(send, "tp", tp_pairs(1))
+        chosen = here % 2 ^ middle
+        keep = lax.dynamic_index_in_dim(summed, chosen, 0, keepdims=False)
+        send = lax.dynamic_index_in_dim(summed, 1 - chosen, 0, keepdims=False)
+        return keep + lax.ppermute(send, "tp", tp_pairs(2))
+
+    near = halve_pair((block, across_x))
+    far = halve_pair((across_y, diagonal))
+    both = jnp.stack([near, far])
+    chosen = here // 2 % 2 ^ high
+    keep = lax.dynamic_index_in_dim(both, chosen, 0, keepdims=False)
+    send = lax.dynamic_index_in_dim(both, 1 - chosen, 0, keepdims=False)
+    return keep + lax.ppermute(send, "tp", tp_pairs(4))
+
+
 def shards(hidden, down_weight, channel_scale):
     seq_count = lax.axis_size("seq")
     tp_count = lax.axis_size("tp")
@@ -110,8 +146,11 @@
         spread = lax.all_to_all(part, "tp", split_axis=0, concat_axis=1, tiled=True)
         turned = rotate(spread)
         rotated = lax.all_to_all(turned, "tp", split_axis=1, concat_axis=0, tiled=True)
-        partial_terms = gathered_product(rotated, down_weight)
-        outputs.append(scatter_sum_tp(partial_terms))
+        if seq_count == 4 and tp_count == 8:
+            outputs.append(product_and_reduce(rotated, down_weight))
+        else:
+            partial_terms = gathered_product(rotated, down_weight)
+            outputs.append(scatter_sum_tp(partial_terms))
     summed = jnp.concatenate(outputs, axis=0)
     return (summed * channel_scale[None, :]).astype(jnp.bfloat16)
 

time: 160 us -> 159 us (level)
  blocking collectives: 56.4 us -> 30.1 us
  waiting for transfers between devices: 68.9 us -> 85.8 us
  starting transfers between devices: 7.53 us -> 12.4 us
  other arithmetic: 4.57 us -> 7.13 us
    all_to_all x1 -> x0, blocking collectives: 26.2 us -> none  [shards(): lax.all_to_all(turned, 'tp', split_axis=1, concat_axis=0, tiled=True)]
    all_to_all x0 -> x1, waiting for transfers between devices: none -> 23.6 us  [shards(): lax.all_to_all(turned, 'tp', split_axis=1, concat_axis=0, tiled=True)]
    ppermute x7 -> x9, waiting for transfers between devices: 68.9 us -> 62.2 us  [the longest x1 24.6 us: product_and_reduce(): return keep + lax.ppermute(send, 'tp', tp_pairs(4))]
    all_to_all x0 -> x1, starting transfers between devices: none -> 4.41 us  [shards(): lax.all_to_all(turned, 'tp', split_axis=1, concat_axis=0, tiled=True)]
    squeeze x0 -> x3, other arithmetic: none -> 2.34 us  [the longest x2 2.23 us: halve_pair(): send = lax.dynamic_index_in_dim(split, 1 - low, 1, keepdims=False)]
    ppermute x7 -> x9, starting transfers between devices: 7.53 us -> 7.95 us  [the longest x1 1.58 us: product_and_reduce(): second = lax.ppermute(across_x[half:], 'seq', seq_pairs(2))]
  transfers between devices with their start and end apart: 7 -> 10, of which waited for: 6 -> 8; matrix products, arithmetic and copies ran while one was open for 8% -> 13% of each run, Pallas kernels for 0% -> 0%
where the time goes in v8:
time: 159 us; the launch traced here: 158 us
  waiting for transfers between devices  85.8 us (54%)
  blocking collectives  30.1 us (19%)
  matrix products  17.6 us (11%)
  starting transfers between devices  12.4 us (8%)
  other arithmetic  7.13 us (4%)
  local copies, waits for them, and re-layouts  5.15 us (3%)
    all_to_all x1, blocking collectives, shards(): spread = lax.all_to_all(part, 'tp', split_axis=0, concat_axis=1, tiled=True)  30.1 us
    ppermute x1, waiting for transfers between devices, product_and_reduce(): return keep + lax.ppermute(send, 'tp', tp_pairs(4))  24.6 us
    all_to_all x1, waiting for transfers between devices, shards(): lax.all_to_all(turned, 'tp', split_axis=1, concat_axis=0, tiled=True)  23.6 us
    ppermute x2, waiting for transfers between devices, halve_pair(): return keep + lax.ppermute(send, 'tp', tp_pairs(2))  21.4 us
    dot_general x4, matrix products, halve_pair(): jnp.dot(piece, down_weight, preferred_element_type=jnp.float32)  14.7 us
    ppermute x1, waiting for transfers between devices, product_and_reduce(): across_y = lax.ppermute(block, 'seq', seq_pairs(2))  11.4 us
    all_to_all x1, starting transfers between devices, shards(): lax.all_to_all(turned, 'tp', split_axis=1, concat_axis=0, tiled=True)  4.41 us
  transfers between devices with their start and end apart: 10, of which 8 were waited for; matrix products, arithmetic and copies ran while one was open for 13% of the time, Pallas kernels for 0%

profile of v8, /device:TPU:0, one launch (start us, length us, event | category | flops | bytes accessed | tf_op | source)
XLA Modules:
  0.0 158.4 jit_solution(14576403173758184576)
XLA Ops:
  0.0 30.1 %all_to_all.35 = bf16[8,16,3584]{2,1,0:T(8,128)(2,1)S(1)} all-to-all(bf16[8,16,3584]{2,1,0:T(8,128)(2,1)} %bitcast.84), channel_id=1, replica_groups=mesh['seq'=4,'tp'=8] {'tp'}, dimensions={0} | all-to-all | bytes 1835008 | tf_op jit(solution)/shard_map/all_to_all | solution.py:146
  30.6 0.5 reshape.30
  31.5 1.2 fusion.36
  32.8 1.7 %fusion.9 = bf16[16,32,896]{2,1,0:T(8,128)(2,1)S(1)} fusion(f32[32,32,1]{0,1,2:T(8,128)S(1)} %copy-done.6, f32[896,16,32]{0,2,1:T(8,128)S(1)} %fusion.36), kind=kOutput, calls=%fused_computation.14 | convolution fusion | flops 177078272 | bytes 2756608 | tf_op jit(solution)/shard_map/rbm,bc->rcm/dot_general | solution.py:50
  35.1 1.2 copy.10
  36.3 4.4 %all-to-all-start.1 = ((bf16[16,8,3584]{2,0,1:T(8,128)(2,1)}), bf16[16,8,3584]{2,0,1:T(8,128)(2,1)}, u32[]{:S(2)}, u32[]{:S(2)}) async-start(bf16[16,8,3584]{2,0,1:T(8,128)(2,1)} %copy.10), calls=%async_computation.1 | async-start | bytes 1835008 | tf_op jit(solution)/shard_map/all_to_all | solution.py:148
  40.7 23.6 %all-to-all-done.1 = bf16[16,8,3584]{2,0,1:T(8,128)(2,1)} async-done(((bf16[16,8,3584]{2,0,1:T(8,128)(2,1)}), bf16[16,8,3584]{2,0,1:T(8,128)(2,1)}, u32[]{:S(2)}, u32[]{:S(2)}) %all-to-all-start.1) | async-done | bytes 917536 | tf_op jit(solution)/shard_map/all_to_all | solution.py:148
  64.3 1.5 collective-permute-start.3
  65.8 1.5 collective-permute-start
  67.3 7.7 %fusion.2 = f32[1,2,64,2048]{3,2,1,0:T(8,128)S(1)} fusion(bf16[2,64,3584]{2,1,0:T(8,128)(2,1)} %bitcast.7, bf16[3584,2048]{1,0:T(8,128)(2,1)} %param.6), kind=kOutput, calls=%fused_computation.10 | convolution fusion | flops 1879048192 | bytes 16646144 | tf_op jit(solution)/shard_map/dot_general | solution.py:115
  75.0 11.4 %collective-permute-done.3 = bf16[128,3584]{1,0:T(8,128)(2,1)S(1)} collective-permute-done((bf16[128,3584]{1,0:T(8,128)(2,1)}, bf16[128,3584]{1,0:T(8,128)(2,1)S(1)}, u32[]{:S(2)}, u32[]{:S(2)}) %collective-permute-start.3) | collective-permute-done | bytes 917536 | tf_op jit(solution)/shard_map/ppermute | solution.py:108
  86.4 1.6 collective-permute-start.4
  88.0 1.6 %collective-permute-start.5 = (bf16[64,3584]{1,0:T(8,128)(2,1)S(1)}, bf16[64,3584]{1,0:T(8,128)(2,1)S(1)}, u32[]{:S(2)}, u32[]{:S(2)}) collective-permute-start(bf16[64,3584]{1,0:T(8,128)(2,1)S(1)} %slice.9), channel_id=1, source_target_pairs={{0,16},{8,24},{16,0},{24,8},{1,17},{9,25},{17,1},{25,9},{2,18},{10... | collective-permute-start | bytes 1376264 | tf_op jit(solution)/shard_map/ppermute | solution.py:110
  89.6 2.3 %fusion.37 = f32[128,2048]{1,0:T(8,128)S(1)} fusion(bf16[128,3584]{1,0:T(8,128)(2,1)S(1)} %collective-permute-done, bf16[3584,2048]{1,0:T(8,128)(2,1)S(1)} %bitcast.76), kind=kOutput, calls=%fused_computation.48 | convolution fusion | flops 1879048192 | bytes 16646144 | tf_op jit(solution)/shard_map/dot_general | solution.py:115
  92.0 1.2 fusion.18
  93.2 2.3 %fusion.38 = f32[128,2048]{1,0:T(8,128)S(1)} fusion(bf16[128,3584]{1,0:T(8,128)(2,1)S(1)} %collective-permute-done.3, bf16[3584,2048]{1,0:T(8,128)(2,1)S(1)} %bitcast.76), kind=kOutput, calls=%fused_computation.49 | convolution fusion | flops 1879048192 | bytes 16646144 | tf_op jit(solution)/shard_map/dot_general | solution.py:115
  95.6 2.1 %collective-permute-done.4 = bf16[64,3584]{1,0:T(8,128)(2,1)S(1)} collective-permute-done((bf16[64,3584]{1,0:T(8,128)(2,1)S(1)}, bf16[64,3584]{1,0:T(8,128)(2,1)S(1)}, u32[]{:S(2)}, u32[]{:S(2)}) %collective-permute-start.4) | collective-permute-done | bytes 458784 | tf_op jit(solution)/shard_map/ppermute | solution.py:109
  97.7 1.3 collective-permute-done.5
  99.0 2.3 %fusion.22 = f32[128,2048]{1,0:T(8,128)S(1)} fusion(bf16[3584,2048]{1,0:T(8,128)(2,1)S(1)} %bitcast.76, bf16[64,3584]{1,0:T(8,128)(2,1)S(1)} %collective-permute-done.5, bf16[64,3584]{1,0:T(8,128)(2,1)S(1)} %collective-permute-done.4), kind=kOutput, calls=%fused_computation.29 | convolution fusion | flops 1880883200 | bytes 16646144 | tf_op jit(solution)/shard_map/dot_general | solution.py:115
  101.4 1.0 copy-done
  102.3 1.1 fusion.13
  103.4 1.5 fusion.21
  105.1 1.4 collective-permute-done.6
  106.4 1.3 fusion.16
  107.8 0.9 dynamic-slice_bitcast_fusion
  108.6 0.7 collective-permute-start.7
  109.3 10.5 %collective-permute-done.2 = f32[64,2048]{1,0:T(8,128)S(1)} collective-permute-done((f32[64,2048]{1,0:T(8,128)S(1)}, f32[64,2048]{1,0:T(8,128)S(1)}, u32[]{:S(2)}, u32[]{:S(2)}) %collective-permute-start.2) | collective-permute-done | bytes 524320 | tf_op jit(solution)/shard_map/ppermute | solution.py:124
  119.8 10.9 %collective-permute-done.7 = f32[64,2048]{1,0:T(8,128)} collective-permute-done((f32[64,2048]{1,0:T(8,128)}, f32[64,2048]{1,0:T(8,128)}, u32[]{:S(2)}, u32[]{:S(2)}) %collective-permute-start.7) | collective-permute-done | bytes 524320 | tf_op jit(solution)/shard_map/ppermute | solution.py:124
  130.7 1.1 fusion.33
  131.9 1.0 collective-permute-start.8
  133.0 24.6 %collective-permute-done.8 = f32[64,2048]{1,0:T(8,128)S(1)} collective-permute-done((f32[64,2048]{1,0:T(8,128)S(1)}, f32[64,2048]{1,0:T(8,128)S(1)}, u32[]{:S(2)}, u32[]{:S(2)}) %collective-permute-start.8) | collective-permute-done | bytes 524320 | tf_op jit(solution)/shard_map/ppermute | solution.py:132
  157.6 0.8 fusion.32
  (38 shorter events, 1.8 us)
Async XLA Ops:
  30.1 1.4 copy-start.8
  31.5 1.2 copy-start.6
  35.0 54.6 %slice-start = ((s8[14680064]{0:T(1024)(128)(4,1)}), s8[2097152]{0:T(1024)(128)(4,1)S(1)}, s32[]{:S(2)}) async-start(s8[14680064]{0:T(1024)(128)(4,1)} %bitcast.75), calls=%async_computation.2 | async-start | bytes 4194304
  36.3 28.0 %all-to-all-start.1 = ((bf16[16,8,3584]{2,0,1:T(8,128)(2,1)}), bf16[16,8,3584]{2,0,1:T(8,128)(2,1)}, u32[]{:S(2)}, u32[]{:S(2)}) async-start(bf16[16,8,3584]{2,0,1:T(8,128)(2,1)} %copy.10), calls=%async_computation.1 | async-start | bytes 1835008 | tf_op jit(solution)/shard_map/all_to_all | solution.py:148
  64.3 22.1 %collective-permute-start.3 = (bf16[128,3584]{1,0:T(8,128)(2,1)}, bf16[128,3584]{1,0:T(8,128)(2,1)S(1)}, u32[]{:S(2)}, u32[]{:S(2)}) collective-permute-start(bf16[128,3584]{1,0:T(8,128)(2,1)} %bitcast.10), channel_id=1, source_target_pairs={{0,16},{8,24},{16,0},{24,8},{1,17},{9,25},{17,1},{25,9},{2,18},{10... | collective-permute-start | bytes 2752520 | tf_op jit(solution)/shard_map/ppermute | solution.py:108
  65.8 22.2 %collective-permute-start = (bf16[128,3584]{1,0:T(8,128)(2,1)}, bf16[128,3584]{1,0:T(8,128)(2,1)S(1)}, u32[]{:S(2)}, u32[]{:S(2)}) collective-permute-start(bf16[128,3584]{1,0:T(8,128)(2,1)} %bitcast.10), channel_id=1, source_target_pairs={{0,8},{8,0},{16,24},{24,16},{1,9},{9,1},{17,25},{25,17},{2,10},{10... | collective-permute-start | bytes 2752520 | tf_op jit(solution)/shard_map/ppermute | solution.py:107
  67.3 22.3 %slice-start.1 = ((s8[14680064]{0:T(1024)(128)(4,1)}), s8[4194304]{0:T(1024)(128)(4,1)S(1)}, s32[]{:S(2)}) async-start(s8[14680064]{0:T(1024)(128)(4,1)} %bitcast.75), calls=%async_computation.3 | async-start | bytes 8388608
  67.3 22.3 %slice-start.2 = ((s8[14680064]{0:T(1024)(128)(4,1)}), s8[4194304]{0:T(1024)(128)(4,1)S(1)}, s32[]{:S(2)}) async-start(s8[14680064]{0:T(1024)(128)(4,1)} %bitcast.75), calls=%async_computation.4 | async-start | bytes 8388608
  67.3 22.3 %slice-start.3 = ((s8[14680064]{0:T(1024)(128)(4,1)}), s8[4194304]{0:T(1024)(128)(4,1)S(1)}, s32[]{:S(2)}) async-start(s8[14680064]{0:T(1024)(128)(4,1)} %bitcast.75), calls=%async_computation.5 | async-start | bytes 8388608
  86.4 11.2 %collective-permute-start.4 = (bf16[64,3584]{1,0:T(8,128)(2,1)S(1)}, bf16[64,3584]{1,0:T(8,128)(2,1)S(1)}, u32[]{:S(2)}, u32[]{:S(2)}) collective-permute-start(bf16[64,3584]{1,0:T(8,128)(2,1)S(1)} %slice.8), channel_id=1, source_target_pairs={{0,8},{8,0},{16,24},{24,16},{1,9},{9,1},{17,25},{25,17},{2,10},{10... | collective-permute-start | bytes 1376264 | tf_op jit(solution)/shard_map/ppermute | solution.py:109
  88.0 10.9 %collective-permute-start.5 = (bf16[64,3584]{1,0:T(8,128)(2,1)S(1)}, bf16[64,3584]{1,0:T(8,128)(2,1)S(1)}, u32[]{:S(2)}, u32[]{:S(2)}) collective-permute-start(bf16[64,3584]{1,0:T(8,128)(2,1)S(1)} %slice.9), channel_id=1, source_target_pairs={{0,16},{8,24},{16,0},{24,8},{1,17},{9,25},{17,1},{25,9},{2,18},{10... | collective-permute-start | bytes 1376264 | tf_op jit(solution)/shard_map/ppermute | solution.py:110
  92.0 3.5 %copy-start.4 = (f32[128,2048]{1,0:T(8,128)}, f32[128,2048]{1,0:T(8,128)S(1)}, u32[]{:S(2)}) copy-start(f32[128,2048]{1,0:T(8,128)S(1)} %fusion.37) | copy-start | bytes 3145732
  93.2 10.2 %collective-permute-start.1 = (f32[2,64,2048]{2,1,0:T(8,128)}, f32[2,64,2048]{2,1,0:T(8,128)}, u32[]{:S(2)}, u32[]{:S(2)}) collective-permute-start(f32[2,64,2048]{2,1,0:T(8,128)} %fusion.18), channel_id=1, source_target_pairs={{0,1},{1,0},{2,3},{3,2},{4,5},{5,4},{6,7},{7,6},{8,9},{9,8},{10,11... | collective-permute-start | bytes 3145736 | tf_op jit(solution)/shard_map/ppermute | solution.py:120
  95.6 5.8 %copy-start.2 = (f32[128,2048]{1,0:T(8,128)}, f32[128,2048]{1,0:T(8,128)S(1)}, u32[]{:S(2)}) copy-start(f32[128,2048]{1,0:T(8,128)S(1)} %fusion.38) | copy-start | bytes 3145732
  101.3 1.0 copy-start
  101.4 2.1 %copy-start.5 = (f32[128,2048]{1,0:T(8,128)S(1)}, f32[128,2048]{1,0:T(8,128)}, u32[]{:S(2)}) copy-start(f32[128,2048]{1,0:T(8,128)} %copy-done.4) | copy-start | bytes 3145732
  103.4 3.0 %collective-permute-start.6 = (f32[2,64,2048]{2,1,0:T(8,128)}, f32[2,64,2048]{2,1,0:T(8,128)}, u32[]{:S(2)}, u32[]{:S(2)}) collective-permute-start(f32[2,64,2048]{2,1,0:T(8,128)} %fusion.13), channel_id=1, source_target_pairs={{0,1},{1,0},{2,3},{3,2},{4,5},{5,4},{6,7},{7,6},{8,9},{9,8},{10,11... | collective-permute-start | bytes 3145736 | tf_op jit(solution)/shard_map/ppermute | solution.py:120
  103.4 3.0 %copy-start.1 = (f32[128,2048]{1,0:T(8,128)S(1)}, f32[128,2048]{1,0:T(8,128)}, u32[]{:S(2)}) copy-start(f32[128,2048]{1,0:T(8,128)} %copy-done) | copy-start | bytes 3145732
  103.4 3.0 %copy-start.3 = (f32[128,2048]{1,0:T(8,128)S(1)}, f32[128,2048]{1,0:T(8,128)}, u32[]{:S(2)}) copy-start(f32[128,2048]{1,0:T(8,128)} %copy-done.2) | copy-start | bytes 3145732
  105.0 14.8 %collective-permute-start.2 = (f32[64,2048]{1,0:T(8,128)S(1)}, f32[64,2048]{1,0:T(8,128)S(1)}, u32[]{:S(2)}, u32[]{:S(2)}) collective-permute-start(f32[64,2048]{1,0:T(8,128)S(1)} %dynamic-slice_bitcast_fusion.1), channel_id=1, source_target_pairs={{0,2},{1,3},{2,0},{3,1},{4,6},{5,7},{6,4},{7,5},{8,10},{9,11},{10,... | collective-permute-start | bytes 1572872 | tf_op jit(solution)/shard_map/ppermute | solution.py:124
  108.6 22.1 %collective-permute-start.7 = (f32[64,2048]{1,0:T(8,128)}, f32[64,2048]{1,0:T(8,128)}, u32[]{:S(2)}, u32[]{:S(2)}) collective-permute-start(f32[64,2048]{1,0:T(8,128)} %dynamic-slice_bitcast_fusion), channel_id=1, source_target_pairs={{0,2},{1,3},{2,0},{3,1},{4,6},{5,7},{6,4},{7,5},{8,10},{9,11},{10,... | collective-permute-start | bytes 1572872 | tf_op jit(solution)/shard_map/ppermute | solution.py:124
  109.3 48.3 %copy-start.7 = (f32[2048]{0:T(1024)S(1)}, f32[2048]{0:T(1024)}, u32[]{:S(2)}) copy-start(f32[2048]{0:T(1024)} %param.7) | copy-start | bytes 24580
  131.9 25.7 %collective-permute-start.8 = (f32[64,2048]{1,0:T(8,128)S(1)}, f32[64,2048]{1,0:T(8,128)S(1)}, u32[]{:S(2)}, u32[]{:S(2)}) collective-permute-start(f32[64,2048]{1,0:T(8,128)S(1)} %fusion.27), channel_id=1, source_target_pairs={{0,4},{1,5},{2,6},{3,7},{4,0},{5,1},{6,2},{7,3},{8,12},{9,13},{10,... | collective-permute-start | bytes 1572872 | tf_op jit(solution)/shard_map/ppermute | solution.py:132

commit v9 on v8

--- a/solution.py
+++ b/solution.py
@@ -8,7 +8,7 @@
 
 PALEY = 28
 INNER = 32
-CHUNKS = 1
+CHUNKS = 2
 
 
 def paley_table():
@@ -140,17 +140,24 @@
     owned = tokens // groups
     piece = owned // CHUNKS
     grouped = hidden.reshape(groups, CHUNKS, piece, units)
+    fast_path = seq_count == 4 and tp_count == 8
     outputs = []
+    pending = None
     for chunk in range(CHUNKS):
         part = grouped[:, chunk].reshape(groups * piece, units)
+        if pending is not None:
+            pending, part = lax.optimization_barrier((pending, part))
+            outputs.append(product_and_reduce(pending, down_weight))
         spread = lax.all_to_all(part, "tp", split_axis=0, concat_axis=1, tiled=True)
         turned = rotate(spread)
         rotated = lax.all_to_all(turned, "tp", split_axis=1, concat_axis=0, tiled=True)
-        if seq_count == 4 and tp_count == 8:
-            outputs.append(product_and_reduce(rotated, down_weight))
+        if fast_path:
+            pending = rotated
         else:
             partial_terms = gathered_product(rotated, down_weight)
             outputs.append(scatter_sum_tp(partial_terms))
+    if pending is not None:
+        outputs.append(product_and_reduce(pending, down_weight))
     summed = jnp.concatenate(outputs, axis=0)
     return (summed * channel_scale[None, :]).astype(jnp.bfloat16)
 

time: 159 us -> 171 us (1.075)
  matrix products: 17.6 us -> 47.4 us
  waiting for transfers between devices: 85.8 us -> 57.5 us
  starting transfers between devices: 12.4 us -> 30.7 us
  blocking collectives: 30.1 us -> 20.1 us
  local copies, waits for them, and re-layouts: 5.15 us -> 7.36 us
    dot_general x4 -> x8, matrix products: 14.7 us -> 40.4 us  [halve_pair(): jnp.dot(piece, down_weight, preferred_element_type=jnp.float32)]
    ppermute x1 -> x2, waiting for transfers between devices: 24.6 us -> 13.4 us  [product_and_reduce(): return keep + lax.ppermute(send, 'tp', tp_pairs(4))]
    ppermute x1 -> x2, waiting for transfers between devices: 11.4 us -> 0.8 us  [product_and_reduce(): across_y = lax.ppermute(block, 'seq', seq_pairs(2))]
    all_to_all x1, blocking collectives: 30.1 us -> 20.1 us  [shards(): spread = lax.all_to_all(part, 'tp', split_axis=0, concat_axis=1, tiled=True)]
    all_to_all x1 -> x2, waiting for transfers between devices: 23.6 us -> 13.8 us  [shards(): lax.all_to_all(turned, 'tp', split_axis=1, concat_axis=0, tiled=True)]
    ppermute x2 -> x4, waiting for transfers between devices: 21.4 us -> 28.8 us  [halve_pair(): return keep + lax.ppermute(send, 'tp', tp_pairs(2))]
    all_to_all x0 -> x1, starting transfers between devices: none -> 4.3 us  [shards(): spread = lax.all_to_all(part, 'tp', split_axis=0, concat_axis=1, tiled=True)]
    all_to_all x1 -> x2, starting transfers between devices: 4.41 us -> 8.27 us  [shards(): lax.all_to_all(turned, 'tp', split_axis=1, concat_axis=0, tiled=True)]
  transfers between devices with their start and end apart: 10 -> 21, of which waited for: 8 -> 8; matrix products, arithmetic and copies ran while one was open for 13% -> 31% of each run, Pallas kernels for 0% -> 0%
where the time goes in v9:
time: 171 us; the launch traced here: 170 us
  waiting for transfers between devices  57.5 us (34%)
  matrix products  47.4 us (28%)
  starting transfers between devices  30.7 us (18%)
  blocking collectives  20.1 us (12%)
  local copies, waits for them, and re-layouts  7.36 us (4%)
  other arithmetic  6.39 us (4%)
    dot_general x8, matrix products, halve_pair(): jnp.dot(piece, down_weight, preferred_element_type=jnp.float32)  40.4 us
    ppermute x4, waiting for transfers between devices, halve_pair(): return keep + lax.ppermute(send, 'tp', tp_pairs(2))  28.8 us
    all_to_all x1, blocking collectives, shards(): spread = lax.all_to_all(part, 'tp', split_axis=0, concat_axis=1, tiled=True)  20.1 us
    all_to_all x2, waiting for transfers between devices, shards(): lax.all_to_all(turned, 'tp', split_axis=1, concat_axis=0, tiled=True)  13.8 us
    ppermute x2, waiting for transfers between devices, product_and_reduce(): return keep + lax.ppermute(send, 'tp', tp_pairs(4))  13.4 us
    all_to_all x2, starting transfers between devices, shards(): lax.all_to_all(turned, 'tp', split_axis=1, concat_axis=0, tiled=True)  8.27 us
    all_to_all x1, starting transfers between devices, shards(): spread = lax.all_to_all(part, 'tp', split_axis=0, concat_axis=1, tiled=True)  4.3 us
    dot_general x2, matrix products, rotate(): jnp.einsum('rbl,lm->rbm', blocks, inner_table, preferred_element_type=jnp...  4.22 us
  transfers between devices with their start and end apart: 21, of which 8 were waited for; matrix products, arithmetic and copies ran while one was open for 31% of the time, Pallas kernels for 0%

profile of v9, /device:TPU:0, one launch (start us, length us, event | category | flops | bytes accessed | tf_op | source)
XLA Modules:
  0.0 170.0 jit_solution(16226957812745517323)
XLA Ops:
  0.0 2.0 %fusion.54 = (bf16[2,1,32,3584]{3,2,1,0:T(8,128)(2,1)}, bf16[2,1,32,3584]{3,2,1,0:T(8,128)(2,1)S(1)}) fusion(bf16[2,2,32,3584]{3,2,1,0:T(8,128)(2,1)} %bitcast.149), kind=kLoop, calls=%fused_computation.88 | loop fusion | bytes 1835008 | tf_op jit(solution)/shard_map/slice | solution.py:147
  2.0 20.1 %all_to_all.70 = bf16[8,8,3584]{2,1,0:T(8,128)(2,1)S(1)} all-to-all(bf16[8,8,3584]{2,1,0:T(8,128)(2,1)S(1)} %bitcast.147), channel_id=1, replica_groups=mesh['seq'=4,'tp'=8] {'tp'}, dimensions={0} | all-to-all | bytes 917504 | tf_op jit(solution)/shard_map/all_to_all | solution.py:151
  22.5 2.1 %convolution_bitcast_fusion = f32[8,32,896]{2,1,0:T(8,128)S(1)} fusion(bf16[896,896,1]{1,0,2:T(8,128)(2,1)} %constant.141, bf16[8,32,896]{2,1,0:T(8,128)(2,1)S(1)} %reshape.57), kind=kOutput, calls=%fused_computation.5 | convolution fusion | flops 411041792 | bytes 2981888 | tf_op jit(solution)/shard_map/rbl,lm->rbm/dot_general | solution.py:49
  24.6 1.8 %fusion.8 = bf16[8,32,896]{2,1,0:T(8,128)(2,1)S(1)} fusion(f32[8,32,896]{2,1,0:T(8,128)S(1)} %convolution_bitcast_fusion, f32[32,32,1]{0,1,2:T(8,128)} %constant.142), kind=kOutput, calls=%fused_computation.25 | convolution fusion | flops 88539136 | bytes 1380352 | tf_op jit(solution)/shard_map/rbm,bc->rcm/dot_general | solution.py:50
  27.6 3.5 %all-to-all-start.1 = ((bf16[8,8,3584]{2,0,1:T(8,128)(2,1)}), bf16[8,8,3584]{2,0,1:T(8,128)(2,1)S(1)}, u32[]{:S(2)}, u32[]{:S(2)}) async-start(bf16[8,8,3584]{2,0,1:T(8,128)(2,1)} %copy.16), calls=%async_computation.1 | async-start | bytes 917504 | tf_op jit(solution)/shard_map/all_to_all | solution.py:153
  31.2 13.8 %all-to-all-done.1 = bf16[8,8,3584]{2,0,1:T(8,128)(2,1)S(1)} async-done(((bf16[8,8,3584]{2,0,1:T(8,128)(2,1)}), bf16[8,8,3584]{2,0,1:T(8,128)(2,1)S(1)}, u32[]{:S(2)}, u32[]{:S(2)}) %all-to-all-start.1) | async-done | bytes 458784 | tf_op jit(solution)/shard_map/all_to_all | solution.py:153
  44.9 1.5 collective-permute-start.3
  46.5 1.5 collective-permute-start
  47.9 4.3 %all-to-all-start.2 = ((bf16[8,8,3584]{2,1,0:T(8,128)(2,1)}), bf16[8,8,3584]{2,1,0:T(8,128)(2,1)}, u32[]{:S(2)}, u32[]{:S(2)}) async-start(bf16[8,8,3584]{2,1,0:T(8,128)(2,1)} %bitcast.26), calls=%async_computation.2 | async-start | bytes 917504 | tf_op jit(solution)/shard_map/all_to_all | solution.py:151
  52.3 8.0 %fusion.55 = f32[64,2048]{1,0:T(8,128)S(1)} fusion(bf16[64,3584]{1,0:T(8,128)(2,1)S(1)} %bitcast.143, bf16[3584,2048]{1,0:T(8,128)(2,1)} %param.8), kind=kOutput, calls=%fused_computation.89 | convolution fusion | flops 939524096 | bytes 15663104 | tf_op jit(solution)/shard_map/dot_general | solution.py:115
  62.5 3.7 %fusion.56 = f32[64,2048]{1,0:T(8,128)S(1)} fusion(bf16[64,3584]{1,0:T(8,128)(2,1)} %collective-permute-done, bf16[3584,2048]{1,0:T(8,128)(2,1)S(1)} %bitcast.126), kind=kOutput, calls=%fused_computation.90 | convolution fusion | flops 939524096 | bytes 15663104 | tf_op jit(solution)/shard_map/dot_general | solution.py:115
  67.1 3.7 %fusion.57 = f32[64,2048]{1,0:T(8,128)S(1)} fusion(bf16[64,3584]{1,0:T(8,128)(2,1)} %copy-done.1, bf16[3584,2048]{1,0:T(8,128)(2,1)S(1)} %bitcast.126), kind=kOutput, calls=%fused_computation.91 | convolution fusion | flops 939524096 | bytes 15663104 | tf_op jit(solution)/shard_map/dot_general | solution.py:115
  70.8 3.6 %fusion.30 = f32[64,2048]{1,0:T(8,128)} fusion(bf16[3584,2048]{1,0:T(8,128)(2,1)S(1)} %bitcast.126, bf16[32,3584]{1,0:T(8,128)(2,1)S(1)} %collective-permute-done.5, bf16[32,3584]{1,0:T(8,128)(2,1)S(1)} %collective-permute-done.4), kind=kOutput, calls=%fused_computation.56 | convolution fusion | flops 940441600 | bytes 15663104 | tf_op jit(solution)/shard_map/dot_general | solution.py:115
  74.4 1.8 %fusion.20 = f32[2,32,2048]{2,1,0:T(8,128)} fusion(s32[]{:T(128)S(6)} %select_n.86, f32[1,2,32,2048]{3,2,1,0:T(8,128)S(1)} %bitcast.131, f32[1,2,32,2048]{3,2,1,0:T(8,128)} %bitcast.18), kind=kLoop, calls=%fused_computation.45 | loop fusion | flops 131072 | bytes 1572868 | tf_op jit(solution)/shard_map/jit(dynamic_index_in_dim)/squeeze | solution.py:119
  78.1 2.1 %fusion.58 = f32[8,32,896]{2,1,0:T(8,128)S(1)} fusion(bf16[8,32,896]{2,1,0:T(8,128)(2,1)S(1)} %reshape.58, bf16[896,896,1]{1,0,2:T(8,128)(2,1)} %constant.141), kind=kOutput, calls=%fused_computation.92 | convolution fusion | flops 411041792 | bytes 2981888 | tf_op jit(solution)/shard_map/rbl,lm->rbm/dot_general | solution.py:49
  82.4 4.8 %all-to-all-start.3 = ((bf16[8,8,3584]{2,0,1:T(8,128)(2,1)}), bf16[8,8,3584]{2,0,1:T(8,128)(2,1)S(1)}, u32[]{:S(2)}, u32[]{:S(2)}) async-start(bf16[8,8,3584]{2,0,1:T(8,128)(2,1)} %copy.18), calls=%async_computation.3 | async-start | bytes 917504 | tf_op jit(solution)/shard_map/all_to_all | solution.py:153
  87.2 1.2 fusion.28
  88.4 2.1 %collective-permute-start.2 = (f32[32,2048]{1,0:T(8,128)S(1)}, f32[32,2048]{1,0:T(8,128)S(1)}, u32[]{:S(2)}, u32[]{:S(2)}) collective-permute-start(f32[32,2048]{1,0:T(8,128)S(1)} %dynamic-slice_bitcast_fusion.3), channel_id=1, source_target_pairs={{0,2},{1,3},{2,0},{3,1},{4,6},{5,7},{6,4},{7,5},{8,10},{9,11},{10,... | collective-permute-start | bytes 786440 | tf_op jit(solution)/shard_map/ppermute | solution.py:124
  91.7 12.1 %collective-permute-done.2 = f32[32,2048]{1,0:T(8,128)S(1)} collective-permute-done((f32[32,2048]{1,0:T(8,128)S(1)}, f32[32,2048]{1,0:T(8,128)S(1)}, u32[]{:S(2)}, u32[]{:S(2)}) %collective-permute-start.2) | collective-permute-done | bytes 262176 | tf_op jit(solution)/shard_map/ppermute | solution.py:124
  103.9 5.1 %collective-permute-done.7 = f32[32,2048]{1,0:T(8,128)S(1)} collective-permute-done((f32[32,2048]{1,0:T(8,128)S(1)}, f32[32,2048]{1,0:T(8,128)S(1)}, u32[]{:S(2)}, u32[]{:S(2)}) %collective-permute-start.7) | collective-permute-done | bytes 262176 | tf_op jit(solution)/shard_map/ppermute | solution.py:124
  109.1 2.5 %collective-permute-start.8 = (f32[32,2048]{1,0:T(8,128)S(1)}, f32[32,2048]{1,0:T(8,128)S(1)}, u32[]{:S(2)}, u32[]{:S(2)}) collective-permute-start(f32[32,2048]{1,0:T(8,128)S(1)} %fusion.44), channel_id=1, source_target_pairs={{0,4},{1,5},{2,6},{3,7},{4,0},{5,1},{6,2},{7,3},{8,12},{9,13},{10,... | collective-permute-start | bytes 786440 | tf_op jit(solution)/shard_map/ppermute | solution.py:132
  111.7 1.5 collective-permute-start.12
  113.2 1.5 collective-permute-start.9
  114.7 8.0 %fusion.2 = f32[1,2,32,2048]{3,2,1,0:T(8,128)S(1)} fusion(bf16[2,32,3584]{2,1,0:T(8,128)(2,1)S(1)} %bitcast.146, bf16[3584,2048]{1,0:T(8,128)(2,1)} %param.8), kind=kOutput, calls=%fused_computation.2 | convolution fusion | flops 939524096 | bytes 15663104 | tf_op jit(solution)/shard_map/dot_general | solution.py:115
  123.5 1.5 collective-permute-start.13
  125.1 1.6 collective-permute-start.14
  126.6 8.2 %fusion.59 = f32[64,2048]{1,0:T(8,128)S(1)} fusion(bf16[64,3584]{1,0:T(8,128)(2,1)S(1)} %collective-permute-done.9, bf16[3584,2048]{1,0:T(8,128)(2,1)} %param.8), kind=kOutput, calls=%fused_computation.93 | convolution fusion | flops 939524096 | bytes 15663104 | tf_op jit(solution)/shard_map/dot_general | solution.py:115
  135.0 2.7 %fusion.60 = f32[64,2048]{1,0:T(8,128)S(1)} fusion(bf16[64,3584]{1,0:T(8,128)(2,1)S(1)} %collective-permute-done.12, bf16[3584,2048]{1,0:T(8,128)(2,1)S(1)} %bitcast.128), kind=kOutput, calls=%fused_computation.94 | convolution fusion | flops 939524096 | bytes 15663104 | tf_op jit(solution)/shard_map/dot_general | solution.py:115
  137.8 2.7 %fusion.34 = f32[64,2048]{1,0:T(8,128)S(1)} fusion(bf16[3584,2048]{1,0:T(8,128)(2,1)S(1)} %bitcast.128, bf16[32,3584]{1,0:T(8,128)(2,1)S(1)} %collective-permute-done.14, bf16[32,3584]{1,0:T(8,128)(2,1)S(1)} %collective-permute-done.13), kind=kOutput, calls=%fused_computation.60 | convolution fusion | flops 940441600 | bytes 15663104 | tf_op jit(solution)/shard_map/dot_general | solution.py:115
  143.4 7.0 %collective-permute-done.11 = f32[32,2048]{1,0:T(8,128)S(1)} collective-permute-done((f32[32,2048]{1,0:T(8,128)S(1)}, f32[32,2048]{1,0:T(8,128)S(1)}, u32[]{:S(2)}, u32[]{:S(2)}) %collective-permute-start.11) | collective-permute-done | bytes 262176 | tf_op jit(solution)/shard_map/ppermute | solution.py:124
  150.4 4.7 %collective-permute-done.16 = f32[32,2048]{1,0:T(8,128)S(1)} collective-permute-done((f32[32,2048]{1,0:T(8,128)S(1)}, f32[32,2048]{1,0:T(8,128)S(1)}, u32[]{:S(2)}, u32[]{:S(2)}) %collective-permute-start.16) | collective-permute-done | bytes 262176 | tf_op jit(solution)/shard_map/ppermute | solution.py:124
  155.8 13.4 %collective-permute-done.17 = f32[32,2048]{1,0:T(8,128)S(1)} collective-permute-done((f32[32,2048]{1,0:T(8,128)S(1)}, f32[32,2048]{1,0:T(8,128)S(1)}, u32[]{:S(2)}, u32[]{:S(2)}) %collective-permute-start.17) | collective-permute-done | bytes 262176 | tf_op jit(solution)/shard_map/ppermute | solution.py:132
  (83 shorter events, 15.6 us)
Async XLA Ops:
  24.6 37.9 %slice-start = ((s8[14680064]{0:T(1024)(128)(4,1)}), s8[2097152]{0:T(1024)(128)(4,1)S(1)}, s32[]{:S(2)}) async-start(s8[14680064]{0:T(1024)(128)(4,1)} %bitcast.125), calls=%async_computation.4 | async-start | bytes 4194304
  27.6 17.4 %all-to-all-start.1 = ((bf16[8,8,3584]{2,0,1:T(8,128)(2,1)}), bf16[8,8,3584]{2,0,1:T(8,128)(2,1)S(1)}, u32[]{:S(2)}, u32[]{:S(2)}) async-start(bf16[8,8,3584]{2,0,1:T(8,128)(2,1)} %copy.16), calls=%async_computation.1 | async-start | bytes 917504 | tf_op jit(solution)/shard_map/all_to_all | solution.py:153
  44.9 15.3 %collective-permute-start.3 = (bf16[64,3584]{1,0:T(8,128)(2,1)S(1)}, bf16[64,3584]{1,0:T(8,128)(2,1)S(1)}, u32[]{:S(2)}, u32[]{:S(2)}) collective-permute-start(bf16[64,3584]{1,0:T(8,128)(2,1)S(1)} %bitcast.141), channel_id=1, source_target_pairs={{0,16},{8,24},{16,0},{24,8},{1,17},{9,25},{17,1},{25,9},{2,18},{10... | collective-permute-start | bytes 1376264 | tf_op jit(solution)/shard_map/ppermute | solution.py:108
  46.5 14.5 %collective-permute-start = (bf16[64,3584]{1,0:T(8,128)(2,1)S(1)}, bf16[64,3584]{1,0:T(8,128)(2,1)}, u32[]{:S(2)}, u32[]{:S(2)}) collective-permute-start(bf16[64,3584]{1,0:T(8,128)(2,1)S(1)} %bitcast.142), channel_id=1, source_target_pairs={{0,8},{8,0},{16,24},{24,16},{1,9},{9,1},{17,25},{25,17},{2,10},{10... | collective-permute-start | bytes 1376264 | tf_op jit(solution)/shard_map/ppermute | solution.py:107
  47.9 28.7 %all-to-all-start.2 = ((bf16[8,8,3584]{2,1,0:T(8,128)(2,1)}), bf16[8,8,3584]{2,1,0:T(8,128)(2,1)}, u32[]{:S(2)}, u32[]{:S(2)}) async-start(bf16[8,8,3584]{2,1,0:T(8,128)(2,1)} %bitcast.26), calls=%async_computation.2 | async-start | bytes 917504 | tf_op jit(solution)/shard_map/all_to_all | solution.py:151
  52.3 10.2 %slice-start.1 = ((s8[14680064]{0:T(1024)(128)(4,1)}), s8[4194304]{0:T(1024)(128)(4,1)S(1)}, s32[]{:S(2)}) async-start(s8[14680064]{0:T(1024)(128)(4,1)} %bitcast.125), calls=%async_computation.5 | async-start | bytes 8388608
  52.3 10.2 %slice-start.2 = ((s8[14680064]{0:T(1024)(128)(4,1)}), s8[4194304]{0:T(1024)(128)(4,1)S(1)}, s32[]{:S(2)}) async-start(s8[14680064]{0:T(1024)(128)(4,1)} %bitcast.125), calls=%async_computation.6 | async-start | bytes 8388608
  52.3 10.2 %slice-start.3 = ((s8[14680064]{0:T(1024)(128)(4,1)}), s8[4194304]{0:T(1024)(128)(4,1)S(1)}, s32[]{:S(2)}) async-start(s8[14680064]{0:T(1024)(128)(4,1)} %bitcast.125), calls=%async_computation.7 | async-start | bytes 8388608
  60.3 10.5 %collective-permute-start.4 = (bf16[32,3584]{1,0:T(8,128)(2,1)S(1)}, bf16[32,3584]{1,0:T(8,128)(2,1)S(1)}, u32[]{:S(2)}, u32[]{:S(2)}) collective-permute-start(bf16[32,3584]{1,0:T(8,128)(2,1)S(1)} %slice.26), channel_id=1, source_target_pairs={{0,8},{8,0},{16,24},{24,16},{1,9},{9,1},{17,25},{25,17},{2,10},{10... | collective-permute-start | bytes 688136 | tf_op jit(solution)/shard_map/ppermute | solution.py:109
  61.9 8.9 %collective-permute-start.5 = (bf16[32,3584]{1,0:T(8,128)(2,1)S(1)}, bf16[32,3584]{1,0:T(8,128)(2,1)S(1)}, u32[]{:S(2)}, u32[]{:S(2)}) collective-permute-start(bf16[32,3584]{1,0:T(8,128)(2,1)S(1)} %slice.27), channel_id=1, source_target_pairs={{0,16},{8,24},{16,0},{24,8},{1,17},{9,25},{17,1},{25,9},{2,18},{10... | collective-permute-start | bytes 688136 | tf_op jit(solution)/shard_map/ppermute | solution.py:110
  66.2 8.2 %copy-start = (f32[64,2048]{1,0:T(8,128)}, f32[64,2048]{1,0:T(8,128)S(1)}, u32[]{:S(2)}) copy-start(f32[64,2048]{1,0:T(8,128)S(1)} %fusion.56) | copy-start | bytes 1572868
  67.1 20.0 %collective-permute-start.1 = (f32[2,32,2048]{2,1,0:T(8,128)}, f32[2,32,2048]{2,1,0:T(8,128)}, u32[]{:S(2)}, u32[]{:S(2)}) collective-permute-start(f32[2,32,2048]{2,1,0:T(8,128)} %fusion.25), channel_id=1, source_target_pairs={{0,1},{1,0},{2,3},{3,2},{4,5},{5,4},{6,7},{7,6},{8,9},{9,8},{10,11... | collective-permute-start | bytes 1572872 | tf_op jit(solution)/shard_map/ppermute | solution.py:120
  70.8 9.5 %copy-start.2 = (f32[32,32,1]{0,1,2:T(8,128)S(1)}, f32[32,32,1]{0,1,2:T(8,128)}, u32[]{:S(2)}) copy-start(f32[32,32,1]{0,1,2:T(8,128)} %constant.142) | copy-start | bytes 12292
  76.2 14.3 %collective-permute-start.6 = (f32[2,32,2048]{2,1,0:T(8,128)}, f32[2,32,2048]{2,1,0:T(8,128)}, u32[]{:S(2)}, u32[]{:S(2)}) collective-permute-start(f32[2,32,2048]{2,1,0:T(8,128)} %fusion.20), channel_id=1, source_target_pairs={{0,1},{1,0},{2,3},{3,2},{4,5},{5,4},{6,7},{7,6},{8,9},{9,8},{10,11... | collective-permute-start | bytes 1572872 | tf_op jit(solution)/shard_map/ppermute | solution.py:120
  82.4 29.3 %all-to-all-start.3 = ((bf16[8,8,3584]{2,0,1:T(8,128)(2,1)}), bf16[8,8,3584]{2,0,1:T(8,128)(2,1)S(1)}, u32[]{:S(2)}, u32[]{:S(2)}) async-start(bf16[8,8,3584]{2,0,1:T(8,128)(2,1)} %copy.18), calls=%async_computation.3 | async-start | bytes 917504 | tf_op jit(solution)/shard_map/all_to_all | solution.py:153
  88.4 15.5 %collective-permute-start.2 = (f32[32,2048]{1,0:T(8,128)S(1)}, f32[32,2048]{1,0:T(8,128)S(1)}, u32[]{:S(2)}, u32[]{:S(2)}) collective-permute-start(f32[32,2048]{1,0:T(8,128)S(1)} %dynamic-slice_bitcast_fusion.3), channel_id=1, source_target_pairs={{0,2},{1,3},{2,0},{3,1},{4,6},{5,7},{6,4},{7,5},{8,10},{9,11},{10,... | collective-permute-start | bytes 786440 | tf_op jit(solution)/shard_map/ppermute | solution.py:124
  91.7 17.3 %collective-permute-start.7 = (f32[32,2048]{1,0:T(8,128)S(1)}, f32[32,2048]{1,0:T(8,128)S(1)}, u32[]{:S(2)}, u32[]{:S(2)}) collective-permute-start(f32[32,2048]{1,0:T(8,128)S(1)} %dynamic-slice_bitcast_fusion.2), channel_id=1, source_target_pairs={{0,2},{1,3},{2,0},{3,1},{4,6},{5,7},{6,4},{7,5},{8,10},{9,11},{10,... | collective-permute-start | bytes 786440 | tf_op jit(solution)/shard_map/ppermute | solution.py:124
  109.1 46.6 %collective-permute-start.8 = (f32[32,2048]{1,0:T(8,128)S(1)}, f32[32,2048]{1,0:T(8,128)S(1)}, u32[]{:S(2)}, u32[]{:S(2)}) collective-permute-start(f32[32,2048]{1,0:T(8,128)S(1)} %fusion.44), channel_id=1, source_target_pairs={{0,4},{1,5},{2,6},{3,7},{4,0},{5,1},{6,2},{7,3},{8,12},{9,13},{10,... | collective-permute-start | bytes 786440 | tf_op jit(solution)/shard_map/ppermute | solution.py:132
  111.7 11.8 %collective-permute-start.12 = (bf16[64,3584]{1,0:T(8,128)(2,1)S(1)}, bf16[64,3584]{1,0:T(8,128)(2,1)S(1)}, u32[]{:S(2)}, u32[]{:S(2)}) collective-permute-start(bf16[64,3584]{1,0:T(8,128)(2,1)S(1)} %bitcast.144), channel_id=1, source_target_pairs={{0,16},{8,24},{16,0},{24,8},{1,17},{9,25},{17,1},{25,9},{2,18},{10... | collective-permute-start | bytes 1376264 | tf_op jit(solution)/shard_map/ppermute | solution.py:108
  113.2 11.8 %collective-permute-start.9 = (bf16[64,3584]{1,0:T(8,128)(2,1)S(1)}, bf16[64,3584]{1,0:T(8,128)(2,1)S(1)}, u32[]{:S(2)}, u32[]{:S(2)}) collective-permute-start(bf16[64,3584]{1,0:T(8,128)(2,1)S(1)} %bitcast.145), channel_id=1, source_target_pairs={{0,8},{8,0},{16,24},{24,16},{1,9},{9,1},{17,25},{25,17},{2,10},{10... | collective-permute-start | bytes 1376264 | tf_op jit(solution)/shard_map/ppermute | solution.py:107
  114.7 20.3 %slice-start.4 = ((s8[14680064]{0:T(1024)(128)(4,1)}), s8[4194304]{0:T(1024)(128)(4,1)S(1)}, s32[]{:S(2)}) async-start(s8[14680064]{0:T(1024)(128)(4,1)} %bitcast.127), calls=%async_computation.8 | async-start | bytes 8388608
  114.7 20.3 %slice-start.5 = ((s8[14680064]{0:T(1024)(128)(4,1)}), s8[4194304]{0:T(1024)(128)(4,1)S(1)}, s32[]{:S(2)}) async-start(s8[14680064]{0:T(1024)(128)(4,1)} %bitcast.127), calls=%async_computation.9 | async-start | bytes 8388608
  123.5 14.3 %collective-permute-start.13 = (bf16[32,3584]{1,0:T(8,128)(2,1)S(1)}, bf16[32,3584]{1,0:T(8,128)(2,1)S(1)}, u32[]{:S(2)}, u32[]{:S(2)}) collective-permute-start(bf16[32,3584]{1,0:T(8,128)(2,1)S(1)} %slice.28), channel_id=1, source_target_pairs={{0,8},{8,0},{16,24},{24,16},{1,9},{9,1},{17,25},{25,17},{2,10},{10... | collective-permute-start | bytes 688136 | tf_op jit(solution)/shard_map/ppermute | solution.py:109
  125.0 9.9 %slice-start.6 = ((s8[14680064]{0:T(1024)(128)(4,1)}), s8[4194304]{0:T(1024)(128)(4,1)S(1)}, s32[]{:S(2)}) async-start(s8[14680064]{0:T(1024)(128)(4,1)} %bitcast.127), calls=%async_computation.10 | async-start | bytes 8388608
  125.0 9.9 %slice-start.7 = ((s8[14680064]{0:T(1024)(128)(4,1)}), s8[2097152]{0:T(1024)(128)(4,1)S(1)}, s32[]{:S(2)}) async-start(s8[14680064]{0:T(1024)(128)(4,1)} %bitcast.127), calls=%async_computation.11 | async-start | bytes 4194304
  125.1 12.7 %collective-permute-start.14 = (bf16[32,3584]{1,0:T(8,128)(2,1)S(1)}, bf16[32,3584]{1,0:T(8,128)(2,1)S(1)}, u32[]{:S(2)}, u32[]{:S(2)}) collective-permute-start(bf16[32,3584]{1,0:T(8,128)(2,1)S(1)} %slice.29), channel_id=1, source_target_pairs={{0,16},{8,24},{16,0},{24,8},{1,17},{9,25},{17,1},{25,9},{2,18},{10... | collective-permute-start | bytes 688136 | tf_op jit(solution)/shard_map/ppermute | solution.py:110
  134.9 6.2 %collective-permute-start.10 = (f32[2,32,2048]{2,1,0:T(8,128)S(1)}, f32[2,32,2048]{2,1,0:T(8,128)S(1)}, u32[]{:S(2)}, u32[]{:S(2)}) collective-permute-start(f32[2,32,2048]{2,1,0:T(8,128)S(1)} %fusion.15), channel_id=1, source_target_pairs={{0,1},{1,0},{2,3},{3,2},{4,5},{5,4},{6,7},{7,6},{8,9},{9,8},{10,11... | collective-permute-start | bytes 1572872 | tf_op jit(solution)/shard_map/ppermute | solution.py:120
  137.7 31.5 %copy-start.3 = (f32[2048]{0:T(1024)S(1)}, f32[2048]{0:T(1024)}, u32[]{:S(2)}) copy-start(f32[2048]{0:T(1024)} %param.9) | copy-start | bytes 24580
  140.5 2.1 %collective-permute-start.15 = (f32[2,32,2048]{2,1,0:T(8,128)S(1)}, f32[2,32,2048]{2,1,0:T(8,128)S(1)}, u32[]{:S(2)}, u32[]{:S(2)}) collective-permute-start(f32[2,32,2048]{2,1,0:T(8,128)S(1)} %fusion.10), channel_id=1, source_target_pairs={{0,1},{1,0},{2,3},{3,2},{4,5},{5,4},{6,7},{7,6},{8,9},{9,8},{10,11... | collective-permute-start | bytes 1572872 | tf_op jit(solution)/shard_map/ppermute | solution.py:120
  141.2 9.2 %collective-permute-start.11 = (f32[32,2048]{1,0:T(8,128)S(1)}, f32[32,2048]{1,0:T(8,128)S(1)}, u32[]{:S(2)}, u32[]{:S(2)}) collective-permute-start(f32[32,2048]{1,0:T(8,128)S(1)} %dynamic-slice_bitcast_fusion.1), channel_id=1, source_target_pairs={{0,2},{1,3},{2,0},{3,1},{4,6},{5,7},{6,4},{7,5},{8,10},{9,11},{10,... | collective-permute-start | bytes 786440 | tf_op jit(solution)/shard_map/ppermute | solution.py:124
  142.7 12.4 %collective-permute-start.16 = (f32[32,2048]{1,0:T(8,128)S(1)}, f32[32,2048]{1,0:T(8,128)S(1)}, u32[]{:S(2)}, u32[]{:S(2)}) collective-permute-start(f32[32,2048]{1,0:T(8,128)S(1)} %dynamic-slice_bitcast_fusion), channel_id=1, source_target_pairs={{0,2},{1,3},{2,0},{3,1},{4,6},{5,7},{6,4},{7,5},{8,10},{9,11},{10,... | collective-permute-start | bytes 786440 | tf_op jit(solution)/shard_map/ppermute | solution.py:124
  155.2 14.0 %collective-permute-start.17 = (f32[32,2048]{1,0:T(8,128)S(1)}, f32[32,2048]{1,0:T(8,128)S(1)}, u32[]{:S(2)}, u32[]{:S(2)}) collective-permute-start(f32[32,2048]{1,0:T(8,128)S(1)} %fusion.39), channel_id=1, source_target_pairs={{0,4},{1,5},{2,6},{3,7},{4,0},{5,1},{6,2},{7,3},{8,12},{9,13},{10,... | collective-permute-start | bytes 786440 | tf_op jit(solution)/shard_map/ppermute | solution.py:132
  (1 other events, 6.8 us)

commit v10 on v8

--- a/solution.py
+++ b/solution.py
@@ -96,7 +96,7 @@
     return keep + lax.ppermute(send, "tp", pairs(4))
 
 
-def product_and_reduce(block, down_weight):
+def product_and_reduce(block, down_weight, channel_scale):
     rows = block.shape[0]
     half = rows // 2
     seq_pairs = lambda distance: [(s, s ^ distance) for s in range(4)]
@@ -125,11 +125,30 @@
 
     near = halve_pair((block, across_x))
     far = halve_pair((across_y, diagonal))
-    both = jnp.stack([near, far])
-    chosen = here // 2 % 2 ^ high
-    keep = lax.dynamic_index_in_dim(both, chosen, 0, keepdims=False)
-    send = lax.dynamic_index_in_dim(both, 1 - chosen, 0, keepdims=False)
-    return keep + lax.ppermute(send, "tp", tp_pairs(4))
+    columns = near.shape[-1]
+    split = columns // 2
+    owns_near = here // 2 % 2 == high
+    both = ("seq", "tp")
+    side_pairs = lambda owner: [
+        (s * 8 + k, s * 8 + (k ^ 4))
+        for s in range(4)
+        for k in range(8)
+        if (k // 4 % 2 == s // 2 % 2) == owner
+    ]
+    from_far_side = side_pairs(False)
+    from_near_side = side_pairs(True)
+    near_in = lax.ppermute(near, both, from_far_side)
+    far_first_in = lax.ppermute(far[:, :split], both, from_near_side)
+    far_second_in = lax.ppermute(far[:, split:], both, from_far_side)
+    scale_first, scale_second = channel_scale[:split], channel_scale[split:]
+    near_sum = near + near_in
+    finished = ((far[:, split:] + far_second_in) * scale_second[None, :]).astype(jnp.bfloat16)
+    finished_in = lax.ppermute(finished, both, from_near_side)
+    first = jnp.where(owns_near, near_sum[:, :split], far[:, :split] + far_first_in)
+    second_near = (near_sum[:, split:] * scale_second[None, :]).astype(jnp.bfloat16)
+    second = jnp.where(owns_near, second_near, finished_in)
+    first = (first * scale_first[None, :]).astype(jnp.bfloat16)
+    return jnp.concatenate([first, second], axis=1)
 
 
 def shards(hidden, down_weight, channel_scale):
@@ -147,12 +166,12 @@
         turned = rotate(spread)
         rotated = lax.all_to_all(turned, "tp", split_axis=1, concat_axis=0, tiled=True)
         if seq_count == 4 and tp_count == 8:
-            outputs.append(product_and_reduce(rotated, down_weight))
+            outputs.append(product_and_reduce(rotated, down_weight, channel_scale))
         else:
             partial_terms = gathered_product(rotated, down_weight)
-            outputs.append(scatter_sum_tp(partial_terms))
-    summed = jnp.concatenate(outputs, axis=0)
-    return (summed * channel_scale[None, :]).astype(jnp.bfloat16)
+            summed = scatter_sum_tp(partial_terms)
+            outputs.append((summed * channel_scale[None, :]).astype(jnp.bfloat16))
+    return jnp.concatenate(outputs, axis=0)
 
 
 def solution(mesh):

time: 159 us -> 166 us (1.044); the launches traced: 158 us -> 163 us
  starting transfers between devices: 12.4 us -> 20.8 us
  waiting for transfers between devices: 85.8 us -> 81.9 us
    ppermute x1 -> x4, waiting for transfers between devices: 24.6 us -> 15.5 us  [the longest x1 9.06 us: product_and_reduce(): near_in = lax.ppermute(near, both, from_far_side)]
    ppermute x1 -> x4, starting transfers between devices: 1.05 us -> 9.51 us  [the longest x1 5.47 us: product_and_reduce(): far_first_in = lax.ppermute(far[:, :split], both, from_near_side)]
    ppermute x2, waiting for transfers between devices: 21.4 us -> 26.6 us  [halve_pair(): return keep + lax.ppermute(send, 'tp', tp_pairs(2))]
  transfers between devices with their start and end apart: 10 -> 13, of which waited for: 8 -> 10; matrix products, arithmetic and copies ran while one was open for 13% -> 13% of each run, Pallas kernels for 0% -> 0%
where the time goes in v10:
time: 166 us; the launch traced here: 163 us
  waiting for transfers between devices  81.9 us (49%)
  blocking collectives  30.1 us (18%)
  starting transfers between devices  20.8 us (13%)
  matrix products  17.6 us (11%)
  other arithmetic  7.12 us (4%)
  local copies, waits for them, and re-layouts  5.19 us (3%)
    all_to_all x1, blocking collectives, shards(): spread = lax.all_to_all(part, 'tp', split_axis=0, concat_axis=1, tiled=True)  30.1 us
    ppermute x2, waiting for transfers between devices, halve_pair(): return keep + lax.ppermute(send, 'tp', tp_pairs(2))  26.6 us
    all_to_all x1, waiting for transfers between devices, shards(): lax.all_to_all(turned, 'tp', split_axis=1, concat_axis=0, tiled=True)  23.6 us
    dot_general x4, matrix products, halve_pair(): jnp.dot(piece, down_weight, preferred_element_type=jnp.float32)  14.7 us
    ppermute x1, waiting for transfers between devices, product_and_reduce(): across_y = lax.ppermute(block, 'seq', seq_pairs(2))  11.4 us
    ppermute x1, waiting for transfers between devices, product_and_reduce(): near_in = lax.ppermute(near, both, from_far_side)  9.06 us
    ppermute x1, starting transfers between devices, product_and_reduce(): far_first_in = lax.ppermute(far[:, :split], both, from_near_side)  5.47 us
    all_to_all x1, starting transfers between devices, shards(): lax.all_to_all(turned, 'tp', split_axis=1, concat_axis=0, tiled=True)  4.42 us
  transfers between devices with their start and end apart: 13, of which 10 were waited for; matrix products, arithmetic and copies ran while one was open for 13% of the time, Pallas kernels for 0%

profile of v10, /device:TPU:0, one launch (start us, length us, event | category | flops | bytes accessed | tf_op | source)
XLA Modules:
  0.0 163.1 jit_solution(2541522387709963949)
XLA Ops:
  0.0 30.1 %all_to_all.35 = bf16[8,16,3584]{2,1,0:T(8,128)(2,1)S(1)} all-to-all(bf16[8,16,3584]{2,1,0:T(8,128)(2,1)} %bitcast.66), channel_id=1, replica_groups=mesh['seq'=4,'tp'=8] {'tp'}, dimensions={0} | all-to-all | bytes 1835008 | tf_op jit(solution)/shard_map/all_to_all | solution.py:165
  31.5 1.2 fusion.33
  32.8 1.7 %fusion.9 = bf16[16,32,896]{2,1,0:T(8,128)(2,1)S(1)} fusion(f32[32,32,1]{0,1,2:T(8,128)S(1)} %copy-done.6, f32[896,16,32]{0,2,1:T(8,128)S(1)} %fusion.33), kind=kOutput, calls=%fused_computation.14 | convolution fusion | flops 177078272 | bytes 2756608 | tf_op jit(solution)/shard_map/rbm,bc->rcm/dot_general | solution.py:50
  35.1 1.2 copy.10
  36.3 4.4 %all-to-all-start.1 = ((bf16[16,8,3584]{2,0,1:T(8,128)(2,1)}), bf16[16,8,3584]{2,0,1:T(8,128)(2,1)}, u32[]{:S(2)}, u32[]{:S(2)}) async-start(bf16[16,8,3584]{2,0,1:T(8,128)(2,1)} %copy.10), calls=%async_computation.1 | async-start | bytes 1835008 | tf_op jit(solution)/shard_map/all_to_all | solution.py:167
  40.7 23.6 %all-to-all-done.1 = bf16[16,8,3584]{2,0,1:T(8,128)(2,1)} async-done(((bf16[16,8,3584]{2,0,1:T(8,128)(2,1)}), bf16[16,8,3584]{2,0,1:T(8,128)(2,1)}, u32[]{:S(2)}, u32[]{:S(2)}) %all-to-all-start.1) | async-done | bytes 917536 | tf_op jit(solution)/shard_map/all_to_all | solution.py:167
  64.3 1.5 collective-permute-start.4
  65.8 1.5 collective-permute-start
  67.3 7.7 %fusion.2 = f32[1,2,64,2048]{3,2,1,0:T(8,128)S(1)} fusion(bf16[2,64,3584]{2,1,0:T(8,128)(2,1)} %bitcast.7, bf16[3584,2048]{1,0:T(8,128)(2,1)} %param.6), kind=kOutput, calls=%fused_computation.10 | convolution fusion | flops 1879048192 | bytes 16646144 | tf_op jit(solution)/shard_map/dot_general | solution.py:115
  75.0 11.4 %collective-permute-done.4 = bf16[128,3584]{1,0:T(8,128)(2,1)S(1)} collective-permute-done((bf16[128,3584]{1,0:T(8,128)(2,1)}, bf16[128,3584]{1,0:T(8,128)(2,1)S(1)}, u32[]{:S(2)}, u32[]{:S(2)}) %collective-permute-start.4) | collective-permute-done | bytes 917536 | tf_op jit(solution)/shard_map/ppermute | solution.py:108
  86.4 1.6 collective-permute-start.5
  88.0 1.6 collective-permute-start.6
  89.6 2.3 %fusion.34 = f32[128,2048]{1,0:T(8,128)S(1)} fusion(bf16[128,3584]{1,0:T(8,128)(2,1)S(1)} %collective-permute-done, bf16[3584,2048]{1,0:T(8,128)(2,1)S(1)} %bitcast.58), kind=kOutput, calls=%fused_computation.45 | convolution fusion | flops 1879048192 | bytes 16646144 | tf_op jit(solution)/shard_map/dot_general | solution.py:115
  92.0 1.2 fusion.18
  93.2 2.3 %fusion.35 = f32[128,2048]{1,0:T(8,128)S(1)} fusion(bf16[128,3584]{1,0:T(8,128)(2,1)S(1)} %collective-permute-done.4, bf16[3584,2048]{1,0:T(8,128)(2,1)S(1)} %bitcast.58), kind=kOutput, calls=%fused_computation.46 | convolution fusion | flops 1879048192 | bytes 16646144 | tf_op jit(solution)/shard_map/dot_general | solution.py:115
  95.6 2.1 %collective-permute-done.5 = bf16[64,3584]{1,0:T(8,128)(2,1)S(1)} collective-permute-done((bf16[64,3584]{1,0:T(8,128)(2,1)S(1)}, bf16[64,3584]{1,0:T(8,128)(2,1)S(1)}, u32[]{:S(2)}, u32[]{:S(2)}) %collective-permute-start.5) | collective-permute-done | bytes 458784 | tf_op jit(solution)/shard_map/ppermute | solution.py:109
  97.7 1.3 collective-permute-done.6
  99.0 2.3 %fusion.22 = f32[128,2048]{1,0:T(8,128)S(1)} fusion(bf16[3584,2048]{1,0:T(8,128)(2,1)S(1)} %bitcast.58, bf16[64,3584]{1,0:T(8,128)(2,1)S(1)} %collective-permute-done.6, bf16[64,3584]{1,0:T(8,128)(2,1)S(1)} %collective-permute-done.5), kind=kOutput, calls=%fused_computation.25 | convolution fusion | flops 1880883200 | bytes 16646144 | tf_op jit(solution)/shard_map/dot_general | solution.py:115
  102.4 1.0 fusion.13
  103.4 1.5 fusion.21
  105.1 1.4 collective-permute-done.7
  106.4 1.3 fusion.16
  109.3 10.5 %collective-permute-done.2 = f32[64,2048]{1,0:T(8,128)S(1)} collective-permute-done((f32[64,2048]{1,0:T(8,128)S(1)}, f32[64,2048]{1,0:T(8,128)S(1)}, u32[]{:S(2)}, u32[]{:S(2)}) %collective-permute-start.2) | collective-permute-done | bytes 524320 | tf_op jit(solution)/shard_map/ppermute | solution.py:124
  119.8 1.3 collective-permute-start.3
  121.1 16.1 %collective-permute-done.8 = f32[64,2048]{1,0:T(8,128)} collective-permute-done((f32[64,2048]{1,0:T(8,128)}, f32[64,2048]{1,0:T(8,128)}, u32[]{:S(2)}, u32[]{:S(2)}) %collective-permute-start.8) | collective-permute-done | bytes 524320 | tf_op jit(solution)/shard_map/ppermute | solution.py:124
  137.3 1.1 bitcast_add_fusion
  138.4 1.3 collective-permute-start.10
  139.7 5.5 %collective-permute-start.9 = (f32[64,1024]{1,0:T(8,128)S(1)}, f32[64,1024]{1,0:T(8,128)S(1)}, u32[]{:S(2)}, u32[]{:S(2)}) collective-permute-start(f32[64,1024]{1,0:T(8,128)S(1)} %get-tuple-element.7), channel_id=1, source_target_pairs={{0,4},{1,5},{2,6},{3,7},{8,12},{9,13},{10,14},{11,15},{20,16},{21,... | collective-permute-start | bytes 786440 | tf_op jit(solution)/shard_map/ppermute | solution.py:141
  145.3 9.1 %collective-permute-done.3 = f32[64,2048]{1,0:T(8,128)S(1)} collective-permute-done((f32[64,2048]{1,0:T(8,128)S(1)}, f32[64,2048]{1,0:T(8,128)S(1)}, u32[]{:S(2)}, u32[]{:S(2)}) %collective-permute-start.3) | collective-permute-done | bytes 524320 | tf_op jit(solution)/shard_map/ppermute | solution.py:140
  154.4 3.9 %collective-permute-done.10 = f32[64,1024]{1,0:T(8,128)S(1)} collective-permute-done((f32[64,1024]{1,0:T(8,128)S(1)}, f32[64,1024]{1,0:T(8,128)S(1)}, u32[]{:S(2)}, u32[]{:S(2)}) %collective-permute-start.10) | collective-permute-done | bytes 262176 | tf_op jit(solution)/shard_map/ppermute | solution.py:142
  158.4 1.5 collective-permute-start.11
  159.9 2.5 %collective-permute-done.11 = bf16[64,1024]{1,0:T(8,128)(2,1)S(1)} collective-permute-done((bf16[64,1024]{1,0:T(8,128)(2,1)S(1)}, bf16[64,1024]{1,0:T(8,128)(2,1)S(1)}, u32[]{:S(2)}, u32[]{:S(2)}) %collective-permute-start.11) | collective-permute-done | bytes 131104 | tf_op jit(solution)/shard_map/ppermute | solution.py:146
  (48 shorter events, 5.7 us)
Async XLA Ops:
  30.1 1.4 copy-start.8
  31.5 1.2 copy-start.6
  35.0 54.6 %slice-start = ((s8[14680064]{0:T(1024)(128)(4,1)}), s8[2097152]{0:T(1024)(128)(4,1)S(1)}, s32[]{:S(2)}) async-start(s8[14680064]{0:T(1024)(128)(4,1)} %bitcast.57), calls=%async_computation.2 | async-start | bytes 4194304
  36.3 28.0 %all-to-all-start.1 = ((bf16[16,8,3584]{2,0,1:T(8,128)(2,1)}), bf16[16,8,3584]{2,0,1:T(8,128)(2,1)}, u32[]{:S(2)}, u32[]{:S(2)}) async-start(bf16[16,8,3584]{2,0,1:T(8,128)(2,1)} %copy.10), calls=%async_computation.1 | async-start | bytes 1835008 | tf_op jit(solution)/shard_map/all_to_all | solution.py:167
  64.3 22.1 %collective-permute-start.4 = (bf16[128,3584]{1,0:T(8,128)(2,1)}, bf16[128,3584]{1,0:T(8,128)(2,1)S(1)}, u32[]{:S(2)}, u32[]{:S(2)}) collective-permute-start(bf16[128,3584]{1,0:T(8,128)(2,1)} %bitcast.10), channel_id=1, source_target_pairs={{0,16},{8,24},{16,0},{24,8},{1,17},{9,25},{17,1},{25,9},{2,18},{10... | collective-permute-start | bytes 2752520 | tf_op jit(solution)/shard_map/ppermute | solution.py:108
  65.8 22.2 %collective-permute-start = (bf16[128,3584]{1,0:T(8,128)(2,1)}, bf16[128,3584]{1,0:T(8,128)(2,1)S(1)}, u32[]{:S(2)}, u32[]{:S(2)}) collective-permute-start(bf16[128,3584]{1,0:T(8,128)(2,1)} %bitcast.10), channel_id=1, source_target_pairs={{0,8},{8,0},{16,24},{24,16},{1,9},{9,1},{17,25},{25,17},{2,10},{10... | collective-permute-start | bytes 2752520 | tf_op jit(solution)/shard_map/ppermute | solution.py:107
  67.3 22.3 %slice-start.1 = ((s8[14680064]{0:T(1024)(128)(4,1)}), s8[4194304]{0:T(1024)(128)(4,1)S(1)}, s32[]{:S(2)}) async-start(s8[14680064]{0:T(1024)(128)(4,1)} %bitcast.57), calls=%async_computation.3 | async-start | bytes 8388608
  67.3 22.3 %slice-start.2 = ((s8[14680064]{0:T(1024)(128)(4,1)}), s8[4194304]{0:T(1024)(128)(4,1)S(1)}, s32[]{:S(2)}) async-start(s8[14680064]{0:T(1024)(128)(4,1)} %bitcast.57), calls=%async_computation.4 | async-start | bytes 8388608
  67.3 22.3 %slice-start.3 = ((s8[14680064]{0:T(1024)(128)(4,1)}), s8[4194304]{0:T(1024)(128)(4,1)S(1)}, s32[]{:S(2)}) async-start(s8[14680064]{0:T(1024)(128)(4,1)} %bitcast.57), calls=%async_computation.5 | async-start | bytes 8388608
  86.4 11.2 %collective-permute-start.5 = (bf16[64,3584]{1,0:T(8,128)(2,1)S(1)}, bf16[64,3584]{1,0:T(8,128)(2,1)S(1)}, u32[]{:S(2)}, u32[]{:S(2)}) collective-permute-start(bf16[64,3584]{1,0:T(8,128)(2,1)S(1)} %slice.35), channel_id=1, source_target_pairs={{0,8},{8,0},{16,24},{24,16},{1,9},{9,1},{17,25},{25,17},{2,10},{10... | collective-permute-start | bytes 1376264 | tf_op jit(solution)/shard_map/ppermute | solution.py:109
  88.0 10.9 %collective-permute-start.6 = (bf16[64,3584]{1,0:T(8,128)(2,1)S(1)}, bf16[64,3584]{1,0:T(8,128)(2,1)S(1)}, u32[]{:S(2)}, u32[]{:S(2)}) collective-permute-start(bf16[64,3584]{1,0:T(8,128)(2,1)S(1)} %slice.36), channel_id=1, source_target_pairs={{0,16},{8,24},{16,0},{24,8},{1,17},{9,25},{17,1},{25,9},{2,18},{10... | collective-permute-start | bytes 1376264 | tf_op jit(solution)/shard_map/ppermute | solution.py:110
  92.0 3.5 %copy-start.4 = (f32[128,2048]{1,0:T(8,128)}, f32[128,2048]{1,0:T(8,128)S(1)}, u32[]{:S(2)}) copy-start(f32[128,2048]{1,0:T(8,128)S(1)} %fusion.34) | copy-start | bytes 3145732
  93.2 10.2 %collective-permute-start.1 = (f32[2,64,2048]{2,1,0:T(8,128)}, f32[2,64,2048]{2,1,0:T(8,128)}, u32[]{:S(2)}, u32[]{:S(2)}) collective-permute-start(f32[2,64,2048]{2,1,0:T(8,128)} %fusion.18), channel_id=1, source_target_pairs={{0,1},{1,0},{2,3},{3,2},{4,5},{5,4},{6,7},{7,6},{8,9},{9,8},{10,11... | collective-permute-start | bytes 3145736 | tf_op jit(solution)/shard_map/ppermute | solution.py:120
  95.5 5.8 %copy-start.2 = (f32[128,2048]{1,0:T(8,128)}, f32[128,2048]{1,0:T(8,128)S(1)}, u32[]{:S(2)}) copy-start(f32[128,2048]{1,0:T(8,128)S(1)} %fusion.35) | copy-start | bytes 3145732
  101.3 1.0 copy-start
  101.3 2.1 %copy-start.5 = (f32[128,2048]{1,0:T(8,128)S(1)}, f32[128,2048]{1,0:T(8,128)}, u32[]{:S(2)}) copy-start(f32[128,2048]{1,0:T(8,128)} %copy-done.4) | copy-start | bytes 3145732
  103.4 3.0 %collective-permute-start.7 = (f32[2,64,2048]{2,1,0:T(8,128)}, f32[2,64,2048]{2,1,0:T(8,128)}, u32[]{:S(2)}, u32[]{:S(2)}) collective-permute-start(f32[2,64,2048]{2,1,0:T(8,128)} %fusion.13), channel_id=1, source_target_pairs={{0,1},{1,0},{2,3},{3,2},{4,5},{5,4},{6,7},{7,6},{8,9},{9,8},{10,11... | collective-permute-start | bytes 3145736 | tf_op jit(solution)/shard_map/ppermute | solution.py:120
  103.4 3.0 %copy-start.1 = (f32[128,2048]{1,0:T(8,128)S(1)}, f32[128,2048]{1,0:T(8,128)}, u32[]{:S(2)}) copy-start(f32[128,2048]{1,0:T(8,128)} %copy-done) | copy-start | bytes 3145732
  103.4 3.0 %copy-start.3 = (f32[128,2048]{1,0:T(8,128)S(1)}, f32[128,2048]{1,0:T(8,128)}, u32[]{:S(2)}) copy-start(f32[128,2048]{1,0:T(8,128)} %copy-done.2) | copy-start | bytes 3145732
  105.0 14.8 %collective-permute-start.2 = (f32[64,2048]{1,0:T(8,128)S(1)}, f32[64,2048]{1,0:T(8,128)S(1)}, u32[]{:S(2)}, u32[]{:S(2)}) collective-permute-start(f32[64,2048]{1,0:T(8,128)S(1)} %dynamic-slice_bitcast_fusion.1), channel_id=1, source_target_pairs={{0,2},{1,3},{2,0},{3,1},{4,6},{5,7},{6,4},{7,5},{8,10},{9,11},{10,... | collective-permute-start | bytes 1572872 | tf_op jit(solution)/shard_map/ppermute | solution.py:124
  108.6 28.7 %collective-permute-start.8 = (f32[64,2048]{1,0:T(8,128)}, f32[64,2048]{1,0:T(8,128)}, u32[]{:S(2)}, u32[]{:S(2)}) collective-permute-start(f32[64,2048]{1,0:T(8,128)} %dynamic-slice_bitcast_fusion), channel_id=1, source_target_pairs={{0,2},{1,3},{2,0},{3,1},{4,6},{5,7},{6,4},{7,5},{8,10},{9,11},{10,... | collective-permute-start | bytes 1572872 | tf_op jit(solution)/shard_map/ppermute | solution.py:124
  109.3 36.0 %copy-start.7 = (f32[2048]{0:T(1024)S(1)}, f32[2048]{0:T(1024)}, u32[]{:S(2)}) copy-start(f32[2048]{0:T(1024)} %param.7) | copy-start | bytes 24580
  119.8 34.5 %collective-permute-start.3 = (f32[64,2048]{1,0:T(8,128)S(1)}, f32[64,2048]{1,0:T(8,128)S(1)}, u32[]{:S(2)}, u32[]{:S(2)}) collective-permute-start(f32[64,2048]{1,0:T(8,128)S(1)} %bitcast_add_fusion.1), channel_id=1, source_target_pairs={{4,0},{5,1},{6,2},{7,3},{12,8},{13,9},{14,10},{15,11},{16,20},{17,... | collective-permute-start | bytes 1572872 | tf_op jit(solution)/shard_map/ppermute | solution.py:140
  138.4 19.9 %collective-permute-start.10 = (f32[64,1024]{1,0:T(8,128)S(1)}, f32[64,1024]{1,0:T(8,128)S(1)}, u32[]{:S(2)}, u32[]{:S(2)}) collective-permute-start(f32[64,1024]{1,0:T(8,128)S(1)} %get-tuple-element.8), channel_id=1, source_target_pairs={{4,0},{5,1},{6,2},{7,3},{12,8},{13,9},{14,10},{15,11},{16,20},{17,... | collective-permute-start | bytes 786440 | tf_op jit(solution)/shard_map/ppermute | solution.py:142
  139.7 18.6 %collective-permute-start.9 = (f32[64,1024]{1,0:T(8,128)S(1)}, f32[64,1024]{1,0:T(8,128)S(1)}, u32[]{:S(2)}, u32[]{:S(2)}) collective-permute-start(f32[64,1024]{1,0:T(8,128)S(1)} %get-tuple-element.7), channel_id=1, source_target_pairs={{0,4},{1,5},{2,6},{3,7},{8,12},{9,13},{10,14},{11,15},{20,16},{21,... | collective-permute-start | bytes 786440 | tf_op jit(solution)/shard_map/ppermute | solution.py:141
  158.4 4.0 %collective-permute-start.11 = (bf16[64,1024]{1,0:T(8,128)(2,1)S(1)}, bf16[64,1024]{1,0:T(8,128)(2,1)S(1)}, u32[]{:S(2)}, u32[]{:S(2)}) collective-permute-start(bf16[64,1024]{1,0:T(8,128)(2,1)S(1)} %get-tuple-element.6), channel_id=1, source_target_pairs={{0,4},{1,5},{2,6},{3,7},{8,12},{9,13},{10,14},{11,15},{20,16},{21,... | collective-permute-start | bytes 393224 | tf_op jit(solution)/shard_map/ppermute | solution.py:146

commit v11 on v8

--- a/solution.py
+++ b/solution.py
@@ -96,6 +96,45 @@
     return keep + lax.ppermute(send, "tp", pairs(4))
 
 
+def spread_rotate_return(part):
+    tp_count = lax.axis_size("tp")
+    rows, units = part.shape
+    share = rows // tp_count
+    width = INNER * PALEY
+    sub = units // width
+    me = lax.axis_index("tp")
+    pairs = lambda distance: [(k, k ^ distance) for k in range(tp_count)]
+    inner_table = jnp.asarray(np.kron(walsh_table(INNER), paley_table()), jnp.bfloat16)
+    landed = []
+    for distance in range(tp_count):
+        send = lax.dynamic_slice_in_dim(part, (me ^ distance) * share, share, 0)
+        if distance:
+            send = lax.ppermute(send, "tp", pairs(distance))
+        landed.append(
+            jnp.einsum(
+                "rbl,lm->rbm",
+                send.reshape(share, sub, width),
+                inner_table,
+                preferred_element_type=jnp.float32,
+            )
+        )
+    inner = jnp.stack(landed, axis=1).reshape(share, tp_count * sub, width)
+    order = jnp.arange(tp_count, dtype=jnp.int32)
+    source = me ^ order
+    signs = 1 - 2 * (lax.population_count(source[:, None] & source[None, :]) % 2)
+    mixing = jnp.kron(signs.astype(jnp.float32), jnp.asarray(walsh_table(sub), jnp.float32))
+    outer = jnp.einsum("rbm,bc->rcm", inner, mixing, precision=lax.Precision.HIGHEST)
+    factor = 1.0 / math.sqrt(units * tp_count)
+    turned = (outer * factor).astype(jnp.bfloat16).reshape(share, tp_count, units)
+    result = jnp.zeros((rows, units), jnp.bfloat16)
+    for distance in range(tp_count):
+        block = turned[:, distance]
+        if distance:
+            block = lax.ppermute(block, "tp", pairs(distance))
+        result = lax.dynamic_update_slice_in_dim(result, block, (me ^ distance) * share, 0)
+    return result
+
+
 def product_and_reduce(block, down_weight):
     rows = block.shape[0]
     half = rows // 2
@@ -143,9 +182,12 @@
     outputs = []
     for chunk in range(CHUNKS):
         part = grouped[:, chunk].reshape(groups * piece, units)
-        spread = lax.all_to_all(part, "tp", split_axis=0, concat_axis=1, tiled=True)
-        turned = rotate(spread)
-        rotated = lax.all_to_all(turned, "tp", split_axis=1, concat_axis=0, tiled=True)
+        if tp_count == 8:
+            rotated = spread_rotate_return(part)
+        else:
+            spread = lax.all_to_all(part, "tp", split_axis=0, concat_axis=1, tiled=True)
+            turned = rotate(spread)
+            rotated = lax.all_to_all(turned, "tp", split_axis=1, concat_axis=0, tiled=True)
         if seq_count == 4 and tp_count == 8:
             outputs.append(product_and_reduce(rotated, down_weight))
         else:

time: 159 us -> 158 us (level)
  blocking collectives: 30.1 us -> 0 us
  starting transfers between devices: 12.4 us -> 34.2 us
  waiting for transfers between devices: 85.8 us -> 74.8 us
  matrix products: 17.6 us -> 27.4 us
  local copies, waits for them, and re-layouts: 5.15 us -> 12.3 us
    all_to_all x1 -> x0, blocking collectives: 30.1 us -> none  [shards(): spread = lax.all_to_all(part, 'tp', split_axis=0, concat_axis=1, tiled=True)]
    all_to_all x1 -> x0, waiting for transfers between devices: 23.6 us -> none  [shards(): lax.all_to_all(turned, 'tp', split_axis=1, concat_axis=0, tiled=True)]
    ppermute x0 -> x14, starting transfers between devices: none -> 20.8 us  [the longest x7 11.2 us: spread_rotate_return(): block = lax.ppermute(block, 'tp', pairs(distance))]
    ppermute x0 -> x14, waiting for transfers between devices: none -> 16.3 us  [the longest x7 11.7 us: spread_rotate_return(): block = lax.ppermute(block, 'tp', pairs(distance))]
    dot_general x2 -> x9, matrix products: 2.94 us -> 11 us  [the longest x8 7.47 us: spread_rotate_return(): jnp.einsum('rbl,lm->rbm', send.reshape(share, sub, width), inner_table, p...]
    all_to_all x1 -> x0, starting transfers between devices: 4.41 us -> none  [shards(): lax.all_to_all(turned, 'tp', split_axis=1, concat_axis=0, tiled=True)]
    ppermute x2, starting transfers between devices: 0.74 us -> 4.55 us  [halve_pair(): return keep + lax.ppermute(send, 'tp', tp_pairs(2))]
    all_to_all x3 -> x0, local copies, waits for them, and re-layouts: 2.27 us -> none  [the longest x2 1.76 us: shards(): lax.all_to_all(turned, 'tp', split_axis=1, concat_axis=0, tiled=True)]
  transfers between devices with their start and end apart: 10 -> 23, of which waited for: 8 -> 9; matrix products, arithmetic and copies ran while one was open for 13% -> 23% of each run, Pallas kernels for 0% -> 0%
where the time goes in v11:
time: 158 us; the launch traced here: 157 us
  waiting for transfers between devices  74.8 us (47%)
  starting transfers between devices  34.2 us (22%)
  matrix products  27.4 us (17%)
  local copies, waits for them, and re-layouts  12.3 us (8%)
  other arithmetic  8.14 us (5%)
    ppermute x1, waiting for transfers between devices, product_and_reduce(): return keep + lax.ppermute(send, 'tp', tp_pairs(4))  23.1 us
    ppermute x2, waiting for transfers between devices, halve_pair(): return keep + lax.ppermute(send, 'tp', tp_pairs(2))  19.9 us
    dot_general x4, matrix products, halve_pair(): jnp.dot(piece, down_weight, preferred_element_type=jnp.float32)  16.4 us
    ppermute x1, waiting for transfers between devices, product_and_reduce(): across_y = lax.ppermute(block, 'seq', seq_pairs(2))  12.8 us
    ppermute x7, waiting for transfers between devices, spread_rotate_return(): block = lax.ppermute(block, 'tp', pairs(distance))  11.7 us
    ppermute x7, starting transfers between devices, spread_rotate_return(): block = lax.ppermute(block, 'tp', pairs(distance))  11.2 us
    ppermute x7, starting transfers between devices, spread_rotate_return(): send = lax.ppermute(send, 'tp', pairs(distance))  9.62 us
    dot_general x8, matrix products, spread_rotate_return(): jnp.einsum('rbl,lm->rbm', send.reshape(share, sub, width), inner_table, p...  7.47 us
  transfers between devices with their start and end apart: 23, of which 9 were waited for; matrix products, arithmetic and copies ran while one was open for 23% of the time, Pallas kernels for 0%

profile of v11, /device:TPU:0, one launch (start us, length us, event | category | flops | bytes accessed | tf_op | source)
XLA Modules:
  0.0 157.3 jit_solution(15591720845594099094)
XLA Ops:
  0.0 2.2 %constant_dynamic-slice_fusion = (bf16[16,3584]{1,0:T(8,128)(2,1)S(1)}, bf16[16,3584]{1,0:T(8,128)(2,1)}, bf16[16,3584]{1,0:T(8,128)(2,1)}, bf16[16,3584]{1,0:T(...) fusion(bf16[128,3584]{1,0:T(8,128)(2,1)} %param.5, ...), kind=kLoop, calls=%fused_computation.85 | loop fusion | bytes 1835040 | tf_op jit(solution)/shard_map/dynamic_slice | solution.py:110
  2.7 2.6 %collective-permute-start.1 = (bf16[16,3584]{1,0:T(8,128)(2,1)}, bf16[16,3584]{1,0:T(8,128)(2,1)}, u32[]{:S(2)}, u32[]{:S(2)}) collective-permute-start(bf16[16,3584]{1,0:T(8,128)(2,1)} %get-tuple-element.17), channel_id=1, source_target_pairs={{0,2},{1,3},{2,0},{3,1},{4,6},{5,7},{6,4},{7,5},{8,10},{9,11},{10,... | collective-permute-start | bytes 344072 | tf_op jit(solution)/shard_map/ppermute | solution.py:112
  5.4 2.7 %collective-permute-start.3 = (bf16[16,3584]{1,0:T(8,128)(2,1)}, bf16[16,3584]{1,0:T(8,128)(2,1)}, u32[]{:S(2)}, u32[]{:S(2)}) collective-permute-start(bf16[16,3584]{1,0:T(8,128)(2,1)} %get-tuple-element.15), channel_id=1, source_target_pairs={{0,4},{1,5},{2,6},{3,7},{4,0},{5,1},{6,2},{7,3},{8,12},{9,13},{10,... | collective-permute-start | bytes 344072 | tf_op jit(solution)/shard_map/ppermute | solution.py:112
  9.4 1.6 %mul.89 = f32[32,32]{1,0:T(8,128)} reshape(f32[8,4,8,4]{3,2,1,0:T(8,128)} %broadcast_multiply_fusion) | data formatting | bytes 8192 | tf_op jit(solution)/shard_map/jit(kron)/mul | solution.py:125
  11.0 3.6 %collective-permute-start.5 = (bf16[16,3584]{1,0:T(8,128)(2,1)}, bf16[16,3584]{1,0:T(8,128)(2,1)S(1)}, u32[]{:S(2)}, u32[]{:S(2)}) collective-permute-start(bf16[16,3584]{1,0:T(8,128)(2,1)} %get-tuple-element.20), channel_id=1, source_target_pairs={{0,6},{1,7},{2,4},{3,5},{4,2},{5,3},{6,0},{7,1},{8,14},{9,15},{10,... | collective-permute-start | bytes 344072 | tf_op jit(solution)/shard_map/ppermute | solution.py:112
  17.3 1.3 fusion.11
  18.5 1.3 fusion.10
  19.8 4.6 %collective-permute-done.4 = bf16[16,3584]{1,0:T(8,128)(2,1)} collective-permute-done((bf16[16,3584]{1,0:T(8,128)(2,1)}, bf16[16,3584]{1,0:T(8,128)(2,1)}, u32[]{:S(2)}, u32[]{:S(2)}) %collective-permute-start.4) | collective-permute-done | bytes 114720 | tf_op jit(solution)/shard_map/ppermute | solution.py:112
  27.8 3.5 %fusion.4 = bf16[16,32,896]{2,1,0:T(8,128)(2,1)S(1)} fusion(f32[16,32,896]{2,0,1:T(8,128)} %bitcast.165, f32[32,32]{1,0:T(8,128)S(1)} %copy-done.10), kind=kOutput, calls=%fused_computation.11 | convolution fusion | flops 177078272 | bytes 2756608 | tf_op jit(solution)/shard_map/rbm,bc->rcm/dot_general | solution.py:126
  31.9 1.7 %fusion.45 = (bf16[16,1,3584]{2,1,0:T(2,128)(2,1)S(1)}, bf16[16,1,3584]{2,1,0:T(2,128)(2,1)S(1)}, bf16[16,1,3584]{2,1,0:T(2,128)(2,1)S(1)}, bf16[16,1,3584]{2,1,...) fusion(bf16[16,8,3584]{2,1,0:T(8,128)(2,1)S(1)} %reshape.114), kind=kLoop, calls=%fused_computation.102 | loop fusion | bytes 1835008 | tf_op jit(solution)/shard_map/slice | solution.py:131
  33.9 3.8 %collective-permute-start.8 = (bf16[16,3584]{1,0:T(8,128)(2,1)S(1)}, bf16[16,3584]{1,0:T(8,128)(2,1)S(1)}, u32[]{:S(2)}, u32[]{:S(2)}) collective-permute-start(bf16[16,3584]{1,0:T(8,128)(2,1)S(1)} %bitcast.172), channel_id=1, source_target_pairs={{0,2},{1,3},{2,0},{3,1},{4,6},{5,7},{6,4},{7,5},{8,10},{9,11},{10,... | collective-permute-start | bytes 344072 | tf_op jit(solution)/shard_map/ppermute | solution.py:133
  37.9 3.1 %collective-permute-start.10 = (bf16[16,3584]{1,0:T(8,128)(2,1)S(1)}, bf16[16,3584]{1,0:T(8,128)(2,1)S(1)}, u32[]{:S(2)}, u32[]{:S(2)}) collective-permute-start(bf16[16,3584]{1,0:T(8,128)(2,1)S(1)} %bitcast.169), channel_id=1, source_target_pairs={{0,4},{1,5},{2,6},{3,7},{4,0},{5,1},{6,2},{7,3},{8,12},{9,13},{10,... | collective-permute-start | bytes 344072 | tf_op jit(solution)/shard_map/ppermute | solution.py:133
  41.6 2.1 %collective-permute-start.12 = (bf16[16,3584]{1,0:T(8,128)(2,1)S(1)}, bf16[16,3584]{1,0:T(8,128)(2,1)S(1)}, u32[]{:S(2)}, u32[]{:S(2)}) collective-permute-start(bf16[16,3584]{1,0:T(8,128)(2,1)S(1)} %bitcast.171), channel_id=1, source_target_pairs={{0,6},{1,7},{2,4},{3,5},{4,2},{5,3},{6,0},{7,1},{8,14},{9,15},{10,... | collective-permute-start | bytes 344072 | tf_op jit(solution)/shard_map/ppermute | solution.py:133
  45.0 2.7 %collective-permute-done.9 = bf16[16,3584]{1,0:T(8,128)(2,1)S(1)} collective-permute-done((bf16[16,3584]{1,0:T(8,128)(2,1)S(1)}, bf16[16,3584]{1,0:T(8,128)(2,1)S(1)}, u32[]{:S(2)}, u32[]{:S(2)}) %collective-permute-start.9) | collective-permute-done | bytes 114720 | tf_op jit(solution)/shard_map/ppermute | solution.py:133
  47.7 9.0 %collective-permute-done.11 = bf16[16,3584]{1,0:T(8,128)(2,1)S(1)} collective-permute-done((bf16[16,3584]{1,0:T(8,128)(2,1)S(1)}, bf16[16,3584]{1,0:T(8,128)(2,1)S(1)}, u32[]{:S(2)}, u32[]{:S(2)}) %collective-permute-start.11) | collective-permute-done | bytes 114720 | tf_op jit(solution)/shard_map/ppermute | solution.py:133
  56.8 1.6 %collective-permute-start.17 = (bf16[128,3584]{1,0:T(8,128)(2,1)S(1)}, bf16[128,3584]{1,0:T(8,128)(2,1)}, u32[]{:S(2)}, u32[]{:S(2)}) collective-permute-start(bf16[128,3584]{1,0:T(8,128)(2,1)S(1)} %constant_dynamic-update-slice_fusion), channel_id=1, source_target_pairs={{0,16},{8,24},{16,0},{24,8},{1,17},{9,25},{17,1},{25,9},{2,18},{10... | collective-permute-start | bytes 2752520 | tf_op jit(solution)/shard_map/ppermute | solution.py:147
  58.4 1.5 collective-permute-start.14
  59.9 7.4 %fusion.46 = f32[128,2048]{1,0:T(8,128)S(1)} fusion(bf16[128,3584]{1,0:T(8,128)(2,1)S(1)} %constant_dynamic-update-slice_fusion, bf16[3584,2048]{1,0:T(8,128)(2,1)} %param.6), kind=kOutput, calls=%fused_computation.103 | convolution fusion | flops 1879048192 | bytes 16646144 | tf_op jit(solution)/shard_map/dot_general | solution.py:154
  67.3 12.8 %collective-permute-done.17 = bf16[128,3584]{1,0:T(8,128)(2,1)} collective-permute-done((bf16[128,3584]{1,0:T(8,128)(2,1)S(1)}, bf16[128,3584]{1,0:T(8,128)(2,1)}, u32[]{:S(2)}, u32[]{:S(2)}) %collective-permute-start.17) | collective-permute-done | bytes 917536 | tf_op jit(solution)/shard_map/ppermute | solution.py:147
  81.2 1.6 %collective-permute-start.18 = (bf16[64,3584]{1,0:T(8,128)(2,1)S(1)}, bf16[64,3584]{1,0:T(8,128)(2,1)S(1)}, u32[]{:S(2)}, u32[]{:S(2)}) collective-permute-start(bf16[64,3584]{1,0:T(8,128)(2,1)S(1)} %slice.48), channel_id=1, source_target_pairs={{0,8},{8,0},{16,24},{24,16},{1,9},{9,1},{17,25},{25,17},{2,10},{10... | collective-permute-start | bytes 1376264 | tf_op jit(solution)/shard_map/ppermute | solution.py:148
  83.8 1.6 %collective-permute-start.19 = (bf16[64,3584]{1,0:T(8,128)(2,1)S(1)}, bf16[64,3584]{1,0:T(8,128)(2,1)S(1)}, u32[]{:S(2)}, u32[]{:S(2)}) collective-permute-start(bf16[64,3584]{1,0:T(8,128)(2,1)S(1)} %slice.49), channel_id=1, source_target_pairs={{0,16},{8,24},{16,0},{24,8},{1,17},{9,25},{17,1},{25,9},{2,18},{10... | collective-permute-start | bytes 1376264 | tf_op jit(solution)/shard_map/ppermute | solution.py:149
  85.4 3.4 %fusion.47 = f32[128,2048]{1,0:T(8,128)S(1)} fusion(bf16[128,3584]{1,0:T(8,128)(2,1)} %collective-permute-done.14, bf16[3584,2048]{1,0:T(8,128)(2,1)S(1)} %bitcast.156), kind=kOutput, calls=%fused_computation.104 | convolution fusion | flops 1879048192 | bytes 16646144 | tf_op jit(solution)/shard_map/dot_general | solution.py:154
  90.3 3.2 %fusion.48 = f32[128,2048]{1,0:T(8,128)S(1)} fusion(bf16[128,3584]{1,0:T(8,128)(2,1)} %collective-permute-done.17, bf16[3584,2048]{1,0:T(8,128)(2,1)S(1)} %bitcast.156), kind=kOutput, calls=%fused_computation.105 | convolution fusion | flops 1879048192 | bytes 16646144 | tf_op jit(solution)/shard_map/dot_general | solution.py:154
  93.9 2.3 %collective-permute-done.19 = bf16[64,3584]{1,0:T(8,128)(2,1)S(1)} collective-permute-done((bf16[64,3584]{1,0:T(8,128)(2,1)S(1)}, bf16[64,3584]{1,0:T(8,128)(2,1)S(1)}, u32[]{:S(2)}, u32[]{:S(2)}) %collective-permute-start.19) | collective-permute-done | bytes 458784 | tf_op jit(solution)/shard_map/ppermute | solution.py:149
  96.2 2.3 %fusion.25 = f32[128,2048]{1,0:T(8,128)S(1)} fusion(bf16[3584,2048]{1,0:T(8,128)(2,1)S(1)} %bitcast.156, bf16[64,3584]{1,0:T(8,128)(2,1)S(1)} %collective-permute-done.19, bf16[64,3584]{1,0:T(8,128)(2,1)S(1)} %collective-permute-done.18), kind=kOutput, calls=%fused_computation.42 | convolution fusion | flops 1880883200 | bytes 16646144 | tf_op jit(solution)/shard_map/dot_general | solution.py:154
  100.2 1.5 fusion.24
  102.6 4.4 %collective-permute-start.16 = (f32[64,2048]{1,0:T(8,128)}, f32[64,2048]{1,0:T(8,128)}, u32[]{:S(2)}, u32[]{:S(2)}) collective-permute-start(f32[64,2048]{1,0:T(8,128)} %dynamic-slice_bitcast_fusion.1), channel_id=1, source_target_pairs={{0,2},{1,3},{2,0},{3,1},{4,6},{5,7},{6,4},{7,5},{8,10},{9,11},{10,... | collective-permute-start | bytes 1572872 | tf_op jit(solution)/shard_map/ppermute | solution.py:163
  107.0 1.3 fusion.19
  109.5 10.5 %collective-permute-done.16 = f32[64,2048]{1,0:T(8,128)} collective-permute-done((f32[64,2048]{1,0:T(8,128)}, f32[64,2048]{1,0:T(8,128)}, u32[]{:S(2)}, u32[]{:S(2)}) %collective-permute-start.16) | collective-permute-done | bytes 524320 | tf_op jit(solution)/shard_map/ppermute | solution.py:163
  121.3 9.4 %collective-permute-done.21 = f32[64,2048]{1,0:T(8,128)S(1)} collective-permute-done((f32[64,2048]{1,0:T(8,128)S(1)}, f32[64,2048]{1,0:T(8,128)S(1)}, u32[]{:S(2)}, u32[]{:S(2)}) %collective-permute-start.21) | collective-permute-done | bytes 524320 | tf_op jit(solution)/shard_map/ppermute | solution.py:163
  130.8 2.6 %collective-permute-start.22 = (f32[64,2048]{1,0:T(8,128)S(1)}, f32[64,2048]{1,0:T(8,128)S(1)}, u32[]{:S(2)}, u32[]{:S(2)}) collective-permute-start(f32[64,2048]{1,0:T(8,128)S(1)} %fusion.30), channel_id=1, source_target_pairs={{0,4},{1,5},{2,6},{3,7},{4,0},{5,1},{6,2},{7,3},{8,12},{9,13},{10,... | collective-permute-start | bytes 1572872 | tf_op jit(solution)/shard_map/ppermute | solution.py:171
  133.4 23.1 %collective-permute-done.22 = f32[64,2048]{1,0:T(8,128)S(1)} collective-permute-done((f32[64,2048]{1,0:T(8,128)S(1)}, f32[64,2048]{1,0:T(8,128)S(1)}, u32[]{:S(2)}, u32[]{:S(2)}) %collective-permute-start.22) | collective-permute-done | bytes 524320 | tf_op jit(solution)/shard_map/ppermute | solution.py:171
  (97 shorter events, 20.4 us)
Async XLA Ops:
  0.0 8.2 %copy-start = (bf16[896,896,1]{1,0,2:T(8,128)(2,1)S(1)}, bf16[896,896,1]{1,0,2:T(8,128)(2,1)}, u32[]{:S(2)}) copy-start(bf16[896,896,1]{1,0,2:T(8,128)(2,1)} %constant.128) | copy-start | bytes 4816900
  0.0 8.6 %copy-start.12 = (f32[4,4]{1,0:T(4,128)S(1)}, f32[4,4]{1,0:T(4,128)}, u32[]{:S(2)}) copy-start(f32[4,4]{1,0:T(4,128)} %constant.127.clone) | copy-start | bytes 196
  2.2 8.7 %collective-permute-start = (bf16[16,3584]{1,0:T(8,128)(2,1)}, bf16[16,3584]{1,0:T(8,128)(2,1)}, u32[]{:S(2)}, u32[]{:S(2)}) collective-permute-start(bf16[16,3584]{1,0:T(8,128)(2,1)} %get-tuple-element.18), channel_id=1, source_target_pairs={{0,1},{1,0},{2,3},{3,2},{4,5},{5,4},{6,7},{7,6},{8,9},{9,8},{10,11... | collective-permute-start | bytes 344072 | tf_op jit(solution)/shard_map/ppermute | solution.py:112
  2.7 13.1 %collective-permute-start.1 = (bf16[16,3584]{1,0:T(8,128)(2,1)}, bf16[16,3584]{1,0:T(8,128)(2,1)}, u32[]{:S(2)}, u32[]{:S(2)}) collective-permute-start(bf16[16,3584]{1,0:T(8,128)(2,1)} %get-tuple-element.17), channel_id=1, source_target_pairs={{0,2},{1,3},{2,0},{3,1},{4,6},{5,7},{6,4},{7,5},{8,10},{9,11},{10,... | collective-permute-start | bytes 344072 | tf_op jit(solution)/shard_map/ppermute | solution.py:112
  5.3 11.9 %collective-permute-start.2 = (bf16[16,3584]{1,0:T(8,128)(2,1)}, bf16[16,3584]{1,0:T(8,128)(2,1)}, u32[]{:S(2)}, u32[]{:S(2)}) collective-permute-start(bf16[16,3584]{1,0:T(8,128)(2,1)} %get-tuple-element.16), channel_id=1, source_target_pairs={{0,3},{1,2},{2,1},{3,0},{4,7},{5,6},{6,5},{7,4},{8,11},{9,10},{10,... | collective-permute-start | bytes 344072 | tf_op jit(solution)/shard_map/ppermute | solution.py:112
  5.4 13.1 %collective-permute-start.3 = (bf16[16,3584]{1,0:T(8,128)(2,1)}, bf16[16,3584]{1,0:T(8,128)(2,1)}, u32[]{:S(2)}, u32[]{:S(2)}) collective-permute-start(bf16[16,3584]{1,0:T(8,128)(2,1)} %get-tuple-element.15), channel_id=1, source_target_pairs={{0,4},{1,5},{2,6},{3,7},{4,0},{5,1},{6,2},{7,3},{8,12},{9,13},{10,... | collective-permute-start | bytes 344072 | tf_op jit(solution)/shard_map/ppermute | solution.py:112
  8.1 16.3 %collective-permute-start.4 = (bf16[16,3584]{1,0:T(8,128)(2,1)}, bf16[16,3584]{1,0:T(8,128)(2,1)}, u32[]{:S(2)}, u32[]{:S(2)}) collective-permute-start(bf16[16,3584]{1,0:T(8,128)(2,1)} %get-tuple-element.14), channel_id=1, source_target_pairs={{0,5},{1,4},{2,7},{3,6},{4,1},{5,0},{6,3},{7,2},{8,13},{9,12},{10,... | collective-permute-start | bytes 344072 | tf_op jit(solution)/shard_map/ppermute | solution.py:112
  11.0 14.7 %collective-permute-start.5 = (bf16[16,3584]{1,0:T(8,128)(2,1)}, bf16[16,3584]{1,0:T(8,128)(2,1)S(1)}, u32[]{:S(2)}, u32[]{:S(2)}) collective-permute-start(bf16[16,3584]{1,0:T(8,128)(2,1)} %get-tuple-element.20), channel_id=1, source_target_pairs={{0,6},{1,7},{2,4},{3,5},{4,2},{5,3},{6,0},{7,1},{8,14},{9,15},{10,... | collective-permute-start | bytes 344072 | tf_op jit(solution)/shard_map/ppermute | solution.py:112
  15.8 10.3 %collective-permute-start.6 = (bf16[16,3584]{1,0:T(8,128)(2,1)S(1)}, bf16[16,3584]{1,0:T(8,128)(2,1)S(1)}, u32[]{:S(2)}, u32[]{:S(2)}) collective-permute-start(bf16[16,3584]{1,0:T(8,128)(2,1)S(1)} %get-tuple-element.13), channel_id=1, source_target_pairs={{0,7},{1,6},{2,5},{3,4},{4,3},{5,2},{6,1},{7,0},{8,15},{9,14},{10,... | collective-permute-start | bytes 344072 | tf_op jit(solution)/shard_map/ppermute | solution.py:112
  33.5 8.0 %collective-permute-start.7 = (bf16[16,3584]{1,0:T(8,128)(2,1)S(1)}, bf16[16,3584]{1,0:T(8,128)(2,1)S(1)}, u32[]{:S(2)}, u32[]{:S(2)}) collective-permute-start(bf16[16,3584]{1,0:T(8,128)(2,1)S(1)} %bitcast.173), channel_id=1, source_target_pairs={{0,1},{1,0},{2,3},{3,2},{4,5},{5,4},{6,7},{7,6},{8,9},{9,8},{10,11... | collective-permute-start | bytes 344072 | tf_op jit(solution)/shard_map/ppermute | solution.py:133
  33.9 9.9 %collective-permute-start.8 = (bf16[16,3584]{1,0:T(8,128)(2,1)S(1)}, bf16[16,3584]{1,0:T(8,128)(2,1)S(1)}, u32[]{:S(2)}, u32[]{:S(2)}) collective-permute-start(bf16[16,3584]{1,0:T(8,128)(2,1)S(1)} %bitcast.172), channel_id=1, source_target_pairs={{0,2},{1,3},{2,0},{3,1},{4,6},{5,7},{6,4},{7,5},{8,10},{9,11},{10,... | collective-permute-start | bytes 344072 | tf_op jit(solution)/shard_map/ppermute | solution.py:133
  37.7 10.0 %collective-permute-start.9 = (bf16[16,3584]{1,0:T(8,128)(2,1)S(1)}, bf16[16,3584]{1,0:T(8,128)(2,1)S(1)}, u32[]{:S(2)}, u32[]{:S(2)}) collective-permute-start(bf16[16,3584]{1,0:T(8,128)(2,1)S(1)} %bitcast.170), channel_id=1, source_target_pairs={{0,3},{1,2},{2,1},{3,0},{4,7},{5,6},{6,5},{7,4},{8,11},{9,10},{10,... | collective-permute-start | bytes 344072 | tf_op jit(solution)/shard_map/ppermute | solution.py:133
  37.9 9.8 %collective-permute-start.10 = (bf16[16,3584]{1,0:T(8,128)(2,1)S(1)}, bf16[16,3584]{1,0:T(8,128)(2,1)S(1)}, u32[]{:S(2)}, u32[]{:S(2)}) collective-permute-start(bf16[16,3584]{1,0:T(8,128)(2,1)S(1)} %bitcast.169), channel_id=1, source_target_pairs={{0,4},{1,5},{2,6},{3,7},{4,0},{5,1},{6,2},{7,3},{8,12},{9,13},{10,... | collective-permute-start | bytes 344072 | tf_op jit(solution)/shard_map/ppermute | solution.py:133
  41.0 15.7 %collective-permute-start.11 = (bf16[16,3584]{1,0:T(8,128)(2,1)S(1)}, bf16[16,3584]{1,0:T(8,128)(2,1)S(1)}, u32[]{:S(2)}, u32[]{:S(2)}) collective-permute-start(bf16[16,3584]{1,0:T(8,128)(2,1)S(1)} %bitcast.168), channel_id=1, source_target_pairs={{0,5},{1,4},{2,7},{3,6},{4,1},{5,0},{6,3},{7,2},{8,13},{9,12},{10,... | collective-permute-start | bytes 344072 | tf_op jit(solution)/shard_map/ppermute | solution.py:133
  41.5 43.9 %slice-start = ((s8[14680064]{0:T(1024)(128)(4,1)}), s8[2097152]{0:T(1024)(128)(4,1)S(1)}, s32[]{:S(2)}) async-start(s8[14680064]{0:T(1024)(128)(4,1)} %bitcast.155), calls=%async_computation | async-start | bytes 4194304
  41.6 15.2 %collective-permute-start.12 = (bf16[16,3584]{1,0:T(8,128)(2,1)S(1)}, bf16[16,3584]{1,0:T(8,128)(2,1)S(1)}, u32[]{:S(2)}, u32[]{:S(2)}) collective-permute-start(bf16[16,3584]{1,0:T(8,128)(2,1)S(1)} %bitcast.171), channel_id=1, source_target_pairs={{0,6},{1,7},{2,4},{3,5},{4,2},{5,3},{6,0},{7,1},{8,14},{9,15},{10,... | collective-permute-start | bytes 344072 | tf_op jit(solution)/shard_map/ppermute | solution.py:133
  43.8 13.0 %collective-permute-start.13 = (bf16[16,3584]{1,0:T(8,128)(2,1)S(1)}, bf16[16,3584]{1,0:T(8,128)(2,1)S(1)}, u32[]{:S(2)}, u32[]{:S(2)}) collective-permute-start(bf16[16,3584]{1,0:T(8,128)(2,1)S(1)} %bitcast.167), channel_id=1, source_target_pairs={{0,7},{1,6},{2,5},{3,4},{4,3},{5,2},{6,1},{7,0},{8,15},{9,14},{10,... | collective-permute-start | bytes 344072 | tf_op jit(solution)/shard_map/ppermute | solution.py:133
  56.8 23.3 %collective-permute-start.17 = (bf16[128,3584]{1,0:T(8,128)(2,1)S(1)}, bf16[128,3584]{1,0:T(8,128)(2,1)}, u32[]{:S(2)}, u32[]{:S(2)}) collective-permute-start(bf16[128,3584]{1,0:T(8,128)(2,1)S(1)} %constant_dynamic-update-slice_fusion), channel_id=1, source_target_pairs={{0,16},{8,24},{16,0},{24,8},{1,17},{9,25},{17,1},{25,9},{2,18},{10... | collective-permute-start | bytes 2752520 | tf_op jit(solution)/shard_map/ppermute | solution.py:147
  58.4 24.4 %collective-permute-start.14 = (bf16[128,3584]{1,0:T(8,128)(2,1)S(1)}, bf16[128,3584]{1,0:T(8,128)(2,1)}, u32[]{:S(2)}, u32[]{:S(2)}) collective-permute-start(bf16[128,3584]{1,0:T(8,128)(2,1)S(1)} %constant_dynamic-update-slice_fusion), channel_id=1, source_target_pairs={{0,8},{8,0},{16,24},{24,16},{1,9},{9,1},{17,25},{25,17},{2,10},{10... | collective-permute-start | bytes 2752520 | tf_op jit(solution)/shard_map/ppermute | solution.py:146
  59.9 25.5 %slice-start.1 = ((s8[14680064]{0:T(1024)(128)(4,1)}), s8[4194304]{0:T(1024)(128)(4,1)S(1)}, s32[]{:S(2)}) async-start(s8[14680064]{0:T(1024)(128)(4,1)} %bitcast.155), calls=%async_computation.1 | async-start | bytes 8388608
  59.9 25.5 %slice-start.2 = ((s8[14680064]{0:T(1024)(128)(4,1)}), s8[4194304]{0:T(1024)(128)(4,1)S(1)}, s32[]{:S(2)}) async-start(s8[14680064]{0:T(1024)(128)(4,1)} %bitcast.155), calls=%async_computation.2 | async-start | bytes 8388608
  59.9 25.5 %slice-start.3 = ((s8[14680064]{0:T(1024)(128)(4,1)}), s8[4194304]{0:T(1024)(128)(4,1)S(1)}, s32[]{:S(2)}) async-start(s8[14680064]{0:T(1024)(128)(4,1)} %bitcast.155), calls=%async_computation.3 | async-start | bytes 8388608
  67.3 21.6 %copy-start.1 = (f32[128,2048]{1,0:T(8,128)}, f32[128,2048]{1,0:T(8,128)S(1)}, u32[]{:S(2)}) copy-start(f32[128,2048]{1,0:T(8,128)S(1)} %fusion.46) | copy-start | bytes 3145732
  81.2 12.7 %collective-permute-start.18 = (bf16[64,3584]{1,0:T(8,128)(2,1)S(1)}, bf16[64,3584]{1,0:T(8,128)(2,1)S(1)}, u32[]{:S(2)}, u32[]{:S(2)}) collective-permute-start(bf16[64,3584]{1,0:T(8,128)(2,1)S(1)} %slice.48), channel_id=1, source_target_pairs={{0,8},{8,0},{16,24},{24,16},{1,9},{9,1},{17,25},{25,17},{2,10},{10... | collective-permute-start | bytes 1376264 | tf_op jit(solution)/shard_map/ppermute | solution.py:148
  83.8 12.4 %collective-permute-start.19 = (bf16[64,3584]{1,0:T(8,128)(2,1)S(1)}, bf16[64,3584]{1,0:T(8,128)(2,1)S(1)}, u32[]{:S(2)}, u32[]{:S(2)}) collective-permute-start(bf16[64,3584]{1,0:T(8,128)(2,1)S(1)} %slice.49), channel_id=1, source_target_pairs={{0,16},{8,24},{16,0},{24,8},{1,17},{9,25},{17,1},{25,9},{2,18},{10... | collective-permute-start | bytes 1376264 | tf_op jit(solution)/shard_map/ppermute | solution.py:149
  90.3 9.4 %collective-permute-start.15 = (f32[2,64,2048]{2,1,0:T(8,128)}, f32[2,64,2048]{2,1,0:T(8,128)}, u32[]{:S(2)}, u32[]{:S(2)}) collective-permute-start(f32[2,64,2048]{2,1,0:T(8,128)} %fusion.21), channel_id=1, source_target_pairs={{0,1},{1,0},{2,3},{3,2},{4,5},{5,4},{6,7},{7,6},{8,9},{9,8},{10,11... | collective-permute-start | bytes 3145736 | tf_op jit(solution)/shard_map/ppermute | solution.py:159
  99.7 7.3 %collective-permute-start.20 = (f32[2,64,2048]{2,1,0:T(8,128)}, f32[2,64,2048]{2,1,0:T(8,128)}, u32[]{:S(2)}, u32[]{:S(2)}) collective-permute-start(f32[2,64,2048]{2,1,0:T(8,128)} %fusion.16), channel_id=1, source_target_pairs={{0,1},{1,0},{2,3},{3,2},{4,5},{5,4},{6,7},{7,6},{8,9},{9,8},{10,11... | collective-permute-start | bytes 3145736 | tf_op jit(solution)/shard_map/ppermute | solution.py:159
  102.6 17.4 %collective-permute-start.16 = (f32[64,2048]{1,0:T(8,128)}, f32[64,2048]{1,0:T(8,128)}, u32[]{:S(2)}, u32[]{:S(2)}) collective-permute-start(f32[64,2048]{1,0:T(8,128)} %dynamic-slice_bitcast_fusion.1), channel_id=1, source_target_pairs={{0,2},{1,3},{2,0},{3,1},{4,6},{5,7},{6,4},{7,5},{8,10},{9,11},{10,... | collective-permute-start | bytes 1572872 | tf_op jit(solution)/shard_map/ppermute | solution.py:163
  109.4 21.3 %collective-permute-start.21 = (f32[64,2048]{1,0:T(8,128)S(1)}, f32[64,2048]{1,0:T(8,128)S(1)}, u32[]{:S(2)}, u32[]{:S(2)}) collective-permute-start(f32[64,2048]{1,0:T(8,128)S(1)} %dynamic-slice_bitcast_fusion), channel_id=1, source_target_pairs={{0,2},{1,3},{2,0},{3,1},{4,6},{5,7},{6,4},{7,5},{8,10},{9,11},{10,... | collective-permute-start | bytes 1572872 | tf_op jit(solution)/shard_map/ppermute | solution.py:163
  109.5 21.2 %copy-start.8 = (f32[2,64,2048]{2,1,0:T(8,128)S(1)}, f32[2,64,2048]{2,1,0:T(8,128)}, u32[]{:S(2)}) copy-start(f32[2,64,2048]{2,1,0:T(8,128)} %copy-done.7) | copy-start | bytes 3145732
  121.3 35.2 %copy-start.11 = (f32[2048]{0:T(1024)S(1)}, f32[2048]{0:T(1024)}, u32[]{:S(2)}) copy-start(f32[2048]{0:T(1024)} %param.7) | copy-start | bytes 24580
  130.8 25.6 %collective-permute-start.22 = (f32[64,2048]{1,0:T(8,128)S(1)}, f32[64,2048]{1,0:T(8,128)S(1)}, u32[]{:S(2)}, u32[]{:S(2)}) collective-permute-start(f32[64,2048]{1,0:T(8,128)S(1)} %fusion.30), channel_id=1, source_target_pairs={{0,4},{1,5},{2,6},{3,7},{4,0},{5,1},{6,2},{7,3},{8,12},{9,13},{10,... | collective-permute-start | bytes 1572872 | tf_op jit(solution)/shard_map/ppermute | solution.py:171
  (8 other events, 26.4 us)

commit v12 on v11

--- a/solution.py
+++ b/solution.py
@@ -149,26 +149,39 @@
     second = lax.ppermute(across_x[half:], "seq", seq_pairs(2))
     diagonal = jnp.concatenate([first, second], axis=0)
 
-    def halve_pair(pieces):
+    def first_halving(pieces):
         products = jnp.stack(
             [jnp.dot(piece, down_weight, preferred_element_type=jnp.float32) for piece in pieces]
         )
         split = products.reshape(2, 2, half, products.shape[-1])
         keep = lax.dynamic_index_in_dim(split, low, 1, keepdims=False)
         send = lax.dynamic_index_in_dim(split, 1 - low, 1, keepdims=False)
-        summed = keep + lax.ppermute(send, "tp", tp_pairs(1))
+        return keep + lax.ppermute(send, "tp", tp_pairs(1))
+
+    def second_halving(summed):
         chosen = here % 2 ^ middle
         keep = lax.dynamic_index_in_dim(summed, chosen, 0, keepdims=False)
         send = lax.dynamic_index_in_dim(summed, 1 - chosen, 0, keepdims=False)
         return keep + lax.ppermute(send, "tp", tp_pairs(2))
 
-    near = halve_pair((block, across_x))
-    far = halve_pair((across_y, diagonal))
-    both = jnp.stack([near, far])
+    near = second_halving(first_halving((block, across_x)))
+    far_summed = first_halving((across_y, diagonal))
+    columns = near.shape[-1]
+    width = columns // 2
     chosen = here // 2 % 2 ^ high
-    keep = lax.dynamic_index_in_dim(both, chosen, 0, keepdims=False)
-    send = lax.dynamic_index_in_dim(both, 1 - chosen, 0, keepdims=False)
-    return keep + lax.ppermute(send, "tp", tp_pairs(4))
+    results = []
+    previous = None
+    for start in (0, width):
+        piece = far_summed[..., start : start + width]
+        if previous is not None:
+            _, piece = lax.optimization_barrier((previous, piece))
+        far = second_halving(piece)
+        both = jnp.stack([near[:, start : start + width], far])
+        keep = lax.dynamic_index_in_dim(both, chosen, 0, keepdims=False)
+        send = lax.dynamic_index_in_dim(both, 1 - chosen, 0, keepdims=False)
+        results.append(keep + lax.ppermute(send, "tp", tp_pairs(4)))
+        previous = far
+    return jnp.concatenate(results, axis=1)
 
 
 def shards(hidden, down_weight, channel_scale):

time: 158 us -> 151 us (0.956)
  local copies, waits for them, and re-layouts: 12.3 us -> 6.94 us
  other arithmetic: 8.14 us -> 6.31 us
  waiting for transfers between devices: 74.8 us -> 73 us
    ppermute x5 -> x7, waiting for transfers between devices: 43 us -> 39 us  [the longest x3 25.2 us: second_halving(): return keep + lax.ppermute(send, 'tp', tp_pairs(2))]
    unnamed x41 -> x31, local copies, waits for them, and re-layouts: 3.01 us -> 0.74 us
    ppermute x7, waiting for transfers between devices: 4.61 us -> 6.61 us  [spread_rotate_return(): send = lax.ppermute(send, 'tp', pairs(distance))]
    ppermute x5 -> x7, starting transfers between devices: 7.12 us -> 8.43 us  [the longest x3 7.24 us: second_halving(): return keep + lax.ppermute(send, 'tp', tp_pairs(2))]
  transfers between devices with their start and end apart: 23 -> 25, of which waited for: 9 -> 12; matrix products, arithmetic and copies ran while one was open for 23% -> 21% of each run, Pallas kernels for 0% -> 0%
where the time goes in v12:
time: 151 us; the launch traced here: 150 us
  waiting for transfers between devices  73 us (48%)
  starting transfers between devices  35.2 us (23%)
  matrix products  28.5 us (19%)
  local copies, waits for them, and re-layouts  6.94 us (5%)
  other arithmetic  6.31 us (4%)
    ppermute x3, waiting for transfers between devices, second_halving(): return keep + lax.ppermute(send, 'tp', tp_pairs(2))  25.2 us
    dot_general x4, matrix products, first_halving(): jnp.dot(piece, down_weight, preferred_element_type=jnp.float32)  16.4 us
    ppermute x2, waiting for transfers between devices, product_and_reduce(): results.append(keep + lax.ppermute(send, 'tp', tp_pairs(4)))  13.8 us
    ppermute x1, waiting for transfers between devices, product_and_reduce(): across_y = lax.ppermute(block, 'seq', seq_pairs(2))  12.9 us
    ppermute x7, waiting for transfers between devices, spread_rotate_return(): block = lax.ppermute(block, 'tp', pairs(distance))  11.7 us
    ppermute x7, starting transfers between devices, spread_rotate_return(): block = lax.ppermute(block, 'tp', pairs(distance))  10.9 us
    ppermute x7, starting transfers between devices, spread_rotate_return(): send = lax.ppermute(send, 'tp', pairs(distance))  9.71 us
    dot_general x8, matrix products, spread_rotate_return(): jnp.einsum('rbl,lm->rbm', send.reshape(share, sub, width), inner_table, p...  8.53 us
  transfers between devices with their start and end apart: 25, of which 12 were waited for; matrix products, arithmetic and copies ran while one was open for 21% of the time, Pallas kernels for 0%

profile of v12, /device:TPU:0, one launch (start us, length us, event | category | flops | bytes accessed | tf_op | source)
XLA Modules:
  0.0 150.4 jit_solution(11899633906803903528)
XLA Ops:
  0.0 1.4 constant_dynamic-slice_fusion
  2.0 2.6 %collective-permute-start.1 = (bf16[16,3584]{1,0:T(8,128)(2,1)S(1)}, bf16[16,3584]{1,0:T(8,128)(2,1)S(1)}, u32[]{:S(2)}, u32[]{:S(2)}) collective-permute-start(bf16[16,3584]{1,0:T(8,128)(2,1)S(1)} %get-tuple-element.21), channel_id=1, source_target_pairs={{0,2},{1,3},{2,0},{3,1},{4,6},{5,7},{6,4},{7,5},{8,10},{9,11},{10,... | collective-permute-start | bytes 344072 | tf_op jit(solution)/shard_map/ppermute | solution.py:112
  4.7 2.8 %collective-permute-start.3 = (bf16[16,3584]{1,0:T(8,128)(2,1)S(1)}, bf16[16,3584]{1,0:T(8,128)(2,1)S(1)}, u32[]{:S(2)}, u32[]{:S(2)}) collective-permute-start(bf16[16,3584]{1,0:T(8,128)(2,1)S(1)} %get-tuple-element.19), channel_id=1, source_target_pairs={{0,4},{1,5},{2,6},{3,7},{4,0},{5,1},{6,2},{7,3},{8,12},{9,13},{10,... | collective-permute-start | bytes 344072 | tf_op jit(solution)/shard_map/ppermute | solution.py:112
  8.8 3.7 %collective-permute-start.5 = (bf16[16,3584]{1,0:T(8,128)(2,1)S(1)}, bf16[16,3584]{1,0:T(8,128)(2,1)S(1)}, u32[]{:S(2)}, u32[]{:S(2)}) collective-permute-start(bf16[16,3584]{1,0:T(8,128)(2,1)S(1)} %get-tuple-element.24), channel_id=1, source_target_pairs={{0,6},{1,7},{2,4},{3,5},{4,2},{5,3},{6,0},{7,1},{8,14},{9,15},{10,... | collective-permute-start | bytes 344072 | tf_op jit(solution)/shard_map/ppermute | solution.py:112
  16.9 6.4 %collective-permute-done.4 = bf16[16,3584]{1,0:T(8,128)(2,1)S(1)} collective-permute-done((bf16[16,3584]{1,0:T(8,128)(2,1)S(1)}, bf16[16,3584]{1,0:T(8,128)(2,1)S(1)}, u32[]{:S(2)}, u32[]{:S(2)}) %collective-permute-start.4) | collective-permute-done | bytes 114720 | tf_op jit(solution)/shard_map/ppermute | solution.py:112
  26.6 3.5 %fusion.4 = bf16[16,32,896]{2,1,0:T(8,128)(2,1)S(1)} fusion(f32[16,32,896]{2,0,1:T(8,128)} %bitcast.10, f32[32,32]{1,0:T(8,128)S(1)} %mul.89), kind=kOutput, calls=%fused_computation.11 | convolution fusion | flops 177078272 | bytes 2756608 | tf_op jit(solution)/shard_map/rbm,bc->rcm/dot_general | solution.py:126
  30.7 1.7 %fusion.49 = (bf16[16,1,3584]{2,1,0:T(2,128)(2,1)S(1)}, bf16[16,1,3584]{2,1,0:T(2,128)(2,1)S(1)}, bf16[16,1,3584]{2,1,0:T(2,128)(2,1)S(1)}, bf16[16,1,3584]{2,1,...) fusion(bf16[16,8,3584]{2,1,0:T(8,128)(2,1)S(1)} %reshape.114), kind=kLoop, calls=%fused_computation.115 | loop fusion | bytes 1835008 | tf_op jit(solution)/shard_map/slice | solution.py:131
  32.7 3.4 %collective-permute-start.8 = (bf16[16,3584]{1,0:T(8,128)(2,1)S(1)}, bf16[16,3584]{1,0:T(8,128)(2,1)S(1)}, u32[]{:S(2)}, u32[]{:S(2)}) collective-permute-start(bf16[16,3584]{1,0:T(8,128)(2,1)S(1)} %bitcast.180), channel_id=1, source_target_pairs={{0,2},{1,3},{2,0},{3,1},{4,6},{5,7},{6,4},{7,5},{8,10},{9,11},{10,... | collective-permute-start | bytes 344072 | tf_op jit(solution)/shard_map/ppermute | solution.py:133
  36.4 3.1 %collective-permute-start.10 = (bf16[16,3584]{1,0:T(8,128)(2,1)S(1)}, bf16[16,3584]{1,0:T(8,128)(2,1)S(1)}, u32[]{:S(2)}, u32[]{:S(2)}) collective-permute-start(bf16[16,3584]{1,0:T(8,128)(2,1)S(1)} %bitcast.177), channel_id=1, source_target_pairs={{0,4},{1,5},{2,6},{3,7},{4,0},{5,1},{6,2},{7,3},{8,12},{9,13},{10,... | collective-permute-start | bytes 344072 | tf_op jit(solution)/shard_map/ppermute | solution.py:133
  40.1 2.1 %collective-permute-start.12 = (bf16[16,3584]{1,0:T(8,128)(2,1)S(1)}, bf16[16,3584]{1,0:T(8,128)(2,1)S(1)}, u32[]{:S(2)}, u32[]{:S(2)}) collective-permute-start(bf16[16,3584]{1,0:T(8,128)(2,1)S(1)} %bitcast.179), channel_id=1, source_target_pairs={{0,6},{1,7},{2,4},{3,5},{4,2},{5,3},{6,0},{7,1},{8,14},{9,15},{10,... | collective-permute-start | bytes 344072 | tf_op jit(solution)/shard_map/ppermute | solution.py:133
  42.2 1.2 collective-permute-start.13
  43.5 2.7 %collective-permute-done.9 = bf16[16,3584]{1,0:T(8,128)(2,1)S(1)} collective-permute-done((bf16[16,3584]{1,0:T(8,128)(2,1)S(1)}, bf16[16,3584]{1,0:T(8,128)(2,1)S(1)}, u32[]{:S(2)}, u32[]{:S(2)}) %collective-permute-start.9) | collective-permute-done | bytes 114720 | tf_op jit(solution)/shard_map/ppermute | solution.py:133
  46.2 9.0 %collective-permute-done.11 = bf16[16,3584]{1,0:T(8,128)(2,1)S(1)} collective-permute-done((bf16[16,3584]{1,0:T(8,128)(2,1)S(1)}, bf16[16,3584]{1,0:T(8,128)(2,1)S(1)}, u32[]{:S(2)}, u32[]{:S(2)}) %collective-permute-start.11) | collective-permute-done | bytes 114720 | tf_op jit(solution)/shard_map/ppermute | solution.py:133
  55.3 1.6 %collective-permute-start.17 = (bf16[128,3584]{1,0:T(8,128)(2,1)S(1)}, bf16[128,3584]{1,0:T(8,128)(2,1)}, u32[]{:S(2)}, u32[]{:S(2)}) collective-permute-start(bf16[128,3584]{1,0:T(8,128)(2,1)S(1)} %constant_dynamic-update-slice_fusion), channel_id=1, source_target_pairs={{0,16},{8,24},{16,0},{24,8},{1,17},{9,25},{17,1},{25,9},{2,18},{10... | collective-permute-start | bytes 2752520 | tf_op jit(solution)/shard_map/ppermute | solution.py:147
  56.9 1.5 collective-permute-start.14
  58.4 7.4 %fusion.50 = f32[128,2048]{1,0:T(8,128)S(1)} fusion(bf16[128,3584]{1,0:T(8,128)(2,1)S(1)} %constant_dynamic-update-slice_fusion, bf16[3584,2048]{1,0:T(8,128)(2,1)} %param.6), kind=kOutput, calls=%fused_computation.116 | convolution fusion | flops 1879048192 | bytes 16646144 | tf_op jit(solution)/shard_map/dot_general | solution.py:154
  65.8 12.9 %collective-permute-done.17 = bf16[128,3584]{1,0:T(8,128)(2,1)} collective-permute-done((bf16[128,3584]{1,0:T(8,128)(2,1)S(1)}, bf16[128,3584]{1,0:T(8,128)(2,1)}, u32[]{:S(2)}, u32[]{:S(2)}) %collective-permute-start.17) | collective-permute-done | bytes 917536 | tf_op jit(solution)/shard_map/ppermute | solution.py:147
  79.7 1.6 %collective-permute-start.18 = (bf16[64,3584]{1,0:T(8,128)(2,1)S(1)}, bf16[64,3584]{1,0:T(8,128)(2,1)S(1)}, u32[]{:S(2)}, u32[]{:S(2)}) collective-permute-start(bf16[64,3584]{1,0:T(8,128)(2,1)S(1)} %slice.65), channel_id=1, source_target_pairs={{0,8},{8,0},{16,24},{24,16},{1,9},{9,1},{17,25},{25,17},{2,10},{10... | collective-permute-start | bytes 1376264 | tf_op jit(solution)/shard_map/ppermute | solution.py:148
  82.4 1.6 %collective-permute-start.19 = (bf16[64,3584]{1,0:T(8,128)(2,1)S(1)}, bf16[64,3584]{1,0:T(8,128)(2,1)S(1)}, u32[]{:S(2)}, u32[]{:S(2)}) collective-permute-start(bf16[64,3584]{1,0:T(8,128)(2,1)S(1)} %slice.66), channel_id=1, source_target_pairs={{0,16},{8,24},{16,0},{24,8},{1,17},{9,25},{17,1},{25,9},{2,18},{10... | collective-permute-start | bytes 1376264 | tf_op jit(solution)/shard_map/ppermute | solution.py:149
  84.0 3.4 %fusion.51 = f32[128,2048]{1,0:T(8,128)S(1)} fusion(bf16[128,3584]{1,0:T(8,128)(2,1)} %collective-permute-done.14, bf16[3584,2048]{1,0:T(8,128)(2,1)S(1)} %bitcast.163), kind=kOutput, calls=%fused_computation.117 | convolution fusion | flops 1879048192 | bytes 16646144 | tf_op jit(solution)/shard_map/dot_general | solution.py:154
  88.7 3.2 %fusion.52 = f32[128,2048]{1,0:T(8,128)S(1)} fusion(bf16[128,3584]{1,0:T(8,128)(2,1)} %collective-permute-done.17, bf16[3584,2048]{1,0:T(8,128)(2,1)S(1)} %bitcast.163), kind=kOutput, calls=%fused_computation.118 | convolution fusion | flops 1879048192 | bytes 16646144 | tf_op jit(solution)/shard_map/dot_general | solution.py:154
  92.4 2.3 %collective-permute-done.19 = bf16[64,3584]{1,0:T(8,128)(2,1)S(1)} collective-permute-done((bf16[64,3584]{1,0:T(8,128)(2,1)S(1)}, bf16[64,3584]{1,0:T(8,128)(2,1)S(1)}, u32[]{:S(2)}, u32[]{:S(2)}) %collective-permute-start.19) | collective-permute-done | bytes 458784 | tf_op jit(solution)/shard_map/ppermute | solution.py:149
  94.7 2.3 %fusion.25 = f32[128,2048]{1,0:T(8,128)S(1)} fusion(bf16[3584,2048]{1,0:T(8,128)(2,1)S(1)} %bitcast.163, bf16[64,3584]{1,0:T(8,128)(2,1)S(1)} %collective-permute-done.19, bf16[64,3584]{1,0:T(8,128)(2,1)S(1)} %collective-permute-done.18), kind=kOutput, calls=%fused_computation.38 | convolution fusion | flops 1880883200 | bytes 16646144 | tf_op jit(solution)/shard_map/dot_general | solution.py:154
  98.7 1.5 fusion.24
  100.2 4.5 %collective-permute-start.16 = (f32[64,2048]{1,0:T(8,128)S(1)}, f32[64,2048]{1,0:T(8,128)S(1)}, u32[]{:S(2)}, u32[]{:S(2)}) collective-permute-start(f32[64,2048]{1,0:T(8,128)S(1)} %dynamic-slice_bitcast_fusion), channel_id=1, source_target_pairs={{0,2},{1,3},{2,0},{3,1},{4,6},{5,7},{6,4},{7,5},{8,10},{9,11},{10,... | collective-permute-start | bytes 1572872 | tf_op jit(solution)/shard_map/ppermute | solution.py:165
  104.7 1.3 fusion.19
  107.1 10.3 %collective-permute-done.16 = f32[64,2048]{1,0:T(8,128)S(1)} collective-permute-done((f32[64,2048]{1,0:T(8,128)S(1)}, f32[64,2048]{1,0:T(8,128)S(1)}, u32[]{:S(2)}, u32[]{:S(2)}) %collective-permute-start.16) | collective-permute-done | bytes 524320 | tf_op jit(solution)/shard_map/ppermute | solution.py:165
  117.4 5.0 %collective-permute-done.21 = f32[64,1024]{1,0:T(8,128)S(1)} collective-permute-done((f32[64,1024]{1,0:T(8,128)S(1)}, f32[64,1024]{1,0:T(8,128)S(1)}, u32[]{:S(2)}, u32[]{:S(2)}) %collective-permute-start.21) | collective-permute-done | bytes 262176 | tf_op jit(solution)/shard_map/ppermute | solution.py:165
  122.5 1.8 %collective-permute-start.23 = (f32[64,1024]{1,0:T(8,128)S(1)}, f32[64,1024]{1,0:T(8,128)S(1)}, u32[]{:S(2)}, u32[]{:S(2)}) collective-permute-start(f32[64,1024]{1,0:T(8,128)S(1)} %dynamic-slice_bitcast_fusion.1), channel_id=1, source_target_pairs={{0,2},{1,3},{2,0},{3,1},{4,6},{5,7},{6,4},{7,5},{8,10},{9,11},{10,... | collective-permute-start | bytes 786440 | tf_op jit(solution)/shard_map/ppermute | solution.py:165
  125.6 9.9 %collective-permute-done.23 = f32[64,1024]{1,0:T(8,128)S(1)} collective-permute-done((f32[64,1024]{1,0:T(8,128)S(1)}, f32[64,1024]{1,0:T(8,128)S(1)}, u32[]{:S(2)}, u32[]{:S(2)}) %collective-permute-start.23) | collective-permute-done | bytes 262176 | tf_op jit(solution)/shard_map/ppermute | solution.py:165
  135.7 8.8 %collective-permute-done.22 = f32[64,1024]{1,0:T(8,128)S(1)} collective-permute-done((f32[64,1024]{1,0:T(8,128)S(1)}, f32[64,1024]{1,0:T(8,128)S(1)}, u32[]{:S(2)}, u32[]{:S(2)}) %collective-permute-start.22) | collective-permute-done | bytes 262176 | tf_op jit(solution)/shard_map/ppermute | solution.py:182
  144.5 5.1 %collective-permute-done.24 = f32[64,1024]{1,0:T(8,128)S(1)} collective-permute-done((f32[64,1024]{1,0:T(8,128)S(1)}, f32[64,1024]{1,0:T(8,128)S(1)}, u32[]{:S(2)}, u32[]{:S(2)}) %collective-permute-start.24) | collective-permute-done | bytes 262176 | tf_op jit(solution)/shard_map/ppermute | solution.py:182
  (98 shorter events, 20.2 us)
Async XLA Ops:
  0.0 8.6 %copy-start.7 = (f32[4,4]{1,0:T(4,128)S(1)}, f32[4,4]{1,0:T(4,128)}, u32[]{:S(2)}) copy-start(f32[4,4]{1,0:T(4,128)} %constant.139.clone) | copy-start | bytes 196
  1.4 7.3 %collective-permute-start = (bf16[16,3584]{1,0:T(8,128)(2,1)S(1)}, bf16[16,3584]{1,0:T(8,128)(2,1)S(1)}, u32[]{:S(2)}, u32[]{:S(2)}) collective-permute-start(bf16[16,3584]{1,0:T(8,128)(2,1)S(1)} %get-tuple-element.22), channel_id=1, source_target_pairs={{0,1},{1,0},{2,3},{3,2},{4,5},{5,4},{6,7},{7,6},{8,9},{9,8},{10,11... | collective-permute-start | bytes 344072 | tf_op jit(solution)/shard_map/ppermute | solution.py:112
  2.0 11.5 %collective-permute-start.1 = (bf16[16,3584]{1,0:T(8,128)(2,1)S(1)}, bf16[16,3584]{1,0:T(8,128)(2,1)S(1)}, u32[]{:S(2)}, u32[]{:S(2)}) collective-permute-start(bf16[16,3584]{1,0:T(8,128)(2,1)S(1)} %get-tuple-element.21), channel_id=1, source_target_pairs={{0,2},{1,3},{2,0},{3,1},{4,6},{5,7},{6,4},{7,5},{8,10},{9,11},{10,... | collective-permute-start | bytes 344072 | tf_op jit(solution)/shard_map/ppermute | solution.py:112
  4.6 10.2 %collective-permute-start.2 = (bf16[16,3584]{1,0:T(8,128)(2,1)S(1)}, bf16[16,3584]{1,0:T(8,128)(2,1)S(1)}, u32[]{:S(2)}, u32[]{:S(2)}) collective-permute-start(bf16[16,3584]{1,0:T(8,128)(2,1)S(1)} %get-tuple-element.20), channel_id=1, source_target_pairs={{0,3},{1,2},{2,1},{3,0},{4,7},{5,6},{6,5},{7,4},{8,11},{9,10},{10,... | collective-permute-start | bytes 344072 | tf_op jit(solution)/shard_map/ppermute | solution.py:112
  4.7 11.2 %collective-permute-start.3 = (bf16[16,3584]{1,0:T(8,128)(2,1)S(1)}, bf16[16,3584]{1,0:T(8,128)(2,1)S(1)}, u32[]{:S(2)}, u32[]{:S(2)}) collective-permute-start(bf16[16,3584]{1,0:T(8,128)(2,1)S(1)} %get-tuple-element.19), channel_id=1, source_target_pairs={{0,4},{1,5},{2,6},{3,7},{4,0},{5,1},{6,2},{7,3},{8,12},{9,13},{10,... | collective-permute-start | bytes 344072 | tf_op jit(solution)/shard_map/ppermute | solution.py:112
  7.4 15.9 %collective-permute-start.4 = (bf16[16,3584]{1,0:T(8,128)(2,1)S(1)}, bf16[16,3584]{1,0:T(8,128)(2,1)S(1)}, u32[]{:S(2)}, u32[]{:S(2)}) collective-permute-start(bf16[16,3584]{1,0:T(8,128)(2,1)S(1)} %get-tuple-element.18), channel_id=1, source_target_pairs={{0,5},{1,4},{2,7},{3,6},{4,1},{5,0},{6,3},{7,2},{8,13},{9,12},{10,... | collective-permute-start | bytes 344072 | tf_op jit(solution)/shard_map/ppermute | solution.py:112
  8.8 15.7 %collective-permute-start.5 = (bf16[16,3584]{1,0:T(8,128)(2,1)S(1)}, bf16[16,3584]{1,0:T(8,128)(2,1)S(1)}, u32[]{:S(2)}, u32[]{:S(2)}) collective-permute-start(bf16[16,3584]{1,0:T(8,128)(2,1)S(1)} %get-tuple-element.24), channel_id=1, source_target_pairs={{0,6},{1,7},{2,4},{3,5},{4,2},{5,3},{6,0},{7,1},{8,14},{9,15},{10,... | collective-permute-start | bytes 344072 | tf_op jit(solution)/shard_map/ppermute | solution.py:112
  13.5 12.0 %collective-permute-start.6 = (bf16[16,3584]{1,0:T(8,128)(2,1)S(1)}, bf16[16,3584]{1,0:T(8,128)(2,1)S(1)}, u32[]{:S(2)}, u32[]{:S(2)}) collective-permute-start(bf16[16,3584]{1,0:T(8,128)(2,1)S(1)} %get-tuple-element.17), channel_id=1, source_target_pairs={{0,7},{1,6},{2,5},{3,4},{4,3},{5,2},{6,1},{7,0},{8,15},{9,14},{10,... | collective-permute-start | bytes 344072 | tf_op jit(solution)/shard_map/ppermute | solution.py:112
  32.4 7.7 %collective-permute-start.7 = (bf16[16,3584]{1,0:T(8,128)(2,1)S(1)}, bf16[16,3584]{1,0:T(8,128)(2,1)S(1)}, u32[]{:S(2)}, u32[]{:S(2)}) collective-permute-start(bf16[16,3584]{1,0:T(8,128)(2,1)S(1)} %bitcast.181), channel_id=1, source_target_pairs={{0,1},{1,0},{2,3},{3,2},{4,5},{5,4},{6,7},{7,6},{8,9},{9,8},{10,11... | collective-permute-start | bytes 344072 | tf_op jit(solution)/shard_map/ppermute | solution.py:133
  32.7 9.5 %collective-permute-start.8 = (bf16[16,3584]{1,0:T(8,128)(2,1)S(1)}, bf16[16,3584]{1,0:T(8,128)(2,1)S(1)}, u32[]{:S(2)}, u32[]{:S(2)}) collective-permute-start(bf16[16,3584]{1,0:T(8,128)(2,1)S(1)} %bitcast.180), channel_id=1, source_target_pairs={{0,2},{1,3},{2,0},{3,1},{4,6},{5,7},{6,4},{7,5},{8,10},{9,11},{10,... | collective-permute-start | bytes 344072 | tf_op jit(solution)/shard_map/ppermute | solution.py:133
  36.2 10.0 %collective-permute-start.9 = (bf16[16,3584]{1,0:T(8,128)(2,1)S(1)}, bf16[16,3584]{1,0:T(8,128)(2,1)S(1)}, u32[]{:S(2)}, u32[]{:S(2)}) collective-permute-start(bf16[16,3584]{1,0:T(8,128)(2,1)S(1)} %bitcast.178), channel_id=1, source_target_pairs={{0,3},{1,2},{2,1},{3,0},{4,7},{5,6},{6,5},{7,4},{8,11},{9,10},{10,... | collective-permute-start | bytes 344072 | tf_op jit(solution)/shard_map/ppermute | solution.py:133
  36.4 9.8 %collective-permute-start.10 = (bf16[16,3584]{1,0:T(8,128)(2,1)S(1)}, bf16[16,3584]{1,0:T(8,128)(2,1)S(1)}, u32[]{:S(2)}, u32[]{:S(2)}) collective-permute-start(bf16[16,3584]{1,0:T(8,128)(2,1)S(1)} %bitcast.177), channel_id=1, source_target_pairs={{0,4},{1,5},{2,6},{3,7},{4,0},{5,1},{6,2},{7,3},{8,12},{9,13},{10,... | collective-permute-start | bytes 344072 | tf_op jit(solution)/shard_map/ppermute | solution.py:133
  39.5 15.7 %collective-permute-start.11 = (bf16[16,3584]{1,0:T(8,128)(2,1)S(1)}, bf16[16,3584]{1,0:T(8,128)(2,1)S(1)}, u32[]{:S(2)}, u32[]{:S(2)}) collective-permute-start(bf16[16,3584]{1,0:T(8,128)(2,1)S(1)} %bitcast.176), channel_id=1, source_target_pairs={{0,5},{1,4},{2,7},{3,6},{4,1},{5,0},{6,3},{7,2},{8,13},{9,12},{10,... | collective-permute-start | bytes 344072 | tf_op jit(solution)/shard_map/ppermute | solution.py:133
  40.0 44.0 %slice-start = ((s8[14680064]{0:T(1024)(128)(4,1)}), s8[2097152]{0:T(1024)(128)(4,1)S(1)}, s32[]{:S(2)}) async-start(s8[14680064]{0:T(1024)(128)(4,1)} %bitcast.162), calls=%async_computation | async-start | bytes 4194304
  40.1 15.2 %collective-permute-start.12 = (bf16[16,3584]{1,0:T(8,128)(2,1)S(1)}, bf16[16,3584]{1,0:T(8,128)(2,1)S(1)}, u32[]{:S(2)}, u32[]{:S(2)}) collective-permute-start(bf16[16,3584]{1,0:T(8,128)(2,1)S(1)} %bitcast.179), channel_id=1, source_target_pairs={{0,6},{1,7},{2,4},{3,5},{4,2},{5,3},{6,0},{7,1},{8,14},{9,15},{10,... | collective-permute-start | bytes 344072 | tf_op jit(solution)/shard_map/ppermute | solution.py:133
  42.2 13.1 %collective-permute-start.13 = (bf16[16,3584]{1,0:T(8,128)(2,1)S(1)}, bf16[16,3584]{1,0:T(8,128)(2,1)S(1)}, u32[]{:S(2)}, u32[]{:S(2)}) collective-permute-start(bf16[16,3584]{1,0:T(8,128)(2,1)S(1)} %bitcast.175), channel_id=1, source_target_pairs={{0,7},{1,6},{2,5},{3,4},{4,3},{5,2},{6,1},{7,0},{8,15},{9,14},{10,... | collective-permute-start | bytes 344072 | tf_op jit(solution)/shard_map/ppermute | solution.py:133
  55.3 23.4 %collective-permute-start.17 = (bf16[128,3584]{1,0:T(8,128)(2,1)S(1)}, bf16[128,3584]{1,0:T(8,128)(2,1)}, u32[]{:S(2)}, u32[]{:S(2)}) collective-permute-start(bf16[128,3584]{1,0:T(8,128)(2,1)S(1)} %constant_dynamic-update-slice_fusion), channel_id=1, source_target_pairs={{0,16},{8,24},{16,0},{24,8},{1,17},{9,25},{17,1},{25,9},{2,18},{10... | collective-permute-start | bytes 2752520 | tf_op jit(solution)/shard_map/ppermute | solution.py:147
  56.9 24.4 %collective-permute-start.14 = (bf16[128,3584]{1,0:T(8,128)(2,1)S(1)}, bf16[128,3584]{1,0:T(8,128)(2,1)}, u32[]{:S(2)}, u32[]{:S(2)}) collective-permute-start(bf16[128,3584]{1,0:T(8,128)(2,1)S(1)} %constant_dynamic-update-slice_fusion), channel_id=1, source_target_pairs={{0,8},{8,0},{16,24},{24,16},{1,9},{9,1},{17,25},{25,17},{2,10},{10... | collective-permute-start | bytes 2752520 | tf_op jit(solution)/shard_map/ppermute | solution.py:146
  58.4 25.6 %slice-start.1 = ((s8[14680064]{0:T(1024)(128)(4,1)}), s8[4194304]{0:T(1024)(128)(4,1)S(1)}, s32[]{:S(2)}) async-start(s8[14680064]{0:T(1024)(128)(4,1)} %bitcast.162), calls=%async_computation.1 | async-start | bytes 8388608
  58.4 25.6 %slice-start.2 = ((s8[14680064]{0:T(1024)(128)(4,1)}), s8[4194304]{0:T(1024)(128)(4,1)S(1)}, s32[]{:S(2)}) async-start(s8[14680064]{0:T(1024)(128)(4,1)} %bitcast.162), calls=%async_computation.2 | async-start | bytes 8388608
  58.4 25.6 %slice-start.3 = ((s8[14680064]{0:T(1024)(128)(4,1)}), s8[4194304]{0:T(1024)(128)(4,1)S(1)}, s32[]{:S(2)}) async-start(s8[14680064]{0:T(1024)(128)(4,1)} %bitcast.162), calls=%async_computation.3 | async-start | bytes 8388608
  65.8 21.6 %copy-start.1 = (f32[128,2048]{1,0:T(8,128)}, f32[128,2048]{1,0:T(8,128)S(1)}, u32[]{:S(2)}) copy-start(f32[128,2048]{1,0:T(8,128)S(1)} %fusion.50) | copy-start | bytes 3145732
  79.7 12.6 %collective-permute-start.18 = (bf16[64,3584]{1,0:T(8,128)(2,1)S(1)}, bf16[64,3584]{1,0:T(8,128)(2,1)S(1)}, u32[]{:S(2)}, u32[]{:S(2)}) collective-permute-start(bf16[64,3584]{1,0:T(8,128)(2,1)S(1)} %slice.65), channel_id=1, source_target_pairs={{0,8},{8,0},{16,24},{24,16},{1,9},{9,1},{17,25},{25,17},{2,10},{10... | collective-permute-start | bytes 1376264 | tf_op jit(solution)/shard_map/ppermute | solution.py:148
  82.4 12.3 %collective-permute-start.19 = (bf16[64,3584]{1,0:T(8,128)(2,1)S(1)}, bf16[64,3584]{1,0:T(8,128)(2,1)S(1)}, u32[]{:S(2)}, u32[]{:S(2)}) collective-permute-start(bf16[64,3584]{1,0:T(8,128)(2,1)S(1)} %slice.66), channel_id=1, source_target_pairs={{0,16},{8,24},{16,0},{24,8},{1,17},{9,25},{17,1},{25,9},{2,18},{10... | collective-permute-start | bytes 1376264 | tf_op jit(solution)/shard_map/ppermute | solution.py:149
  88.7 9.5 %collective-permute-start.15 = (f32[2,64,2048]{2,1,0:T(8,128)}, f32[2,64,2048]{2,1,0:T(8,128)}, u32[]{:S(2)}, u32[]{:S(2)}) collective-permute-start(f32[2,64,2048]{2,1,0:T(8,128)} %fusion.21), channel_id=1, source_target_pairs={{0,1},{1,0},{2,3},{3,2},{4,5},{5,4},{6,7},{7,6},{8,9},{9,8},{10,11... | collective-permute-start | bytes 3145736 | tf_op jit(solution)/shard_map/ppermute | solution.py:159
  98.2 6.5 %collective-permute-start.20 = (f32[2,64,2048]{2,1,0:T(8,128)}, f32[2,64,2048]{2,1,0:T(8,128)}, u32[]{:S(2)}, u32[]{:S(2)}) collective-permute-start(f32[2,64,2048]{2,1,0:T(8,128)} %fusion.16), channel_id=1, source_target_pairs={{0,1},{1,0},{2,3},{3,2},{4,5},{5,4},{6,7},{7,6},{8,9},{9,8},{10,11... | collective-permute-start | bytes 3145736 | tf_op jit(solution)/shard_map/ppermute | solution.py:159
  100.2 17.2 %collective-permute-start.16 = (f32[64,2048]{1,0:T(8,128)S(1)}, f32[64,2048]{1,0:T(8,128)S(1)}, u32[]{:S(2)}, u32[]{:S(2)}) collective-permute-start(f32[64,2048]{1,0:T(8,128)S(1)} %dynamic-slice_bitcast_fusion), channel_id=1, source_target_pairs={{0,2},{1,3},{2,0},{3,1},{4,6},{5,7},{6,4},{7,5},{8,10},{9,11},{10,... | collective-permute-start | bytes 1572872 | tf_op jit(solution)/shard_map/ppermute | solution.py:165
  106.1 16.4 %collective-permute-start.21 = (f32[64,1024]{1,0:T(8,128)S(1)}, f32[64,1024]{1,0:T(8,128)S(1)}, u32[]{:S(2)}, u32[]{:S(2)}) collective-permute-start(f32[64,1024]{1,0:T(8,128)S(1)} %dynamic-slice_bitcast_fusion.2), channel_id=1, source_target_pairs={{0,2},{1,3},{2,0},{3,1},{4,6},{5,7},{6,4},{7,5},{8,10},{9,11},{10,... | collective-permute-start | bytes 786440 | tf_op jit(solution)/shard_map/ppermute | solution.py:165
  122.5 12.9 %collective-permute-start.23 = (f32[64,1024]{1,0:T(8,128)S(1)}, f32[64,1024]{1,0:T(8,128)S(1)}, u32[]{:S(2)}, u32[]{:S(2)}) collective-permute-start(f32[64,1024]{1,0:T(8,128)S(1)} %dynamic-slice_bitcast_fusion.1), channel_id=1, source_target_pairs={{0,2},{1,3},{2,0},{3,1},{4,6},{5,7},{6,4},{7,5},{8,10},{9,11},{10,... | collective-permute-start | bytes 786440 | tf_op jit(solution)/shard_map/ppermute | solution.py:165
  124.5 25.2 %copy-start.6 = (f32[2048]{0:T(1024)S(1)}, f32[2048]{0:T(1024)}, u32[]{:S(2)}) copy-start(f32[2048]{0:T(1024)} %param.7) | copy-start | bytes 24580
  124.5 20.0 %collective-permute-start.22 = (f32[64,1024]{1,0:T(8,128)S(1)}, f32[64,1024]{1,0:T(8,128)S(1)}, u32[]{:S(2)}, u32[]{:S(2)}) collective-permute-start(f32[64,1024]{1,0:T(8,128)S(1)} %fusion.36), channel_id=1, source_target_pairs={{0,4},{1,5},{2,6},{3,7},{4,0},{5,1},{6,2},{7,3},{8,12},{9,13},{10,... | collective-permute-start | bytes 786440 | tf_op jit(solution)/shard_map/ppermute | solution.py:182
  135.6 14.0 %collective-permute-start.24 = (f32[64,1024]{1,0:T(8,128)S(1)}, f32[64,1024]{1,0:T(8,128)S(1)}, u32[]{:S(2)}, u32[]{:S(2)}) collective-permute-start(f32[64,1024]{1,0:T(8,128)S(1)} %fusion.31), channel_id=1, source_target_pairs={{0,4},{1,5},{2,6},{3,7},{4,0},{5,1},{6,2},{7,3},{8,12},{9,13},{10,... | collective-permute-start | bytes 786440 | tf_op jit(solution)/shard_map/ppermute | solution.py:182
  (5 other events, 22.0 us)

commit v13 on v12

--- a/solution.py
+++ b/solution.py
@@ -9,6 +9,7 @@
 PALEY = 28
 INNER = 32
 CHUNKS = 1
+TAIL_PIECES = 4
 
 
 def paley_table():
@@ -167,11 +168,11 @@
     near = second_halving(first_halving((block, across_x)))
     far_summed = first_halving((across_y, diagonal))
     columns = near.shape[-1]
-    width = columns // 2
+    width = columns // TAIL_PIECES
     chosen = here // 2 % 2 ^ high
     results = []
     previous = None
-    for start in (0, width):
+    for start in range(0, columns, width):
         piece = far_summed[..., start : start + width]
         if previous is not None:
             _, piece = lax.optimization_barrier((previous, piece))

time: 151 us -> 150 us (level)
  waiting for transfers between devices: 73 us -> 65.3 us
  starting transfers between devices: 35.2 us -> 42.3 us
    ppermute x2 -> x4, starting transfers between devices: 1.18 us -> 7.14 us  [product_and_reduce(): results.append(keep + lax.ppermute(send, 'tp', tp_pairs(4)))]
    ppermute x3 -> x5, waiting for transfers between devices: 25.2 us -> 20.4 us  [second_halving(): return keep + lax.ppermute(send, 'tp', tp_pairs(2))]
    ppermute x2 -> x4, waiting for transfers between devices: 13.8 us -> 11.1 us  [product_and_reduce(): results.append(keep + lax.ppermute(send, 'tp', tp_pairs(4)))]
    ppermute x3 -> x5, starting transfers between devices: 7.24 us -> 8.23 us  [second_halving(): return keep + lax.ppermute(send, 'tp', tp_pairs(2))]
  transfers between devices with their start and end apart: 25 -> 29, of which waited for: 12 -> 15; matrix products, arithmetic and copies ran while one was open for 21% -> 21% of each run, Pallas kernels for 0% -> 0%
where the time goes in v13:
time: 150 us
  waiting for transfers between devices  65.3 us (44%)
  starting transfers between devices  42.3 us (28%)
  matrix products  28.5 us (19%)
  local copies, waits for them, and re-layouts  6.98 us (5%)
  other arithmetic  6.34 us (4%)
    ppermute x5, waiting for transfers between devices, second_halving(): return keep + lax.ppermute(send, 'tp', tp_pairs(2))  20.4 us
    dot_general x4, matrix products, first_halving(): jnp.dot(piece, down_weight, preferred_element_type=jnp.float32)  16.4 us
    ppermute x1, waiting for transfers between devices, product_and_reduce(): across_y = lax.ppermute(block, 'seq', seq_pairs(2))  12.8 us
    ppermute x7, waiting for transfers between devices, spread_rotate_return(): block = lax.ppermute(block, 'tp', pairs(distance))  11.7 us
    ppermute x4, waiting for transfers between devices, product_and_reduce(): results.append(keep + lax.ppermute(send, 'tp', tp_pairs(4)))  11.1 us
    ppermute x7, starting transfers between devices, spread_rotate_return(): block = lax.ppermute(block, 'tp', pairs(distance))  10.9 us
    ppermute x7, starting transfers between devices, spread_rotate_return(): send = lax.ppermute(send, 'tp', pairs(distance))  9.71 us
    dot_general x8, matrix products, spread_rotate_return(): jnp.einsum('rbl,lm->rbm', send.reshape(share, sub, width), inner_table, p...  8.56 us
  transfers between devices with their start and end apart: 29, of which 15 were waited for; matrix products, arithmetic and copies ran while one was open for 21% of the time, Pallas kernels for 0%

profile of v13, /device:TPU:0, one launch (start us, length us, event | category | flops | bytes accessed | tf_op | source)
XLA Modules:
  0.0 149.9 jit_solution(6431934289155796781)
XLA Ops:
  2.0 2.6 %collective-permute-start.1 = (bf16[16,3584]{1,0:T(8,128)(2,1)S(1)}, bf16[16,3584]{1,0:T(8,128)(2,1)S(1)}, u32[]{:S(2)}, u32[]{:S(2)}) collective-permute-start(bf16[16,3584]{1,0:T(8,128)(2,1)S(1)} %get-tuple-element.27), channel_id=1, source_target_pairs={{0,2},{1,3},{2,0},{3,1},{4,6},{5,7},{6,4},{7,5},{8,10},{9,11},{10,... | collective-permute-start | bytes 344072 | tf_op jit(solution)/shard_map/ppermute | solution.py:113
  4.7 2.8 %collective-permute-start.3 = (bf16[16,3584]{1,0:T(8,128)(2,1)S(1)}, bf16[16,3584]{1,0:T(8,128)(2,1)S(1)}, u32[]{:S(2)}, u32[]{:S(2)}) collective-permute-start(bf16[16,3584]{1,0:T(8,128)(2,1)S(1)} %get-tuple-element.25), channel_id=1, source_target_pairs={{0,4},{1,5},{2,6},{3,7},{4,0},{5,1},{6,2},{7,3},{8,12},{9,13},{10,... | collective-permute-start | bytes 344072 | tf_op jit(solution)/shard_map/ppermute | solution.py:113
  8.8 3.7 %collective-permute-start.5 = (bf16[16,3584]{1,0:T(8,128)(2,1)S(1)}, bf16[16,3584]{1,0:T(8,128)(2,1)S(1)}, u32[]{:S(2)}, u32[]{:S(2)}) collective-permute-start(bf16[16,3584]{1,0:T(8,128)(2,1)S(1)} %get-tuple-element.30), channel_id=1, source_target_pairs={{0,6},{1,7},{2,4},{3,5},{4,2},{5,3},{6,0},{7,1},{8,14},{9,15},{10,... | collective-permute-start | bytes 344072 | tf_op jit(solution)/shard_map/ppermute | solution.py:113
  16.9 6.5 %collective-permute-done.4 = bf16[16,3584]{1,0:T(8,128)(2,1)S(1)} collective-permute-done((bf16[16,3584]{1,0:T(8,128)(2,1)S(1)}, bf16[16,3584]{1,0:T(8,128)(2,1)S(1)}, u32[]{:S(2)}, u32[]{:S(2)}) %collective-permute-start.4) | collective-permute-done | bytes 114720 | tf_op jit(solution)/shard_map/ppermute | solution.py:113
  26.6 3.5 %fusion.4 = bf16[16,32,896]{2,1,0:T(8,128)(2,1)S(1)} fusion(f32[16,32,896]{2,0,1:T(8,128)} %bitcast.10, f32[32,32]{1,0:T(8,128)S(1)} %mul.89), kind=kOutput, calls=%fused_computation.11 | convolution fusion | flops 177078272 | bytes 2756608 | tf_op jit(solution)/shard_map/rbm,bc->rcm/dot_general | solution.py:127
  30.7 1.7 %fusion.59 = (bf16[16,1,3584]{2,1,0:T(2,128)(2,1)S(1)}, bf16[16,1,3584]{2,1,0:T(2,128)(2,1)S(1)}, bf16[16,1,3584]{2,1,0:T(2,128)(2,1)S(1)}, bf16[16,1,3584]{2,1,...) fusion(bf16[16,8,3584]{2,1,0:T(8,128)(2,1)S(1)} %reshape.114), kind=kLoop, calls=%fused_computation.139 | loop fusion | bytes 1835008 | tf_op jit(solution)/shard_map/slice | solution.py:132
  32.7 3.5 %collective-permute-start.8 = (bf16[16,3584]{1,0:T(8,128)(2,1)S(1)}, bf16[16,3584]{1,0:T(8,128)(2,1)S(1)}, u32[]{:S(2)}, u32[]{:S(2)}) collective-permute-start(bf16[16,3584]{1,0:T(8,128)(2,1)S(1)} %bitcast.210), channel_id=1, source_target_pairs={{0,2},{1,3},{2,0},{3,1},{4,6},{5,7},{6,4},{7,5},{8,10},{9,11},{10,... | collective-permute-start | bytes 344072 | tf_op jit(solution)/shard_map/ppermute | solution.py:134
  36.4 3.1 %collective-permute-start.10 = (bf16[16,3584]{1,0:T(8,128)(2,1)S(1)}, bf16[16,3584]{1,0:T(8,128)(2,1)S(1)}, u32[]{:S(2)}, u32[]{:S(2)}) collective-permute-start(bf16[16,3584]{1,0:T(8,128)(2,1)S(1)} %bitcast.207), channel_id=1, source_target_pairs={{0,4},{1,5},{2,6},{3,7},{4,0},{5,1},{6,2},{7,3},{8,12},{9,13},{10,... | collective-permute-start | bytes 344072 | tf_op jit(solution)/shard_map/ppermute | solution.py:134
  40.1 2.1 %collective-permute-start.12 = (bf16[16,3584]{1,0:T(8,128)(2,1)S(1)}, bf16[16,3584]{1,0:T(8,128)(2,1)S(1)}, u32[]{:S(2)}, u32[]{:S(2)}) collective-permute-start(bf16[16,3584]{1,0:T(8,128)(2,1)S(1)} %bitcast.209), channel_id=1, source_target_pairs={{0,6},{1,7},{2,4},{3,5},{4,2},{5,3},{6,0},{7,1},{8,14},{9,15},{10,... | collective-permute-start | bytes 344072 | tf_op jit(solution)/shard_map/ppermute | solution.py:134
  43.5 2.7 %collective-permute-done.9 = bf16[16,3584]{1,0:T(8,128)(2,1)S(1)} collective-permute-done((bf16[16,3584]{1,0:T(8,128)(2,1)S(1)}, bf16[16,3584]{1,0:T(8,128)(2,1)S(1)}, u32[]{:S(2)}, u32[]{:S(2)}) %collective-permute-start.9) | collective-permute-done | bytes 114720 | tf_op jit(solution)/shard_map/ppermute | solution.py:134
  46.2 9.0 %collective-permute-done.11 = bf16[16,3584]{1,0:T(8,128)(2,1)S(1)} collective-permute-done((bf16[16,3584]{1,0:T(8,128)(2,1)S(1)}, bf16[16,3584]{1,0:T(8,128)(2,1)S(1)}, u32[]{:S(2)}, u32[]{:S(2)}) %collective-permute-start.11) | collective-permute-done | bytes 114720 | tf_op jit(solution)/shard_map/ppermute | solution.py:134
  55.3 1.6 %collective-permute-start.17 = (bf16[128,3584]{1,0:T(8,128)(2,1)S(1)}, bf16[128,3584]{1,0:T(8,128)(2,1)}, u32[]{:S(2)}, u32[]{:S(2)}) collective-permute-start(bf16[128,3584]{1,0:T(8,128)(2,1)S(1)} %constant_dynamic-update-slice_fusion), channel_id=1, source_target_pairs={{0,16},{8,24},{16,0},{24,8},{1,17},{9,25},{17,1},{25,9},{2,18},{10... | collective-permute-start | bytes 2752520 | tf_op jit(solution)/shard_map/ppermute | solution.py:148
  56.9 1.5 collective-permute-start.14
  58.4 7.4 %fusion.60 = f32[128,2048]{1,0:T(8,128)S(1)} fusion(bf16[128,3584]{1,0:T(8,128)(2,1)S(1)} %constant_dynamic-update-slice_fusion, bf16[3584,2048]{1,0:T(8,128)(2,1)} %param.6), kind=kOutput, calls=%fused_computation.140 | convolution fusion | flops 1879048192 | bytes 16646144 | tf_op jit(solution)/shard_map/dot_general | solution.py:155
  65.8 12.8 %collective-permute-done.17 = bf16[128,3584]{1,0:T(8,128)(2,1)} collective-permute-done((bf16[128,3584]{1,0:T(8,128)(2,1)S(1)}, bf16[128,3584]{1,0:T(8,128)(2,1)}, u32[]{:S(2)}, u32[]{:S(2)}) %collective-permute-start.17) | collective-permute-done | bytes 917536 | tf_op jit(solution)/shard_map/ppermute | solution.py:148
  79.7 1.6 %collective-permute-start.18 = (bf16[64,3584]{1,0:T(8,128)(2,1)S(1)}, bf16[64,3584]{1,0:T(8,128)(2,1)S(1)}, u32[]{:S(2)}, u32[]{:S(2)}) collective-permute-start(bf16[64,3584]{1,0:T(8,128)(2,1)S(1)} %slice.81), channel_id=1, source_target_pairs={{0,8},{8,0},{16,24},{24,16},{1,9},{9,1},{17,25},{25,17},{2,10},{10... | collective-permute-start | bytes 1376264 | tf_op jit(solution)/shard_map/ppermute | solution.py:149
  82.4 1.6 %collective-permute-start.19 = (bf16[64,3584]{1,0:T(8,128)(2,1)S(1)}, bf16[64,3584]{1,0:T(8,128)(2,1)S(1)}, u32[]{:S(2)}, u32[]{:S(2)}) collective-permute-start(bf16[64,3584]{1,0:T(8,128)(2,1)S(1)} %slice.82), channel_id=1, source_target_pairs={{0,16},{8,24},{16,0},{24,8},{1,17},{9,25},{17,1},{25,9},{2,18},{10... | collective-permute-start | bytes 1376264 | tf_op jit(solution)/shard_map/ppermute | solution.py:150
  84.0 3.4 %fusion.61 = f32[128,2048]{1,0:T(8,128)S(1)} fusion(bf16[128,3584]{1,0:T(8,128)(2,1)} %collective-permute-done.14, bf16[3584,2048]{1,0:T(8,128)(2,1)S(1)} %bitcast.189), kind=kOutput, calls=%fused_computation.141 | convolution fusion | flops 1879048192 | bytes 16646144 | tf_op jit(solution)/shard_map/dot_general | solution.py:155
  88.8 3.2 %fusion.62 = f32[128,2048]{1,0:T(8,128)S(1)} fusion(bf16[128,3584]{1,0:T(8,128)(2,1)} %collective-permute-done.17, bf16[3584,2048]{1,0:T(8,128)(2,1)S(1)} %bitcast.189), kind=kOutput, calls=%fused_computation.142 | convolution fusion | flops 1879048192 | bytes 16646144 | tf_op jit(solution)/shard_map/dot_general | solution.py:155
  92.4 2.4 %collective-permute-done.19 = bf16[64,3584]{1,0:T(8,128)(2,1)S(1)} collective-permute-done((bf16[64,3584]{1,0:T(8,128)(2,1)S(1)}, bf16[64,3584]{1,0:T(8,128)(2,1)S(1)}, u32[]{:S(2)}, u32[]{:S(2)}) %collective-permute-start.19) | collective-permute-done | bytes 458784 | tf_op jit(solution)/shard_map/ppermute | solution.py:150
  94.7 2.3 %fusion.25 = f32[128,2048]{1,0:T(8,128)S(1)} fusion(bf16[3584,2048]{1,0:T(8,128)(2,1)S(1)} %bitcast.189, bf16[64,3584]{1,0:T(8,128)(2,1)S(1)} %collective-permute-done.19, bf16[64,3584]{1,0:T(8,128)(2,1)S(1)} %collective-permute-done.18), kind=kOutput, calls=%fused_computation.38 | convolution fusion | flops 1880883200 | bytes 16646144 | tf_op jit(solution)/shard_map/dot_general | solution.py:155
  100.2 4.5 %collective-permute-start.16 = (f32[64,2048]{1,0:T(8,128)S(1)}, f32[64,2048]{1,0:T(8,128)S(1)}, u32[]{:S(2)}, u32[]{:S(2)}) collective-permute-start(f32[64,2048]{1,0:T(8,128)S(1)} %dynamic-slice_bitcast_fusion), channel_id=1, source_target_pairs={{0,2},{1,3},{2,0},{3,1},{4,6},{5,7},{6,4},{7,5},{8,10},{9,11},{10,... | collective-permute-start | bytes 1572872 | tf_op jit(solution)/shard_map/ppermute | solution.py:166
  107.1 10.3 %collective-permute-done.16 = f32[64,2048]{1,0:T(8,128)S(1)} collective-permute-done((f32[64,2048]{1,0:T(8,128)S(1)}, f32[64,2048]{1,0:T(8,128)S(1)}, u32[]{:S(2)}, u32[]{:S(2)}) %collective-permute-start.16) | collective-permute-done | bytes 524320 | tf_op jit(solution)/shard_map/ppermute | solution.py:166
  117.5 2.2 %collective-permute-done.21 = f32[64,512]{1,0:T(8,128)S(1)} collective-permute-done((f32[64,512]{1,0:T(8,128)S(1)}, f32[64,512]{1,0:T(8,128)S(1)}, u32[]{:S(2)}, u32[]{:S(2)}) %collective-permute-start.21) | collective-permute-done | bytes 131104 | tf_op jit(solution)/shard_map/ppermute | solution.py:166
  119.7 1.8 %collective-permute-start.23 = (f32[64,512]{1,0:T(8,128)S(1)}, f32[64,512]{1,0:T(8,128)S(1)}, u32[]{:S(2)}, u32[]{:S(2)}) collective-permute-start(f32[64,512]{1,0:T(8,128)S(1)} %dynamic-slice_bitcast_fusion.3), channel_id=1, source_target_pairs={{0,2},{1,3},{2,0},{3,1},{4,6},{5,7},{6,4},{7,5},{8,10},{9,11},{10,... | collective-permute-start | bytes 393224 | tf_op jit(solution)/shard_map/ppermute | solution.py:166
  122.7 3.1 %collective-permute-done.23 = f32[64,512]{1,0:T(8,128)S(1)} collective-permute-done((f32[64,512]{1,0:T(8,128)S(1)}, f32[64,512]{1,0:T(8,128)S(1)}, u32[]{:S(2)}, u32[]{:S(2)}) %collective-permute-start.23) | collective-permute-done | bytes 131104 | tf_op jit(solution)/shard_map/ppermute | solution.py:166
  126.0 2.6 %collective-permute-start.24 = (f32[64,512]{1,0:T(8,128)S(1)}, f32[64,512]{1,0:T(8,128)S(1)}, u32[]{:S(2)}, u32[]{:S(2)}) collective-permute-start(f32[64,512]{1,0:T(8,128)S(1)} %fusion.41), channel_id=1, source_target_pairs={{0,4},{1,5},{2,6},{3,7},{4,0},{5,1},{6,2},{7,3},{8,12},{9,13},{10,... | collective-permute-start | bytes 393224 | tf_op jit(solution)/shard_map/ppermute | solution.py:183
  128.7 5.2 %collective-permute-done.22 = f32[64,512]{1,0:T(8,128)S(1)} collective-permute-done((f32[64,512]{1,0:T(8,128)S(1)}, f32[64,512]{1,0:T(8,128)S(1)}, u32[]{:S(2)}, u32[]{:S(2)}) %collective-permute-start.22) | collective-permute-done | bytes 131104 | tf_op jit(solution)/shard_map/ppermute | solution.py:183
  136.7 1.5 %collective-permute-done.24 = f32[64,512]{1,0:T(8,128)S(1)} collective-permute-done((f32[64,512]{1,0:T(8,128)S(1)}, f32[64,512]{1,0:T(8,128)S(1)}, u32[]{:S(2)}, u32[]{:S(2)}) %collective-permute-start.24) | collective-permute-done | bytes 131104 | tf_op jit(solution)/shard_map/ppermute | solution.py:183
  138.2 3.5 %collective-permute-done.27 = f32[64,512]{1,0:T(8,128)S(1)} collective-permute-done((f32[64,512]{1,0:T(8,128)S(1)}, f32[64,512]{1,0:T(8,128)S(1)}, u32[]{:S(2)}, u32[]{:S(2)}) %collective-permute-start.27) | collective-permute-done | bytes 131104 | tf_op jit(solution)/shard_map/ppermute | solution.py:166
  141.8 3.0 %collective-permute-start.28 = (f32[64,512]{1,0:T(8,128)S(1)}, f32[64,512]{1,0:T(8,128)S(1)}, u32[]{:S(2)}, u32[]{:S(2)}) collective-permute-start(f32[64,512]{1,0:T(8,128)S(1)} %fusion.31), channel_id=1, source_target_pairs={{0,4},{1,5},{2,6},{3,7},{4,0},{5,1},{6,2},{7,3},{8,12},{9,13},{10,... | collective-permute-start | bytes 393224 | tf_op jit(solution)/shard_map/ppermute | solution.py:183
  144.8 4.3 %collective-permute-done.28 = f32[64,512]{1,0:T(8,128)S(1)} collective-permute-done((f32[64,512]{1,0:T(8,128)S(1)}, f32[64,512]{1,0:T(8,128)S(1)}, u32[]{:S(2)}, u32[]{:S(2)}) %collective-permute-start.28) | collective-permute-done | bytes 131104 | tf_op jit(solution)/shard_map/ppermute | solution.py:183
  (114 shorter events, 28.3 us)
Async XLA Ops:
  1.4 7.4 %collective-permute-start = (bf16[16,3584]{1,0:T(8,128)(2,1)S(1)}, bf16[16,3584]{1,0:T(8,128)(2,1)S(1)}, u32[]{:S(2)}, u32[]{:S(2)}) collective-permute-start(bf16[16,3584]{1,0:T(8,128)(2,1)S(1)} %get-tuple-element.28), channel_id=1, source_target_pairs={{0,1},{1,0},{2,3},{3,2},{4,5},{5,4},{6,7},{7,6},{8,9},{9,8},{10,11... | collective-permute-start | bytes 344072 | tf_op jit(solution)/shard_map/ppermute | solution.py:113
  2.0 11.6 %collective-permute-start.1 = (bf16[16,3584]{1,0:T(8,128)(2,1)S(1)}, bf16[16,3584]{1,0:T(8,128)(2,1)S(1)}, u32[]{:S(2)}, u32[]{:S(2)}) collective-permute-start(bf16[16,3584]{1,0:T(8,128)(2,1)S(1)} %get-tuple-element.27), channel_id=1, source_target_pairs={{0,2},{1,3},{2,0},{3,1},{4,6},{5,7},{6,4},{7,5},{8,10},{9,11},{10,... | collective-permute-start | bytes 344072 | tf_op jit(solution)/shard_map/ppermute | solution.py:113
  4.6 10.2 %collective-permute-start.2 = (bf16[16,3584]{1,0:T(8,128)(2,1)S(1)}, bf16[16,3584]{1,0:T(8,128)(2,1)S(1)}, u32[]{:S(2)}, u32[]{:S(2)}) collective-permute-start(bf16[16,3584]{1,0:T(8,128)(2,1)S(1)} %get-tuple-element.26), channel_id=1, source_target_pairs={{0,3},{1,2},{2,1},{3,0},{4,7},{5,6},{6,5},{7,4},{8,11},{9,10},{10,... | collective-permute-start | bytes 344072 | tf_op jit(solution)/shard_map/ppermute | solution.py:113
  4.7 11.2 %collective-permute-start.3 = (bf16[16,3584]{1,0:T(8,128)(2,1)S(1)}, bf16[16,3584]{1,0:T(8,128)(2,1)S(1)}, u32[]{:S(2)}, u32[]{:S(2)}) collective-permute-start(bf16[16,3584]{1,0:T(8,128)(2,1)S(1)} %get-tuple-element.25), channel_id=1, source_target_pairs={{0,4},{1,5},{2,6},{3,7},{4,0},{5,1},{6,2},{7,3},{8,12},{9,13},{10,... | collective-permute-start | bytes 344072 | tf_op jit(solution)/shard_map/ppermute | solution.py:113
  7.4 15.9 %collective-permute-start.4 = (bf16[16,3584]{1,0:T(8,128)(2,1)S(1)}, bf16[16,3584]{1,0:T(8,128)(2,1)S(1)}, u32[]{:S(2)}, u32[]{:S(2)}) collective-permute-start(bf16[16,3584]{1,0:T(8,128)(2,1)S(1)} %get-tuple-element.24), channel_id=1, source_target_pairs={{0,5},{1,4},{2,7},{3,6},{4,1},{5,0},{6,3},{7,2},{8,13},{9,12},{10,... | collective-permute-start | bytes 344072 | tf_op jit(solution)/shard_map/ppermute | solution.py:113
  8.8 15.6 %collective-permute-start.5 = (bf16[16,3584]{1,0:T(8,128)(2,1)S(1)}, bf16[16,3584]{1,0:T(8,128)(2,1)S(1)}, u32[]{:S(2)}, u32[]{:S(2)}) collective-permute-start(bf16[16,3584]{1,0:T(8,128)(2,1)S(1)} %get-tuple-element.30), channel_id=1, source_target_pairs={{0,6},{1,7},{2,4},{3,5},{4,2},{5,3},{6,0},{7,1},{8,14},{9,15},{10,... | collective-permute-start | bytes 344072 | tf_op jit(solution)/shard_map/ppermute | solution.py:113
  13.5 12.0 %collective-permute-start.6 = (bf16[16,3584]{1,0:T(8,128)(2,1)S(1)}, bf16[16,3584]{1,0:T(8,128)(2,1)S(1)}, u32[]{:S(2)}, u32[]{:S(2)}) collective-permute-start(bf16[16,3584]{1,0:T(8,128)(2,1)S(1)} %get-tuple-element.23), channel_id=1, source_target_pairs={{0,7},{1,6},{2,5},{3,4},{4,3},{5,2},{6,1},{7,0},{8,15},{9,14},{10,... | collective-permute-start | bytes 344072 | tf_op jit(solution)/shard_map/ppermute | solution.py:113
  32.4 7.7 %collective-permute-start.7 = (bf16[16,3584]{1,0:T(8,128)(2,1)S(1)}, bf16[16,3584]{1,0:T(8,128)(2,1)S(1)}, u32[]{:S(2)}, u32[]{:S(2)}) collective-permute-start(bf16[16,3584]{1,0:T(8,128)(2,1)S(1)} %bitcast.211), channel_id=1, source_target_pairs={{0,1},{1,0},{2,3},{3,2},{4,5},{5,4},{6,7},{7,6},{8,9},{9,8},{10,11... | collective-permute-start | bytes 344072 | tf_op jit(solution)/shard_map/ppermute | solution.py:134
  32.7 9.5 %collective-permute-start.8 = (bf16[16,3584]{1,0:T(8,128)(2,1)S(1)}, bf16[16,3584]{1,0:T(8,128)(2,1)S(1)}, u32[]{:S(2)}, u32[]{:S(2)}) collective-permute-start(bf16[16,3584]{1,0:T(8,128)(2,1)S(1)} %bitcast.210), channel_id=1, source_target_pairs={{0,2},{1,3},{2,0},{3,1},{4,6},{5,7},{6,4},{7,5},{8,10},{9,11},{10,... | collective-permute-start | bytes 344072 | tf_op jit(solution)/shard_map/ppermute | solution.py:134
  36.2 10.0 %collective-permute-start.9 = (bf16[16,3584]{1,0:T(8,128)(2,1)S(1)}, bf16[16,3584]{1,0:T(8,128)(2,1)S(1)}, u32[]{:S(2)}, u32[]{:S(2)}) collective-permute-start(bf16[16,3584]{1,0:T(8,128)(2,1)S(1)} %bitcast.208), channel_id=1, source_target_pairs={{0,3},{1,2},{2,1},{3,0},{4,7},{5,6},{6,5},{7,4},{8,11},{9,10},{10,... | collective-permute-start | bytes 344072 | tf_op jit(solution)/shard_map/ppermute | solution.py:134
  36.4 9.8 %collective-permute-start.10 = (bf16[16,3584]{1,0:T(8,128)(2,1)S(1)}, bf16[16,3584]{1,0:T(8,128)(2,1)S(1)}, u32[]{:S(2)}, u32[]{:S(2)}) collective-permute-start(bf16[16,3584]{1,0:T(8,128)(2,1)S(1)} %bitcast.207), channel_id=1, source_target_pairs={{0,4},{1,5},{2,6},{3,7},{4,0},{5,1},{6,2},{7,3},{8,12},{9,13},{10,... | collective-permute-start | bytes 344072 | tf_op jit(solution)/shard_map/ppermute | solution.py:134
  39.6 15.7 %collective-permute-start.11 = (bf16[16,3584]{1,0:T(8,128)(2,1)S(1)}, bf16[16,3584]{1,0:T(8,128)(2,1)S(1)}, u32[]{:S(2)}, u32[]{:S(2)}) collective-permute-start(bf16[16,3584]{1,0:T(8,128)(2,1)S(1)} %bitcast.206), channel_id=1, source_target_pairs={{0,5},{1,4},{2,7},{3,6},{4,1},{5,0},{6,3},{7,2},{8,13},{9,12},{10,... | collective-permute-start | bytes 344072 | tf_op jit(solution)/shard_map/ppermute | solution.py:134
  40.0 44.0 %slice-start = ((s8[14680064]{0:T(1024)(128)(4,1)}), s8[2097152]{0:T(1024)(128)(4,1)S(1)}, s32[]{:S(2)}) async-start(s8[14680064]{0:T(1024)(128)(4,1)} %bitcast.188), calls=%async_computation | async-start | bytes 4194304
  40.1 15.2 %collective-permute-start.12 = (bf16[16,3584]{1,0:T(8,128)(2,1)S(1)}, bf16[16,3584]{1,0:T(8,128)(2,1)S(1)}, u32[]{:S(2)}, u32[]{:S(2)}) collective-permute-start(bf16[16,3584]{1,0:T(8,128)(2,1)S(1)} %bitcast.209), channel_id=1, source_target_pairs={{0,6},{1,7},{2,4},{3,5},{4,2},{5,3},{6,0},{7,1},{8,14},{9,15},{10,... | collective-permute-start | bytes 344072 | tf_op jit(solution)/shard_map/ppermute | solution.py:134
  42.3 13.0 %collective-permute-start.13 = (bf16[16,3584]{1,0:T(8,128)(2,1)S(1)}, bf16[16,3584]{1,0:T(8,128)(2,1)S(1)}, u32[]{:S(2)}, u32[]{:S(2)}) collective-permute-start(bf16[16,3584]{1,0:T(8,128)(2,1)S(1)} %bitcast.205), channel_id=1, source_target_pairs={{0,7},{1,6},{2,5},{3,4},{4,3},{5,2},{6,1},{7,0},{8,15},{9,14},{10,... | collective-permute-start | bytes 344072 | tf_op jit(solution)/shard_map/ppermute | solution.py:134
  55.3 23.3 %collective-permute-start.17 = (bf16[128,3584]{1,0:T(8,128)(2,1)S(1)}, bf16[128,3584]{1,0:T(8,128)(2,1)}, u32[]{:S(2)}, u32[]{:S(2)}) collective-permute-start(bf16[128,3584]{1,0:T(8,128)(2,1)S(1)} %constant_dynamic-update-slice_fusion), channel_id=1, source_target_pairs={{0,16},{8,24},{16,0},{24,8},{1,17},{9,25},{17,1},{25,9},{2,18},{10... | collective-permute-start | bytes 2752520 | tf_op jit(solution)/shard_map/ppermute | solution.py:148
  56.9 24.4 %collective-permute-start.14 = (bf16[128,3584]{1,0:T(8,128)(2,1)S(1)}, bf16[128,3584]{1,0:T(8,128)(2,1)}, u32[]{:S(2)}, u32[]{:S(2)}) collective-permute-start(bf16[128,3584]{1,0:T(8,128)(2,1)S(1)} %constant_dynamic-update-slice_fusion), channel_id=1, source_target_pairs={{0,8},{8,0},{16,24},{24,16},{1,9},{9,1},{17,25},{25,17},{2,10},{10... | collective-permute-start | bytes 2752520 | tf_op jit(solution)/shard_map/ppermute | solution.py:147
  58.4 25.6 %slice-start.2 = ((s8[14680064]{0:T(1024)(128)(4,1)}), s8[4194304]{0:T(1024)(128)(4,1)S(1)}, s32[]{:S(2)}) async-start(s8[14680064]{0:T(1024)(128)(4,1)} %bitcast.188), calls=%async_computation.2 | async-start | bytes 8388608
  58.4 25.6 %slice-start.3 = ((s8[14680064]{0:T(1024)(128)(4,1)}), s8[4194304]{0:T(1024)(128)(4,1)S(1)}, s32[]{:S(2)}) async-start(s8[14680064]{0:T(1024)(128)(4,1)} %bitcast.188), calls=%async_computation.3 | async-start | bytes 8388608
  79.7 12.7 %collective-permute-start.18 = (bf16[64,3584]{1,0:T(8,128)(2,1)S(1)}, bf16[64,3584]{1,0:T(8,128)(2,1)S(1)}, u32[]{:S(2)}, u32[]{:S(2)}) collective-permute-start(bf16[64,3584]{1,0:T(8,128)(2,1)S(1)} %slice.81), channel_id=1, source_target_pairs={{0,8},{8,0},{16,24},{24,16},{1,9},{9,1},{17,25},{25,17},{2,10},{10... | collective-permute-start | bytes 1376264 | tf_op jit(solution)/shard_map/ppermute | solution.py:149
  82.4 12.3 %collective-permute-start.19 = (bf16[64,3584]{1,0:T(8,128)(2,1)S(1)}, bf16[64,3584]{1,0:T(8,128)(2,1)S(1)}, u32[]{:S(2)}, u32[]{:S(2)}) collective-permute-start(bf16[64,3584]{1,0:T(8,128)(2,1)S(1)} %slice.82), channel_id=1, source_target_pairs={{0,16},{8,24},{16,0},{24,8},{1,17},{9,25},{17,1},{25,9},{2,18},{10... | collective-permute-start | bytes 1376264 | tf_op jit(solution)/shard_map/ppermute | solution.py:150
  88.8 9.5 %collective-permute-start.15 = (f32[2,64,2048]{2,1,0:T(8,128)}, f32[2,64,2048]{2,1,0:T(8,128)}, u32[]{:S(2)}, u32[]{:S(2)}) collective-permute-start(f32[2,64,2048]{2,1,0:T(8,128)} %fusion.21), channel_id=1, source_target_pairs={{0,1},{1,0},{2,3},{3,2},{4,5},{5,4},{6,7},{7,6},{8,9},{9,8},{10,11... | collective-permute-start | bytes 3145736 | tf_op jit(solution)/shard_map/ppermute | solution.py:160
  98.2 6.5 %collective-permute-start.20 = (f32[2,64,2048]{2,1,0:T(8,128)}, f32[2,64,2048]{2,1,0:T(8,128)}, u32[]{:S(2)}, u32[]{:S(2)}) collective-permute-start(f32[2,64,2048]{2,1,0:T(8,128)} %fusion.16), channel_id=1, source_target_pairs={{0,1},{1,0},{2,3},{3,2},{4,5},{5,4},{6,7},{7,6},{8,9},{9,8},{10,11... | collective-permute-start | bytes 3145736 | tf_op jit(solution)/shard_map/ppermute | solution.py:160
  100.2 17.2 %collective-permute-start.16 = (f32[64,2048]{1,0:T(8,128)S(1)}, f32[64,2048]{1,0:T(8,128)S(1)}, u32[]{:S(2)}, u32[]{:S(2)}) collective-permute-start(f32[64,2048]{1,0:T(8,128)S(1)} %dynamic-slice_bitcast_fusion), channel_id=1, source_target_pairs={{0,2},{1,3},{2,0},{3,1},{4,6},{5,7},{6,4},{7,5},{8,10},{9,11},{10,... | collective-permute-start | bytes 1572872 | tf_op jit(solution)/shard_map/ppermute | solution.py:166
  106.1 13.5 %collective-permute-start.21 = (f32[64,512]{1,0:T(8,128)S(1)}, f32[64,512]{1,0:T(8,128)S(1)}, u32[]{:S(2)}, u32[]{:S(2)}) collective-permute-start(f32[64,512]{1,0:T(8,128)S(1)} %dynamic-slice_bitcast_fusion.4), channel_id=1, source_target_pairs={{0,2},{1,3},{2,0},{3,1},{4,6},{5,7},{6,4},{7,5},{8,10},{9,11},{10,... | collective-permute-start | bytes 393224 | tf_op jit(solution)/shard_map/ppermute | solution.py:166
  119.7 6.2 %collective-permute-start.23 = (f32[64,512]{1,0:T(8,128)S(1)}, f32[64,512]{1,0:T(8,128)S(1)}, u32[]{:S(2)}, u32[]{:S(2)}) collective-permute-start(f32[64,512]{1,0:T(8,128)S(1)} %dynamic-slice_bitcast_fusion.3), channel_id=1, source_target_pairs={{0,2},{1,3},{2,0},{3,1},{4,6},{5,7},{6,4},{7,5},{8,10},{9,11},{10,... | collective-permute-start | bytes 393224 | tf_op jit(solution)/shard_map/ppermute | solution.py:166
  121.6 12.3 %collective-permute-start.22 = (f32[64,512]{1,0:T(8,128)S(1)}, f32[64,512]{1,0:T(8,128)S(1)}, u32[]{:S(2)}, u32[]{:S(2)}) collective-permute-start(f32[64,512]{1,0:T(8,128)S(1)} %fusion.46), channel_id=1, source_target_pairs={{0,4},{1,5},{2,6},{3,7},{4,0},{5,1},{6,2},{7,3},{8,12},{9,13},{10,... | collective-permute-start | bytes 393224 | tf_op jit(solution)/shard_map/ppermute | solution.py:183
  126.0 12.2 %collective-permute-start.24 = (f32[64,512]{1,0:T(8,128)S(1)}, f32[64,512]{1,0:T(8,128)S(1)}, u32[]{:S(2)}, u32[]{:S(2)}) collective-permute-start(f32[64,512]{1,0:T(8,128)S(1)} %fusion.41), channel_id=1, source_target_pairs={{0,4},{1,5},{2,6},{3,7},{4,0},{5,1},{6,2},{7,3},{8,12},{9,13},{10,... | collective-permute-start | bytes 393224 | tf_op jit(solution)/shard_map/ppermute | solution.py:183
  128.6 6.6 %collective-permute-start.25 = (f32[64,512]{1,0:T(8,128)S(1)}, f32[64,512]{1,0:T(8,128)S(1)}, u32[]{:S(2)}, u32[]{:S(2)}) collective-permute-start(f32[64,512]{1,0:T(8,128)S(1)} %dynamic-slice_bitcast_fusion.2), channel_id=1, source_target_pairs={{0,2},{1,3},{2,0},{3,1},{4,6},{5,7},{6,4},{7,5},{8,10},{9,11},{10,... | collective-permute-start | bytes 393224 | tf_op jit(solution)/shard_map/ppermute | solution.py:166
  135.3 9.4 %collective-permute-start.26 = (f32[64,512]{1,0:T(8,128)S(1)}, f32[64,512]{1,0:T(8,128)S(1)}, u32[]{:S(2)}, u32[]{:S(2)}) collective-permute-start(f32[64,512]{1,0:T(8,128)S(1)} %fusion.36), channel_id=1, source_target_pairs={{0,4},{1,5},{2,6},{3,7},{4,0},{5,1},{6,2},{7,3},{8,12},{9,13},{10,... | collective-permute-start | bytes 393224 | tf_op jit(solution)/shard_map/ppermute | solution.py:183
  135.7 6.0 %collective-permute-start.27 = (f32[64,512]{1,0:T(8,128)S(1)}, f32[64,512]{1,0:T(8,128)S(1)}, u32[]{:S(2)}, u32[]{:S(2)}) collective-permute-start(f32[64,512]{1,0:T(8,128)S(1)} %dynamic-slice_bitcast_fusion.1), channel_id=1, source_target_pairs={{0,2},{1,3},{2,0},{3,1},{4,6},{5,7},{6,4},{7,5},{8,10},{9,11},{10,... | collective-permute-start | bytes 393224 | tf_op jit(solution)/shard_map/ppermute | solution.py:166
  141.8 7.3 %collective-permute-start.28 = (f32[64,512]{1,0:T(8,128)S(1)}, f32[64,512]{1,0:T(8,128)S(1)}, u32[]{:S(2)}, u32[]{:S(2)}) collective-permute-start(f32[64,512]{1,0:T(8,128)S(1)} %fusion.31), channel_id=1, source_target_pairs={{0,4},{1,5},{2,6},{3,7},{4,0},{5,1},{6,2},{7,3},{8,12},{9,13},{10,... | collective-permute-start | bytes 393224 | tf_op jit(solution)/shard_map/ppermute | solution.py:183
  (9 other events, 93.0 us)

commit v14 on v13

--- a/solution.py
+++ b/solution.py
@@ -150,9 +150,9 @@
     second = lax.ppermute(across_x[half:], "seq", seq_pairs(2))
     diagonal = jnp.concatenate([first, second], axis=0)
 
-    def first_halving(pieces):
+    def first_halving(pieces, weight=down_weight):
         products = jnp.stack(
-            [jnp.dot(piece, down_weight, preferred_element_type=jnp.float32) for piece in pieces]
+            [jnp.dot(piece, weight, preferred_element_type=jnp.float32) for piece in pieces]
         )
         split = products.reshape(2, 2, half, products.shape[-1])
         keep = lax.dynamic_index_in_dim(split, low, 1, keepdims=False)
@@ -165,7 +165,12 @@
         send = lax.dynamic_index_in_dim(summed, 1 - chosen, 0, keepdims=False)
         return keep + lax.ppermute(send, "tp", tp_pairs(2))
 
-    near = second_halving(first_halving((block, across_x)))
+    near_width = down_weight.shape[1] // 2
+    near_parts = []
+    for start in (0, near_width):
+        summed = first_halving((block, across_x), down_weight[:, start : start + near_width])
+        near_parts.append(second_halving(summed))
+    near = jnp.concatenate(near_parts, axis=1)
     far_summed = first_halving((across_y, diagonal))
     columns = near.shape[-1]
     width = columns // TAIL_PIECES

time: 150 us -> 154 us (1.027)
  waiting for transfers between devices: 65.3 us -> 69.4 us
  matrix products: 28.5 us -> 26.5 us
  local copies, waits for them, and re-layouts: 6.98 us -> 8.67 us
    ppermute x7, starting transfers between devices: 10.9 us -> 6.39 us  [spread_rotate_return(): block = lax.ppermute(block, 'tp', pairs(distance))]
    ppermute x1, waiting for transfers between devices: 0.37 us -> 3.94 us  [product_and_reduce(): first = lax.ppermute(across_y[:half], 'seq', seq_pairs(1))]
    ppermute x5 -> x6, starting transfers between devices: 8.23 us -> 11.3 us  [second_halving(): return keep + lax.ppermute(send, 'tp', tp_pairs(2))]
    ppermute x4, waiting for transfers between devices: 11.1 us -> 8.92 us  [product_and_reduce(): results.append(keep + lax.ppermute(send, 'tp', tp_pairs(4)))]
    add x4 -> x5, other arithmetic: 0.11 us -> 2.02 us  [second_halving(): return keep + lax.ppermute(send, 'tp', tp_pairs(2))]
    ppermute x7, waiting for transfers between devices: 6.58 us -> 8.42 us  [spread_rotate_return(): send = lax.ppermute(send, 'tp', pairs(distance))]
    ppermute x7, waiting for transfers between devices: 11.7 us -> 13.4 us  [spread_rotate_return(): block = lax.ppermute(block, 'tp', pairs(distance))]
    ppermute x4, starting transfers between devices: 7.14 us -> 5.41 us  [product_and_reduce(): results.append(keep + lax.ppermute(send, 'tp', tp_pairs(4)))]
  transfers between devices with their start and end apart: 29 -> 31, of which waited for: 15 -> 17; matrix products, arithmetic and copies ran while one was open for 21% -> 19% of each run, Pallas kernels for 0% -> 0%
where the time goes in v14:
time: 154 us; the launch traced here: 153 us
  waiting for transfers between devices  69.4 us (45%)
  starting transfers between devices  41 us (27%)
  matrix products  26.5 us (17%)
  local copies, waits for them, and re-layouts  8.67 us (6%)
  other arithmetic  7.24 us (5%)
    ppermute x6, waiting for transfers between devices, second_halving(): return keep + lax.ppermute(send, 'tp', tp_pairs(2))  21.8 us
    dot_general x6, matrix products, first_halving(): jnp.dot(piece, weight, preferred_element_type=jnp.float32)  15.5 us
    ppermute x7, waiting for transfers between devices, spread_rotate_return(): block = lax.ppermute(block, 'tp', pairs(distance))  13.4 us
    ppermute x1, waiting for transfers between devices, product_and_reduce(): across_y = lax.ppermute(block, 'seq', seq_pairs(2))  11.6 us
    ppermute x6, starting transfers between devices, second_halving(): return keep + lax.ppermute(send, 'tp', tp_pairs(2))  11.3 us
    ppermute x7, starting transfers between devices, spread_rotate_return(): send = lax.ppermute(send, 'tp', pairs(distance))  11 us
    ppermute x4, waiting for transfers between devices, product_and_reduce(): results.append(keep + lax.ppermute(send, 'tp', tp_pairs(4)))  8.92 us
    ppermute x7, waiting for transfers between devices, spread_rotate_return(): send = lax.ppermute(send, 'tp', pairs(distance))  8.42 us
  transfers between devices with their start and end apart: 31, of which 17 were waited for; matrix products, arithmetic and copies ran while one was open for 19% of the time, Pallas kernels for 0%

profile of v14, /device:TPU:0, one launch (start us, length us, event | category | flops | bytes accessed | tf_op | source)
XLA Modules:
  0.0 153.4 jit_solution(10730359334892380689)
XLA Ops:
  0.0 2.3 %constant_dynamic-slice_fusion = (bf16[16,3584]{1,0:T(8,128)(2,1)}, bf16[16,3584]{1,0:T(8,128)(2,1)}, bf16[16,3584]{1,0:T(8,128)(2,1)}, bf16[16,3584]{1,0:T(8,12...) fusion(bf16[128,3584]{1,0:T(8,128)(2,1)} %param.5, ...), kind=kLoop, calls=%fused_computation.140 | loop fusion | bytes 1835040 | tf_op jit(solution)/shard_map/dynamic_slice | solution.py:111
  2.3 4.5 %collective-permute-start.6 = (bf16[16,3584]{1,0:T(8,128)(2,1)}, bf16[16,3584]{1,0:T(8,128)(2,1)}, u32[]{:S(2)}, u32[]{:S(2)}) collective-permute-start(bf16[16,3584]{1,0:T(8,128)(2,1)} %get-tuple-element.23), channel_id=1, source_target_pairs={{0,7},{1,6},{2,5},{3,4},{4,3},{5,2},{6,1},{7,0},{8,15},{9,14},{10,... | collective-permute-start | bytes 344072 | tf_op jit(solution)/shard_map/ppermute | solution.py:113
  6.8 3.2 %collective-permute-start.3 = (bf16[16,3584]{1,0:T(8,128)(2,1)}, bf16[16,3584]{1,0:T(8,128)(2,1)}, u32[]{:S(2)}, u32[]{:S(2)}) collective-permute-start(bf16[16,3584]{1,0:T(8,128)(2,1)} %get-tuple-element.25), channel_id=1, source_target_pairs={{0,4},{1,5},{2,6},{3,7},{4,0},{5,1},{6,2},{7,3},{8,12},{9,13},{10,... | collective-permute-start | bytes 344072 | tf_op jit(solution)/shard_map/ppermute | solution.py:113
  11.9 1.6 %mul.89 = f32[32,32]{1,0:T(8,128)} reshape(f32[8,4,8,4]{3,2,1,0:T(8,128)} %broadcast_multiply_fusion) | data formatting | bytes 8192 | tf_op jit(solution)/shard_map/jit(kron)/mul | solution.py:126
  13.5 2.1 %collective-permute-start.1 = (bf16[16,3584]{1,0:T(8,128)(2,1)}, bf16[16,3584]{1,0:T(8,128)(2,1)S(1)}, u32[]{:S(2)}, u32[]{:S(2)}) collective-permute-start(bf16[16,3584]{1,0:T(8,128)(2,1)} %get-tuple-element.27), channel_id=1, source_target_pairs={{0,2},{1,3},{2,0},{3,1},{4,6},{5,7},{6,4},{7,5},{8,10},{9,11},{10,... | collective-permute-start | bytes 344072 | tf_op jit(solution)/shard_map/ppermute | solution.py:113
  16.9 7.3 %collective-permute-done.1 = bf16[16,3584]{1,0:T(8,128)(2,1)S(1)} collective-permute-done((bf16[16,3584]{1,0:T(8,128)(2,1)}, bf16[16,3584]{1,0:T(8,128)(2,1)S(1)}, u32[]{:S(2)}, u32[]{:S(2)}) %collective-permute-start.1) | collective-permute-done | bytes 114720 | tf_op jit(solution)/shard_map/ppermute | solution.py:113
  33.8 3.5 %fusion.12 = bf16[16,32,896]{2,1,0:T(8,128)(2,1)S(1)} fusion(f32[16,32,896]{2,0,1:T(8,128)} %bitcast.206, f32[32,32]{1,0:T(8,128)S(1)} %copy-done.3), kind=kOutput, calls=%fused_computation.15 | convolution fusion | flops 177078272 | bytes 2756608 | tf_op jit(solution)/shard_map/rbm,bc->rcm/dot_general | solution.py:127
  37.9 1.7 %fusion.72 = (bf16[16,1,3584]{2,1,0:T(2,128)(2,1)S(1)}, bf16[16,1,3584]{2,1,0:T(2,128)(2,1)S(1)}, bf16[16,1,3584]{2,1,0:T(2,128)(2,1)S(1)}, bf16[16,1,3584]{2,1,...) fusion(bf16[16,8,3584]{2,1,0:T(8,128)(2,1)S(1)} %reshape.119), kind=kLoop, calls=%fused_computation.158 | loop fusion | bytes 1835008 | tf_op jit(solution)/shard_map/slice | solution.py:132
  39.8 1.8 %collective-permute-start.9 = (bf16[16,3584]{1,0:T(8,128)(2,1)S(1)}, bf16[16,3584]{1,0:T(8,128)(2,1)S(1)}, u32[]{:S(2)}, u32[]{:S(2)}) collective-permute-start(bf16[16,3584]{1,0:T(8,128)(2,1)S(1)} %bitcast.226), channel_id=1, source_target_pairs={{0,3},{1,2},{2,1},{3,0},{4,7},{5,6},{6,5},{7,4},{8,11},{9,10},{10,... | collective-permute-start | bytes 344072 | tf_op jit(solution)/shard_map/ppermute | solution.py:134
  42.0 2.3 %collective-permute-start.11 = (bf16[16,3584]{1,0:T(8,128)(2,1)S(1)}, bf16[16,3584]{1,0:T(8,128)(2,1)S(1)}, u32[]{:S(2)}, u32[]{:S(2)}) collective-permute-start(bf16[16,3584]{1,0:T(8,128)(2,1)S(1)} %bitcast.224), channel_id=1, source_target_pairs={{0,5},{1,4},{2,7},{3,6},{4,1},{5,0},{6,3},{7,2},{8,13},{9,12},{10,... | collective-permute-start | bytes 344072 | tf_op jit(solution)/shard_map/ppermute | solution.py:134
  45.9 1.9 %collective-permute-done.8 = bf16[16,3584]{1,0:T(8,128)(2,1)S(1)} collective-permute-done((bf16[16,3584]{1,0:T(8,128)(2,1)S(1)}, bf16[16,3584]{1,0:T(8,128)(2,1)S(1)}, u32[]{:S(2)}, u32[]{:S(2)}) %collective-permute-start.8) | collective-permute-done | bytes 114720 | tf_op jit(solution)/shard_map/ppermute | solution.py:134
  49.5 8.9 %collective-permute-done.10 = bf16[16,3584]{1,0:T(8,128)(2,1)S(1)} collective-permute-done((bf16[16,3584]{1,0:T(8,128)(2,1)S(1)}, bf16[16,3584]{1,0:T(8,128)(2,1)S(1)}, u32[]{:S(2)}, u32[]{:S(2)}) %collective-permute-start.10) | collective-permute-done | bytes 114720 | tf_op jit(solution)/shard_map/ppermute | solution.py:134
  59.8 1.6 %collective-permute-start.17 = (bf16[128,3584]{1,0:T(8,128)(2,1)S(1)}, bf16[128,3584]{1,0:T(8,128)(2,1)S(1)}, u32[]{:S(2)}, u32[]{:S(2)}) collective-permute-start(bf16[128,3584]{1,0:T(8,128)(2,1)S(1)} %constant_dynamic-update-slice_fusion), channel_id=1, source_target_pairs={{0,16},{8,24},{16,0},{24,8},{1,17},{9,25},{17,1},{25,9},{2,18},{10... | collective-permute-start | bytes 2752520 | tf_op jit(solution)/shard_map/ppermute | solution.py:148
  62.9 4.2 %fusion.2 = f32[128,1024]{1,0:T(8,128)S(1)} fusion(bf16[128,3584]{1,0:T(8,128)(2,1)S(1)} %constant_dynamic-update-slice_fusion, bf16[3584,2048]{1,0:T(8,128)(2,1)} %param.6), kind=kOutput, calls=%fused_computation.2 | convolution fusion | flops 939524096 | bytes 8781824 | tf_op jit(solution)/shard_map/dot_general | solution.py:155
  67.1 4.3 %fusion.6 = f32[128,1024]{1,0:T(8,128)S(1)} fusion(bf16[128,3584]{1,0:T(8,128)(2,1)S(1)} %constant_dynamic-update-slice_fusion, bf16[3584,2048]{1,0:T(8,128)(2,1)} %param.6), kind=kOutput, calls=%fused_computation.6 | convolution fusion | flops 939524096 | bytes 8781824 | tf_op jit(solution)/shard_map/dot_general | solution.py:155
  71.4 11.6 %collective-permute-done.17 = bf16[128,3584]{1,0:T(8,128)(2,1)S(1)} collective-permute-done((bf16[128,3584]{1,0:T(8,128)(2,1)S(1)}, bf16[128,3584]{1,0:T(8,128)(2,1)S(1)}, u32[]{:S(2)}, u32[]{:S(2)}) %collective-permute-start.17) | collective-permute-done | bytes 917536 | tf_op jit(solution)/shard_map/ppermute | solution.py:148
  89.7 2.1 %fusion.73 = f32[128,2048]{1,0:T(8,128)S(1)} fusion(bf16[128,3584]{1,0:T(8,128)(2,1)S(1)} %collective-permute-done.17, bf16[3584,2048]{1,0:T(8,128)(2,1)S(1)} %bitcast.201), kind=kOutput, calls=%fused_computation.159 | convolution fusion | flops 1879048192 | bytes 16646144 | tf_op jit(solution)/shard_map/dot_general | solution.py:155
  91.8 3.9 %collective-permute-done.18 = bf16[64,3584]{1,0:T(8,128)(2,1)S(1)} collective-permute-done((bf16[64,3584]{1,0:T(8,128)(2,1)S(1)}, bf16[64,3584]{1,0:T(8,128)(2,1)S(1)}, u32[]{:S(2)}, u32[]{:S(2)}) %collective-permute-start.18) | collective-permute-done | bytes 458784 | tf_op jit(solution)/shard_map/ppermute | solution.py:149
  97.0 2.2 %fusion.28 = f32[128,2048]{1,0:T(8,128)S(1)} fusion(bf16[3584,2048]{1,0:T(8,128)(2,1)S(1)} %bitcast.201, bf16[64,3584]{1,0:T(8,128)(2,1)S(1)} %collective-permute-done.19, bf16[64,3584]{1,0:T(8,128)(2,1)S(1)} %collective-permute-done.18), kind=kOutput, calls=%fused_computation.45 | convolution fusion | flops 1880883200 | bytes 16646144 | tf_op jit(solution)/shard_map/dot_general | solution.py:155
  100.4 4.5 %collective-permute-start.16 = (f32[64,1024]{1,0:T(8,128)S(1)}, f32[64,1024]{1,0:T(8,128)}, u32[]{:S(2)}, u32[]{:S(2)}) collective-permute-start(f32[64,1024]{1,0:T(8,128)S(1)} %dynamic-slice_bitcast_fusion.1), channel_id=1, source_target_pairs={{0,2},{1,3},{2,0},{3,1},{4,6},{5,7},{6,4},{7,5},{8,10},{9,11},{10,... | collective-permute-start | bytes 786440 | tf_op jit(solution)/shard_map/ppermute | solution.py:166
  105.7 6.4 %collective-permute-done.16 = f32[64,1024]{1,0:T(8,128)} collective-permute-done((f32[64,1024]{1,0:T(8,128)S(1)}, f32[64,1024]{1,0:T(8,128)}, u32[]{:S(2)}, u32[]{:S(2)}) %collective-permute-start.16) | collective-permute-done | bytes 262176 | tf_op jit(solution)/shard_map/ppermute | solution.py:166
  113.1 4.5 %collective-permute-done.26 = f32[64,1024]{1,0:T(8,128)} collective-permute-done((f32[64,1024]{1,0:T(8,128)}, f32[64,1024]{1,0:T(8,128)}, u32[]{:S(2)}, u32[]{:S(2)}) %collective-permute-start.26) | collective-permute-done | bytes 262176 | tf_op jit(solution)/shard_map/ppermute | solution.py:166
  120.0 1.8 %collective-permute-start.21 = (f32[64,512]{1,0:T(8,128)S(1)}, f32[64,512]{1,0:T(8,128)S(1)}, u32[]{:S(2)}, u32[]{:S(2)}) collective-permute-start(f32[64,512]{1,0:T(8,128)S(1)} %dynamic-slice_bitcast_fusion.5), channel_id=1, source_target_pairs={{0,2},{1,3},{2,0},{3,1},{4,6},{5,7},{6,4},{7,5},{8,10},{9,11},{10,... | collective-permute-start | bytes 393224 | tf_op jit(solution)/shard_map/ppermute | solution.py:166
  121.9 3.6 %collective-permute-done.21 = f32[64,512]{1,0:T(8,128)S(1)} collective-permute-done((f32[64,512]{1,0:T(8,128)S(1)}, f32[64,512]{1,0:T(8,128)S(1)}, u32[]{:S(2)}, u32[]{:S(2)}) %collective-permute-start.21) | collective-permute-done | bytes 131104 | tf_op jit(solution)/shard_map/ppermute | solution.py:166
  125.5 1.6 %collective-permute-start.23 = (f32[64,512]{1,0:T(8,128)S(1)}, f32[64,512]{1,0:T(8,128)S(1)}, u32[]{:S(2)}, u32[]{:S(2)}) collective-permute-start(f32[64,512]{1,0:T(8,128)S(1)} %dynamic-slice_bitcast_fusion.4), channel_id=1, source_target_pairs={{0,2},{1,3},{2,0},{3,1},{4,6},{5,7},{6,4},{7,5},{8,10},{9,11},{10,... | collective-permute-start | bytes 393224 | tf_op jit(solution)/shard_map/ppermute | solution.py:166
  127.6 3.7 %collective-permute-done.23 = f32[64,512]{1,0:T(8,128)S(1)} collective-permute-done((f32[64,512]{1,0:T(8,128)S(1)}, f32[64,512]{1,0:T(8,128)S(1)}, u32[]{:S(2)}, u32[]{:S(2)}) %collective-permute-start.23) | collective-permute-done | bytes 131104 | tf_op jit(solution)/shard_map/ppermute | solution.py:166
  134.1 4.7 %collective-permute-done.22 = f32[64,512]{1,0:T(8,128)S(1)} collective-permute-done((f32[64,512]{1,0:T(8,128)S(1)}, f32[64,512]{1,0:T(8,128)S(1)}, u32[]{:S(2)}, u32[]{:S(2)}) %collective-permute-start.22) | collective-permute-done | bytes 131104 | tf_op jit(solution)/shard_map/ppermute | solution.py:188
  138.9 1.7 %collective-permute-start.28 = (f32[64,512]{1,0:T(8,128)S(1)}, f32[64,512]{1,0:T(8,128)S(1)}, u32[]{:S(2)}, u32[]{:S(2)}) collective-permute-start(f32[64,512]{1,0:T(8,128)S(1)} %fusion.49), channel_id=1, source_target_pairs={{0,4},{1,5},{2,6},{3,7},{4,0},{5,1},{6,2},{7,3},{8,12},{9,13},{10,... | collective-permute-start | bytes 393224 | tf_op jit(solution)/shard_map/ppermute | solution.py:188
  140.6 2.3 %collective-permute-start.29 = (f32[64,512]{1,0:T(8,128)S(1)}, f32[64,512]{1,0:T(8,128)S(1)}, u32[]{:S(2)}, u32[]{:S(2)}) collective-permute-start(f32[64,512]{1,0:T(8,128)S(1)} %dynamic-slice_bitcast_fusion.2), channel_id=1, source_target_pairs={{0,2},{1,3},{2,0},{3,1},{4,6},{5,7},{6,4},{7,5},{8,10},{9,11},{10,... | collective-permute-start | bytes 393224 | tf_op jit(solution)/shard_map/ppermute | solution.py:166
  143.0 3.6 %collective-permute-done.29 = f32[64,512]{1,0:T(8,128)S(1)} collective-permute-done((f32[64,512]{1,0:T(8,128)S(1)}, f32[64,512]{1,0:T(8,128)S(1)}, u32[]{:S(2)}, u32[]{:S(2)}) %collective-permute-start.29) | collective-permute-done | bytes 131104 | tf_op jit(solution)/shard_map/ppermute | solution.py:166
  146.7 1.8 %collective-permute-start.30 = (f32[64,512]{1,0:T(8,128)S(1)}, f32[64,512]{1,0:T(8,128)S(1)}, u32[]{:S(2)}, u32[]{:S(2)}) collective-permute-start(f32[64,512]{1,0:T(8,128)S(1)} %fusion.44), channel_id=1, source_target_pairs={{0,4},{1,5},{2,6},{3,7},{4,0},{5,1},{6,2},{7,3},{8,12},{9,13},{10,... | collective-permute-start | bytes 393224 | tf_op jit(solution)/shard_map/ppermute | solution.py:188
  148.5 4.1 %collective-permute-done.30 = f32[64,512]{1,0:T(8,128)S(1)} collective-permute-done((f32[64,512]{1,0:T(8,128)S(1)}, f32[64,512]{1,0:T(8,128)S(1)}, u32[]{:S(2)}, u32[]{:S(2)}) %collective-permute-start.30) | collective-permute-done | bytes 131104 | tf_op jit(solution)/shard_map/ppermute | solution.py:188
  (119 shorter events, 37.7 us)
Async XLA Ops:
  2.3 28.9 %collective-permute-start.6 = (bf16[16,3584]{1,0:T(8,128)(2,1)}, bf16[16,3584]{1,0:T(8,128)(2,1)}, u32[]{:S(2)}, u32[]{:S(2)}) collective-permute-start(bf16[16,3584]{1,0:T(8,128)(2,1)} %get-tuple-element.23), channel_id=1, source_target_pairs={{0,7},{1,6},{2,5},{3,4},{4,3},{5,2},{6,1},{7,0},{8,15},{9,14},{10,... | collective-permute-start | bytes 344072 | tf_op jit(solution)/shard_map/ppermute | solution.py:113
  6.8 21.6 %collective-permute-start.4 = (bf16[16,3584]{1,0:T(8,128)(2,1)}, bf16[16,3584]{1,0:T(8,128)(2,1)}, u32[]{:S(2)}, u32[]{:S(2)}) collective-permute-start(bf16[16,3584]{1,0:T(8,128)(2,1)} %get-tuple-element.24), channel_id=1, source_target_pairs={{0,5},{1,4},{2,7},{3,6},{4,1},{5,0},{6,3},{7,2},{8,13},{9,12},{10,... | collective-permute-start | bytes 344072 | tf_op jit(solution)/shard_map/ppermute | solution.py:113
  6.8 20.3 %collective-permute-start.3 = (bf16[16,3584]{1,0:T(8,128)(2,1)}, bf16[16,3584]{1,0:T(8,128)(2,1)}, u32[]{:S(2)}, u32[]{:S(2)}) collective-permute-start(bf16[16,3584]{1,0:T(8,128)(2,1)} %get-tuple-element.25), channel_id=1, source_target_pairs={{0,4},{1,5},{2,6},{3,7},{4,0},{5,1},{6,2},{7,3},{8,12},{9,13},{10,... | collective-permute-start | bytes 344072 | tf_op jit(solution)/shard_map/ppermute | solution.py:113
  10.0 15.8 %collective-permute-start.2 = (bf16[16,3584]{1,0:T(8,128)(2,1)}, bf16[16,3584]{1,0:T(8,128)(2,1)}, u32[]{:S(2)}, u32[]{:S(2)}) collective-permute-start(bf16[16,3584]{1,0:T(8,128)(2,1)} %get-tuple-element.26), channel_id=1, source_target_pairs={{0,3},{1,2},{2,1},{3,0},{4,7},{5,6},{6,5},{7,4},{8,11},{9,10},{10,... | collective-permute-start | bytes 344072 | tf_op jit(solution)/shard_map/ppermute | solution.py:113
  10.0 3.5 %collective-permute-start = (bf16[16,3584]{1,0:T(8,128)(2,1)}, bf16[16,3584]{1,0:T(8,128)(2,1)}, u32[]{:S(2)}, u32[]{:S(2)}) collective-permute-start(bf16[16,3584]{1,0:T(8,128)(2,1)} %get-tuple-element.28), channel_id=1, source_target_pairs={{0,1},{1,0},{2,3},{3,2},{4,5},{5,4},{6,7},{7,6},{8,9},{9,8},{10,11... | collective-permute-start | bytes 344072 | tf_op jit(solution)/shard_map/ppermute | solution.py:113
  13.5 10.7 %collective-permute-start.1 = (bf16[16,3584]{1,0:T(8,128)(2,1)}, bf16[16,3584]{1,0:T(8,128)(2,1)S(1)}, u32[]{:S(2)}, u32[]{:S(2)}) collective-permute-start(bf16[16,3584]{1,0:T(8,128)(2,1)} %get-tuple-element.27), channel_id=1, source_target_pairs={{0,2},{1,3},{2,0},{3,1},{4,6},{5,7},{6,4},{7,5},{8,10},{9,11},{10,... | collective-permute-start | bytes 344072 | tf_op jit(solution)/shard_map/ppermute | solution.py:113
  24.2 6.6 %collective-permute-start.5 = (bf16[16,3584]{1,0:T(8,128)(2,1)S(1)}, bf16[16,3584]{1,0:T(8,128)(2,1)S(1)}, u32[]{:S(2)}, u32[]{:S(2)}) collective-permute-start(bf16[16,3584]{1,0:T(8,128)(2,1)S(1)} %copy-done.2), channel_id=1, source_target_pairs={{0,6},{1,7},{2,4},{3,5},{4,2},{5,3},{6,0},{7,1},{8,14},{9,15},{10,... | collective-permute-start | bytes 344072 | tf_op jit(solution)/shard_map/ppermute | solution.py:113
  39.7 4.6 %collective-permute-start.7 = (bf16[16,3584]{1,0:T(8,128)(2,1)S(1)}, bf16[16,3584]{1,0:T(8,128)(2,1)S(1)}, u32[]{:S(2)}, u32[]{:S(2)}) collective-permute-start(bf16[16,3584]{1,0:T(8,128)(2,1)S(1)} %bitcast.228), channel_id=1, source_target_pairs={{0,1},{1,0},{2,3},{3,2},{4,5},{5,4},{6,7},{7,6},{8,9},{9,8},{10,11... | collective-permute-start | bytes 344072 | tf_op jit(solution)/shard_map/ppermute | solution.py:134
  39.8 8.0 %collective-permute-start.8 = (bf16[16,3584]{1,0:T(8,128)(2,1)S(1)}, bf16[16,3584]{1,0:T(8,128)(2,1)S(1)}, u32[]{:S(2)}, u32[]{:S(2)}) collective-permute-start(bf16[16,3584]{1,0:T(8,128)(2,1)S(1)} %bitcast.227), channel_id=1, source_target_pairs={{0,2},{1,3},{2,0},{3,1},{4,6},{5,7},{6,4},{7,5},{8,10},{9,11},{10,... | collective-permute-start | bytes 344072 | tf_op jit(solution)/shard_map/ppermute | solution.py:134
  39.8 9.6 %collective-permute-start.9 = (bf16[16,3584]{1,0:T(8,128)(2,1)S(1)}, bf16[16,3584]{1,0:T(8,128)(2,1)S(1)}, u32[]{:S(2)}, u32[]{:S(2)}) collective-permute-start(bf16[16,3584]{1,0:T(8,128)(2,1)S(1)} %bitcast.226), channel_id=1, source_target_pairs={{0,3},{1,2},{2,1},{3,0},{4,7},{5,6},{6,5},{7,4},{8,11},{9,10},{10,... | collective-permute-start | bytes 344072 | tf_op jit(solution)/shard_map/ppermute | solution.py:134
  41.6 16.8 %collective-permute-start.10 = (bf16[16,3584]{1,0:T(8,128)(2,1)S(1)}, bf16[16,3584]{1,0:T(8,128)(2,1)S(1)}, u32[]{:S(2)}, u32[]{:S(2)}) collective-permute-start(bf16[16,3584]{1,0:T(8,128)(2,1)S(1)} %bitcast.225), channel_id=1, source_target_pairs={{0,4},{1,5},{2,6},{3,7},{4,0},{5,1},{6,2},{7,3},{8,12},{9,13},{10,... | collective-permute-start | bytes 344072 | tf_op jit(solution)/shard_map/ppermute | solution.py:134
  42.0 17.7 %collective-permute-start.11 = (bf16[16,3584]{1,0:T(8,128)(2,1)S(1)}, bf16[16,3584]{1,0:T(8,128)(2,1)S(1)}, u32[]{:S(2)}, u32[]{:S(2)}) collective-permute-start(bf16[16,3584]{1,0:T(8,128)(2,1)S(1)} %bitcast.224), channel_id=1, source_target_pairs={{0,5},{1,4},{2,7},{3,6},{4,1},{5,0},{6,3},{7,2},{8,13},{9,12},{10,... | collective-permute-start | bytes 344072 | tf_op jit(solution)/shard_map/ppermute | solution.py:134
  44.2 42.0 %slice-start = ((s8[14680064]{0:T(1024)(128)(4,1)}), s8[4194304]{0:T(1024)(128)(4,1)S(1)}, s32[]{:S(2)}) async-start(s8[14680064]{0:T(1024)(128)(4,1)} %bitcast.200), calls=%async_computation | async-start | bytes 8388608
  44.3 15.4 %collective-permute-start.12 = (bf16[16,3584]{1,0:T(8,128)(2,1)S(1)}, bf16[16,3584]{1,0:T(8,128)(2,1)S(1)}, u32[]{:S(2)}, u32[]{:S(2)}) collective-permute-start(bf16[16,3584]{1,0:T(8,128)(2,1)S(1)} %bitcast.223), channel_id=1, source_target_pairs={{0,6},{1,7},{2,4},{3,5},{4,2},{5,3},{6,0},{7,1},{8,14},{9,15},{10,... | collective-permute-start | bytes 344072 | tf_op jit(solution)/shard_map/ppermute | solution.py:134
  47.8 11.9 %collective-permute-start.13 = (bf16[16,3584]{1,0:T(8,128)(2,1)S(1)}, bf16[16,3584]{1,0:T(8,128)(2,1)S(1)}, u32[]{:S(2)}, u32[]{:S(2)}) collective-permute-start(bf16[16,3584]{1,0:T(8,128)(2,1)S(1)} %bitcast.222), channel_id=1, source_target_pairs={{0,7},{1,6},{2,5},{3,4},{4,3},{5,2},{6,1},{7,0},{8,15},{9,14},{10,... | collective-permute-start | bytes 344072 | tf_op jit(solution)/shard_map/ppermute | solution.py:134
  59.8 23.3 %collective-permute-start.17 = (bf16[128,3584]{1,0:T(8,128)(2,1)S(1)}, bf16[128,3584]{1,0:T(8,128)(2,1)S(1)}, u32[]{:S(2)}, u32[]{:S(2)}) collective-permute-start(bf16[128,3584]{1,0:T(8,128)(2,1)S(1)} %constant_dynamic-update-slice_fusion), channel_id=1, source_target_pairs={{0,16},{8,24},{16,0},{24,8},{1,17},{9,25},{17,1},{25,9},{2,18},{10... | collective-permute-start | bytes 2752520 | tf_op jit(solution)/shard_map/ppermute | solution.py:148
  61.4 23.3 %collective-permute-start.14 = (bf16[128,3584]{1,0:T(8,128)(2,1)S(1)}, bf16[128,3584]{1,0:T(8,128)(2,1)S(1)}, u32[]{:S(2)}, u32[]{:S(2)}) collective-permute-start(bf16[128,3584]{1,0:T(8,128)(2,1)S(1)} %constant_dynamic-update-slice_fusion), channel_id=1, source_target_pairs={{0,8},{8,0},{16,24},{24,16},{1,9},{9,1},{17,25},{25,17},{2,10},{10... | collective-permute-start | bytes 2752520 | tf_op jit(solution)/shard_map/ppermute | solution.py:147
  83.1 12.6 %collective-permute-start.18 = (bf16[64,3584]{1,0:T(8,128)(2,1)S(1)}, bf16[64,3584]{1,0:T(8,128)(2,1)S(1)}, u32[]{:S(2)}, u32[]{:S(2)}) collective-permute-start(bf16[64,3584]{1,0:T(8,128)(2,1)S(1)} %slice.89), channel_id=1, source_target_pairs={{0,8},{8,0},{16,24},{24,16},{1,9},{9,1},{17,25},{25,17},{2,10},{10... | collective-permute-start | bytes 1376264 | tf_op jit(solution)/shard_map/ppermute | solution.py:149
  84.7 12.3 %collective-permute-start.19 = (bf16[64,3584]{1,0:T(8,128)(2,1)S(1)}, bf16[64,3584]{1,0:T(8,128)(2,1)S(1)}, u32[]{:S(2)}, u32[]{:S(2)}) collective-permute-start(bf16[64,3584]{1,0:T(8,128)(2,1)S(1)} %slice.90), channel_id=1, source_target_pairs={{0,16},{8,24},{16,0},{24,8},{1,17},{9,25},{17,1},{25,9},{2,18},{10... | collective-permute-start | bytes 1376264 | tf_op jit(solution)/shard_map/ppermute | solution.py:150
  87.6 12.7 %collective-permute-start.15 = (f32[2,64,1024]{2,1,0:T(8,128)S(1)}, f32[2,64,1024]{2,1,0:T(8,128)S(1)}, u32[]{:S(2)}, u32[]{:S(2)}) collective-permute-start(f32[2,64,1024]{2,1,0:T(8,128)S(1)} %fusion.38), channel_id=1, source_target_pairs={{0,1},{1,0},{2,3},{3,2},{4,5},{5,4},{6,7},{7,6},{8,9},{9,8},{10,11... | collective-permute-start | bytes 1572872 | tf_op jit(solution)/shard_map/ppermute | solution.py:160
  89.1 15.7 %collective-permute-start.25 = (f32[2,64,1024]{2,1,0:T(8,128)S(1)}, f32[2,64,1024]{2,1,0:T(8,128)S(1)}, u32[]{:S(2)}, u32[]{:S(2)}) collective-permute-start(f32[2,64,1024]{2,1,0:T(8,128)S(1)} %fusion.33), channel_id=1, source_target_pairs={{0,1},{1,0},{2,3},{3,2},{4,5},{5,4},{6,7},{7,6},{8,9},{9,8},{10,11... | collective-permute-start | bytes 1572872 | tf_op jit(solution)/shard_map/ppermute | solution.py:160
  100.3 18.3 %collective-permute-start.20 = (f32[2,64,2048]{2,1,0:T(8,128)}, f32[2,64,2048]{2,1,0:T(8,128)}, u32[]{:S(2)}, u32[]{:S(2)}) collective-permute-start(f32[2,64,2048]{2,1,0:T(8,128)} %fusion.24), channel_id=1, source_target_pairs={{0,1},{1,0},{2,3},{3,2},{4,5},{5,4},{6,7},{7,6},{8,9},{9,8},{10,11... | collective-permute-start | bytes 3145736 | tf_op jit(solution)/shard_map/ppermute | solution.py:160
  100.4 11.7 %collective-permute-start.16 = (f32[64,1024]{1,0:T(8,128)S(1)}, f32[64,1024]{1,0:T(8,128)}, u32[]{:S(2)}, u32[]{:S(2)}) collective-permute-start(f32[64,1024]{1,0:T(8,128)S(1)} %dynamic-slice_bitcast_fusion.1), channel_id=1, source_target_pairs={{0,2},{1,3},{2,0},{3,1},{4,6},{5,7},{6,4},{7,5},{8,10},{9,11},{10,... | collective-permute-start | bytes 786440 | tf_op jit(solution)/shard_map/ppermute | solution.py:166
  105.7 11.9 %collective-permute-start.26 = (f32[64,1024]{1,0:T(8,128)}, f32[64,1024]{1,0:T(8,128)}, u32[]{:S(2)}, u32[]{:S(2)}) collective-permute-start(f32[64,1024]{1,0:T(8,128)} %dynamic-slice_bitcast_fusion), channel_id=1, source_target_pairs={{0,2},{1,3},{2,0},{3,1},{4,6},{5,7},{6,4},{7,5},{8,10},{9,11},{10,... | collective-permute-start | bytes 786440 | tf_op jit(solution)/shard_map/ppermute | solution.py:166
  120.0 5.4 %collective-permute-start.21 = (f32[64,512]{1,0:T(8,128)S(1)}, f32[64,512]{1,0:T(8,128)S(1)}, u32[]{:S(2)}, u32[]{:S(2)}) collective-permute-start(f32[64,512]{1,0:T(8,128)S(1)} %dynamic-slice_bitcast_fusion.5), channel_id=1, source_target_pairs={{0,2},{1,3},{2,0},{3,1},{4,6},{5,7},{6,4},{7,5},{8,10},{9,11},{10,... | collective-permute-start | bytes 393224 | tf_op jit(solution)/shard_map/ppermute | solution.py:166
  125.5 5.9 %collective-permute-start.23 = (f32[64,512]{1,0:T(8,128)S(1)}, f32[64,512]{1,0:T(8,128)S(1)}, u32[]{:S(2)}, u32[]{:S(2)}) collective-permute-start(f32[64,512]{1,0:T(8,128)S(1)} %dynamic-slice_bitcast_fusion.4), channel_id=1, source_target_pairs={{0,2},{1,3},{2,0},{3,1},{4,6},{5,7},{6,4},{7,5},{8,10},{9,11},{10,... | collective-permute-start | bytes 393224 | tf_op jit(solution)/shard_map/ppermute | solution.py:166
  127.1 11.6 %collective-permute-start.22 = (f32[64,512]{1,0:T(8,128)S(1)}, f32[64,512]{1,0:T(8,128)S(1)}, u32[]{:S(2)}, u32[]{:S(2)}) collective-permute-start(f32[64,512]{1,0:T(8,128)S(1)} %fusion.59), channel_id=1, source_target_pairs={{0,4},{1,5},{2,6},{3,7},{4,0},{5,1},{6,2},{7,3},{8,12},{9,13},{10,... | collective-permute-start | bytes 393224 | tf_op jit(solution)/shard_map/ppermute | solution.py:188
  131.4 11.5 %collective-permute-start.24 = (f32[64,512]{1,0:T(8,128)S(1)}, f32[64,512]{1,0:T(8,128)S(1)}, u32[]{:S(2)}, u32[]{:S(2)}) collective-permute-start(f32[64,512]{1,0:T(8,128)S(1)} %fusion.54), channel_id=1, source_target_pairs={{0,4},{1,5},{2,6},{3,7},{4,0},{5,1},{6,2},{7,3},{8,12},{9,13},{10,... | collective-permute-start | bytes 393224 | tf_op jit(solution)/shard_map/ppermute | solution.py:188
  132.9 5.9 %collective-permute-start.27 = (f32[64,512]{1,0:T(8,128)S(1)}, f32[64,512]{1,0:T(8,128)S(1)}, u32[]{:S(2)}, u32[]{:S(2)}) collective-permute-start(f32[64,512]{1,0:T(8,128)S(1)} %dynamic-slice_bitcast_fusion.3), channel_id=1, source_target_pairs={{0,2},{1,3},{2,0},{3,1},{4,6},{5,7},{6,4},{7,5},{8,10},{9,11},{10,... | collective-permute-start | bytes 393224 | tf_op jit(solution)/shard_map/ppermute | solution.py:166
  138.9 9.5 %collective-permute-start.28 = (f32[64,512]{1,0:T(8,128)S(1)}, f32[64,512]{1,0:T(8,128)S(1)}, u32[]{:S(2)}, u32[]{:S(2)}) collective-permute-start(f32[64,512]{1,0:T(8,128)S(1)} %fusion.49), channel_id=1, source_target_pairs={{0,4},{1,5},{2,6},{3,7},{4,0},{5,1},{6,2},{7,3},{8,12},{9,13},{10,... | collective-permute-start | bytes 393224 | tf_op jit(solution)/shard_map/ppermute | solution.py:188
  140.6 6.0 %collective-permute-start.29 = (f32[64,512]{1,0:T(8,128)S(1)}, f32[64,512]{1,0:T(8,128)S(1)}, u32[]{:S(2)}, u32[]{:S(2)}) collective-permute-start(f32[64,512]{1,0:T(8,128)S(1)} %dynamic-slice_bitcast_fusion.2), channel_id=1, source_target_pairs={{0,2},{1,3},{2,0},{3,1},{4,6},{5,7},{6,4},{7,5},{8,10},{9,11},{10,... | collective-permute-start | bytes 393224 | tf_op jit(solution)/shard_map/ppermute | solution.py:166
  146.7 5.9 %collective-permute-start.30 = (f32[64,512]{1,0:T(8,128)S(1)}, f32[64,512]{1,0:T(8,128)S(1)}, u32[]{:S(2)}, u32[]{:S(2)}) collective-permute-start(f32[64,512]{1,0:T(8,128)S(1)} %fusion.44), channel_id=1, source_target_pairs={{0,4},{1,5},{2,6},{3,7},{4,0},{5,1},{6,2},{7,3},{8,12},{9,13},{10,... | collective-permute-start | bytes 393224 | tf_op jit(solution)/shard_map/ppermute | solution.py:188
  (8 other events, 114.1 us)

commit v15 on v13

--- a/solution.py
+++ b/solution.py
@@ -150,10 +150,12 @@
     second = lax.ppermute(across_x[half:], "seq", seq_pairs(2))
     diagonal = jnp.concatenate([first, second], axis=0)
 
-    def first_halving(pieces):
-        products = jnp.stack(
+    def multiply(pieces):
+        return jnp.stack(
             [jnp.dot(piece, down_weight, preferred_element_type=jnp.float32) for piece in pieces]
         )
+
+    def first_halving(products):
         split = products.reshape(2, 2, half, products.shape[-1])
         keep = lax.dynamic_index_in_dim(split, low, 1, keepdims=False)
         send = lax.dynamic_index_in_dim(split, 1 - low, 1, keepdims=False)
@@ -165,15 +167,15 @@
         send = lax.dynamic_index_in_dim(summed, 1 - chosen, 0, keepdims=False)
         return keep + lax.ppermute(send, "tp", tp_pairs(2))
 
-    near = second_halving(first_halving((block, across_x)))
-    far_summed = first_halving((across_y, diagonal))
+    near = second_halving(first_halving(multiply((block, across_x))))
+    far_products = multiply((across_y, diagonal))
     columns = near.shape[-1]
     width = columns // TAIL_PIECES
     chosen = here // 2 % 2 ^ high
     results = []
     previous = None
     for start in range(0, columns, width):
-        piece = far_summed[..., start : start + width]
+        piece = first_halving(far_products[..., start : start + width])
         if previous is not None:
             _, piece = lax.optimization_barrier((previous, piece))
         far = second_halving(piece)

time: 150 us -> 158 us (1.053)
  waiting for transfers between devices: 65.3 us -> 71.8 us
  other arithmetic: 6.34 us -> 2.54 us
  local copies, waits for them, and re-layouts: 6.98 us -> 10 us
  starting transfers between devices: 42.3 us -> 44.7 us
    ppermute x4, waiting for transfers between devices: 11.1 us -> 17.5 us  [product_and_reduce(): results.append(keep + lax.ppermute(send, 'tp', tp_pairs(4)))]
    add x2 -> x5, other arithmetic: 2.81 us -> 0.28 us  [first_halving(): return keep + lax.ppermute(send, 'tp', tp_pairs(1))]
    squeeze x2 -> x1, other arithmetic: 2.22 us -> 0.1 us  [first_halving(): send = lax.dynamic_index_in_dim(split, 1 - low, 1, keepdims=False)]
    ppermute x7, waiting for transfers between devices: 6.58 us -> 4.57 us  [spread_rotate_return(): send = lax.ppermute(send, 'tp', pairs(distance))]
    ppermute x5, starting transfers between devices: 8.23 us -> 10.2 us  [second_halving(): return keep + lax.ppermute(send, 'tp', tp_pairs(2))]
  transfers between devices with their start and end apart: 29 -> 32, of which waited for: 15 -> 15; matrix products, arithmetic and copies ran while one was open for 21% -> 19% of each run, Pallas kernels for 0% -> 0%
where the time goes in v15:
time: 158 us; the launch traced here: 157 us
  waiting for transfers between devices  71.8 us (45%)
  starting transfers between devices  44.7 us (28%)
  matrix products  27.4 us (17%)
  local copies, waits for them, and re-layouts  10 us (6%)
  other arithmetic  2.54 us (2%)
    ppermute x5, waiting for transfers between devices, second_halving(): return keep + lax.ppermute(send, 'tp', tp_pairs(2))  21.1 us
    ppermute x4, waiting for transfers between devices, product_and_reduce(): results.append(keep + lax.ppermute(send, 'tp', tp_pairs(4)))  17.5 us
    dot_general x4, matrix products, multiply(): jnp.dot(piece, down_weight, preferred_element_type=jnp.float32)  16.4 us
    ppermute x1, waiting for transfers between devices, product_and_reduce(): across_y = lax.ppermute(block, 'seq', seq_pairs(2))  12.9 us
    ppermute x7, waiting for transfers between devices, spread_rotate_return(): block = lax.ppermute(block, 'tp', pairs(distance))  11.7 us
    ppermute x7, starting transfers between devices, spread_rotate_return(): block = lax.ppermute(block, 'tp', pairs(distance))  11.2 us
    ppermute x5, starting transfers between devices, second_halving(): return keep + lax.ppermute(send, 'tp', tp_pairs(2))  10.2 us
    ppermute x7, starting transfers between devices, spread_rotate_return(): send = lax.ppermute(send, 'tp', pairs(distance))  9.65 us
  transfers between devices with their start and end apart: 32, of which 15 were waited for; matrix products, arithmetic and copies ran while one was open for 19% of the time, Pallas kernels for 0%

profile of v15, /device:TPU:0, one launch (start us, length us, event | category | flops | bytes accessed | tf_op | source)
XLA Modules:
  0.0 157.0 jit_solution(13238649656390064093)
XLA Ops:
  0.0 2.3 %constant_dynamic-slice_fusion = (bf16[16,3584]{1,0:T(8,128)(2,1)S(1)}, bf16[16,3584]{1,0:T(8,128)(2,1)}, bf16[16,3584]{1,0:T(8,128)(2,1)}, bf16[16,3584]{1,0:T(...) fusion(bf16[128,3584]{1,0:T(8,128)(2,1)} %param.5, ...), kind=kLoop, calls=%fused_computation.131 | loop fusion | bytes 1835040 | tf_op jit(solution)/shard_map/dynamic_slice | solution.py:111
  2.7 2.6 %collective-permute-start.1 = (bf16[16,3584]{1,0:T(8,128)(2,1)}, bf16[16,3584]{1,0:T(8,128)(2,1)}, u32[]{:S(2)}, u32[]{:S(2)}) collective-permute-start(bf16[16,3584]{1,0:T(8,128)(2,1)} %get-tuple-element.27), channel_id=1, source_target_pairs={{0,2},{1,3},{2,0},{3,1},{4,6},{5,7},{6,4},{7,5},{8,10},{9,11},{10,... | collective-permute-start | bytes 344072 | tf_op jit(solution)/shard_map/ppermute | solution.py:113
  5.5 2.7 %collective-permute-start.3 = (bf16[16,3584]{1,0:T(8,128)(2,1)}, bf16[16,3584]{1,0:T(8,128)(2,1)}, u32[]{:S(2)}, u32[]{:S(2)}) collective-permute-start(bf16[16,3584]{1,0:T(8,128)(2,1)} %get-tuple-element.25), channel_id=1, source_target_pairs={{0,4},{1,5},{2,6},{3,7},{4,0},{5,1},{6,2},{7,3},{8,12},{9,13},{10,... | collective-permute-start | bytes 344072 | tf_op jit(solution)/shard_map/ppermute | solution.py:113
  11.0 3.6 %collective-permute-start.5 = (bf16[16,3584]{1,0:T(8,128)(2,1)}, bf16[16,3584]{1,0:T(8,128)(2,1)S(1)}, u32[]{:S(2)}, u32[]{:S(2)}) collective-permute-start(bf16[16,3584]{1,0:T(8,128)(2,1)} %get-tuple-element.30), channel_id=1, source_target_pairs={{0,6},{1,7},{2,4},{3,5},{4,2},{5,3},{6,0},{7,1},{8,14},{9,15},{10,... | collective-permute-start | bytes 344072 | tf_op jit(solution)/shard_map/ppermute | solution.py:113
  19.9 4.6 %collective-permute-done.4 = bf16[16,3584]{1,0:T(8,128)(2,1)} collective-permute-done((bf16[16,3584]{1,0:T(8,128)(2,1)}, bf16[16,3584]{1,0:T(8,128)(2,1)}, u32[]{:S(2)}, u32[]{:S(2)}) %collective-permute-start.4) | collective-permute-done | bytes 114720 | tf_op jit(solution)/shard_map/ppermute | solution.py:113
  27.8 3.5 %fusion.4 = bf16[16,32,896]{2,1,0:T(8,128)(2,1)S(1)} fusion(f32[16,32,896]{2,0,1:T(8,128)} %bitcast.210, f32[32,32]{1,0:T(8,128)S(1)} %copy-done.2), kind=kOutput, calls=%fused_computation.15 | convolution fusion | flops 177078272 | bytes 2756608 | tf_op jit(solution)/shard_map/rbm,bc->rcm/dot_general | solution.py:127
  31.9 1.7 %fusion.55 = (bf16[16,1,3584]{2,1,0:T(2,128)(2,1)S(1)}, bf16[16,1,3584]{2,1,0:T(2,128)(2,1)S(1)}, bf16[16,1,3584]{2,1,0:T(2,128)(2,1)S(1)}, bf16[16,1,3584]{2,1,...) fusion(bf16[16,8,3584]{2,1,0:T(8,128)(2,1)S(1)} %reshape.121), kind=kLoop, calls=%fused_computation.148 | loop fusion | bytes 1835008 | tf_op jit(solution)/shard_map/slice | solution.py:132
  33.9 3.8 %collective-permute-start.8 = (bf16[16,3584]{1,0:T(8,128)(2,1)S(1)}, bf16[16,3584]{1,0:T(8,128)(2,1)S(1)}, u32[]{:S(2)}, u32[]{:S(2)}) collective-permute-start(bf16[16,3584]{1,0:T(8,128)(2,1)S(1)} %bitcast.231), channel_id=1, source_target_pairs={{0,2},{1,3},{2,0},{3,1},{4,6},{5,7},{6,4},{7,5},{8,10},{9,11},{10,... | collective-permute-start | bytes 344072 | tf_op jit(solution)/shard_map/ppermute | solution.py:134
  37.9 3.1 %collective-permute-start.10 = (bf16[16,3584]{1,0:T(8,128)(2,1)S(1)}, bf16[16,3584]{1,0:T(8,128)(2,1)S(1)}, u32[]{:S(2)}, u32[]{:S(2)}) collective-permute-start(bf16[16,3584]{1,0:T(8,128)(2,1)S(1)} %bitcast.228), channel_id=1, source_target_pairs={{0,4},{1,5},{2,6},{3,7},{4,0},{5,1},{6,2},{7,3},{8,12},{9,13},{10,... | collective-permute-start | bytes 344072 | tf_op jit(solution)/shard_map/ppermute | solution.py:134
  41.6 2.1 %collective-permute-start.12 = (bf16[16,3584]{1,0:T(8,128)(2,1)S(1)}, bf16[16,3584]{1,0:T(8,128)(2,1)S(1)}, u32[]{:S(2)}, u32[]{:S(2)}) collective-permute-start(bf16[16,3584]{1,0:T(8,128)(2,1)S(1)} %bitcast.230), channel_id=1, source_target_pairs={{0,6},{1,7},{2,4},{3,5},{4,2},{5,3},{6,0},{7,1},{8,14},{9,15},{10,... | collective-permute-start | bytes 344072 | tf_op jit(solution)/shard_map/ppermute | solution.py:134
  45.1 2.7 %collective-permute-done.9 = bf16[16,3584]{1,0:T(8,128)(2,1)S(1)} collective-permute-done((bf16[16,3584]{1,0:T(8,128)(2,1)S(1)}, bf16[16,3584]{1,0:T(8,128)(2,1)S(1)}, u32[]{:S(2)}, u32[]{:S(2)}) %collective-permute-start.9) | collective-permute-done | bytes 114720 | tf_op jit(solution)/shard_map/ppermute | solution.py:134
  47.8 9.0 %collective-permute-done.11 = bf16[16,3584]{1,0:T(8,128)(2,1)S(1)} collective-permute-done((bf16[16,3584]{1,0:T(8,128)(2,1)S(1)}, bf16[16,3584]{1,0:T(8,128)(2,1)S(1)}, u32[]{:S(2)}, u32[]{:S(2)}) %collective-permute-start.11) | collective-permute-done | bytes 114720 | tf_op jit(solution)/shard_map/ppermute | solution.py:134
  59.9 7.4 %fusion.56 = f32[128,2048]{1,0:T(8,128)S(1)} fusion(bf16[128,3584]{1,0:T(8,128)(2,1)S(1)} %constant_dynamic-update-slice_fusion, bf16[3584,2048]{1,0:T(8,128)(2,1)} %param.6), kind=kOutput, calls=%fused_computation.149 | convolution fusion | flops 1879048192 | bytes 16646144 | tf_op jit(solution)/shard_map/dot_general | solution.py:155
  67.3 12.9 %collective-permute-done.17 = bf16[128,3584]{1,0:T(8,128)(2,1)} collective-permute-done((bf16[128,3584]{1,0:T(8,128)(2,1)S(1)}, bf16[128,3584]{1,0:T(8,128)(2,1)}, u32[]{:S(2)}, u32[]{:S(2)}) %collective-permute-start.17) | collective-permute-done | bytes 917536 | tf_op jit(solution)/shard_map/ppermute | solution.py:148
  85.5 3.4 %fusion.57 = f32[128,2048]{1,0:T(8,128)S(1)} fusion(bf16[128,3584]{1,0:T(8,128)(2,1)} %collective-permute-done.14, bf16[3584,2048]{1,0:T(8,128)(2,1)S(1)} %bitcast.205), kind=kOutput, calls=%fused_computation.150 | convolution fusion | flops 1879048192 | bytes 16646144 | tf_op jit(solution)/shard_map/dot_general | solution.py:155
  89.1 3.2 %convolution_bitcast_fusion.1 = f32[1,128,2048]{2,1,0:T(8,128)S(1)} fusion(bf16[128,3584]{1,0:T(8,128)(2,1)} %collective-permute-done.17, bf16[3584,2048]{1,0:T(8,128)(2,1)S(1)} %bitcast.205), kind=kOutput, calls=%fused_computation.11 | convolution fusion | flops 1879048192 | bytes 16646144 | tf_op jit(solution)/shard_map/dot_general | solution.py:155
  93.9 2.3 %collective-permute-done.19 = bf16[64,3584]{1,0:T(8,128)(2,1)S(1)} collective-permute-done((bf16[64,3584]{1,0:T(8,128)(2,1)S(1)}, bf16[64,3584]{1,0:T(8,128)(2,1)S(1)}, u32[]{:S(2)}, u32[]{:S(2)}) %collective-permute-start.19) | collective-permute-done | bytes 458784 | tf_op jit(solution)/shard_map/ppermute | solution.py:150
  96.3 2.3 %convolution_bitcast_fusion = f32[1,128,2048]{2,1,0:T(8,128)S(1)} fusion(bf16[3584,2048]{1,0:T(8,128)(2,1)S(1)} %bitcast.205, bf16[64,3584]{1,0:T(8,128)(2,1)S(1)} %collective-permute-done.19, bf16[64,3584]{1,0:T(8,128)(2,1)S(1)} %collective-permute-done.18), kind=kOutput, calls=%fused_computation.10 | convolution fusion | flops 1880883200 | bytes 16646144 | tf_op jit(solution)/shard_map/dot_general | solution.py:155
  100.5 4.5 %collective-permute-start.21 = (f32[64,512]{1,0:T(8,128)S(1)}, f32[64,512]{1,0:T(8,128)S(1)}, u32[]{:S(2)}, u32[]{:S(2)}) collective-permute-start(f32[64,512]{1,0:T(8,128)S(1)} %dynamic-slice_bitcast_fusion.8), channel_id=1, source_target_pairs={{0,2},{1,3},{2,0},{3,1},{4,6},{5,7},{6,4},{7,5},{8,10},{9,11},{10,... | collective-permute-start | bytes 393224 | tf_op jit(solution)/shard_map/ppermute | solution.py:168
  105.1 3.7 %collective-permute-done.21 = f32[64,512]{1,0:T(8,128)S(1)} collective-permute-done((f32[64,512]{1,0:T(8,128)S(1)}, f32[64,512]{1,0:T(8,128)S(1)}, u32[]{:S(2)}, u32[]{:S(2)}) %collective-permute-start.21) | collective-permute-done | bytes 131104 | tf_op jit(solution)/shard_map/ppermute | solution.py:168
  108.9 1.8 %collective-permute-start.24 = (f32[64,512]{1,0:T(8,128)S(1)}, f32[64,512]{1,0:T(8,128)S(1)}, u32[]{:S(2)}, u32[]{:S(2)}) collective-permute-start(f32[64,512]{1,0:T(8,128)S(1)} %dynamic-slice_bitcast_fusion.7), channel_id=1, source_target_pairs={{0,2},{1,3},{2,0},{3,1},{4,6},{5,7},{6,4},{7,5},{8,10},{9,11},{10,... | collective-permute-start | bytes 393224 | tf_op jit(solution)/shard_map/ppermute | solution.py:168
  110.7 3.2 %collective-permute-done.24 = f32[64,512]{1,0:T(8,128)S(1)} collective-permute-done((f32[64,512]{1,0:T(8,128)S(1)}, f32[64,512]{1,0:T(8,128)S(1)}, u32[]{:S(2)}, u32[]{:S(2)}) %collective-permute-start.24) | collective-permute-done | bytes 131104 | tf_op jit(solution)/shard_map/ppermute | solution.py:168
  114.0 1.7 %collective-permute-start.27 = (f32[64,512]{1,0:T(8,128)S(1)}, f32[64,512]{1,0:T(8,128)S(1)}, u32[]{:S(2)}, u32[]{:S(2)}) collective-permute-start(f32[64,512]{1,0:T(8,128)S(1)} %dynamic-slice_bitcast_fusion.6), channel_id=1, source_target_pairs={{0,2},{1,3},{2,0},{3,1},{4,6},{5,7},{6,4},{7,5},{8,10},{9,11},{10,... | collective-permute-start | bytes 393224 | tf_op jit(solution)/shard_map/ppermute | solution.py:168
  116.3 4.2 %collective-permute-done.27 = f32[64,512]{1,0:T(8,128)S(1)} collective-permute-done((f32[64,512]{1,0:T(8,128)S(1)}, f32[64,512]{1,0:T(8,128)S(1)}, u32[]{:S(2)}, u32[]{:S(2)}) %collective-permute-start.27) | collective-permute-done | bytes 131104 | tf_op jit(solution)/shard_map/ppermute | solution.py:168
  120.5 1.7 %collective-permute-start.30 = (f32[64,512]{1,0:T(8,128)S(1)}, f32[64,512]{1,0:T(8,128)S(1)}, u32[]{:S(2)}, u32[]{:S(2)}) collective-permute-start(f32[64,512]{1,0:T(8,128)S(1)} %dynamic-slice_bitcast_fusion.5), channel_id=1, source_target_pairs={{0,2},{1,3},{2,0},{3,1},{4,6},{5,7},{6,4},{7,5},{8,10},{9,11},{10,... | collective-permute-start | bytes 393224 | tf_op jit(solution)/shard_map/ppermute | solution.py:168
  122.3 9.9 %collective-permute-done.30 = f32[64,512]{1,0:T(8,128)S(1)} collective-permute-done((f32[64,512]{1,0:T(8,128)S(1)}, f32[64,512]{1,0:T(8,128)S(1)}, u32[]{:S(2)}, u32[]{:S(2)}) %collective-permute-start.30) | collective-permute-done | bytes 131104 | tf_op jit(solution)/shard_map/ppermute | solution.py:168
  132.4 2.0 %collective-permute-start.22 = (f32[64,512]{1,0:T(8,128)S(1)}, f32[64,512]{1,0:T(8,128)S(1)}, u32[]{:S(2)}, u32[]{:S(2)}) collective-permute-start(f32[64,512]{1,0:T(8,128)S(1)} %fusion.43), channel_id=1, source_target_pairs={{0,4},{1,5},{2,6},{3,7},{4,0},{5,1},{6,2},{7,3},{8,12},{9,13},{10,... | collective-permute-start | bytes 393224 | tf_op jit(solution)/shard_map/ppermute | solution.py:185
  135.6 2.0 %collective-permute-start.28 = (f32[64,512]{1,0:T(8,128)S(1)}, f32[64,512]{1,0:T(8,128)S(1)}, u32[]{:S(2)}, u32[]{:S(2)}) collective-permute-start(f32[64,512]{1,0:T(8,128)S(1)} %fusion.33), channel_id=1, source_target_pairs={{0,4},{1,5},{2,6},{3,7},{4,0},{5,1},{6,2},{7,3},{8,12},{9,13},{10,... | collective-permute-start | bytes 393224 | tf_op jit(solution)/shard_map/ppermute | solution.py:185
  138.7 10.0 %collective-permute-done.22 = f32[64,512]{1,0:T(8,128)S(1)} collective-permute-done((f32[64,512]{1,0:T(8,128)S(1)}, f32[64,512]{1,0:T(8,128)S(1)}, u32[]{:S(2)}, u32[]{:S(2)}) %collective-permute-start.22) | collective-permute-done | bytes 131104 | tf_op jit(solution)/shard_map/ppermute | solution.py:185
  148.7 2.8 %collective-permute-done.25 = f32[64,512]{1,0:T(8,128)S(1)} collective-permute-done((f32[64,512]{1,0:T(8,128)S(1)}, f32[64,512]{1,0:T(8,128)S(1)}, u32[]{:S(2)}, u32[]{:S(2)}) %collective-permute-start.25) | collective-permute-done | bytes 131104 | tf_op jit(solution)/shard_map/ppermute | solution.py:185
  151.5 2.8 %collective-permute-done.28 = f32[64,512]{1,0:T(8,128)S(1)} collective-permute-done((f32[64,512]{1,0:T(8,128)S(1)}, f32[64,512]{1,0:T(8,128)S(1)}, u32[]{:S(2)}, u32[]{:S(2)}) %collective-permute-start.28) | collective-permute-done | bytes 131104 | tf_op jit(solution)/shard_map/ppermute | solution.py:185
  154.3 1.9 %collective-permute-done.31 = f32[64,512]{1,0:T(8,128)S(1)} collective-permute-done((f32[64,512]{1,0:T(8,128)S(1)}, f32[64,512]{1,0:T(8,128)S(1)}, u32[]{:S(2)}, u32[]{:S(2)}) %collective-permute-start.31) | collective-permute-done | bytes 131104 | tf_op jit(solution)/shard_map/ppermute | solution.py:185
  (120 shorter events, 30.9 us)
Async XLA Ops:
  2.3 8.7 %collective-permute-start = (bf16[16,3584]{1,0:T(8,128)(2,1)}, bf16[16,3584]{1,0:T(8,128)(2,1)}, u32[]{:S(2)}, u32[]{:S(2)}) collective-permute-start(bf16[16,3584]{1,0:T(8,128)(2,1)} %get-tuple-element.28), channel_id=1, source_target_pairs={{0,1},{1,0},{2,3},{3,2},{4,5},{5,4},{6,7},{7,6},{8,9},{9,8},{10,11... | collective-permute-start | bytes 344072 | tf_op jit(solution)/shard_map/ppermute | solution.py:113
  2.7 13.1 %collective-permute-start.1 = (bf16[16,3584]{1,0:T(8,128)(2,1)}, bf16[16,3584]{1,0:T(8,128)(2,1)}, u32[]{:S(2)}, u32[]{:S(2)}) collective-permute-start(bf16[16,3584]{1,0:T(8,128)(2,1)} %get-tuple-element.27), channel_id=1, source_target_pairs={{0,2},{1,3},{2,0},{3,1},{4,6},{5,7},{6,4},{7,5},{8,10},{9,11},{10,... | collective-permute-start | bytes 344072 | tf_op jit(solution)/shard_map/ppermute | solution.py:113
  5.4 12.0 %collective-permute-start.2 = (bf16[16,3584]{1,0:T(8,128)(2,1)}, bf16[16,3584]{1,0:T(8,128)(2,1)}, u32[]{:S(2)}, u32[]{:S(2)}) collective-permute-start(bf16[16,3584]{1,0:T(8,128)(2,1)} %get-tuple-element.26), channel_id=1, source_target_pairs={{0,3},{1,2},{2,1},{3,0},{4,7},{5,6},{6,5},{7,4},{8,11},{9,10},{10,... | collective-permute-start | bytes 344072 | tf_op jit(solution)/shard_map/ppermute | solution.py:113
  5.5 13.1 %collective-permute-start.3 = (bf16[16,3584]{1,0:T(8,128)(2,1)}, bf16[16,3584]{1,0:T(8,128)(2,1)}, u32[]{:S(2)}, u32[]{:S(2)}) collective-permute-start(bf16[16,3584]{1,0:T(8,128)(2,1)} %get-tuple-element.25), channel_id=1, source_target_pairs={{0,4},{1,5},{2,6},{3,7},{4,0},{5,1},{6,2},{7,3},{8,12},{9,13},{10,... | collective-permute-start | bytes 344072 | tf_op jit(solution)/shard_map/ppermute | solution.py:113
  8.2 16.3 %collective-permute-start.4 = (bf16[16,3584]{1,0:T(8,128)(2,1)}, bf16[16,3584]{1,0:T(8,128)(2,1)}, u32[]{:S(2)}, u32[]{:S(2)}) collective-permute-start(bf16[16,3584]{1,0:T(8,128)(2,1)} %get-tuple-element.24), channel_id=1, source_target_pairs={{0,5},{1,4},{2,7},{3,6},{4,1},{5,0},{6,3},{7,2},{8,13},{9,12},{10,... | collective-permute-start | bytes 344072 | tf_op jit(solution)/shard_map/ppermute | solution.py:113
  11.0 14.7 %collective-permute-start.5 = (bf16[16,3584]{1,0:T(8,128)(2,1)}, bf16[16,3584]{1,0:T(8,128)(2,1)S(1)}, u32[]{:S(2)}, u32[]{:S(2)}) collective-permute-start(bf16[16,3584]{1,0:T(8,128)(2,1)} %get-tuple-element.30), channel_id=1, source_target_pairs={{0,6},{1,7},{2,4},{3,5},{4,2},{5,3},{6,0},{7,1},{8,14},{9,15},{10,... | collective-permute-start | bytes 344072 | tf_op jit(solution)/shard_map/ppermute | solution.py:113
  15.9 10.3 %collective-permute-start.6 = (bf16[16,3584]{1,0:T(8,128)(2,1)S(1)}, bf16[16,3584]{1,0:T(8,128)(2,1)S(1)}, u32[]{:S(2)}, u32[]{:S(2)}) collective-permute-start(bf16[16,3584]{1,0:T(8,128)(2,1)S(1)} %get-tuple-element.23), channel_id=1, source_target_pairs={{0,7},{1,6},{2,5},{3,4},{4,3},{5,2},{6,1},{7,0},{8,15},{9,14},{10,... | collective-permute-start | bytes 344072 | tf_op jit(solution)/shard_map/ppermute | solution.py:113
  33.6 8.0 %collective-permute-start.7 = (bf16[16,3584]{1,0:T(8,128)(2,1)S(1)}, bf16[16,3584]{1,0:T(8,128)(2,1)S(1)}, u32[]{:S(2)}, u32[]{:S(2)}) collective-permute-start(bf16[16,3584]{1,0:T(8,128)(2,1)S(1)} %bitcast.232), channel_id=1, source_target_pairs={{0,1},{1,0},{2,3},{3,2},{4,5},{5,4},{6,7},{7,6},{8,9},{9,8},{10,11... | collective-permute-start | bytes 344072 | tf_op jit(solution)/shard_map/ppermute | solution.py:134
  33.9 9.9 %collective-permute-start.8 = (bf16[16,3584]{1,0:T(8,128)(2,1)S(1)}, bf16[16,3584]{1,0:T(8,128)(2,1)S(1)}, u32[]{:S(2)}, u32[]{:S(2)}) collective-permute-start(bf16[16,3584]{1,0:T(8,128)(2,1)S(1)} %bitcast.231), channel_id=1, source_target_pairs={{0,2},{1,3},{2,0},{3,1},{4,6},{5,7},{6,4},{7,5},{8,10},{9,11},{10,... | collective-permute-start | bytes 344072 | tf_op jit(solution)/shard_map/ppermute | solution.py:134
  37.8 10.0 %collective-permute-start.9 = (bf16[16,3584]{1,0:T(8,128)(2,1)S(1)}, bf16[16,3584]{1,0:T(8,128)(2,1)S(1)}, u32[]{:S(2)}, u32[]{:S(2)}) collective-permute-start(bf16[16,3584]{1,0:T(8,128)(2,1)S(1)} %bitcast.229), channel_id=1, source_target_pairs={{0,3},{1,2},{2,1},{3,0},{4,7},{5,6},{6,5},{7,4},{8,11},{9,10},{10,... | collective-permute-start | bytes 344072 | tf_op jit(solution)/shard_map/ppermute | solution.py:134
  37.9 9.8 %collective-permute-start.10 = (bf16[16,3584]{1,0:T(8,128)(2,1)S(1)}, bf16[16,3584]{1,0:T(8,128)(2,1)S(1)}, u32[]{:S(2)}, u32[]{:S(2)}) collective-permute-start(bf16[16,3584]{1,0:T(8,128)(2,1)S(1)} %bitcast.228), channel_id=1, source_target_pairs={{0,4},{1,5},{2,6},{3,7},{4,0},{5,1},{6,2},{7,3},{8,12},{9,13},{10,... | collective-permute-start | bytes 344072 | tf_op jit(solution)/shard_map/ppermute | solution.py:134
  41.1 15.7 %collective-permute-start.11 = (bf16[16,3584]{1,0:T(8,128)(2,1)S(1)}, bf16[16,3584]{1,0:T(8,128)(2,1)S(1)}, u32[]{:S(2)}, u32[]{:S(2)}) collective-permute-start(bf16[16,3584]{1,0:T(8,128)(2,1)S(1)} %bitcast.227), channel_id=1, source_target_pairs={{0,5},{1,4},{2,7},{3,6},{4,1},{5,0},{6,3},{7,2},{8,13},{9,12},{10,... | collective-permute-start | bytes 344072 | tf_op jit(solution)/shard_map/ppermute | solution.py:134
  41.6 15.2 %collective-permute-start.12 = (bf16[16,3584]{1,0:T(8,128)(2,1)S(1)}, bf16[16,3584]{1,0:T(8,128)(2,1)S(1)}, u32[]{:S(2)}, u32[]{:S(2)}) collective-permute-start(bf16[16,3584]{1,0:T(8,128)(2,1)S(1)} %bitcast.230), channel_id=1, source_target_pairs={{0,6},{1,7},{2,4},{3,5},{4,2},{5,3},{6,0},{7,1},{8,14},{9,15},{10,... | collective-permute-start | bytes 344072 | tf_op jit(solution)/shard_map/ppermute | solution.py:134
  43.8 13.0 %collective-permute-start.13 = (bf16[16,3584]{1,0:T(8,128)(2,1)S(1)}, bf16[16,3584]{1,0:T(8,128)(2,1)S(1)}, u32[]{:S(2)}, u32[]{:S(2)}) collective-permute-start(bf16[16,3584]{1,0:T(8,128)(2,1)S(1)} %bitcast.226), channel_id=1, source_target_pairs={{0,7},{1,6},{2,5},{3,4},{4,3},{5,2},{6,1},{7,0},{8,15},{9,14},{10,... | collective-permute-start | bytes 344072 | tf_op jit(solution)/shard_map/ppermute | solution.py:134
  56.9 23.4 %collective-permute-start.17 = (bf16[128,3584]{1,0:T(8,128)(2,1)S(1)}, bf16[128,3584]{1,0:T(8,128)(2,1)}, u32[]{:S(2)}, u32[]{:S(2)}) collective-permute-start(bf16[128,3584]{1,0:T(8,128)(2,1)S(1)} %constant_dynamic-update-slice_fusion), channel_id=1, source_target_pairs={{0,16},{8,24},{16,0},{24,8},{1,17},{9,25},{17,1},{25,9},{2,18},{10... | collective-permute-start | bytes 2752520 | tf_op jit(solution)/shard_map/ppermute | solution.py:148
  58.5 24.4 %collective-permute-start.14 = (bf16[128,3584]{1,0:T(8,128)(2,1)S(1)}, bf16[128,3584]{1,0:T(8,128)(2,1)}, u32[]{:S(2)}, u32[]{:S(2)}) collective-permute-start(bf16[128,3584]{1,0:T(8,128)(2,1)S(1)} %constant_dynamic-update-slice_fusion), channel_id=1, source_target_pairs={{0,8},{8,0},{16,24},{24,16},{1,9},{9,1},{17,25},{25,17},{2,10},{10... | collective-permute-start | bytes 2752520 | tf_op jit(solution)/shard_map/ppermute | solution.py:147
  81.3 12.6 %collective-permute-start.18 = (bf16[64,3584]{1,0:T(8,128)(2,1)S(1)}, bf16[64,3584]{1,0:T(8,128)(2,1)S(1)}, u32[]{:S(2)}, u32[]{:S(2)}) collective-permute-start(bf16[64,3584]{1,0:T(8,128)(2,1)S(1)} %slice.81), channel_id=1, source_target_pairs={{0,8},{8,0},{16,24},{24,16},{1,9},{9,1},{17,25},{25,17},{2,10},{10... | collective-permute-start | bytes 1376264 | tf_op jit(solution)/shard_map/ppermute | solution.py:149
  83.9 12.3 %collective-permute-start.19 = (bf16[64,3584]{1,0:T(8,128)(2,1)S(1)}, bf16[64,3584]{1,0:T(8,128)(2,1)S(1)}, u32[]{:S(2)}, u32[]{:S(2)}) collective-permute-start(bf16[64,3584]{1,0:T(8,128)(2,1)S(1)} %slice.82), channel_id=1, source_target_pairs={{0,16},{8,24},{16,0},{24,8},{1,17},{9,25},{17,1},{25,9},{2,18},{10... | collective-permute-start | bytes 1376264 | tf_op jit(solution)/shard_map/ppermute | solution.py:150
  89.1 26.7 %collective-permute-start.15 = (f32[2,64,2048]{2,1,0:T(8,128)S(1)}, f32[2,64,2048]{2,1,0:T(8,128)S(1)}, u32[]{:S(2)}, u32[]{:S(2)}) collective-permute-start(f32[2,64,2048]{2,1,0:T(8,128)S(1)} %fusion.16), channel_id=1, source_target_pairs={{0,1},{1,0},{2,3},{3,2},{4,5},{5,4},{6,7},{7,6},{8,9},{9,8},{10,11... | collective-permute-start | bytes 3145736 | tf_op jit(solution)/shard_map/ppermute | solution.py:162
  98.9 1.6 %collective-permute-start.20 = (f32[2,64,512]{2,1,0:T(8,128)S(1)}, f32[2,64,512]{2,1,0:T(8,128)S(1)}, u32[]{:S(2)}, u32[]{:S(2)}) collective-permute-start(f32[2,64,512]{2,1,0:T(8,128)S(1)} %dynamic-slice_bitcast_fusion.4), channel_id=1, source_target_pairs={{0,1},{1,0},{2,3},{3,2},{4,5},{5,4},{6,7},{7,6},{8,9},{9,8},{10,11... | collective-permute-start | bytes 786440 | tf_op jit(solution)/shard_map/ppermute | solution.py:162
  99.0 6.0 %collective-permute-start.23 = (f32[2,64,512]{2,1,0:T(8,128)S(1)}, f32[2,64,512]{2,1,0:T(8,128)S(1)}, u32[]{:S(2)}, u32[]{:S(2)}) collective-permute-start(f32[2,64,512]{2,1,0:T(8,128)S(1)} %dynamic-slice_bitcast_fusion.3), channel_id=1, source_target_pairs={{0,1},{1,0},{2,3},{3,2},{4,5},{5,4},{6,7},{7,6},{8,9},{9,8},{10,11... | collective-permute-start | bytes 786440 | tf_op jit(solution)/shard_map/ppermute | solution.py:162
  99.6 5.5 %collective-permute-start.26 = (f32[2,64,512]{2,1,0:T(8,128)S(1)}, f32[2,64,512]{2,1,0:T(8,128)S(1)}, u32[]{:S(2)}, u32[]{:S(2)}) collective-permute-start(f32[2,64,512]{2,1,0:T(8,128)S(1)} %dynamic-slice_bitcast_fusion.2), channel_id=1, source_target_pairs={{0,1},{1,0},{2,3},{3,2},{4,5},{5,4},{6,7},{7,6},{8,9},{9,8},{10,11... | collective-permute-start | bytes 786440 | tf_op jit(solution)/shard_map/ppermute | solution.py:162
  99.7 11.0 %collective-permute-start.29 = (f32[2,64,512]{2,1,0:T(8,128)S(1)}, f32[2,64,512]{2,1,0:T(8,128)S(1)}, u32[]{:S(2)}, u32[]{:S(2)}) collective-permute-start(f32[2,64,512]{2,1,0:T(8,128)S(1)} %dynamic-slice_bitcast_fusion.1), channel_id=1, source_target_pairs={{0,1},{1,0},{2,3},{3,2},{4,5},{5,4},{6,7},{7,6},{8,9},{9,8},{10,11... | collective-permute-start | bytes 786440 | tf_op jit(solution)/shard_map/ppermute | solution.py:162
  100.5 8.3 %collective-permute-start.21 = (f32[64,512]{1,0:T(8,128)S(1)}, f32[64,512]{1,0:T(8,128)S(1)}, u32[]{:S(2)}, u32[]{:S(2)}) collective-permute-start(f32[64,512]{1,0:T(8,128)S(1)} %dynamic-slice_bitcast_fusion.8), channel_id=1, source_target_pairs={{0,2},{1,3},{2,0},{3,1},{4,6},{5,7},{6,4},{7,5},{8,10},{9,11},{10,... | collective-permute-start | bytes 393224 | tf_op jit(solution)/shard_map/ppermute | solution.py:168
  108.9 5.1 %collective-permute-start.24 = (f32[64,512]{1,0:T(8,128)S(1)}, f32[64,512]{1,0:T(8,128)S(1)}, u32[]{:S(2)}, u32[]{:S(2)}) collective-permute-start(f32[64,512]{1,0:T(8,128)S(1)} %dynamic-slice_bitcast_fusion.7), channel_id=1, source_target_pairs={{0,2},{1,3},{2,0},{3,1},{4,6},{5,7},{6,4},{7,5},{8,10},{9,11},{10,... | collective-permute-start | bytes 393224 | tf_op jit(solution)/shard_map/ppermute | solution.py:168
  114.0 6.5 %collective-permute-start.27 = (f32[64,512]{1,0:T(8,128)S(1)}, f32[64,512]{1,0:T(8,128)S(1)}, u32[]{:S(2)}, u32[]{:S(2)}) collective-permute-start(f32[64,512]{1,0:T(8,128)S(1)} %dynamic-slice_bitcast_fusion.6), channel_id=1, source_target_pairs={{0,2},{1,3},{2,0},{3,1},{4,6},{5,7},{6,4},{7,5},{8,10},{9,11},{10,... | collective-permute-start | bytes 393224 | tf_op jit(solution)/shard_map/ppermute | solution.py:168
  115.9 16.3 %collective-permute-start.16 = (f32[64,2048]{1,0:T(8,128)S(1)}, f32[64,2048]{1,0:T(8,128)S(1)}, u32[]{:S(2)}, u32[]{:S(2)}) collective-permute-start(f32[64,2048]{1,0:T(8,128)S(1)} %dynamic-slice_bitcast_fusion), channel_id=1, source_target_pairs={{0,2},{1,3},{2,0},{3,1},{4,6},{5,7},{6,4},{7,5},{8,10},{9,11},{10,... | collective-permute-start | bytes 1572872 | tf_op jit(solution)/shard_map/ppermute | solution.py:168
  120.5 11.7 %collective-permute-start.30 = (f32[64,512]{1,0:T(8,128)S(1)}, f32[64,512]{1,0:T(8,128)S(1)}, u32[]{:S(2)}, u32[]{:S(2)}) collective-permute-start(f32[64,512]{1,0:T(8,128)S(1)} %dynamic-slice_bitcast_fusion.5), channel_id=1, source_target_pairs={{0,2},{1,3},{2,0},{3,1},{4,6},{5,7},{6,4},{7,5},{8,10},{9,11},{10,... | collective-permute-start | bytes 393224 | tf_op jit(solution)/shard_map/ppermute | solution.py:168
  132.4 16.2 %collective-permute-start.22 = (f32[64,512]{1,0:T(8,128)S(1)}, f32[64,512]{1,0:T(8,128)S(1)}, u32[]{:S(2)}, u32[]{:S(2)}) collective-permute-start(f32[64,512]{1,0:T(8,128)S(1)} %fusion.43), channel_id=1, source_target_pairs={{0,4},{1,5},{2,6},{3,7},{4,0},{5,1},{6,2},{7,3},{8,12},{9,13},{10,... | collective-permute-start | bytes 393224 | tf_op jit(solution)/shard_map/ppermute | solution.py:185
  134.4 17.0 %collective-permute-start.25 = (f32[64,512]{1,0:T(8,128)S(1)}, f32[64,512]{1,0:T(8,128)S(1)}, u32[]{:S(2)}, u32[]{:S(2)}) collective-permute-start(f32[64,512]{1,0:T(8,128)S(1)} %fusion.38), channel_id=1, source_target_pairs={{0,4},{1,5},{2,6},{3,7},{4,0},{5,1},{6,2},{7,3},{8,12},{9,13},{10,... | collective-permute-start | bytes 393224 | tf_op jit(solution)/shard_map/ppermute | solution.py:185
  135.6 18.7 %collective-permute-start.28 = (f32[64,512]{1,0:T(8,128)S(1)}, f32[64,512]{1,0:T(8,128)S(1)}, u32[]{:S(2)}, u32[]{:S(2)}) collective-permute-start(f32[64,512]{1,0:T(8,128)S(1)} %fusion.33), channel_id=1, source_target_pairs={{0,4},{1,5},{2,6},{3,7},{4,0},{5,1},{6,2},{7,3},{8,12},{9,13},{10,... | collective-permute-start | bytes 393224 | tf_op jit(solution)/shard_map/ppermute | solution.py:185
  137.6 18.7 %collective-permute-start.31 = (f32[64,512]{1,0:T(8,128)S(1)}, f32[64,512]{1,0:T(8,128)S(1)}, u32[]{:S(2)}, u32[]{:S(2)}) collective-permute-start(f32[64,512]{1,0:T(8,128)S(1)} %fusion.28), channel_id=1, source_target_pairs={{0,4},{1,5},{2,6},{3,7},{4,0},{5,1},{6,2},{7,3},{8,12},{9,13},{10,... | collective-permute-start | bytes 393224 | tf_op jit(solution)/shard_map/ppermute | solution.py:185
  (9 other events, 164.8 us)

commit v16 on v13

--- a/solution.py
+++ b/solution.py
@@ -165,7 +165,14 @@
         send = lax.dynamic_index_in_dim(summed, 1 - chosen, 0, keepdims=False)
         return keep + lax.ppermute(send, "tp", tp_pairs(2))
 
-    near = second_halving(first_halving((block, across_x)))
+    def first_halving_one(piece):
+        product = jnp.dot(piece, down_weight, preferred_element_type=jnp.float32)
+        split = product.reshape(2, half, product.shape[-1])
+        keep = lax.dynamic_index_in_dim(split, low, 0, keepdims=False)
+        send = lax.dynamic_index_in_dim(split, 1 - low, 0, keepdims=False)
+        return keep + lax.ppermute(send, "tp", tp_pairs(1))
+
+    near = second_halving(jnp.stack([first_halving_one(block), first_halving_one(across_x)]))
     far_summed = first_halving((across_y, diagonal))
     columns = near.shape[-1]
     width = columns // TAIL_PIECES

time: 150 us -> 148 us (0.987)
  matrix products: 28.5 us -> 24.9 us
  starting transfers between devices: 42.3 us -> 45.6 us
  other arithmetic: 6.34 us -> 3.2 us
    ppermute x1, waiting for transfers between devices: 12.8 us -> 0.01 us  [product_and_reduce(): across_y = lax.ppermute(block, 'seq', seq_pairs(2))]
    dot_general x4 -> x2, matrix products: 16.4 us -> 4.12 us  [first_halving(): jnp.dot(piece, down_weight, preferred_element_type=jnp.float32)]
    ppermute x1, waiting for transfers between devices: 0.01 us -> 11.5 us  [product_and_reduce(): across_x = lax.ppermute(block, 'seq', seq_pairs(1))]
    dot_general x0 -> x2, matrix products: none -> 9.78 us  [first_halving_one(): product = jnp.dot(piece, down_weight, preferred_element_type=jnp.float32)]
    ppermute x1, waiting for transfers between devices: 2.36 us -> 7.53 us  [product_and_reduce(): second = lax.ppermute(across_x[half:], 'seq', seq_pairs(2))]
    ppermute x5, starting transfers between devices: 8.23 us -> 12.3 us  [second_halving(): return keep + lax.ppermute(send, 'tp', tp_pairs(2))]
    ppermute x7, waiting for transfers between devices: 6.58 us -> 3.89 us  [spread_rotate_return(): send = lax.ppermute(send, 'tp', pairs(distance))]
    add x2 -> x1, other arithmetic: 2.81 us -> 0.15 us  [first_halving(): return keep + lax.ppermute(send, 'tp', tp_pairs(1))]
  transfers between devices with their start and end apart: 29 -> 30, of which waited for: 15 -> 15; matrix products, arithmetic and copies ran while one was open for 21% -> 17% of each run, Pallas kernels for 0% -> 0%
where the time goes in v16:
time: 148 us
  waiting for transfers between devices  65.7 us (44%)
  starting transfers between devices  45.6 us (31%)
  matrix products  24.9 us (17%)
  local copies, waits for them, and re-layouts  7.85 us (5%)
  other arithmetic  3.2 us (2%)
    ppermute x5, waiting for transfers between devices, second_halving(): return keep + lax.ppermute(send, 'tp', tp_pairs(2))  20.2 us
    ppermute x5, starting transfers between devices, second_halving(): return keep + lax.ppermute(send, 'tp', tp_pairs(2))  12.3 us
    ppermute x7, waiting for transfers between devices, spread_rotate_return(): block = lax.ppermute(block, 'tp', pairs(distance))  11.7 us
    ppermute x1, waiting for transfers between devices, product_and_reduce(): across_x = lax.ppermute(block, 'seq', seq_pairs(1))  11.5 us
    ppermute x7, starting transfers between devices, spread_rotate_return(): block = lax.ppermute(block, 'tp', pairs(distance))  11.2 us
    dot_general x2, matrix products, first_halving_one(): product = jnp.dot(piece, down_weight, preferred_element_type=jnp.float32)  9.78 us
    ppermute x7, starting transfers between devices, spread_rotate_return(): send = lax.ppermute(send, 'tp', pairs(distance))  9.62 us
    ppermute x4, waiting for transfers between devices, product_and_reduce(): results.append(keep + lax.ppermute(send, 'tp', tp_pairs(4)))  9.59 us
  transfers between devices with their start and end apart: 30, of which 15 were waited for; matrix products, arithmetic and copies ran while one was open for 17% of the time, Pallas kernels for 0%

profile of v16, /device:TPU:0, one launch (start us, length us, event | category | flops | bytes accessed | tf_op | source)
XLA Modules:
  0.0 147.9 jit_solution(17055061763461518477)
XLA Ops:
  0.0 2.3 %constant_dynamic-slice_fusion = (bf16[16,3584]{1,0:T(8,128)(2,1)}, bf16[16,3584]{1,0:T(8,128)(2,1)}, bf16[16,3584]{1,0:T(8,128)(2,1)}, bf16[16,3584]{1,0:T(8,12...) fusion(bf16[128,3584]{1,0:T(8,128)(2,1)} %param.5, ...), kind=kLoop, calls=%fused_computation.125 | loop fusion | bytes 1835040 | tf_op jit(solution)/shard_map/dynamic_slice | solution.py:111
  2.7 2.6 %collective-permute-start.1 = (bf16[16,3584]{1,0:T(8,128)(2,1)}, bf16[16,3584]{1,0:T(8,128)(2,1)}, u32[]{:S(2)}, u32[]{:S(2)}) collective-permute-start(bf16[16,3584]{1,0:T(8,128)(2,1)} %get-tuple-element.27), channel_id=1, source_target_pairs={{0,2},{1,3},{2,0},{3,1},{4,6},{5,7},{6,4},{7,5},{8,10},{9,11},{10,... | collective-permute-start | bytes 344072 | tf_op jit(solution)/shard_map/ppermute | solution.py:113
  5.4 2.7 %collective-permute-start.3 = (bf16[16,3584]{1,0:T(8,128)(2,1)}, bf16[16,3584]{1,0:T(8,128)(2,1)}, u32[]{:S(2)}, u32[]{:S(2)}) collective-permute-start(bf16[16,3584]{1,0:T(8,128)(2,1)} %get-tuple-element.25), channel_id=1, source_target_pairs={{0,4},{1,5},{2,6},{3,7},{4,0},{5,1},{6,2},{7,3},{8,12},{9,13},{10,... | collective-permute-start | bytes 344072 | tf_op jit(solution)/shard_map/ppermute | solution.py:113
  10.1 1.6 %mul.89 = f32[32,32]{1,0:T(8,128)} reshape(f32[8,4,8,4]{3,2,1,0:T(8,128)} %broadcast_multiply_fusion) | data formatting | bytes 8192 | tf_op jit(solution)/shard_map/jit(kron)/mul | solution.py:126
  11.7 3.6 %collective-permute-start.5 = (bf16[16,3584]{1,0:T(8,128)(2,1)}, bf16[16,3584]{1,0:T(8,128)(2,1)S(1)}, u32[]{:S(2)}, u32[]{:S(2)}) collective-permute-start(bf16[16,3584]{1,0:T(8,128)(2,1)} %get-tuple-element.30), channel_id=1, source_target_pairs={{0,6},{1,7},{2,4},{3,5},{4,2},{5,3},{6,0},{7,1},{8,14},{9,15},{10,... | collective-permute-start | bytes 344072 | tf_op jit(solution)/shard_map/ppermute | solution.py:113
  20.6 3.9 %collective-permute-done.4 = bf16[16,3584]{1,0:T(8,128)(2,1)} collective-permute-done((bf16[16,3584]{1,0:T(8,128)(2,1)}, bf16[16,3584]{1,0:T(8,128)(2,1)}, u32[]{:S(2)}, u32[]{:S(2)}) %collective-permute-start.4) | collective-permute-done | bytes 114720 | tf_op jit(solution)/shard_map/ppermute | solution.py:113
  27.8 3.5 %fusion.4 = bf16[16,32,896]{2,1,0:T(8,128)(2,1)S(1)} fusion(f32[16,32,896]{2,0,1:T(8,128)} %bitcast.210, f32[32,32]{1,0:T(8,128)S(1)} %copy-done.3), kind=kOutput, calls=%fused_computation.7 | convolution fusion | flops 177078272 | bytes 2756608 | tf_op jit(solution)/shard_map/rbm,bc->rcm/dot_general | solution.py:127
  33.8 3.8 %collective-permute-start.8 = (bf16[16,3584]{1,0:T(8,128)(2,1)S(1)}, bf16[16,3584]{1,0:T(8,128)(2,1)S(1)}, u32[]{:S(2)}, u32[]{:S(2)}) collective-permute-start(bf16[16,3584]{1,0:T(8,128)(2,1)S(1)} %bitcast.223), channel_id=1, source_target_pairs={{0,2},{1,3},{2,0},{3,1},{4,6},{5,7},{6,4},{7,5},{8,10},{9,11},{10,... | collective-permute-start | bytes 344072 | tf_op jit(solution)/shard_map/ppermute | solution.py:134
  37.8 3.1 %collective-permute-start.10 = (bf16[16,3584]{1,0:T(8,128)(2,1)S(1)}, bf16[16,3584]{1,0:T(8,128)(2,1)S(1)}, u32[]{:S(2)}, u32[]{:S(2)}) collective-permute-start(bf16[16,3584]{1,0:T(8,128)(2,1)S(1)} %bitcast.220), channel_id=1, source_target_pairs={{0,4},{1,5},{2,6},{3,7},{4,0},{5,1},{6,2},{7,3},{8,12},{9,13},{10,... | collective-permute-start | bytes 344072 | tf_op jit(solution)/shard_map/ppermute | solution.py:134
  41.5 2.1 %collective-permute-start.12 = (bf16[16,3584]{1,0:T(8,128)(2,1)S(1)}, bf16[16,3584]{1,0:T(8,128)(2,1)S(1)}, u32[]{:S(2)}, u32[]{:S(2)}) collective-permute-start(bf16[16,3584]{1,0:T(8,128)(2,1)S(1)} %bitcast.222), channel_id=1, source_target_pairs={{0,6},{1,7},{2,4},{3,5},{4,2},{5,3},{6,0},{7,1},{8,14},{9,15},{10,... | collective-permute-start | bytes 344072 | tf_op jit(solution)/shard_map/ppermute | solution.py:134
  44.9 2.7 %collective-permute-done.9 = bf16[16,3584]{1,0:T(8,128)(2,1)S(1)} collective-permute-done((bf16[16,3584]{1,0:T(8,128)(2,1)S(1)}, bf16[16,3584]{1,0:T(8,128)(2,1)S(1)}, u32[]{:S(2)}, u32[]{:S(2)}) %collective-permute-start.9) | collective-permute-done | bytes 114720 | tf_op jit(solution)/shard_map/ppermute | solution.py:134
  47.6 9.0 %collective-permute-done.11 = bf16[16,3584]{1,0:T(8,128)(2,1)S(1)} collective-permute-done((bf16[16,3584]{1,0:T(8,128)(2,1)S(1)}, bf16[16,3584]{1,0:T(8,128)(2,1)S(1)}, u32[]{:S(2)}, u32[]{:S(2)}) %collective-permute-start.11) | collective-permute-done | bytes 114720 | tf_op jit(solution)/shard_map/ppermute | solution.py:134
  59.9 7.5 %fusion.62 = f32[128,2048]{1,0:T(8,128)S(1)} fusion(bf16[128,3584]{1,0:T(8,128)(2,1)S(1)} %constant_dynamic-update-slice_fusion, bf16[3584,2048]{1,0:T(8,128)(2,1)} %param.6), kind=kOutput, calls=%fused_computation.144 | convolution fusion | flops 1879048192 | bytes 16646144 | tf_op jit(solution)/shard_map/dot_general | solution.py:169
  68.5 11.5 %collective-permute-done.15 = bf16[128,3584]{1,0:T(8,128)(2,1)S(1)} collective-permute-done((bf16[128,3584]{1,0:T(8,128)(2,1)S(1)}, bf16[128,3584]{1,0:T(8,128)(2,1)S(1)}, u32[]{:S(2)}, u32[]{:S(2)}) %collective-permute-start.15) | collective-permute-done | bytes 917536 | tf_op jit(solution)/shard_map/ppermute | solution.py:147
  80.0 2.3 %fusion.63 = f32[128,2048]{1,0:T(8,128)S(1)} fusion(bf16[128,3584]{1,0:T(8,128)(2,1)S(1)} %collective-permute-done.15, bf16[3584,2048]{1,0:T(8,128)(2,1)S(1)} %bitcast.201), kind=kOutput, calls=%fused_computation.145 | convolution fusion | flops 1879048192 | bytes 16646144 | tf_op jit(solution)/shard_map/dot_general | solution.py:169
  82.6 1.6 %collective-permute-start.20 = (bf16[64,3584]{1,0:T(8,128)(2,1)S(1)}, bf16[64,3584]{1,0:T(8,128)(2,1)S(1)}, u32[]{:S(2)}, u32[]{:S(2)}) collective-permute-start(bf16[64,3584]{1,0:T(8,128)(2,1)S(1)} %slice.82), channel_id=1, source_target_pairs={{0,16},{8,24},{16,0},{24,8},{1,17},{9,25},{17,1},{25,9},{2,18},{10... | collective-permute-start | bytes 1376264 | tf_op jit(solution)/shard_map/ppermute | solution.py:150
  84.2 1.6 %collective-permute-start.19 = (bf16[64,3584]{1,0:T(8,128)(2,1)S(1)}, bf16[64,3584]{1,0:T(8,128)(2,1)S(1)}, u32[]{:S(2)}, u32[]{:S(2)}) collective-permute-start(bf16[64,3584]{1,0:T(8,128)(2,1)S(1)} %slice.81), channel_id=1, source_target_pairs={{0,8},{8,0},{16,24},{24,16},{1,9},{9,1},{17,25},{25,17},{2,10},{10... | collective-permute-start | bytes 1376264 | tf_op jit(solution)/shard_map/ppermute | solution.py:149
  85.9 2.1 %fusion.64 = f32[128,2048]{1,0:T(8,128)S(1)} fusion(bf16[128,3584]{1,0:T(8,128)(2,1)S(1)} %collective-permute-done.18, bf16[3584,2048]{1,0:T(8,128)(2,1)S(1)} %bitcast.201), kind=kOutput, calls=%fused_computation.146 | convolution fusion | flops 1879048192 | bytes 16646144 | tf_op jit(solution)/shard_map/dot_general | solution.py:155
  87.9 7.5 %collective-permute-done.20 = bf16[64,3584]{1,0:T(8,128)(2,1)S(1)} collective-permute-done((bf16[64,3584]{1,0:T(8,128)(2,1)S(1)}, bf16[64,3584]{1,0:T(8,128)(2,1)S(1)}, u32[]{:S(2)}, u32[]{:S(2)}) %collective-permute-start.20) | collective-permute-done | bytes 458784 | tf_op jit(solution)/shard_map/ppermute | solution.py:150
  96.8 2.1 %fusion.20 = f32[128,2048]{1,0:T(8,128)S(1)} fusion(bf16[3584,2048]{1,0:T(8,128)(2,1)S(1)} %bitcast.201, bf16[64,3584]{1,0:T(8,128)(2,1)S(1)} %collective-permute-done.20, bf16[64,3584]{1,0:T(8,128)(2,1)S(1)} %collective-permute-done.19), kind=kOutput, calls=%fused_computation.33 | convolution fusion | flops 1880883200 | bytes 16646144 | tf_op jit(solution)/shard_map/dot_general | solution.py:155
  99.3 5.0 %collective-permute-start.17 = (f32[64,2048]{1,0:T(8,128)S(1)}, f32[64,2048]{1,0:T(8,128)S(1)}, u32[]{:S(2)}, u32[]{:S(2)}) collective-permute-start(f32[64,2048]{1,0:T(8,128)S(1)} %fusion.25), channel_id=1, source_target_pairs={{0,2},{1,3},{2,0},{3,1},{4,6},{5,7},{6,4},{7,5},{8,10},{9,11},{10,... | collective-permute-start | bytes 1572872 | tf_op jit(solution)/shard_map/ppermute | solution.py:166
  104.6 2.4 %collective-permute-start.22 = (f32[64,512]{1,0:T(8,128)S(1)}, f32[64,512]{1,0:T(8,128)S(1)}, u32[]{:S(2)}, u32[]{:S(2)}) collective-permute-start(f32[64,512]{1,0:T(8,128)S(1)} %dynamic-slice_bitcast_fusion.5), channel_id=1, source_target_pairs={{0,2},{1,3},{2,0},{3,1},{4,6},{5,7},{6,4},{7,5},{8,10},{9,11},{10,... | collective-permute-start | bytes 393224 | tf_op jit(solution)/shard_map/ppermute | solution.py:166
  107.0 10.1 %collective-permute-done.17 = f32[64,2048]{1,0:T(8,128)S(1)} collective-permute-done((f32[64,2048]{1,0:T(8,128)S(1)}, f32[64,2048]{1,0:T(8,128)S(1)}, u32[]{:S(2)}, u32[]{:S(2)}) %collective-permute-start.17) | collective-permute-done | bytes 524320 | tf_op jit(solution)/shard_map/ppermute | solution.py:166
  117.2 2.5 %collective-permute-done.22 = f32[64,512]{1,0:T(8,128)S(1)} collective-permute-done((f32[64,512]{1,0:T(8,128)S(1)}, f32[64,512]{1,0:T(8,128)S(1)}, u32[]{:S(2)}, u32[]{:S(2)}) %collective-permute-start.22) | collective-permute-done | bytes 131104 | tf_op jit(solution)/shard_map/ppermute | solution.py:166
  119.7 1.8 %collective-permute-start.24 = (f32[64,512]{1,0:T(8,128)S(1)}, f32[64,512]{1,0:T(8,128)S(1)}, u32[]{:S(2)}, u32[]{:S(2)}) collective-permute-start(f32[64,512]{1,0:T(8,128)S(1)} %dynamic-slice_bitcast_fusion.4), channel_id=1, source_target_pairs={{0,2},{1,3},{2,0},{3,1},{4,6},{5,7},{6,4},{7,5},{8,10},{9,11},{10,... | collective-permute-start | bytes 393224 | tf_op jit(solution)/shard_map/ppermute | solution.py:166
  122.6 3.8 %collective-permute-done.24 = f32[64,512]{1,0:T(8,128)S(1)} collective-permute-done((f32[64,512]{1,0:T(8,128)S(1)}, f32[64,512]{1,0:T(8,128)S(1)}, u32[]{:S(2)}, u32[]{:S(2)}) %collective-permute-start.24) | collective-permute-done | bytes 131104 | tf_op jit(solution)/shard_map/ppermute | solution.py:166
  126.5 1.6 %collective-permute-start.26 = (f32[64,512]{1,0:T(8,128)S(1)}, f32[64,512]{1,0:T(8,128)S(1)}, u32[]{:S(2)}, u32[]{:S(2)}) collective-permute-start(f32[64,512]{1,0:T(8,128)S(1)} %dynamic-slice_bitcast_fusion.3), channel_id=1, source_target_pairs={{0,2},{1,3},{2,0},{3,1},{4,6},{5,7},{6,4},{7,5},{8,10},{9,11},{10,... | collective-permute-start | bytes 393224 | tf_op jit(solution)/shard_map/ppermute | solution.py:166
  130.4 1.8 %collective-permute-done.26 = f32[64,512]{1,0:T(8,128)S(1)} collective-permute-done((f32[64,512]{1,0:T(8,128)S(1)}, f32[64,512]{1,0:T(8,128)S(1)}, u32[]{:S(2)}, u32[]{:S(2)}) %collective-permute-start.26) | collective-permute-done | bytes 131104 | tf_op jit(solution)/shard_map/ppermute | solution.py:166
  135.9 1.9 %collective-permute-done.28 = f32[64,512]{1,0:T(8,128)S(1)} collective-permute-done((f32[64,512]{1,0:T(8,128)S(1)}, f32[64,512]{1,0:T(8,128)S(1)}, u32[]{:S(2)}, u32[]{:S(2)}) %collective-permute-start.28) | collective-permute-done | bytes 131104 | tf_op jit(solution)/shard_map/ppermute | solution.py:166
  137.9 2.1 %collective-permute-start.29 = (f32[64,512]{1,0:T(8,128)S(1)}, f32[64,512]{1,0:T(8,128)S(1)}, u32[]{:S(2)}, u32[]{:S(2)}) collective-permute-start(f32[64,512]{1,0:T(8,128)S(1)} %fusion.33), channel_id=1, source_target_pairs={{0,4},{1,5},{2,6},{3,7},{4,0},{5,1},{6,2},{7,3},{8,12},{9,13},{10,... | collective-permute-start | bytes 393224 | tf_op jit(solution)/shard_map/ppermute | solution.py:190
  140.1 4.8 %collective-permute-done.27 = f32[64,512]{1,0:T(8,128)S(1)} collective-permute-done((f32[64,512]{1,0:T(8,128)S(1)}, f32[64,512]{1,0:T(8,128)S(1)}, u32[]{:S(2)}, u32[]{:S(2)}) %collective-permute-start.27) | collective-permute-done | bytes 131104 | tf_op jit(solution)/shard_map/ppermute | solution.py:190
  144.9 2.2 %collective-permute-done.29 = f32[64,512]{1,0:T(8,128)S(1)} collective-permute-done((f32[64,512]{1,0:T(8,128)S(1)}, f32[64,512]{1,0:T(8,128)S(1)}, u32[]{:S(2)}, u32[]{:S(2)}) %collective-permute-start.29) | collective-permute-done | bytes 131104 | tf_op jit(solution)/shard_map/ppermute | solution.py:190
  (112 shorter events, 30.1 us)
Async XLA Ops:
  2.3 9.5 %collective-permute-start = (bf16[16,3584]{1,0:T(8,128)(2,1)}, bf16[16,3584]{1,0:T(8,128)(2,1)}, u32[]{:S(2)}, u32[]{:S(2)}) collective-permute-start(bf16[16,3584]{1,0:T(8,128)(2,1)} %get-tuple-element.28), channel_id=1, source_target_pairs={{0,1},{1,0},{2,3},{3,2},{4,5},{5,4},{6,7},{7,6},{8,9},{9,8},{10,11... | collective-permute-start | bytes 344072 | tf_op jit(solution)/shard_map/ppermute | solution.py:113
  2.7 13.9 %collective-permute-start.1 = (bf16[16,3584]{1,0:T(8,128)(2,1)}, bf16[16,3584]{1,0:T(8,128)(2,1)}, u32[]{:S(2)}, u32[]{:S(2)}) collective-permute-start(bf16[16,3584]{1,0:T(8,128)(2,1)} %get-tuple-element.27), channel_id=1, source_target_pairs={{0,2},{1,3},{2,0},{3,1},{4,6},{5,7},{6,4},{7,5},{8,10},{9,11},{10,... | collective-permute-start | bytes 344072 | tf_op jit(solution)/shard_map/ppermute | solution.py:113
  5.4 12.7 %collective-permute-start.2 = (bf16[16,3584]{1,0:T(8,128)(2,1)}, bf16[16,3584]{1,0:T(8,128)(2,1)}, u32[]{:S(2)}, u32[]{:S(2)}) collective-permute-start(bf16[16,3584]{1,0:T(8,128)(2,1)} %get-tuple-element.26), channel_id=1, source_target_pairs={{0,3},{1,2},{2,1},{3,0},{4,7},{5,6},{6,5},{7,4},{8,11},{9,10},{10,... | collective-permute-start | bytes 344072 | tf_op jit(solution)/shard_map/ppermute | solution.py:113
  5.4 13.8 %collective-permute-start.3 = (bf16[16,3584]{1,0:T(8,128)(2,1)}, bf16[16,3584]{1,0:T(8,128)(2,1)}, u32[]{:S(2)}, u32[]{:S(2)}) collective-permute-start(bf16[16,3584]{1,0:T(8,128)(2,1)} %get-tuple-element.25), channel_id=1, source_target_pairs={{0,4},{1,5},{2,6},{3,7},{4,0},{5,1},{6,2},{7,3},{8,12},{9,13},{10,... | collective-permute-start | bytes 344072 | tf_op jit(solution)/shard_map/ppermute | solution.py:113
  8.2 16.3 %collective-permute-start.4 = (bf16[16,3584]{1,0:T(8,128)(2,1)}, bf16[16,3584]{1,0:T(8,128)(2,1)}, u32[]{:S(2)}, u32[]{:S(2)}) collective-permute-start(bf16[16,3584]{1,0:T(8,128)(2,1)} %get-tuple-element.24), channel_id=1, source_target_pairs={{0,5},{1,4},{2,7},{3,6},{4,1},{5,0},{6,3},{7,2},{8,13},{9,12},{10,... | collective-permute-start | bytes 344072 | tf_op jit(solution)/shard_map/ppermute | solution.py:113
  11.7 14.0 %collective-permute-start.5 = (bf16[16,3584]{1,0:T(8,128)(2,1)}, bf16[16,3584]{1,0:T(8,128)(2,1)S(1)}, u32[]{:S(2)}, u32[]{:S(2)}) collective-permute-start(bf16[16,3584]{1,0:T(8,128)(2,1)} %get-tuple-element.30), channel_id=1, source_target_pairs={{0,6},{1,7},{2,4},{3,5},{4,2},{5,3},{6,0},{7,1},{8,14},{9,15},{10,... | collective-permute-start | bytes 344072 | tf_op jit(solution)/shard_map/ppermute | solution.py:113
  16.6 9.5 %collective-permute-start.6 = (bf16[16,3584]{1,0:T(8,128)(2,1)S(1)}, bf16[16,3584]{1,0:T(8,128)(2,1)S(1)}, u32[]{:S(2)}, u32[]{:S(2)}) collective-permute-start(bf16[16,3584]{1,0:T(8,128)(2,1)S(1)} %copy-done.2), channel_id=1, source_target_pairs={{0,7},{1,6},{2,5},{3,4},{4,3},{5,2},{6,1},{7,0},{8,15},{9,14},{10,... | collective-permute-start | bytes 344072 | tf_op jit(solution)/shard_map/ppermute | solution.py:113
  33.4 8.0 %collective-permute-start.7 = (bf16[16,3584]{1,0:T(8,128)(2,1)S(1)}, bf16[16,3584]{1,0:T(8,128)(2,1)S(1)}, u32[]{:S(2)}, u32[]{:S(2)}) collective-permute-start(bf16[16,3584]{1,0:T(8,128)(2,1)S(1)} %bitcast.224), channel_id=1, source_target_pairs={{0,1},{1,0},{2,3},{3,2},{4,5},{5,4},{6,7},{7,6},{8,9},{9,8},{10,11... | collective-permute-start | bytes 344072 | tf_op jit(solution)/shard_map/ppermute | solution.py:134
  33.8 9.8 %collective-permute-start.8 = (bf16[16,3584]{1,0:T(8,128)(2,1)S(1)}, bf16[16,3584]{1,0:T(8,128)(2,1)S(1)}, u32[]{:S(2)}, u32[]{:S(2)}) collective-permute-start(bf16[16,3584]{1,0:T(8,128)(2,1)S(1)} %bitcast.223), channel_id=1, source_target_pairs={{0,2},{1,3},{2,0},{3,1},{4,6},{5,7},{6,4},{7,5},{8,10},{9,11},{10,... | collective-permute-start | bytes 344072 | tf_op jit(solution)/shard_map/ppermute | solution.py:134
  37.6 10.0 %collective-permute-start.9 = (bf16[16,3584]{1,0:T(8,128)(2,1)S(1)}, bf16[16,3584]{1,0:T(8,128)(2,1)S(1)}, u32[]{:S(2)}, u32[]{:S(2)}) collective-permute-start(bf16[16,3584]{1,0:T(8,128)(2,1)S(1)} %bitcast.221), channel_id=1, source_target_pairs={{0,3},{1,2},{2,1},{3,0},{4,7},{5,6},{6,5},{7,4},{8,11},{9,10},{10,... | collective-permute-start | bytes 344072 | tf_op jit(solution)/shard_map/ppermute | solution.py:134
  37.8 9.8 %collective-permute-start.10 = (bf16[16,3584]{1,0:T(8,128)(2,1)S(1)}, bf16[16,3584]{1,0:T(8,128)(2,1)S(1)}, u32[]{:S(2)}, u32[]{:S(2)}) collective-permute-start(bf16[16,3584]{1,0:T(8,128)(2,1)S(1)} %bitcast.220), channel_id=1, source_target_pairs={{0,4},{1,5},{2,6},{3,7},{4,0},{5,1},{6,2},{7,3},{8,12},{9,13},{10,... | collective-permute-start | bytes 344072 | tf_op jit(solution)/shard_map/ppermute | solution.py:134
  41.0 15.7 %collective-permute-start.11 = (bf16[16,3584]{1,0:T(8,128)(2,1)S(1)}, bf16[16,3584]{1,0:T(8,128)(2,1)S(1)}, u32[]{:S(2)}, u32[]{:S(2)}) collective-permute-start(bf16[16,3584]{1,0:T(8,128)(2,1)S(1)} %bitcast.219), channel_id=1, source_target_pairs={{0,5},{1,4},{2,7},{3,6},{4,1},{5,0},{6,3},{7,2},{8,13},{9,12},{10,... | collective-permute-start | bytes 344072 | tf_op jit(solution)/shard_map/ppermute | solution.py:134
  41.3 38.7 %slice-start = ((s8[14680064]{0:T(1024)(128)(4,1)}), s8[4194304]{0:T(1024)(128)(4,1)S(1)}, s32[]{:S(2)}) async-start(s8[14680064]{0:T(1024)(128)(4,1)} %bitcast.200), calls=%async_computation | async-start | bytes 8388608
  41.5 15.2 %collective-permute-start.12 = (bf16[16,3584]{1,0:T(8,128)(2,1)S(1)}, bf16[16,3584]{1,0:T(8,128)(2,1)S(1)}, u32[]{:S(2)}, u32[]{:S(2)}) collective-permute-start(bf16[16,3584]{1,0:T(8,128)(2,1)S(1)} %bitcast.222), channel_id=1, source_target_pairs={{0,6},{1,7},{2,4},{3,5},{4,2},{5,3},{6,0},{7,1},{8,14},{9,15},{10,... | collective-permute-start | bytes 344072 | tf_op jit(solution)/shard_map/ppermute | solution.py:134
  43.7 13.1 %collective-permute-start.13 = (bf16[16,3584]{1,0:T(8,128)(2,1)S(1)}, bf16[16,3584]{1,0:T(8,128)(2,1)S(1)}, u32[]{:S(2)}, u32[]{:S(2)}) collective-permute-start(bf16[16,3584]{1,0:T(8,128)(2,1)S(1)} %bitcast.218), channel_id=1, source_target_pairs={{0,7},{1,6},{2,5},{3,4},{4,3},{5,2},{6,1},{7,0},{8,15},{9,14},{10,... | collective-permute-start | bytes 344072 | tf_op jit(solution)/shard_map/ppermute | solution.py:134
  56.7 23.3 %slice-start.1 = ((s8[14680064]{0:T(1024)(128)(4,1)}), s8[4194304]{0:T(1024)(128)(4,1)S(1)}, s32[]{:S(2)}) async-start(s8[14680064]{0:T(1024)(128)(4,1)} %bitcast.200), calls=%async_computation.1 | async-start | bytes 8388608
  56.8 23.2 %collective-permute-start.15 = (bf16[128,3584]{1,0:T(8,128)(2,1)S(1)}, bf16[128,3584]{1,0:T(8,128)(2,1)S(1)}, u32[]{:S(2)}, u32[]{:S(2)}) collective-permute-start(bf16[128,3584]{1,0:T(8,128)(2,1)S(1)} %constant_dynamic-update-slice_fusion), channel_id=1, source_target_pairs={{0,8},{8,0},{16,24},{24,16},{1,9},{9,1},{17,25},{25,17},{2,10},{10... | collective-permute-start | bytes 2752520 | tf_op jit(solution)/shard_map/ppermute | solution.py:147
  58.3 25.9 %collective-permute-start.18 = (bf16[128,3584]{1,0:T(8,128)(2,1)S(1)}, bf16[128,3584]{1,0:T(8,128)(2,1)S(1)}, u32[]{:S(2)}, u32[]{:S(2)}) collective-permute-start(bf16[128,3584]{1,0:T(8,128)(2,1)S(1)} %constant_dynamic-update-slice_fusion), channel_id=1, source_target_pairs={{0,16},{8,24},{16,0},{24,8},{1,17},{9,25},{17,1},{25,9},{2,18},{10... | collective-permute-start | bytes 2752520 | tf_op jit(solution)/shard_map/ppermute | solution.py:148
  67.4 31.6 %collective-permute-start.14 = (f32[64,2048]{1,0:T(8,128)S(1)}, f32[64,2048]{1,0:T(8,128)S(1)}, u32[]{:S(2)}, u32[]{:S(2)}) collective-permute-start(f32[64,2048]{1,0:T(8,128)S(1)} %dynamic-slice_bitcast_fusion.1), channel_id=1, source_target_pairs={{0,1},{1,0},{2,3},{3,2},{4,5},{5,4},{6,7},{7,6},{8,9},{9,8},{10,11... | collective-permute-start | bytes 1572872 | tf_op jit(solution)/shard_map/ppermute | solution.py:173
  82.4 16.8 %collective-permute-start.16 = (f32[64,2048]{1,0:T(8,128)S(1)}, f32[64,2048]{1,0:T(8,128)S(1)}, u32[]{:S(2)}, u32[]{:S(2)}) collective-permute-start(f32[64,2048]{1,0:T(8,128)S(1)} %dynamic-slice_bitcast_fusion), channel_id=1, source_target_pairs={{0,1},{1,0},{2,3},{3,2},{4,5},{5,4},{6,7},{7,6},{8,9},{9,8},{10,11... | collective-permute-start | bytes 1572872 | tf_op jit(solution)/shard_map/ppermute | solution.py:173
  82.6 12.8 %collective-permute-start.20 = (bf16[64,3584]{1,0:T(8,128)(2,1)S(1)}, bf16[64,3584]{1,0:T(8,128)(2,1)S(1)}, u32[]{:S(2)}, u32[]{:S(2)}) collective-permute-start(bf16[64,3584]{1,0:T(8,128)(2,1)S(1)} %slice.82), channel_id=1, source_target_pairs={{0,16},{8,24},{16,0},{24,8},{1,17},{9,25},{17,1},{25,9},{2,18},{10... | collective-permute-start | bytes 1376264 | tf_op jit(solution)/shard_map/ppermute | solution.py:150
  84.2 12.5 %collective-permute-start.19 = (bf16[64,3584]{1,0:T(8,128)(2,1)S(1)}, bf16[64,3584]{1,0:T(8,128)(2,1)S(1)}, u32[]{:S(2)}, u32[]{:S(2)}) collective-permute-start(bf16[64,3584]{1,0:T(8,128)(2,1)S(1)} %slice.81), channel_id=1, source_target_pairs={{0,8},{8,0},{16,24},{24,16},{1,9},{9,1},{17,25},{25,17},{2,10},{10... | collective-permute-start | bytes 1376264 | tf_op jit(solution)/shard_map/ppermute | solution.py:149
  98.9 5.4 %collective-permute-start.21 = (f32[2,64,2048]{2,1,0:T(8,128)S(1)}, f32[2,64,2048]{2,1,0:T(8,128)S(1)}, u32[]{:S(2)}, u32[]{:S(2)}) collective-permute-start(f32[2,64,2048]{2,1,0:T(8,128)S(1)} %fusion.16), channel_id=1, source_target_pairs={{0,1},{1,0},{2,3},{3,2},{4,5},{5,4},{6,7},{7,6},{8,9},{9,8},{10,11... | collective-permute-start | bytes 3145736 | tf_op jit(solution)/shard_map/ppermute | solution.py:160
  99.3 17.8 %collective-permute-start.17 = (f32[64,2048]{1,0:T(8,128)S(1)}, f32[64,2048]{1,0:T(8,128)S(1)}, u32[]{:S(2)}, u32[]{:S(2)}) collective-permute-start(f32[64,2048]{1,0:T(8,128)S(1)} %fusion.25), channel_id=1, source_target_pairs={{0,2},{1,3},{2,0},{3,1},{4,6},{5,7},{6,4},{7,5},{8,10},{9,11},{10,... | collective-permute-start | bytes 1572872 | tf_op jit(solution)/shard_map/ppermute | solution.py:166
  104.6 15.1 %collective-permute-start.22 = (f32[64,512]{1,0:T(8,128)S(1)}, f32[64,512]{1,0:T(8,128)S(1)}, u32[]{:S(2)}, u32[]{:S(2)}) collective-permute-start(f32[64,512]{1,0:T(8,128)S(1)} %dynamic-slice_bitcast_fusion.5), channel_id=1, source_target_pairs={{0,2},{1,3},{2,0},{3,1},{4,6},{5,7},{6,4},{7,5},{8,10},{9,11},{10,... | collective-permute-start | bytes 393224 | tf_op jit(solution)/shard_map/ppermute | solution.py:166
  119.7 6.7 %collective-permute-start.24 = (f32[64,512]{1,0:T(8,128)S(1)}, f32[64,512]{1,0:T(8,128)S(1)}, u32[]{:S(2)}, u32[]{:S(2)}) collective-permute-start(f32[64,512]{1,0:T(8,128)S(1)} %dynamic-slice_bitcast_fusion.4), channel_id=1, source_target_pairs={{0,2},{1,3},{2,0},{3,1},{4,6},{5,7},{6,4},{7,5},{8,10},{9,11},{10,... | collective-permute-start | bytes 393224 | tf_op jit(solution)/shard_map/ppermute | solution.py:166
  121.6 8.7 %collective-permute-start.23 = (f32[64,512]{1,0:T(8,128)S(1)}, f32[64,512]{1,0:T(8,128)S(1)}, u32[]{:S(2)}, u32[]{:S(2)}) collective-permute-start(f32[64,512]{1,0:T(8,128)S(1)} %fusion.48), channel_id=1, source_target_pairs={{0,4},{1,5},{2,6},{3,7},{4,0},{5,1},{6,2},{7,3},{8,12},{9,13},{10,... | collective-permute-start | bytes 393224 | tf_op jit(solution)/shard_map/ppermute | solution.py:190
  126.5 5.8 %collective-permute-start.26 = (f32[64,512]{1,0:T(8,128)S(1)}, f32[64,512]{1,0:T(8,128)S(1)}, u32[]{:S(2)}, u32[]{:S(2)}) collective-permute-start(f32[64,512]{1,0:T(8,128)S(1)} %dynamic-slice_bitcast_fusion.3), channel_id=1, source_target_pairs={{0,2},{1,3},{2,0},{3,1},{4,6},{5,7},{6,4},{7,5},{8,10},{9,11},{10,... | collective-permute-start | bytes 393224 | tf_op jit(solution)/shard_map/ppermute | solution.py:166
  128.1 7.8 %collective-permute-start.25 = (f32[64,512]{1,0:T(8,128)S(1)}, f32[64,512]{1,0:T(8,128)S(1)}, u32[]{:S(2)}, u32[]{:S(2)}) collective-permute-start(f32[64,512]{1,0:T(8,128)S(1)} %fusion.43), channel_id=1, source_target_pairs={{0,4},{1,5},{2,6},{3,7},{4,0},{5,1},{6,2},{7,3},{8,12},{9,13},{10,... | collective-permute-start | bytes 393224 | tf_op jit(solution)/shard_map/ppermute | solution.py:190
  132.3 5.6 %collective-permute-start.28 = (f32[64,512]{1,0:T(8,128)S(1)}, f32[64,512]{1,0:T(8,128)S(1)}, u32[]{:S(2)}, u32[]{:S(2)}) collective-permute-start(f32[64,512]{1,0:T(8,128)S(1)} %dynamic-slice_bitcast_fusion.2), channel_id=1, source_target_pairs={{0,2},{1,3},{2,0},{3,1},{4,6},{5,7},{6,4},{7,5},{8,10},{9,11},{10,... | collective-permute-start | bytes 393224 | tf_op jit(solution)/shard_map/ppermute | solution.py:166
  133.8 11.0 %collective-permute-start.27 = (f32[64,512]{1,0:T(8,128)S(1)}, f32[64,512]{1,0:T(8,128)S(1)}, u32[]{:S(2)}, u32[]{:S(2)}) collective-permute-start(f32[64,512]{1,0:T(8,128)S(1)} %fusion.38), channel_id=1, source_target_pairs={{0,4},{1,5},{2,6},{3,7},{4,0},{5,1},{6,2},{7,3},{8,12},{9,13},{10,... | collective-permute-start | bytes 393224 | tf_op jit(solution)/shard_map/ppermute | solution.py:190
  137.9 9.2 %collective-permute-start.29 = (f32[64,512]{1,0:T(8,128)S(1)}, f32[64,512]{1,0:T(8,128)S(1)}, u32[]{:S(2)}, u32[]{:S(2)}) collective-permute-start(f32[64,512]{1,0:T(8,128)S(1)} %fusion.33), channel_id=1, source_target_pairs={{0,4},{1,5},{2,6},{3,7},{4,0},{5,1},{6,2},{7,3},{8,12},{9,13},{10,... | collective-permute-start | bytes 393224 | tf_op jit(solution)/shard_map/ppermute | solution.py:190
  (7 other events, 82.8 us)

commit v17 on v16

--- a/solution.py
+++ b/solution.py
@@ -173,7 +173,7 @@
         return keep + lax.ppermute(send, "tp", tp_pairs(1))
 
     near = second_halving(jnp.stack([first_halving_one(block), first_halving_one(across_x)]))
-    far_summed = first_halving((across_y, diagonal))
+    far_summed = jnp.stack([first_halving_one(across_y), first_halving_one(diagonal)])
     columns = near.shape[-1]
     width = columns // TAIL_PIECES
     chosen = here // 2 % 2 ^ high

time: 148 us -> 164 us (1.11)
  waiting for transfers between devices: 65.7 us -> 76.6 us
  matrix products: 24.9 us -> 29.8 us
    ppermute x1, waiting for transfers between devices: 0.01 us -> 19.1 us  [product_and_reduce(): across_y = lax.ppermute(block, 'seq', seq_pairs(2))]
    ppermute x1, waiting for transfers between devices: 11.5 us -> 0.01 us  [product_and_reduce(): across_x = lax.ppermute(block, 'seq', seq_pairs(1))]
    dot_general x2 -> x4, matrix products: 9.78 us -> 18.8 us  [first_halving_one(): product = jnp.dot(piece, down_weight, preferred_element_type=jnp.float32)]
    ppermute x1, waiting for transfers between devices: 1.32 us -> 7.57 us  [product_and_reduce(): first = lax.ppermute(across_y[:half], 'seq', seq_pairs(1))]
    ppermute x1, waiting for transfers between devices: 7.53 us -> 1.31 us  [product_and_reduce(): second = lax.ppermute(across_x[half:], 'seq', seq_pairs(2))]
    dot_general x2 -> x0, matrix products: 4.12 us -> none  [first_halving(): jnp.dot(piece, down_weight, preferred_element_type=jnp.float32)]
    ppermute x5, starting transfers between devices: 12.3 us -> 9.61 us  [second_halving(): return keep + lax.ppermute(send, 'tp', tp_pairs(2))]
    ppermute x5, waiting for transfers between devices: 20.2 us -> 22.4 us  [second_halving(): return keep + lax.ppermute(send, 'tp', tp_pairs(2))]
  transfers between devices with their start and end apart: 30 -> 31, of which waited for: 15 -> 14; matrix products, arithmetic and copies ran while one was open for 17% -> 14% of each run, Pallas kernels for 0% -> 0%
where the time goes in v17:
time: 164 us; the launch traced here: 163 us
  waiting for transfers between devices  76.6 us (47%)
  starting transfers between devices  44.3 us (27%)
  matrix products  29.8 us (18%)
  local copies, waits for them, and re-layouts  8.78 us (5%)
  other arithmetic  3.19 us (2%)
    ppermute x5, waiting for transfers between devices, second_halving(): return keep + lax.ppermute(send, 'tp', tp_pairs(2))  22.4 us
    ppermute x1, waiting for transfers between devices, product_and_reduce(): across_y = lax.ppermute(block, 'seq', seq_pairs(2))  19.1 us
    dot_general x4, matrix products, first_halving_one(): product = jnp.dot(piece, down_weight, preferred_element_type=jnp.float32)  18.8 us
    ppermute x7, waiting for transfers between devices, spread_rotate_return(): block = lax.ppermute(block, 'tp', pairs(distance))  11.7 us
    ppermute x7, starting transfers between devices, spread_rotate_return(): block = lax.ppermute(block, 'tp', pairs(distance))  11.2 us
    ppermute x4, waiting for transfers between devices, product_and_reduce(): results.append(keep + lax.ppermute(send, 'tp', tp_pairs(4)))  10.6 us
    ppermute x7, starting transfers between devices, spread_rotate_return(): send = lax.ppermute(send, 'tp', pairs(distance))  9.65 us
    ppermute x5, starting transfers between devices, second_halving(): return keep + lax.ppermute(send, 'tp', tp_pairs(2))  9.61 us
  transfers between devices with their start and end apart: 31, of which 14 were waited for; matrix products, arithmetic and copies ran while one was open for 14% of the time, Pallas kernels for 0%

profile of v17, /device:TPU:0, one launch (start us, length us, event | category | flops | bytes accessed | tf_op | source)
XLA Modules:
  0.0 163.3 jit_solution(7273673469075964745)
XLA Ops:
  0.0 2.3 %constant_dynamic-slice_fusion = (bf16[16,3584]{1,0:T(8,128)(2,1)}, bf16[16,3584]{1,0:T(8,128)(2,1)}, bf16[16,3584]{1,0:T(8,128)(2,1)}, bf16[16,3584]{1,0:T(8,12...) fusion(bf16[128,3584]{1,0:T(8,128)(2,1)} %param.5, ...), kind=kLoop, calls=%fused_computation.132 | loop fusion | bytes 1835040 | tf_op jit(solution)/shard_map/dynamic_slice | solution.py:111
  2.7 2.6 %collective-permute-start.1 = (bf16[16,3584]{1,0:T(8,128)(2,1)}, bf16[16,3584]{1,0:T(8,128)(2,1)}, u32[]{:S(2)}, u32[]{:S(2)}) collective-permute-start(bf16[16,3584]{1,0:T(8,128)(2,1)} %get-tuple-element.27), channel_id=1, source_target_pairs={{0,2},{1,3},{2,0},{3,1},{4,6},{5,7},{6,4},{7,5},{8,10},{9,11},{10,... | collective-permute-start | bytes 344072 | tf_op jit(solution)/shard_map/ppermute | solution.py:113
  5.5 2.7 %collective-permute-start.3 = (bf16[16,3584]{1,0:T(8,128)(2,1)}, bf16[16,3584]{1,0:T(8,128)(2,1)}, u32[]{:S(2)}, u32[]{:S(2)}) collective-permute-start(bf16[16,3584]{1,0:T(8,128)(2,1)} %get-tuple-element.25), channel_id=1, source_target_pairs={{0,4},{1,5},{2,6},{3,7},{4,0},{5,1},{6,2},{7,3},{8,12},{9,13},{10,... | collective-permute-start | bytes 344072 | tf_op jit(solution)/shard_map/ppermute | solution.py:113
  10.1 1.6 mul.89
  11.7 3.6 %collective-permute-start.5 = (bf16[16,3584]{1,0:T(8,128)(2,1)}, bf16[16,3584]{1,0:T(8,128)(2,1)S(1)}, u32[]{:S(2)}, u32[]{:S(2)}) collective-permute-start(bf16[16,3584]{1,0:T(8,128)(2,1)} %get-tuple-element.30), channel_id=1, source_target_pairs={{0,6},{1,7},{2,4},{3,5},{4,2},{5,3},{6,0},{7,1},{8,14},{9,15},{10,... | collective-permute-start | bytes 344072 | tf_op jit(solution)/shard_map/ppermute | solution.py:113
  20.6 3.8 %collective-permute-done.4 = bf16[16,3584]{1,0:T(8,128)(2,1)} collective-permute-done((bf16[16,3584]{1,0:T(8,128)(2,1)}, bf16[16,3584]{1,0:T(8,128)(2,1)}, u32[]{:S(2)}, u32[]{:S(2)}) %collective-permute-start.4) | collective-permute-done | bytes 114720 | tf_op jit(solution)/shard_map/ppermute | solution.py:113
  27.8 3.5 %fusion.4 = bf16[16,32,896]{2,1,0:T(8,128)(2,1)S(1)} fusion(f32[16,32,896]{2,0,1:T(8,128)} %bitcast.220, f32[32,32]{1,0:T(8,128)S(1)} %copy-done.3), kind=kOutput, calls=%fused_computation.9 | convolution fusion | flops 177078272 | bytes 2756608 | tf_op jit(solution)/shard_map/rbm,bc->rcm/dot_general | solution.py:127
  31.9 1.7 %fusion.60 = (bf16[16,1,3584]{2,1,0:T(2,128)(2,1)S(1)}, bf16[16,1,3584]{2,1,0:T(2,128)(2,1)S(1)}, bf16[16,1,3584]{2,1,0:T(2,128)(2,1)S(1)}, bf16[16,1,3584]{2,1,...) fusion(bf16[16,8,3584]{2,1,0:T(8,128)(2,1)S(1)} %reshape.116), kind=kLoop, calls=%fused_computation.149 | loop fusion | bytes 1835008 | tf_op jit(solution)/shard_map/slice | solution.py:132
  33.9 3.8 %collective-permute-start.8 = (bf16[16,3584]{1,0:T(8,128)(2,1)S(1)}, bf16[16,3584]{1,0:T(8,128)(2,1)S(1)}, u32[]{:S(2)}, u32[]{:S(2)}) collective-permute-start(bf16[16,3584]{1,0:T(8,128)(2,1)S(1)} %bitcast.233), channel_id=1, source_target_pairs={{0,2},{1,3},{2,0},{3,1},{4,6},{5,7},{6,4},{7,5},{8,10},{9,11},{10,... | collective-permute-start | bytes 344072 | tf_op jit(solution)/shard_map/ppermute | solution.py:134
  37.9 3.1 %collective-permute-start.10 = (bf16[16,3584]{1,0:T(8,128)(2,1)S(1)}, bf16[16,3584]{1,0:T(8,128)(2,1)S(1)}, u32[]{:S(2)}, u32[]{:S(2)}) collective-permute-start(bf16[16,3584]{1,0:T(8,128)(2,1)S(1)} %bitcast.230), channel_id=1, source_target_pairs={{0,4},{1,5},{2,6},{3,7},{4,0},{5,1},{6,2},{7,3},{8,12},{9,13},{10,... | collective-permute-start | bytes 344072 | tf_op jit(solution)/shard_map/ppermute | solution.py:134
  41.6 2.1 %collective-permute-start.12 = (bf16[16,3584]{1,0:T(8,128)(2,1)S(1)}, bf16[16,3584]{1,0:T(8,128)(2,1)S(1)}, u32[]{:S(2)}, u32[]{:S(2)}) collective-permute-start(bf16[16,3584]{1,0:T(8,128)(2,1)S(1)} %bitcast.232), channel_id=1, source_target_pairs={{0,6},{1,7},{2,4},{3,5},{4,2},{5,3},{6,0},{7,1},{8,14},{9,15},{10,... | collective-permute-start | bytes 344072 | tf_op jit(solution)/shard_map/ppermute | solution.py:134
  45.0 2.7 %collective-permute-done.9 = bf16[16,3584]{1,0:T(8,128)(2,1)S(1)} collective-permute-done((bf16[16,3584]{1,0:T(8,128)(2,1)S(1)}, bf16[16,3584]{1,0:T(8,128)(2,1)S(1)}, u32[]{:S(2)}, u32[]{:S(2)}) %collective-permute-start.9) | collective-permute-done | bytes 114720 | tf_op jit(solution)/shard_map/ppermute | solution.py:134
  47.8 9.0 %collective-permute-done.11 = bf16[16,3584]{1,0:T(8,128)(2,1)S(1)} collective-permute-done((bf16[16,3584]{1,0:T(8,128)(2,1)S(1)}, bf16[16,3584]{1,0:T(8,128)(2,1)S(1)}, u32[]{:S(2)}, u32[]{:S(2)}) %collective-permute-start.11) | collective-permute-done | bytes 114720 | tf_op jit(solution)/shard_map/ppermute | solution.py:134
  56.9 7.2 %fusion.61 = f32[128,2048]{1,0:T(8,128)S(1)} fusion(bf16[128,3584]{1,0:T(8,128)(2,1)S(1)} %constant_dynamic-update-slice_fusion, bf16[3584,2048]{1,0:T(8,128)(2,1)} %param.6), kind=kOutput, calls=%fused_computation.150 | convolution fusion | flops 1879048192 | bytes 16646144 | tf_op jit(solution)/shard_map/dot_general | solution.py:169
  69.1 19.1 %collective-permute-done.18 = bf16[128,3584]{1,0:T(8,128)(2,1)S(1)} collective-permute-done((bf16[128,3584]{1,0:T(8,128)(2,1)S(1)}, bf16[128,3584]{1,0:T(8,128)(2,1)S(1)}, u32[]{:S(2)}, u32[]{:S(2)}) %collective-permute-start.18) | collective-permute-done | bytes 917536 | tf_op jit(solution)/shard_map/ppermute | solution.py:148
  88.2 7.4 %fusion.63 = f32[128,2048]{1,0:T(8,128)S(1)} fusion(bf16[128,3584]{1,0:T(8,128)(2,1)S(1)} %collective-permute-done.18, bf16[3584,2048]{1,0:T(8,128)(2,1)} %param.6), kind=kOutput, calls=%fused_computation.152 | convolution fusion | flops 1879048192 | bytes 16646144 | tf_op jit(solution)/shard_map/dot_general | solution.py:169
  95.8 1.6 collective-permute-start.20
  97.4 1.6 collective-permute-start.21
  99.0 2.1 %fusion.62 = f32[128,2048]{1,0:T(8,128)S(1)} fusion(bf16[128,3584]{1,0:T(8,128)(2,1)S(1)} %collective-permute-done.15, bf16[3584,2048]{1,0:T(8,128)(2,1)S(1)} %bitcast.211), kind=kOutput, calls=%fused_computation.151 | convolution fusion | flops 1879048192 | bytes 16646144 | tf_op jit(solution)/shard_map/dot_general | solution.py:169
  101.2 7.6 %collective-permute-done.20 = bf16[64,3584]{1,0:T(8,128)(2,1)S(1)} collective-permute-done((bf16[64,3584]{1,0:T(8,128)(2,1)S(1)}, bf16[64,3584]{1,0:T(8,128)(2,1)S(1)}, u32[]{:S(2)}, u32[]{:S(2)}) %collective-permute-start.20) | collective-permute-done | bytes 458784 | tf_op jit(solution)/shard_map/ppermute | solution.py:149
  110.1 2.1 %fusion.15 = f32[128,2048]{1,0:T(8,128)S(1)} fusion(bf16[3584,2048]{1,0:T(8,128)(2,1)S(1)} %bitcast.211, bf16[64,3584]{1,0:T(8,128)(2,1)S(1)} %collective-permute-done.21, bf16[64,3584]{1,0:T(8,128)(2,1)S(1)} %collective-permute-done.20), kind=kOutput, calls=%fused_computation.30 | convolution fusion | flops 1880883200 | bytes 16646144 | tf_op jit(solution)/shard_map/dot_general | solution.py:169
  112.5 5.0 %collective-permute-start.17 = (f32[64,2048]{1,0:T(8,128)S(1)}, f32[64,2048]{1,0:T(8,128)S(1)}, u32[]{:S(2)}, u32[]{:S(2)}) collective-permute-start(f32[64,2048]{1,0:T(8,128)S(1)} %fusion.20), channel_id=1, source_target_pairs={{0,2},{1,3},{2,0},{3,1},{4,6},{5,7},{6,4},{7,5},{8,10},{9,11},{10,... | collective-permute-start | bytes 1572872 | tf_op jit(solution)/shard_map/ppermute | solution.py:166
  117.8 1.6 collective-permute-start.23
  119.4 10.9 %collective-permute-done.17 = f32[64,2048]{1,0:T(8,128)S(1)} collective-permute-done((f32[64,2048]{1,0:T(8,128)S(1)}, f32[64,2048]{1,0:T(8,128)S(1)}, u32[]{:S(2)}, u32[]{:S(2)}) %collective-permute-start.17) | collective-permute-done | bytes 524320 | tf_op jit(solution)/shard_map/ppermute | solution.py:166
  130.4 2.5 %collective-permute-done.23 = f32[64,512]{1,0:T(8,128)S(1)} collective-permute-done((f32[64,512]{1,0:T(8,128)S(1)}, f32[64,512]{1,0:T(8,128)S(1)}, u32[]{:S(2)}, u32[]{:S(2)}) %collective-permute-start.23) | collective-permute-done | bytes 131104 | tf_op jit(solution)/shard_map/ppermute | solution.py:166
  132.9 1.8 %collective-permute-start.25 = (f32[64,512]{1,0:T(8,128)S(1)}, f32[64,512]{1,0:T(8,128)S(1)}, u32[]{:S(2)}, u32[]{:S(2)}) collective-permute-start(f32[64,512]{1,0:T(8,128)S(1)} %dynamic-slice_bitcast_fusion.6), channel_id=1, source_target_pairs={{0,2},{1,3},{2,0},{3,1},{4,6},{5,7},{6,4},{7,5},{8,10},{9,11},{10,... | collective-permute-start | bytes 393224 | tf_op jit(solution)/shard_map/ppermute | solution.py:166
  135.7 3.8 %collective-permute-done.25 = f32[64,512]{1,0:T(8,128)S(1)} collective-permute-done((f32[64,512]{1,0:T(8,128)S(1)}, f32[64,512]{1,0:T(8,128)S(1)}, u32[]{:S(2)}, u32[]{:S(2)}) %collective-permute-start.25) | collective-permute-done | bytes 131104 | tf_op jit(solution)/shard_map/ppermute | solution.py:166
  139.6 2.2 %collective-permute-start.26 = (f32[64,512]{1,0:T(8,128)S(1)}, f32[64,512]{1,0:T(8,128)S(1)}, u32[]{:S(2)}, u32[]{:S(2)}) collective-permute-start(f32[64,512]{1,0:T(8,128)S(1)} %fusion.43), channel_id=1, source_target_pairs={{0,4},{1,5},{2,6},{3,7},{4,0},{5,1},{6,2},{7,3},{8,12},{9,13},{10,... | collective-permute-start | bytes 393224 | tf_op jit(solution)/shard_map/ppermute | solution.py:190
  142.1 4.9 %collective-permute-done.24 = f32[64,512]{1,0:T(8,128)S(1)} collective-permute-done((f32[64,512]{1,0:T(8,128)S(1)}, f32[64,512]{1,0:T(8,128)S(1)}, u32[]{:S(2)}, u32[]{:S(2)}) %collective-permute-start.24) | collective-permute-done | bytes 131104 | tf_op jit(solution)/shard_map/ppermute | solution.py:190
  151.4 3.7 %collective-permute-done.29 = f32[64,512]{1,0:T(8,128)S(1)} collective-permute-done((f32[64,512]{1,0:T(8,128)S(1)}, f32[64,512]{1,0:T(8,128)S(1)}, u32[]{:S(2)}, u32[]{:S(2)}) %collective-permute-start.29) | collective-permute-done | bytes 131104 | tf_op jit(solution)/shard_map/ppermute | solution.py:166
  155.2 3.0 %collective-permute-start.30 = (f32[64,512]{1,0:T(8,128)S(1)}, f32[64,512]{1,0:T(8,128)S(1)}, u32[]{:S(2)}, u32[]{:S(2)}) collective-permute-start(f32[64,512]{1,0:T(8,128)S(1)} %fusion.33), channel_id=1, source_target_pairs={{0,4},{1,5},{2,6},{3,7},{4,0},{5,1},{6,2},{7,3},{8,12},{9,13},{10,... | collective-permute-start | bytes 393224 | tf_op jit(solution)/shard_map/ppermute | solution.py:190
  158.2 4.3 %collective-permute-done.30 = f32[64,512]{1,0:T(8,128)S(1)} collective-permute-done((f32[64,512]{1,0:T(8,128)S(1)}, f32[64,512]{1,0:T(8,128)S(1)}, u32[]{:S(2)}, u32[]{:S(2)}) %collective-permute-start.30) | collective-permute-done | bytes 131104 | tf_op jit(solution)/shard_map/ppermute | solution.py:190
  (116 shorter events, 27.8 us)
Async XLA Ops:
  2.3 9.4 %collective-permute-start = (bf16[16,3584]{1,0:T(8,128)(2,1)}, bf16[16,3584]{1,0:T(8,128)(2,1)}, u32[]{:S(2)}, u32[]{:S(2)}) collective-permute-start(bf16[16,3584]{1,0:T(8,128)(2,1)} %get-tuple-element.28), channel_id=1, source_target_pairs={{0,1},{1,0},{2,3},{3,2},{4,5},{5,4},{6,7},{7,6},{8,9},{9,8},{10,11... | collective-permute-start | bytes 344072 | tf_op jit(solution)/shard_map/ppermute | solution.py:113
  2.7 13.9 %collective-permute-start.1 = (bf16[16,3584]{1,0:T(8,128)(2,1)}, bf16[16,3584]{1,0:T(8,128)(2,1)}, u32[]{:S(2)}, u32[]{:S(2)}) collective-permute-start(bf16[16,3584]{1,0:T(8,128)(2,1)} %get-tuple-element.27), channel_id=1, source_target_pairs={{0,2},{1,3},{2,0},{3,1},{4,6},{5,7},{6,4},{7,5},{8,10},{9,11},{10,... | collective-permute-start | bytes 344072 | tf_op jit(solution)/shard_map/ppermute | solution.py:113
  5.4 12.7 %collective-permute-start.2 = (bf16[16,3584]{1,0:T(8,128)(2,1)}, bf16[16,3584]{1,0:T(8,128)(2,1)}, u32[]{:S(2)}, u32[]{:S(2)}) collective-permute-start(bf16[16,3584]{1,0:T(8,128)(2,1)} %get-tuple-element.26), channel_id=1, source_target_pairs={{0,3},{1,2},{2,1},{3,0},{4,7},{5,6},{6,5},{7,4},{8,11},{9,10},{10,... | collective-permute-start | bytes 344072 | tf_op jit(solution)/shard_map/ppermute | solution.py:113
  5.5 13.9 %collective-permute-start.3 = (bf16[16,3584]{1,0:T(8,128)(2,1)}, bf16[16,3584]{1,0:T(8,128)(2,1)}, u32[]{:S(2)}, u32[]{:S(2)}) collective-permute-start(bf16[16,3584]{1,0:T(8,128)(2,1)} %get-tuple-element.25), channel_id=1, source_target_pairs={{0,4},{1,5},{2,6},{3,7},{4,0},{5,1},{6,2},{7,3},{8,12},{9,13},{10,... | collective-permute-start | bytes 344072 | tf_op jit(solution)/shard_map/ppermute | solution.py:113
  8.2 16.3 %collective-permute-start.4 = (bf16[16,3584]{1,0:T(8,128)(2,1)}, bf16[16,3584]{1,0:T(8,128)(2,1)}, u32[]{:S(2)}, u32[]{:S(2)}) collective-permute-start(bf16[16,3584]{1,0:T(8,128)(2,1)} %get-tuple-element.24), channel_id=1, source_target_pairs={{0,5},{1,4},{2,7},{3,6},{4,1},{5,0},{6,3},{7,2},{8,13},{9,12},{10,... | collective-permute-start | bytes 344072 | tf_op jit(solution)/shard_map/ppermute | solution.py:113
  11.7 14.0 %collective-permute-start.5 = (bf16[16,3584]{1,0:T(8,128)(2,1)}, bf16[16,3584]{1,0:T(8,128)(2,1)S(1)}, u32[]{:S(2)}, u32[]{:S(2)}) collective-permute-start(bf16[16,3584]{1,0:T(8,128)(2,1)} %get-tuple-element.30), channel_id=1, source_target_pairs={{0,6},{1,7},{2,4},{3,5},{4,2},{5,3},{6,0},{7,1},{8,14},{9,15},{10,... | collective-permute-start | bytes 344072 | tf_op jit(solution)/shard_map/ppermute | solution.py:113
  16.6 9.5 %collective-permute-start.6 = (bf16[16,3584]{1,0:T(8,128)(2,1)S(1)}, bf16[16,3584]{1,0:T(8,128)(2,1)S(1)}, u32[]{:S(2)}, u32[]{:S(2)}) collective-permute-start(bf16[16,3584]{1,0:T(8,128)(2,1)S(1)} %copy-done.2), channel_id=1, source_target_pairs={{0,7},{1,6},{2,5},{3,4},{4,3},{5,2},{6,1},{7,0},{8,15},{9,14},{10,... | collective-permute-start | bytes 344072 | tf_op jit(solution)/shard_map/ppermute | solution.py:113
  33.6 8.0 %collective-permute-start.7 = (bf16[16,3584]{1,0:T(8,128)(2,1)S(1)}, bf16[16,3584]{1,0:T(8,128)(2,1)S(1)}, u32[]{:S(2)}, u32[]{:S(2)}) collective-permute-start(bf16[16,3584]{1,0:T(8,128)(2,1)S(1)} %bitcast.234), channel_id=1, source_target_pairs={{0,1},{1,0},{2,3},{3,2},{4,5},{5,4},{6,7},{7,6},{8,9},{9,8},{10,11... | collective-permute-start | bytes 344072 | tf_op jit(solution)/shard_map/ppermute | solution.py:134
  33.9 9.8 %collective-permute-start.8 = (bf16[16,3584]{1,0:T(8,128)(2,1)S(1)}, bf16[16,3584]{1,0:T(8,128)(2,1)S(1)}, u32[]{:S(2)}, u32[]{:S(2)}) collective-permute-start(bf16[16,3584]{1,0:T(8,128)(2,1)S(1)} %bitcast.233), channel_id=1, source_target_pairs={{0,2},{1,3},{2,0},{3,1},{4,6},{5,7},{6,4},{7,5},{8,10},{9,11},{10,... | collective-permute-start | bytes 344072 | tf_op jit(solution)/shard_map/ppermute | solution.py:134
  37.7 10.0 %collective-permute-start.9 = (bf16[16,3584]{1,0:T(8,128)(2,1)S(1)}, bf16[16,3584]{1,0:T(8,128)(2,1)S(1)}, u32[]{:S(2)}, u32[]{:S(2)}) collective-permute-start(bf16[16,3584]{1,0:T(8,128)(2,1)S(1)} %bitcast.231), channel_id=1, source_target_pairs={{0,3},{1,2},{2,1},{3,0},{4,7},{5,6},{6,5},{7,4},{8,11},{9,10},{10,... | collective-permute-start | bytes 344072 | tf_op jit(solution)/shard_map/ppermute | solution.py:134
  37.9 9.8 %collective-permute-start.10 = (bf16[16,3584]{1,0:T(8,128)(2,1)S(1)}, bf16[16,3584]{1,0:T(8,128)(2,1)S(1)}, u32[]{:S(2)}, u32[]{:S(2)}) collective-permute-start(bf16[16,3584]{1,0:T(8,128)(2,1)S(1)} %bitcast.230), channel_id=1, source_target_pairs={{0,4},{1,5},{2,6},{3,7},{4,0},{5,1},{6,2},{7,3},{8,12},{9,13},{10,... | collective-permute-start | bytes 344072 | tf_op jit(solution)/shard_map/ppermute | solution.py:134
  41.1 15.7 %collective-permute-start.11 = (bf16[16,3584]{1,0:T(8,128)(2,1)S(1)}, bf16[16,3584]{1,0:T(8,128)(2,1)S(1)}, u32[]{:S(2)}, u32[]{:S(2)}) collective-permute-start(bf16[16,3584]{1,0:T(8,128)(2,1)S(1)} %bitcast.229), channel_id=1, source_target_pairs={{0,5},{1,4},{2,7},{3,6},{4,1},{5,0},{6,3},{7,2},{8,13},{9,12},{10,... | collective-permute-start | bytes 344072 | tf_op jit(solution)/shard_map/ppermute | solution.py:134
  41.6 15.2 %collective-permute-start.12 = (bf16[16,3584]{1,0:T(8,128)(2,1)S(1)}, bf16[16,3584]{1,0:T(8,128)(2,1)S(1)}, u32[]{:S(2)}, u32[]{:S(2)}) collective-permute-start(bf16[16,3584]{1,0:T(8,128)(2,1)S(1)} %bitcast.232), channel_id=1, source_target_pairs={{0,6},{1,7},{2,4},{3,5},{4,2},{5,3},{6,0},{7,1},{8,14},{9,15},{10,... | collective-permute-start | bytes 344072 | tf_op jit(solution)/shard_map/ppermute | solution.py:134
  43.8 13.1 %collective-permute-start.13 = (bf16[16,3584]{1,0:T(8,128)(2,1)S(1)}, bf16[16,3584]{1,0:T(8,128)(2,1)S(1)}, u32[]{:S(2)}, u32[]{:S(2)}) collective-permute-start(bf16[16,3584]{1,0:T(8,128)(2,1)S(1)} %bitcast.228), channel_id=1, source_target_pairs={{0,7},{1,6},{2,5},{3,4},{4,3},{5,2},{6,1},{7,0},{8,15},{9,14},{10,... | collective-permute-start | bytes 344072 | tf_op jit(solution)/shard_map/ppermute | solution.py:134
  65.0 4.0 %collective-permute-start.14 = (f32[64,2048]{1,0:T(8,128)}, f32[64,2048]{1,0:T(8,128)S(1)}, u32[]{:S(2)}, u32[]{:S(2)}) collective-permute-start(f32[64,2048]{1,0:T(8,128)} %dynamic-slice_bitcast_fusion.3), channel_id=1, source_target_pairs={{0,1},{1,0},{2,3},{3,2},{4,5},{5,4},{6,7},{7,6},{8,9},{9,8},{10,11... | collective-permute-start | bytes 1572872 | tf_op jit(solution)/shard_map/ppermute | solution.py:173
  65.9 22.3 %collective-permute-start.18 = (bf16[128,3584]{1,0:T(8,128)(2,1)S(1)}, bf16[128,3584]{1,0:T(8,128)(2,1)S(1)}, u32[]{:S(2)}, u32[]{:S(2)}) collective-permute-start(bf16[128,3584]{1,0:T(8,128)(2,1)S(1)} %constant_dynamic-update-slice_fusion), channel_id=1, source_target_pairs={{0,16},{8,24},{16,0},{24,8},{1,17},{9,25},{17,1},{25,9},{2,18},{10... | collective-permute-start | bytes 2752520 | tf_op jit(solution)/shard_map/ppermute | solution.py:148
  67.5 29.9 %collective-permute-start.15 = (bf16[128,3584]{1,0:T(8,128)(2,1)S(1)}, bf16[128,3584]{1,0:T(8,128)(2,1)S(1)}, u32[]{:S(2)}, u32[]{:S(2)}) collective-permute-start(bf16[128,3584]{1,0:T(8,128)(2,1)S(1)} %constant_dynamic-update-slice_fusion), channel_id=1, source_target_pairs={{0,8},{8,0},{16,24},{24,16},{1,9},{9,1},{17,25},{25,17},{2,10},{10... | collective-permute-start | bytes 2752520 | tf_op jit(solution)/shard_map/ppermute | solution.py:147
  69.0 30.0 %slice-start = ((s8[14680064]{0:T(1024)(128)(4,1)}), s8[4194304]{0:T(1024)(128)(4,1)S(1)}, s32[]{:S(2)}) async-start(s8[14680064]{0:T(1024)(128)(4,1)} %bitcast.210), calls=%async_computation | async-start | bytes 8388608
  95.7 21.8 %collective-permute-start.19 = (f32[64,2048]{1,0:T(8,128)S(1)}, f32[64,2048]{1,0:T(8,128)S(1)}, u32[]{:S(2)}, u32[]{:S(2)}) collective-permute-start(f32[64,2048]{1,0:T(8,128)S(1)} %dynamic-slice_bitcast_fusion.1), channel_id=1, source_target_pairs={{0,1},{1,0},{2,3},{3,2},{4,5},{5,4},{6,7},{7,6},{8,9},{9,8},{10,11... | collective-permute-start | bytes 1572872 | tf_op jit(solution)/shard_map/ppermute | solution.py:173
  95.8 13.0 %collective-permute-start.20 = (bf16[64,3584]{1,0:T(8,128)(2,1)S(1)}, bf16[64,3584]{1,0:T(8,128)(2,1)S(1)}, u32[]{:S(2)}, u32[]{:S(2)}) collective-permute-start(bf16[64,3584]{1,0:T(8,128)(2,1)S(1)} %slice.81), channel_id=1, source_target_pairs={{0,8},{8,0},{16,24},{24,16},{1,9},{9,1},{17,25},{25,17},{2,10},{10... | collective-permute-start | bytes 1376264 | tf_op jit(solution)/shard_map/ppermute | solution.py:149
  97.4 12.7 %collective-permute-start.21 = (bf16[64,3584]{1,0:T(8,128)(2,1)S(1)}, bf16[64,3584]{1,0:T(8,128)(2,1)S(1)}, u32[]{:S(2)}, u32[]{:S(2)}) collective-permute-start(bf16[64,3584]{1,0:T(8,128)(2,1)S(1)} %slice.82), channel_id=1, source_target_pairs={{0,16},{8,24},{16,0},{24,8},{1,17},{9,25},{17,1},{25,9},{2,18},{10... | collective-permute-start | bytes 1376264 | tf_op jit(solution)/shard_map/ppermute | solution.py:150
  101.1 11.2 %collective-permute-start.16 = (f32[64,2048]{1,0:T(8,128)S(1)}, f32[64,2048]{1,0:T(8,128)S(1)}, u32[]{:S(2)}, u32[]{:S(2)}) collective-permute-start(f32[64,2048]{1,0:T(8,128)S(1)} %dynamic-slice_bitcast_fusion.2), channel_id=1, source_target_pairs={{0,1},{1,0},{2,3},{3,2},{4,5},{5,4},{6,7},{7,6},{8,9},{9,8},{10,11... | collective-permute-start | bytes 1572872 | tf_op jit(solution)/shard_map/ppermute | solution.py:173
  112.2 5.3 %collective-permute-start.22 = (f32[64,2048]{1,0:T(8,128)S(1)}, f32[64,2048]{1,0:T(8,128)S(1)}, u32[]{:S(2)}, u32[]{:S(2)}) collective-permute-start(f32[64,2048]{1,0:T(8,128)S(1)} %dynamic-slice_bitcast_fusion), channel_id=1, source_target_pairs={{0,1},{1,0},{2,3},{3,2},{4,5},{5,4},{6,7},{7,6},{8,9},{9,8},{10,11... | collective-permute-start | bytes 1572872 | tf_op jit(solution)/shard_map/ppermute | solution.py:173
  112.5 17.8 %collective-permute-start.17 = (f32[64,2048]{1,0:T(8,128)S(1)}, f32[64,2048]{1,0:T(8,128)S(1)}, u32[]{:S(2)}, u32[]{:S(2)}) collective-permute-start(f32[64,2048]{1,0:T(8,128)S(1)} %fusion.20), channel_id=1, source_target_pairs={{0,2},{1,3},{2,0},{3,1},{4,6},{5,7},{6,4},{7,5},{8,10},{9,11},{10,... | collective-permute-start | bytes 1572872 | tf_op jit(solution)/shard_map/ppermute | solution.py:166
  117.8 15.1 %collective-permute-start.23 = (f32[64,512]{1,0:T(8,128)S(1)}, f32[64,512]{1,0:T(8,128)S(1)}, u32[]{:S(2)}, u32[]{:S(2)}) collective-permute-start(f32[64,512]{1,0:T(8,128)S(1)} %dynamic-slice_bitcast_fusion.7), channel_id=1, source_target_pairs={{0,2},{1,3},{2,0},{3,1},{4,6},{5,7},{6,4},{7,5},{8,10},{9,11},{10,... | collective-permute-start | bytes 393224 | tf_op jit(solution)/shard_map/ppermute | solution.py:166
  132.9 6.6 %collective-permute-start.25 = (f32[64,512]{1,0:T(8,128)S(1)}, f32[64,512]{1,0:T(8,128)S(1)}, u32[]{:S(2)}, u32[]{:S(2)}) collective-permute-start(f32[64,512]{1,0:T(8,128)S(1)} %dynamic-slice_bitcast_fusion.6), channel_id=1, source_target_pairs={{0,2},{1,3},{2,0},{3,1},{4,6},{5,7},{6,4},{7,5},{8,10},{9,11},{10,... | collective-permute-start | bytes 393224 | tf_op jit(solution)/shard_map/ppermute | solution.py:166
  134.8 12.2 %collective-permute-start.24 = (f32[64,512]{1,0:T(8,128)S(1)}, f32[64,512]{1,0:T(8,128)S(1)}, u32[]{:S(2)}, u32[]{:S(2)}) collective-permute-start(f32[64,512]{1,0:T(8,128)S(1)} %fusion.48), channel_id=1, source_target_pairs={{0,4},{1,5},{2,6},{3,7},{4,0},{5,1},{6,2},{7,3},{8,12},{9,13},{10,... | collective-permute-start | bytes 393224 | tf_op jit(solution)/shard_map/ppermute | solution.py:190
  139.6 11.8 %collective-permute-start.26 = (f32[64,512]{1,0:T(8,128)S(1)}, f32[64,512]{1,0:T(8,128)S(1)}, u32[]{:S(2)}, u32[]{:S(2)}) collective-permute-start(f32[64,512]{1,0:T(8,128)S(1)} %fusion.43), channel_id=1, source_target_pairs={{0,4},{1,5},{2,6},{3,7},{4,0},{5,1},{6,2},{7,3},{8,12},{9,13},{10,... | collective-permute-start | bytes 393224 | tf_op jit(solution)/shard_map/ppermute | solution.py:190
  141.8 6.8 %collective-permute-start.27 = (f32[64,512]{1,0:T(8,128)S(1)}, f32[64,512]{1,0:T(8,128)S(1)}, u32[]{:S(2)}, u32[]{:S(2)}) collective-permute-start(f32[64,512]{1,0:T(8,128)S(1)} %dynamic-slice_bitcast_fusion.5), channel_id=1, source_target_pairs={{0,2},{1,3},{2,0},{3,1},{4,6},{5,7},{6,4},{7,5},{8,10},{9,11},{10,... | collective-permute-start | bytes 393224 | tf_op jit(solution)/shard_map/ppermute | solution.py:166
  148.7 9.4 %collective-permute-start.28 = (f32[64,512]{1,0:T(8,128)S(1)}, f32[64,512]{1,0:T(8,128)S(1)}, u32[]{:S(2)}, u32[]{:S(2)}) collective-permute-start(f32[64,512]{1,0:T(8,128)S(1)} %fusion.38), channel_id=1, source_target_pairs={{0,4},{1,5},{2,6},{3,7},{4,0},{5,1},{6,2},{7,3},{8,12},{9,13},{10,... | collective-permute-start | bytes 393224 | tf_op jit(solution)/shard_map/ppermute | solution.py:190
  149.1 6.0 %collective-permute-start.29 = (f32[64,512]{1,0:T(8,128)S(1)}, f32[64,512]{1,0:T(8,128)S(1)}, u32[]{:S(2)}, u32[]{:S(2)}) collective-permute-start(f32[64,512]{1,0:T(8,128)S(1)} %dynamic-slice_bitcast_fusion.4), channel_id=1, source_target_pairs={{0,2},{1,3},{2,0},{3,1},{4,6},{5,7},{6,4},{7,5},{8,10},{9,11},{10,... | collective-permute-start | bytes 393224 | tf_op jit(solution)/shard_map/ppermute | solution.py:166
  155.2 7.3 %collective-permute-start.30 = (f32[64,512]{1,0:T(8,128)S(1)}, f32[64,512]{1,0:T(8,128)S(1)}, u32[]{:S(2)}, u32[]{:S(2)}) collective-permute-start(f32[64,512]{1,0:T(8,128)S(1)} %fusion.33), channel_id=1, source_target_pairs={{0,4},{1,5},{2,6},{3,7},{4,0},{5,1},{6,2},{7,3},{8,12},{9,13},{10,... | collective-permute-start | bytes 393224 | tf_op jit(solution)/shard_map/ppermute | solution.py:190
  (8 other events, 124.9 us)

commit v18 on v16

--- a/solution.py
+++ b/solution.py
@@ -9,7 +9,7 @@
 PALEY = 28
 INNER = 32
 CHUNKS = 1
-TAIL_PIECES = 4
+TAIL_PIECES = 2
 
 
 def paley_table():

time: 148 us -> 151 us (1.020)
  waiting for transfers between devices: 65.7 us -> 75.8 us
  starting transfers between devices: 45.6 us -> 38.6 us
    ppermute x5 -> x3, waiting for transfers between devices: 20.2 us -> 25.6 us  [second_halving(): return keep + lax.ppermute(send, 'tp', tp_pairs(2))]
    ppermute x4 -> x2, waiting for transfers between devices: 9.59 us -> 14 us  [product_and_reduce(): results.append(keep + lax.ppermute(send, 'tp', tp_pairs(4)))]
    ppermute x4 -> x2, starting transfers between devices: 4.86 us -> 1.06 us  [product_and_reduce(): results.append(keep + lax.ppermute(send, 'tp', tp_pairs(4)))]
    ppermute x5 -> x3, starting transfers between devices: 12.3 us -> 9.13 us  [second_halving(): return keep + lax.ppermute(send, 'tp', tp_pairs(2))]
  transfers between devices with their start and end apart: 30 -> 26, of which waited for: 15 -> 11; matrix products, arithmetic and copies ran while one was open for 17% -> 17% of each run, Pallas kernels for 0% -> 0%
where the time goes in v18:
time: 151 us
  waiting for transfers between devices  75.8 us (50%)
  starting transfers between devices  38.6 us (26%)
  matrix products  24.9 us (16%)
  local copies, waits for them, and re-layouts  7.83 us (5%)
  other arithmetic  3.17 us (2%)
    ppermute x3, waiting for transfers between devices, second_halving(): return keep + lax.ppermute(send, 'tp', tp_pairs(2))  25.6 us
    ppermute x2, waiting for transfers between devices, product_and_reduce(): results.append(keep + lax.ppermute(send, 'tp', tp_pairs(4)))  14 us
    ppermute x7, waiting for transfers between devices, spread_rotate_return(): block = lax.ppermute(block, 'tp', pairs(distance))  11.7 us
    ppermute x1, waiting for transfers between devices, product_and_reduce(): across_x = lax.ppermute(block, 'seq', seq_pairs(1))  11.6 us
    ppermute x7, starting transfers between devices, spread_rotate_return(): block = lax.ppermute(block, 'tp', pairs(distance))  11.2 us
    dot_general x2, matrix products, first_halving_one(): product = jnp.dot(piece, down_weight, preferred_element_type=jnp.float32)  9.78 us
    ppermute x7, starting transfers between devices, spread_rotate_return(): send = lax.ppermute(send, 'tp', pairs(distance))  9.65 us
    ppermute x3, starting transfers between devices, second_halving(): return keep + lax.ppermute(send, 'tp', tp_pairs(2))  9.13 us
  transfers between devices with their start and end apart: 26, of which 11 were waited for; matrix products, arithmetic and copies ran while one was open for 17% of the time, Pallas kernels for 0%

profile of v18, /device:TPU:0, one launch (start us, length us, event | category | flops | bytes accessed | tf_op | source)
XLA Modules:
  0.0 150.8 jit_solution(16607490786634180374)
XLA Ops:
  0.0 2.3 %constant_dynamic-slice_fusion = (bf16[16,3584]{1,0:T(8,128)(2,1)}, bf16[16,3584]{1,0:T(8,128)(2,1)}, bf16[16,3584]{1,0:T(8,128)(2,1)}, bf16[16,3584]{1,0:T(8,12...) fusion(bf16[128,3584]{1,0:T(8,128)(2,1)} %param.5, ...), kind=kLoop, calls=%fused_computation.101 | loop fusion | bytes 1835040 | tf_op jit(solution)/shard_map/dynamic_slice | solution.py:111
  2.8 2.6 %collective-permute-start.1 = (bf16[16,3584]{1,0:T(8,128)(2,1)}, bf16[16,3584]{1,0:T(8,128)(2,1)}, u32[]{:S(2)}, u32[]{:S(2)}) collective-permute-start(bf16[16,3584]{1,0:T(8,128)(2,1)} %get-tuple-element.21), channel_id=1, source_target_pairs={{0,2},{1,3},{2,0},{3,1},{4,6},{5,7},{6,4},{7,5},{8,10},{9,11},{10,... | collective-permute-start | bytes 344072 | tf_op jit(solution)/shard_map/ppermute | solution.py:113
  5.5 2.7 %collective-permute-start.3 = (bf16[16,3584]{1,0:T(8,128)(2,1)}, bf16[16,3584]{1,0:T(8,128)(2,1)}, u32[]{:S(2)}, u32[]{:S(2)}) collective-permute-start(bf16[16,3584]{1,0:T(8,128)(2,1)} %get-tuple-element.19), channel_id=1, source_target_pairs={{0,4},{1,5},{2,6},{3,7},{4,0},{5,1},{6,2},{7,3},{8,12},{9,13},{10,... | collective-permute-start | bytes 344072 | tf_op jit(solution)/shard_map/ppermute | solution.py:113
  8.7 1.5 broadcast_multiply_fusion
  10.1 1.6 %mul.89 = f32[32,32]{1,0:T(8,128)} reshape(f32[8,4,8,4]{3,2,1,0:T(8,128)} %broadcast_multiply_fusion) | data formatting | bytes 8192 | tf_op jit(solution)/shard_map/jit(kron)/mul | solution.py:126
  11.7 3.6 %collective-permute-start.5 = (bf16[16,3584]{1,0:T(8,128)(2,1)}, bf16[16,3584]{1,0:T(8,128)(2,1)S(1)}, u32[]{:S(2)}, u32[]{:S(2)}) collective-permute-start(bf16[16,3584]{1,0:T(8,128)(2,1)} %get-tuple-element.24), channel_id=1, source_target_pairs={{0,6},{1,7},{2,4},{3,5},{4,2},{5,3},{6,0},{7,1},{8,14},{9,15},{10,... | collective-permute-start | bytes 344072 | tf_op jit(solution)/shard_map/ppermute | solution.py:113
  20.6 3.8 %collective-permute-done.4 = bf16[16,3584]{1,0:T(8,128)(2,1)} collective-permute-done((bf16[16,3584]{1,0:T(8,128)(2,1)}, bf16[16,3584]{1,0:T(8,128)(2,1)}, u32[]{:S(2)}, u32[]{:S(2)}) %collective-permute-start.4) | collective-permute-done | bytes 114720 | tf_op jit(solution)/shard_map/ppermute | solution.py:113
  27.8 3.5 %fusion.4 = bf16[16,32,896]{2,1,0:T(8,128)(2,1)S(1)} fusion(f32[16,32,896]{2,0,1:T(8,128)} %bitcast.186, f32[32,32]{1,0:T(8,128)S(1)} %copy-done.3), kind=kOutput, calls=%fused_computation.7 | convolution fusion | flops 177078272 | bytes 2756608 | tf_op jit(solution)/shard_map/rbm,bc->rcm/dot_general | solution.py:127
  31.9 1.5 %fusion.51 = (bf16[16,1,3584]{2,1,0:T(2,128)(2,1)S(1)}, bf16[16,1,3584]{2,1,0:T(2,128)(2,1)S(1)}, bf16[16,1,3584]{2,1,0:T(2,128)(2,1)S(1)}, bf16[16,1,3584]{2,1,...) fusion(bf16[16,8,3584]{2,1,0:T(8,128)(2,1)S(1)} %reshape.115), kind=kLoop, calls=%fused_computation.119 | loop fusion | bytes 1835008 | tf_op jit(solution)/shard_map/slice | solution.py:132
  33.8 3.8 %collective-permute-start.8 = (bf16[16,3584]{1,0:T(8,128)(2,1)S(1)}, bf16[16,3584]{1,0:T(8,128)(2,1)S(1)}, u32[]{:S(2)}, u32[]{:S(2)}) collective-permute-start(bf16[16,3584]{1,0:T(8,128)(2,1)S(1)} %bitcast.193), channel_id=1, source_target_pairs={{0,2},{1,3},{2,0},{3,1},{4,6},{5,7},{6,4},{7,5},{8,10},{9,11},{10,... | collective-permute-start | bytes 344072 | tf_op jit(solution)/shard_map/ppermute | solution.py:134
  37.8 3.1 %collective-permute-start.10 = (bf16[16,3584]{1,0:T(8,128)(2,1)S(1)}, bf16[16,3584]{1,0:T(8,128)(2,1)S(1)}, u32[]{:S(2)}, u32[]{:S(2)}) collective-permute-start(bf16[16,3584]{1,0:T(8,128)(2,1)S(1)} %bitcast.190), channel_id=1, source_target_pairs={{0,4},{1,5},{2,6},{3,7},{4,0},{5,1},{6,2},{7,3},{8,12},{9,13},{10,... | collective-permute-start | bytes 344072 | tf_op jit(solution)/shard_map/ppermute | solution.py:134
  41.5 2.1 %collective-permute-start.12 = (bf16[16,3584]{1,0:T(8,128)(2,1)S(1)}, bf16[16,3584]{1,0:T(8,128)(2,1)S(1)}, u32[]{:S(2)}, u32[]{:S(2)}) collective-permute-start(bf16[16,3584]{1,0:T(8,128)(2,1)S(1)} %bitcast.192), channel_id=1, source_target_pairs={{0,6},{1,7},{2,4},{3,5},{4,2},{5,3},{6,0},{7,1},{8,14},{9,15},{10,... | collective-permute-start | bytes 344072 | tf_op jit(solution)/shard_map/ppermute | solution.py:134
  44.9 2.7 %collective-permute-done.9 = bf16[16,3584]{1,0:T(8,128)(2,1)S(1)} collective-permute-done((bf16[16,3584]{1,0:T(8,128)(2,1)S(1)}, bf16[16,3584]{1,0:T(8,128)(2,1)S(1)}, u32[]{:S(2)}, u32[]{:S(2)}) %collective-permute-start.9) | collective-permute-done | bytes 114720 | tf_op jit(solution)/shard_map/ppermute | solution.py:134
  47.6 9.0 %collective-permute-done.11 = bf16[16,3584]{1,0:T(8,128)(2,1)S(1)} collective-permute-done((bf16[16,3584]{1,0:T(8,128)(2,1)S(1)}, bf16[16,3584]{1,0:T(8,128)(2,1)S(1)}, u32[]{:S(2)}, u32[]{:S(2)}) %collective-permute-start.11) | collective-permute-done | bytes 114720 | tf_op jit(solution)/shard_map/ppermute | solution.py:134
  56.8 1.6 %collective-permute-start.15 = (bf16[128,3584]{1,0:T(8,128)(2,1)S(1)}, bf16[128,3584]{1,0:T(8,128)(2,1)S(1)}, u32[]{:S(2)}, u32[]{:S(2)}) collective-permute-start(bf16[128,3584]{1,0:T(8,128)(2,1)S(1)} %constant_dynamic-update-slice_fusion), channel_id=1, source_target_pairs={{0,8},{8,0},{16,24},{24,16},{1,9},{9,1},{17,25},{25,17},{2,10},{10... | collective-permute-start | bytes 2752520 | tf_op jit(solution)/shard_map/ppermute | solution.py:147
  58.3 1.5 %collective-permute-start.18 = (bf16[128,3584]{1,0:T(8,128)(2,1)S(1)}, bf16[128,3584]{1,0:T(8,128)(2,1)S(1)}, u32[]{:S(2)}, u32[]{:S(2)}) collective-permute-start(bf16[128,3584]{1,0:T(8,128)(2,1)S(1)} %constant_dynamic-update-slice_fusion), channel_id=1, source_target_pairs={{0,16},{8,24},{16,0},{24,8},{1,17},{9,25},{17,1},{25,9},{2,18},{10... | collective-permute-start | bytes 2752520 | tf_op jit(solution)/shard_map/ppermute | solution.py:148
  59.8 7.5 %fusion.52 = f32[128,2048]{1,0:T(8,128)S(1)} fusion(bf16[128,3584]{1,0:T(8,128)(2,1)S(1)} %constant_dynamic-update-slice_fusion, bf16[3584,2048]{1,0:T(8,128)(2,1)} %param.6), kind=kOutput, calls=%fused_computation.120 | convolution fusion | flops 1879048192 | bytes 16646144 | tf_op jit(solution)/shard_map/dot_general | solution.py:169
  68.4 11.6 %collective-permute-done.15 = bf16[128,3584]{1,0:T(8,128)(2,1)S(1)} collective-permute-done((bf16[128,3584]{1,0:T(8,128)(2,1)S(1)}, bf16[128,3584]{1,0:T(8,128)(2,1)S(1)}, u32[]{:S(2)}, u32[]{:S(2)}) %collective-permute-start.15) | collective-permute-done | bytes 917536 | tf_op jit(solution)/shard_map/ppermute | solution.py:147
  80.1 2.3 %fusion.53 = f32[128,2048]{1,0:T(8,128)S(1)} fusion(bf16[128,3584]{1,0:T(8,128)(2,1)S(1)} %collective-permute-done.15, bf16[3584,2048]{1,0:T(8,128)(2,1)S(1)} %bitcast.175), kind=kOutput, calls=%fused_computation.121 | convolution fusion | flops 1879048192 | bytes 16646144 | tf_op jit(solution)/shard_map/dot_general | solution.py:169
  82.6 1.6 %collective-permute-start.20 = (bf16[64,3584]{1,0:T(8,128)(2,1)S(1)}, bf16[64,3584]{1,0:T(8,128)(2,1)S(1)}, u32[]{:S(2)}, u32[]{:S(2)}) collective-permute-start(bf16[64,3584]{1,0:T(8,128)(2,1)S(1)} %slice.66), channel_id=1, source_target_pairs={{0,16},{8,24},{16,0},{24,8},{1,17},{9,25},{17,1},{25,9},{2,18},{10... | collective-permute-start | bytes 1376264 | tf_op jit(solution)/shard_map/ppermute | solution.py:150
  84.3 1.6 %collective-permute-start.19 = (bf16[64,3584]{1,0:T(8,128)(2,1)S(1)}, bf16[64,3584]{1,0:T(8,128)(2,1)S(1)}, u32[]{:S(2)}, u32[]{:S(2)}) collective-permute-start(bf16[64,3584]{1,0:T(8,128)(2,1)S(1)} %slice.65), channel_id=1, source_target_pairs={{0,8},{8,0},{16,24},{24,16},{1,9},{9,1},{17,25},{25,17},{2,10},{10... | collective-permute-start | bytes 1376264 | tf_op jit(solution)/shard_map/ppermute | solution.py:149
  85.8 2.1 %fusion.54 = f32[128,2048]{1,0:T(8,128)S(1)} fusion(bf16[128,3584]{1,0:T(8,128)(2,1)S(1)} %collective-permute-done.18, bf16[3584,2048]{1,0:T(8,128)(2,1)S(1)} %bitcast.175), kind=kOutput, calls=%fused_computation.122 | convolution fusion | flops 1879048192 | bytes 16646144 | tf_op jit(solution)/shard_map/dot_general | solution.py:155
  87.9 7.6 %collective-permute-done.20 = bf16[64,3584]{1,0:T(8,128)(2,1)S(1)} collective-permute-done((bf16[64,3584]{1,0:T(8,128)(2,1)S(1)}, bf16[64,3584]{1,0:T(8,128)(2,1)S(1)}, u32[]{:S(2)}, u32[]{:S(2)}) %collective-permute-start.20) | collective-permute-done | bytes 458784 | tf_op jit(solution)/shard_map/ppermute | solution.py:150
  96.8 2.1 %fusion.20 = f32[128,2048]{1,0:T(8,128)S(1)} fusion(bf16[3584,2048]{1,0:T(8,128)(2,1)S(1)} %bitcast.175, bf16[64,3584]{1,0:T(8,128)(2,1)S(1)} %collective-permute-done.20, bf16[64,3584]{1,0:T(8,128)(2,1)S(1)} %collective-permute-done.19), kind=kOutput, calls=%fused_computation.33 | convolution fusion | flops 1880883200 | bytes 16646144 | tf_op jit(solution)/shard_map/dot_general | solution.py:155
  99.3 5.0 %collective-permute-start.17 = (f32[64,2048]{1,0:T(8,128)S(1)}, f32[64,2048]{1,0:T(8,128)S(1)}, u32[]{:S(2)}, u32[]{:S(2)}) collective-permute-start(f32[64,2048]{1,0:T(8,128)S(1)} %fusion.25), channel_id=1, source_target_pairs={{0,2},{1,3},{2,0},{3,1},{4,6},{5,7},{6,4},{7,5},{8,10},{9,11},{10,... | collective-permute-start | bytes 1572872 | tf_op jit(solution)/shard_map/ppermute | solution.py:166
  104.6 2.4 %collective-permute-start.22 = (f32[64,1024]{1,0:T(8,128)S(1)}, f32[64,1024]{1,0:T(8,128)S(1)}, u32[]{:S(2)}, u32[]{:S(2)}) collective-permute-start(f32[64,1024]{1,0:T(8,128)S(1)} %dynamic-slice_bitcast_fusion.3), channel_id=1, source_target_pairs={{0,2},{1,3},{2,0},{3,1},{4,6},{5,7},{6,4},{7,5},{8,10},{9,11},{10,... | collective-permute-start | bytes 786440 | tf_op jit(solution)/shard_map/ppermute | solution.py:166
  106.9 10.1 %collective-permute-done.17 = f32[64,2048]{1,0:T(8,128)S(1)} collective-permute-done((f32[64,2048]{1,0:T(8,128)S(1)}, f32[64,2048]{1,0:T(8,128)S(1)}, u32[]{:S(2)}, u32[]{:S(2)}) %collective-permute-start.17) | collective-permute-done | bytes 524320 | tf_op jit(solution)/shard_map/ppermute | solution.py:166
  117.2 5.3 %collective-permute-done.22 = f32[64,1024]{1,0:T(8,128)S(1)} collective-permute-done((f32[64,1024]{1,0:T(8,128)S(1)}, f32[64,1024]{1,0:T(8,128)S(1)}, u32[]{:S(2)}, u32[]{:S(2)}) %collective-permute-start.22) | collective-permute-done | bytes 262176 | tf_op jit(solution)/shard_map/ppermute | solution.py:166
  122.6 1.8 %collective-permute-start.24 = (f32[64,1024]{1,0:T(8,128)S(1)}, f32[64,1024]{1,0:T(8,128)S(1)}, u32[]{:S(2)}, u32[]{:S(2)}) collective-permute-start(f32[64,1024]{1,0:T(8,128)S(1)} %dynamic-slice_bitcast_fusion.2), channel_id=1, source_target_pairs={{0,2},{1,3},{2,0},{3,1},{4,6},{5,7},{6,4},{7,5},{8,10},{9,11},{10,... | collective-permute-start | bytes 786440 | tf_op jit(solution)/shard_map/ppermute | solution.py:166
  125.5 10.2 %collective-permute-done.24 = f32[64,1024]{1,0:T(8,128)S(1)} collective-permute-done((f32[64,1024]{1,0:T(8,128)S(1)}, f32[64,1024]{1,0:T(8,128)S(1)}, u32[]{:S(2)}, u32[]{:S(2)}) %collective-permute-start.24) | collective-permute-done | bytes 262176 | tf_op jit(solution)/shard_map/ppermute | solution.py:166
  135.9 9.1 %collective-permute-done.23 = f32[64,1024]{1,0:T(8,128)S(1)} collective-permute-done((f32[64,1024]{1,0:T(8,128)S(1)}, f32[64,1024]{1,0:T(8,128)S(1)}, u32[]{:S(2)}, u32[]{:S(2)}) %collective-permute-start.23) | collective-permute-done | bytes 262176 | tf_op jit(solution)/shard_map/ppermute | solution.py:190
  145.1 4.9 %collective-permute-done.25 = f32[64,1024]{1,0:T(8,128)S(1)} collective-permute-done((f32[64,1024]{1,0:T(8,128)S(1)}, f32[64,1024]{1,0:T(8,128)S(1)}, u32[]{:S(2)}, u32[]{:S(2)}) %collective-permute-start.25) | collective-permute-done | bytes 262176 | tf_op jit(solution)/shard_map/ppermute | solution.py:190
  (96 shorter events, 18.2 us)
Async XLA Ops:
  0.0 8.3 %copy-start = (bf16[896,896,1]{1,0,2:T(8,128)(2,1)S(1)}, bf16[896,896,1]{1,0,2:T(8,128)(2,1)}, u32[]{:S(2)}) copy-start(bf16[896,896,1]{1,0,2:T(8,128)(2,1)} %constant.144) | copy-start | bytes 4816900
  2.3 9.4 %collective-permute-start = (bf16[16,3584]{1,0:T(8,128)(2,1)}, bf16[16,3584]{1,0:T(8,128)(2,1)}, u32[]{:S(2)}, u32[]{:S(2)}) collective-permute-start(bf16[16,3584]{1,0:T(8,128)(2,1)} %get-tuple-element.22), channel_id=1, source_target_pairs={{0,1},{1,0},{2,3},{3,2},{4,5},{5,4},{6,7},{7,6},{8,9},{9,8},{10,11... | collective-permute-start | bytes 344072 | tf_op jit(solution)/shard_map/ppermute | solution.py:113
  2.8 13.8 %collective-permute-start.1 = (bf16[16,3584]{1,0:T(8,128)(2,1)}, bf16[16,3584]{1,0:T(8,128)(2,1)}, u32[]{:S(2)}, u32[]{:S(2)}) collective-permute-start(bf16[16,3584]{1,0:T(8,128)(2,1)} %get-tuple-element.21), channel_id=1, source_target_pairs={{0,2},{1,3},{2,0},{3,1},{4,6},{5,7},{6,4},{7,5},{8,10},{9,11},{10,... | collective-permute-start | bytes 344072 | tf_op jit(solution)/shard_map/ppermute | solution.py:113
  5.4 12.7 %collective-permute-start.2 = (bf16[16,3584]{1,0:T(8,128)(2,1)}, bf16[16,3584]{1,0:T(8,128)(2,1)}, u32[]{:S(2)}, u32[]{:S(2)}) collective-permute-start(bf16[16,3584]{1,0:T(8,128)(2,1)} %get-tuple-element.20), channel_id=1, source_target_pairs={{0,3},{1,2},{2,1},{3,0},{4,7},{5,6},{6,5},{7,4},{8,11},{9,10},{10,... | collective-permute-start | bytes 344072 | tf_op jit(solution)/shard_map/ppermute | solution.py:113
  5.5 13.9 %collective-permute-start.3 = (bf16[16,3584]{1,0:T(8,128)(2,1)}, bf16[16,3584]{1,0:T(8,128)(2,1)}, u32[]{:S(2)}, u32[]{:S(2)}) collective-permute-start(bf16[16,3584]{1,0:T(8,128)(2,1)} %get-tuple-element.19), channel_id=1, source_target_pairs={{0,4},{1,5},{2,6},{3,7},{4,0},{5,1},{6,2},{7,3},{8,12},{9,13},{10,... | collective-permute-start | bytes 344072 | tf_op jit(solution)/shard_map/ppermute | solution.py:113
  8.2 16.3 %collective-permute-start.4 = (bf16[16,3584]{1,0:T(8,128)(2,1)}, bf16[16,3584]{1,0:T(8,128)(2,1)}, u32[]{:S(2)}, u32[]{:S(2)}) collective-permute-start(bf16[16,3584]{1,0:T(8,128)(2,1)} %get-tuple-element.18), channel_id=1, source_target_pairs={{0,5},{1,4},{2,7},{3,6},{4,1},{5,0},{6,3},{7,2},{8,13},{9,12},{10,... | collective-permute-start | bytes 344072 | tf_op jit(solution)/shard_map/ppermute | solution.py:113
  11.7 14.0 %collective-permute-start.5 = (bf16[16,3584]{1,0:T(8,128)(2,1)}, bf16[16,3584]{1,0:T(8,128)(2,1)S(1)}, u32[]{:S(2)}, u32[]{:S(2)}) collective-permute-start(bf16[16,3584]{1,0:T(8,128)(2,1)} %get-tuple-element.24), channel_id=1, source_target_pairs={{0,6},{1,7},{2,4},{3,5},{4,2},{5,3},{6,0},{7,1},{8,14},{9,15},{10,... | collective-permute-start | bytes 344072 | tf_op jit(solution)/shard_map/ppermute | solution.py:113
  16.6 9.5 %collective-permute-start.6 = (bf16[16,3584]{1,0:T(8,128)(2,1)S(1)}, bf16[16,3584]{1,0:T(8,128)(2,1)S(1)}, u32[]{:S(2)}, u32[]{:S(2)}) collective-permute-start(bf16[16,3584]{1,0:T(8,128)(2,1)S(1)} %copy-done.2), channel_id=1, source_target_pairs={{0,7},{1,6},{2,5},{3,4},{4,3},{5,2},{6,1},{7,0},{8,15},{9,14},{10,... | collective-permute-start | bytes 344072 | tf_op jit(solution)/shard_map/ppermute | solution.py:113
  33.4 8.0 %collective-permute-start.7 = (bf16[16,3584]{1,0:T(8,128)(2,1)S(1)}, bf16[16,3584]{1,0:T(8,128)(2,1)S(1)}, u32[]{:S(2)}, u32[]{:S(2)}) collective-permute-start(bf16[16,3584]{1,0:T(8,128)(2,1)S(1)} %bitcast.194), channel_id=1, source_target_pairs={{0,1},{1,0},{2,3},{3,2},{4,5},{5,4},{6,7},{7,6},{8,9},{9,8},{10,11... | collective-permute-start | bytes 344072 | tf_op jit(solution)/shard_map/ppermute | solution.py:134
  33.8 9.8 %collective-permute-start.8 = (bf16[16,3584]{1,0:T(8,128)(2,1)S(1)}, bf16[16,3584]{1,0:T(8,128)(2,1)S(1)}, u32[]{:S(2)}, u32[]{:S(2)}) collective-permute-start(bf16[16,3584]{1,0:T(8,128)(2,1)S(1)} %bitcast.193), channel_id=1, source_target_pairs={{0,2},{1,3},{2,0},{3,1},{4,6},{5,7},{6,4},{7,5},{8,10},{9,11},{10,... | collective-permute-start | bytes 344072 | tf_op jit(solution)/shard_map/ppermute | solution.py:134
  37.6 10.0 %collective-permute-start.9 = (bf16[16,3584]{1,0:T(8,128)(2,1)S(1)}, bf16[16,3584]{1,0:T(8,128)(2,1)S(1)}, u32[]{:S(2)}, u32[]{:S(2)}) collective-permute-start(bf16[16,3584]{1,0:T(8,128)(2,1)S(1)} %bitcast.191), channel_id=1, source_target_pairs={{0,3},{1,2},{2,1},{3,0},{4,7},{5,6},{6,5},{7,4},{8,11},{9,10},{10,... | collective-permute-start | bytes 344072 | tf_op jit(solution)/shard_map/ppermute | solution.py:134
  37.8 9.8 %collective-permute-start.10 = (bf16[16,3584]{1,0:T(8,128)(2,1)S(1)}, bf16[16,3584]{1,0:T(8,128)(2,1)S(1)}, u32[]{:S(2)}, u32[]{:S(2)}) collective-permute-start(bf16[16,3584]{1,0:T(8,128)(2,1)S(1)} %bitcast.190), channel_id=1, source_target_pairs={{0,4},{1,5},{2,6},{3,7},{4,0},{5,1},{6,2},{7,3},{8,12},{9,13},{10,... | collective-permute-start | bytes 344072 | tf_op jit(solution)/shard_map/ppermute | solution.py:134
  40.9 15.7 %collective-permute-start.11 = (bf16[16,3584]{1,0:T(8,128)(2,1)S(1)}, bf16[16,3584]{1,0:T(8,128)(2,1)S(1)}, u32[]{:S(2)}, u32[]{:S(2)}) collective-permute-start(bf16[16,3584]{1,0:T(8,128)(2,1)S(1)} %bitcast.189), channel_id=1, source_target_pairs={{0,5},{1,4},{2,7},{3,6},{4,1},{5,0},{6,3},{7,2},{8,13},{9,12},{10,... | collective-permute-start | bytes 344072 | tf_op jit(solution)/shard_map/ppermute | solution.py:134
  41.3 38.7 %slice-start = ((s8[14680064]{0:T(1024)(128)(4,1)}), s8[4194304]{0:T(1024)(128)(4,1)S(1)}, s32[]{:S(2)}) async-start(s8[14680064]{0:T(1024)(128)(4,1)} %bitcast.174), calls=%async_computation | async-start | bytes 8388608
  41.5 15.2 %collective-permute-start.12 = (bf16[16,3584]{1,0:T(8,128)(2,1)S(1)}, bf16[16,3584]{1,0:T(8,128)(2,1)S(1)}, u32[]{:S(2)}, u32[]{:S(2)}) collective-permute-start(bf16[16,3584]{1,0:T(8,128)(2,1)S(1)} %bitcast.192), channel_id=1, source_target_pairs={{0,6},{1,7},{2,4},{3,5},{4,2},{5,3},{6,0},{7,1},{8,14},{9,15},{10,... | collective-permute-start | bytes 344072 | tf_op jit(solution)/shard_map/ppermute | solution.py:134
  43.7 13.0 %collective-permute-start.13 = (bf16[16,3584]{1,0:T(8,128)(2,1)S(1)}, bf16[16,3584]{1,0:T(8,128)(2,1)S(1)}, u32[]{:S(2)}, u32[]{:S(2)}) collective-permute-start(bf16[16,3584]{1,0:T(8,128)(2,1)S(1)} %bitcast.188), channel_id=1, source_target_pairs={{0,7},{1,6},{2,5},{3,4},{4,3},{5,2},{6,1},{7,0},{8,15},{9,14},{10,... | collective-permute-start | bytes 344072 | tf_op jit(solution)/shard_map/ppermute | solution.py:134
  56.7 23.3 %slice-start.1 = ((s8[14680064]{0:T(1024)(128)(4,1)}), s8[4194304]{0:T(1024)(128)(4,1)S(1)}, s32[]{:S(2)}) async-start(s8[14680064]{0:T(1024)(128)(4,1)} %bitcast.174), calls=%async_computation.1 | async-start | bytes 8388608
  56.7 23.3 %slice-start.2 = ((s8[14680064]{0:T(1024)(128)(4,1)}), s8[4194304]{0:T(1024)(128)(4,1)S(1)}, s32[]{:S(2)}) async-start(s8[14680064]{0:T(1024)(128)(4,1)} %bitcast.174), calls=%async_computation.2 | async-start | bytes 8388608
  56.8 23.3 %slice-start.3 = ((s8[14680064]{0:T(1024)(128)(4,1)}), s8[2097152]{0:T(1024)(128)(4,1)S(1)}, s32[]{:S(2)}) async-start(s8[14680064]{0:T(1024)(128)(4,1)} %bitcast.174), calls=%async_computation.3 | async-start | bytes 4194304
  56.8 23.3 %collective-permute-start.15 = (bf16[128,3584]{1,0:T(8,128)(2,1)S(1)}, bf16[128,3584]{1,0:T(8,128)(2,1)S(1)}, u32[]{:S(2)}, u32[]{:S(2)}) collective-permute-start(bf16[128,3584]{1,0:T(8,128)(2,1)S(1)} %constant_dynamic-update-slice_fusion), channel_id=1, source_target_pairs={{0,8},{8,0},{16,24},{24,16},{1,9},{9,1},{17,25},{25,17},{2,10},{10... | collective-permute-start | bytes 2752520 | tf_op jit(solution)/shard_map/ppermute | solution.py:147
  58.3 25.9 %collective-permute-start.18 = (bf16[128,3584]{1,0:T(8,128)(2,1)S(1)}, bf16[128,3584]{1,0:T(8,128)(2,1)S(1)}, u32[]{:S(2)}, u32[]{:S(2)}) collective-permute-start(bf16[128,3584]{1,0:T(8,128)(2,1)S(1)} %constant_dynamic-update-slice_fusion), channel_id=1, source_target_pairs={{0,16},{8,24},{16,0},{24,8},{1,17},{9,25},{17,1},{25,9},{2,18},{10... | collective-permute-start | bytes 2752520 | tf_op jit(solution)/shard_map/ppermute | solution.py:148
  67.4 31.7 %collective-permute-start.14 = (f32[64,2048]{1,0:T(8,128)S(1)}, f32[64,2048]{1,0:T(8,128)S(1)}, u32[]{:S(2)}, u32[]{:S(2)}) collective-permute-start(f32[64,2048]{1,0:T(8,128)S(1)} %dynamic-slice_bitcast_fusion.1), channel_id=1, source_target_pairs={{0,1},{1,0},{2,3},{3,2},{4,5},{5,4},{6,7},{7,6},{8,9},{9,8},{10,11... | collective-permute-start | bytes 1572872 | tf_op jit(solution)/shard_map/ppermute | solution.py:173
  82.4 16.8 %collective-permute-start.16 = (f32[64,2048]{1,0:T(8,128)S(1)}, f32[64,2048]{1,0:T(8,128)S(1)}, u32[]{:S(2)}, u32[]{:S(2)}) collective-permute-start(f32[64,2048]{1,0:T(8,128)S(1)} %dynamic-slice_bitcast_fusion), channel_id=1, source_target_pairs={{0,1},{1,0},{2,3},{3,2},{4,5},{5,4},{6,7},{7,6},{8,9},{9,8},{10,11... | collective-permute-start | bytes 1572872 | tf_op jit(solution)/shard_map/ppermute | solution.py:173
  82.6 12.9 %collective-permute-start.20 = (bf16[64,3584]{1,0:T(8,128)(2,1)S(1)}, bf16[64,3584]{1,0:T(8,128)(2,1)S(1)}, u32[]{:S(2)}, u32[]{:S(2)}) collective-permute-start(bf16[64,3584]{1,0:T(8,128)(2,1)S(1)} %slice.66), channel_id=1, source_target_pairs={{0,16},{8,24},{16,0},{24,8},{1,17},{9,25},{17,1},{25,9},{2,18},{10... | collective-permute-start | bytes 1376264 | tf_op jit(solution)/shard_map/ppermute | solution.py:150
  84.3 12.6 %collective-permute-start.19 = (bf16[64,3584]{1,0:T(8,128)(2,1)S(1)}, bf16[64,3584]{1,0:T(8,128)(2,1)S(1)}, u32[]{:S(2)}, u32[]{:S(2)}) collective-permute-start(bf16[64,3584]{1,0:T(8,128)(2,1)S(1)} %slice.65), channel_id=1, source_target_pairs={{0,8},{8,0},{16,24},{24,16},{1,9},{9,1},{17,25},{25,17},{2,10},{10... | collective-permute-start | bytes 1376264 | tf_op jit(solution)/shard_map/ppermute | solution.py:149
  99.0 5.3 %collective-permute-start.21 = (f32[2,64,2048]{2,1,0:T(8,128)S(1)}, f32[2,64,2048]{2,1,0:T(8,128)S(1)}, u32[]{:S(2)}, u32[]{:S(2)}) collective-permute-start(f32[2,64,2048]{2,1,0:T(8,128)S(1)} %fusion.16), channel_id=1, source_target_pairs={{0,1},{1,0},{2,3},{3,2},{4,5},{5,4},{6,7},{7,6},{8,9},{9,8},{10,11... | collective-permute-start | bytes 3145736 | tf_op jit(solution)/shard_map/ppermute | solution.py:160
  99.3 17.7 %collective-permute-start.17 = (f32[64,2048]{1,0:T(8,128)S(1)}, f32[64,2048]{1,0:T(8,128)S(1)}, u32[]{:S(2)}, u32[]{:S(2)}) collective-permute-start(f32[64,2048]{1,0:T(8,128)S(1)} %fusion.25), channel_id=1, source_target_pairs={{0,2},{1,3},{2,0},{3,1},{4,6},{5,7},{6,4},{7,5},{8,10},{9,11},{10,... | collective-permute-start | bytes 1572872 | tf_op jit(solution)/shard_map/ppermute | solution.py:166
  104.6 17.9 %collective-permute-start.22 = (f32[64,1024]{1,0:T(8,128)S(1)}, f32[64,1024]{1,0:T(8,128)S(1)}, u32[]{:S(2)}, u32[]{:S(2)}) collective-permute-start(f32[64,1024]{1,0:T(8,128)S(1)} %dynamic-slice_bitcast_fusion.3), channel_id=1, source_target_pairs={{0,2},{1,3},{2,0},{3,1},{4,6},{5,7},{6,4},{7,5},{8,10},{9,11},{10,... | collective-permute-start | bytes 786440 | tf_op jit(solution)/shard_map/ppermute | solution.py:166
  122.6 13.1 %collective-permute-start.24 = (f32[64,1024]{1,0:T(8,128)S(1)}, f32[64,1024]{1,0:T(8,128)S(1)}, u32[]{:S(2)}, u32[]{:S(2)}) collective-permute-start(f32[64,1024]{1,0:T(8,128)S(1)} %dynamic-slice_bitcast_fusion.2), channel_id=1, source_target_pairs={{0,2},{1,3},{2,0},{3,1},{4,6},{5,7},{6,4},{7,5},{8,10},{9,11},{10,... | collective-permute-start | bytes 786440 | tf_op jit(solution)/shard_map/ppermute | solution.py:166
  124.5 25.6 %copy-start.4 = (f32[2048]{0:T(1024)S(1)}, f32[2048]{0:T(1024)}, u32[]{:S(2)}) copy-start(f32[2048]{0:T(1024)} %param.7) | copy-start | bytes 24580
  124.5 20.5 %collective-permute-start.23 = (f32[64,1024]{1,0:T(8,128)S(1)}, f32[64,1024]{1,0:T(8,128)S(1)}, u32[]{:S(2)}, u32[]{:S(2)}) collective-permute-start(f32[64,1024]{1,0:T(8,128)S(1)} %fusion.38), channel_id=1, source_target_pairs={{0,4},{1,5},{2,6},{3,7},{4,0},{5,1},{6,2},{7,3},{8,12},{9,13},{10,... | collective-permute-start | bytes 786440 | tf_op jit(solution)/shard_map/ppermute | solution.py:190
  135.8 14.2 %collective-permute-start.25 = (f32[64,1024]{1,0:T(8,128)S(1)}, f32[64,1024]{1,0:T(8,128)S(1)}, u32[]{:S(2)}, u32[]{:S(2)}) collective-permute-start(f32[64,1024]{1,0:T(8,128)S(1)} %fusion.33), channel_id=1, source_target_pairs={{0,4},{1,5},{2,6},{3,7},{4,0},{5,1},{6,2},{7,3},{8,12},{9,13},{10,... | collective-permute-start | bytes 786440 | tf_op jit(solution)/shard_map/ppermute | solution.py:190
  (3 other events, 11.2 us)

commit v19 on v18

--- a/solution.py
+++ b/solution.py
@@ -9,7 +9,7 @@
 PALEY = 28
 INNER = 32
 CHUNKS = 1
-TAIL_PIECES = 2
+TAIL_PIECES = 8
 
 
 def paley_table():

time: 151 us -> 188 us (1.25)
  starting transfers between devices: 38.6 us -> 53.5 us
  waiting for transfers between devices: 75.8 us -> 86.8 us
  other arithmetic: 3.17 us -> 8.43 us
  matrix products: 24.9 us -> 29.8 us
    ppermute x3 -> x9, waiting for transfers between devices: 25.6 us -> 39 us  [second_halving(): return keep + lax.ppermute(send, 'tp', tp_pairs(2))]
    ppermute x2 -> x8, starting transfers between devices: 1.06 us -> 11 us  [product_and_reduce(): results.append(keep + lax.ppermute(send, 'tp', tp_pairs(4)))]
    ppermute x2 -> x8, waiting for transfers between devices: 14 us -> 5.18 us  [product_and_reduce(): results.append(keep + lax.ppermute(send, 'tp', tp_pairs(4)))]
    ppermute x1, waiting for transfers between devices: 11.6 us -> 18 us  [product_and_reduce(): across_x = lax.ppermute(block, 'seq', seq_pairs(1))]
    ppermute x3 -> x9, starting transfers between devices: 9.13 us -> 14.3 us  [second_halving(): return keep + lax.ppermute(send, 'tp', tp_pairs(2))]
    dot_general x2, matrix products: 9.78 us -> 14.7 us  [first_halving_one(): product = jnp.dot(piece, down_weight, preferred_element_type=jnp.float32)]
  transfers between devices with their start and end apart: 26 -> 38, of which waited for: 11 -> 17; matrix products, arithmetic and copies ran while one was open for 17% -> 14% of each run, Pallas kernels for 0% -> 0%
where the time goes in v19:
time: 188 us; the launch traced here: 187 us
  waiting for transfers between devices  86.8 us (46%)
  starting transfers between devices  53.5 us (28%)
  matrix products  29.8 us (16%)
  other arithmetic  8.43 us (4%)
  local copies, waits for them, and re-layouts  8.05 us (4%)
    ppermute x9, waiting for transfers between devices, second_halving(): return keep + lax.ppermute(send, 'tp', tp_pairs(2))  39 us
    ppermute x1, waiting for transfers between devices, product_and_reduce(): across_x = lax.ppermute(block, 'seq', seq_pairs(1))  18 us
    dot_general x2, matrix products, first_halving_one(): product = jnp.dot(piece, down_weight, preferred_element_type=jnp.float32)  14.7 us
    ppermute x9, starting transfers between devices, second_halving(): return keep + lax.ppermute(send, 'tp', tp_pairs(2))  14.3 us
    ppermute x7, waiting for transfers between devices, spread_rotate_return(): block = lax.ppermute(block, 'tp', pairs(distance))  11.7 us
    ppermute x7, starting transfers between devices, spread_rotate_return(): block = lax.ppermute(block, 'tp', pairs(distance))  11.2 us
    ppermute x8, starting transfers between devices, product_and_reduce(): results.append(keep + lax.ppermute(send, 'tp', tp_pairs(4)))  11 us
    ppermute x7, starting transfers between devices, spread_rotate_return(): send = lax.ppermute(send, 'tp', pairs(distance))  9.65 us
  transfers between devices with their start and end apart: 38, of which 17 were waited for; matrix products, arithmetic and copies ran while one was open for 14% of the time, Pallas kernels for 0%

profile of v19, /device:TPU:0, one launch (start us, length us, event | category | flops | bytes accessed | tf_op | source)
XLA Modules:
  0.0 187.1 jit_solution(5718811651382338536)
XLA Ops:
  0.0 2.3 %constant_dynamic-slice_fusion = (bf16[16,3584]{1,0:T(8,128)(2,1)}, bf16[16,3584]{1,0:T(8,128)(2,1)}, bf16[16,3584]{1,0:T(8,128)(2,1)}, bf16[16,3584]{1,0:T(8,12...) fusion(bf16[128,3584]{1,0:T(8,128)(2,1)} %param.5, ...), kind=kLoop, calls=%fused_computation.179 | loop fusion | bytes 1835040 | tf_op jit(solution)/shard_map/dynamic_slice | solution.py:111
  2.8 2.6 %collective-permute-start.1 = (bf16[16,3584]{1,0:T(8,128)(2,1)}, bf16[16,3584]{1,0:T(8,128)(2,1)}, u32[]{:S(2)}, u32[]{:S(2)}) collective-permute-start(bf16[16,3584]{1,0:T(8,128)(2,1)} %get-tuple-element.39), channel_id=1, source_target_pairs={{0,2},{1,3},{2,0},{3,1},{4,6},{5,7},{6,4},{7,5},{8,10},{9,11},{10,... | collective-permute-start | bytes 344072 | tf_op jit(solution)/shard_map/ppermute | solution.py:113
  5.5 2.7 %collective-permute-start.3 = (bf16[16,3584]{1,0:T(8,128)(2,1)}, bf16[16,3584]{1,0:T(8,128)(2,1)}, u32[]{:S(2)}, u32[]{:S(2)}) collective-permute-start(bf16[16,3584]{1,0:T(8,128)(2,1)} %get-tuple-element.37), channel_id=1, source_target_pairs={{0,4},{1,5},{2,6},{3,7},{4,0},{5,1},{6,2},{7,3},{8,12},{9,13},{10,... | collective-permute-start | bytes 344072 | tf_op jit(solution)/shard_map/ppermute | solution.py:113
  11.7 3.6 %collective-permute-start.5 = (bf16[16,3584]{1,0:T(8,128)(2,1)}, bf16[16,3584]{1,0:T(8,128)(2,1)S(1)}, u32[]{:S(2)}, u32[]{:S(2)}) collective-permute-start(bf16[16,3584]{1,0:T(8,128)(2,1)} %get-tuple-element.42), channel_id=1, source_target_pairs={{0,6},{1,7},{2,4},{3,5},{4,2},{5,3},{6,0},{7,1},{8,14},{9,15},{10,... | collective-permute-start | bytes 344072 | tf_op jit(solution)/shard_map/ppermute | solution.py:113
  20.6 3.8 %collective-permute-done.4 = bf16[16,3584]{1,0:T(8,128)(2,1)} collective-permute-done((bf16[16,3584]{1,0:T(8,128)(2,1)}, bf16[16,3584]{1,0:T(8,128)(2,1)}, u32[]{:S(2)}, u32[]{:S(2)}) %collective-permute-start.4) | collective-permute-done | bytes 114720 | tf_op jit(solution)/shard_map/ppermute | solution.py:113
  27.8 3.5 %fusion.4 = bf16[16,32,896]{2,1,0:T(8,128)(2,1)S(1)} fusion(f32[16,32,896]{2,0,1:T(8,128)} %bitcast.278, f32[32,32]{1,0:T(8,128)S(1)} %copy-done.3), kind=kOutput, calls=%fused_computation.7 | convolution fusion | flops 177078272 | bytes 2756608 | tf_op jit(solution)/shard_map/rbm,bc->rcm/dot_general | solution.py:127
  34.0 3.8 %collective-permute-start.8 = (bf16[16,3584]{1,0:T(8,128)(2,1)S(1)}, bf16[16,3584]{1,0:T(8,128)(2,1)S(1)}, u32[]{:S(2)}, u32[]{:S(2)}) collective-permute-start(bf16[16,3584]{1,0:T(8,128)(2,1)S(1)} %bitcast.299), channel_id=1, source_target_pairs={{0,2},{1,3},{2,0},{3,1},{4,6},{5,7},{6,4},{7,5},{8,10},{9,11},{10,... | collective-permute-start | bytes 344072 | tf_op jit(solution)/shard_map/ppermute | solution.py:134
  38.0 3.1 %collective-permute-start.10 = (bf16[16,3584]{1,0:T(8,128)(2,1)S(1)}, bf16[16,3584]{1,0:T(8,128)(2,1)S(1)}, u32[]{:S(2)}, u32[]{:S(2)}) collective-permute-start(bf16[16,3584]{1,0:T(8,128)(2,1)S(1)} %bitcast.296), channel_id=1, source_target_pairs={{0,4},{1,5},{2,6},{3,7},{4,0},{5,1},{6,2},{7,3},{8,12},{9,13},{10,... | collective-permute-start | bytes 344072 | tf_op jit(solution)/shard_map/ppermute | solution.py:134
  41.7 2.1 %collective-permute-start.12 = (bf16[16,3584]{1,0:T(8,128)(2,1)S(1)}, bf16[16,3584]{1,0:T(8,128)(2,1)S(1)}, u32[]{:S(2)}, u32[]{:S(2)}) collective-permute-start(bf16[16,3584]{1,0:T(8,128)(2,1)S(1)} %bitcast.298), channel_id=1, source_target_pairs={{0,6},{1,7},{2,4},{3,5},{4,2},{5,3},{6,0},{7,1},{8,14},{9,15},{10,... | collective-permute-start | bytes 344072 | tf_op jit(solution)/shard_map/ppermute | solution.py:134
  45.1 2.7 %collective-permute-done.9 = bf16[16,3584]{1,0:T(8,128)(2,1)S(1)} collective-permute-done((bf16[16,3584]{1,0:T(8,128)(2,1)S(1)}, bf16[16,3584]{1,0:T(8,128)(2,1)S(1)}, u32[]{:S(2)}, u32[]{:S(2)}) %collective-permute-start.9) | collective-permute-done | bytes 114720 | tf_op jit(solution)/shard_map/ppermute | solution.py:134
  47.8 9.0 %collective-permute-done.11 = bf16[16,3584]{1,0:T(8,128)(2,1)S(1)} collective-permute-done((bf16[16,3584]{1,0:T(8,128)(2,1)S(1)}, bf16[16,3584]{1,0:T(8,128)(2,1)S(1)}, u32[]{:S(2)}, u32[]{:S(2)}) %collective-permute-start.11) | collective-permute-done | bytes 114720 | tf_op jit(solution)/shard_map/ppermute | solution.py:134
  56.9 7.2 %fusion.89 = f32[128,2048]{1,0:T(8,128)S(1)} fusion(bf16[128,3584]{1,0:T(8,128)(2,1)S(1)} %constant_dynamic-update-slice_fusion, bf16[3584,2048]{1,0:T(8,128)(2,1)} %param.6), kind=kOutput, calls=%fused_computation.199 | convolution fusion | flops 1879048192 | bytes 16646144 | tf_op jit(solution)/shard_map/dot_general | solution.py:169
  69.6 18.0 %collective-permute-done.15 = bf16[128,3584]{1,0:T(8,128)(2,1)S(1)} collective-permute-done((bf16[128,3584]{1,0:T(8,128)(2,1)S(1)}, bf16[128,3584]{1,0:T(8,128)(2,1)S(1)}, u32[]{:S(2)}, u32[]{:S(2)}) %collective-permute-start.15) | collective-permute-done | bytes 917536 | tf_op jit(solution)/shard_map/ppermute | solution.py:147
  87.6 7.4 %fusion.90 = f32[128,2048]{1,0:T(8,128)S(1)} fusion(bf16[128,3584]{1,0:T(8,128)(2,1)S(1)} %collective-permute-done.15, bf16[3584,2048]{1,0:T(8,128)(2,1)} %param.6), kind=kOutput, calls=%fused_computation.200 | convolution fusion | flops 1879048192 | bytes 16646144 | tf_op jit(solution)/shard_map/dot_general | solution.py:169
  98.4 2.1 %fusion.91 = f32[128,2048]{1,0:T(8,128)S(1)} fusion(bf16[128,3584]{1,0:T(8,128)(2,1)S(1)} %collective-permute-done.18, bf16[3584,2048]{1,0:T(8,128)(2,1)S(1)} %bitcast.269), kind=kOutput, calls=%fused_computation.201 | convolution fusion | flops 1879048192 | bytes 16646144 | tf_op jit(solution)/shard_map/dot_general | solution.py:155
  100.5 7.7 %collective-permute-done.20 = bf16[64,3584]{1,0:T(8,128)(2,1)S(1)} collective-permute-done((bf16[64,3584]{1,0:T(8,128)(2,1)S(1)}, bf16[64,3584]{1,0:T(8,128)(2,1)S(1)}, u32[]{:S(2)}, u32[]{:S(2)}) %collective-permute-start.20) | collective-permute-done | bytes 458784 | tf_op jit(solution)/shard_map/ppermute | solution.py:150
  109.5 2.1 %fusion.20 = f32[128,2048]{1,0:T(8,128)S(1)} fusion(bf16[3584,2048]{1,0:T(8,128)(2,1)S(1)} %bitcast.269, bf16[64,3584]{1,0:T(8,128)(2,1)S(1)} %collective-permute-done.20, bf16[64,3584]{1,0:T(8,128)(2,1)S(1)} %collective-permute-done.19), kind=kOutput, calls=%fused_computation.33 | convolution fusion | flops 1880883200 | bytes 16646144 | tf_op jit(solution)/shard_map/dot_general | solution.py:155
  113.6 4.9 %collective-permute-start.17 = (f32[64,2048]{1,0:T(8,128)}, f32[64,2048]{1,0:T(8,128)}, u32[]{:S(2)}, u32[]{:S(2)}) collective-permute-start(f32[64,2048]{1,0:T(8,128)} %fusion.25), channel_id=1, source_target_pairs={{0,2},{1,3},{2,0},{3,1},{4,6},{5,7},{6,4},{7,5},{8,10},{9,11},{10,... | collective-permute-start | bytes 1572872 | tf_op jit(solution)/shard_map/ppermute | solution.py:166
  118.5 12.9 %collective-permute-done.17 = f32[64,2048]{1,0:T(8,128)} collective-permute-done((f32[64,2048]{1,0:T(8,128)}, f32[64,2048]{1,0:T(8,128)}, u32[]{:S(2)}, u32[]{:S(2)}) %collective-permute-start.17) | collective-permute-done | bytes 524320 | tf_op jit(solution)/shard_map/ppermute | solution.py:166
  134.0 1.8 collective-permute-start.22
  135.9 2.5 %collective-permute-done.22 = f32[64,256]{1,0:T(8,128)S(1)} collective-permute-done((f32[64,256]{1,0:T(8,128)S(1)}, f32[64,256]{1,0:T(8,128)S(1)}, u32[]{:S(2)}, u32[]{:S(2)}) %collective-permute-start.22) | collective-permute-done | bytes 65568 | tf_op jit(solution)/shard_map/ppermute | solution.py:166
  138.4 1.8 collective-permute-start.24
  143.0 2.3 %collective-permute-start.25 = (f32[64,256]{1,0:T(8,128)S(1)}, f32[64,256]{1,0:T(8,128)S(1)}, u32[]{:S(2)}, u32[]{:S(2)}) collective-permute-start(f32[64,256]{1,0:T(8,128)S(1)} %fusion.69), channel_id=1, source_target_pairs={{0,4},{1,5},{2,6},{3,7},{4,0},{5,1},{6,2},{7,3},{8,12},{9,13},{10,... | collective-permute-start | bytes 196616 | tf_op jit(solution)/shard_map/ppermute | solution.py:190
  146.8 3.7 %collective-permute-done.26 = f32[64,256]{1,0:T(8,128)S(1)} collective-permute-done((f32[64,256]{1,0:T(8,128)S(1)}, f32[64,256]{1,0:T(8,128)S(1)}, u32[]{:S(2)}, u32[]{:S(2)}) %collective-permute-start.26) | collective-permute-done | bytes 65568 | tf_op jit(solution)/shard_map/ppermute | solution.py:166
  152.0 3.8 %collective-permute-done.28 = f32[64,256]{1,0:T(8,128)S(1)} collective-permute-done((f32[64,256]{1,0:T(8,128)S(1)}, f32[64,256]{1,0:T(8,128)S(1)}, u32[]{:S(2)}, u32[]{:S(2)}) %collective-permute-start.28) | collective-permute-done | bytes 65568 | tf_op jit(solution)/shard_map/ppermute | solution.py:166
  155.9 2.1 %collective-permute-start.29 = (f32[64,256]{1,0:T(8,128)S(1)}, f32[64,256]{1,0:T(8,128)S(1)}, u32[]{:S(2)}, u32[]{:S(2)}) collective-permute-start(f32[64,256]{1,0:T(8,128)S(1)} %fusion.57), channel_id=1, source_target_pairs={{0,4},{1,5},{2,6},{3,7},{4,0},{5,1},{6,2},{7,3},{8,12},{9,13},{10,... | collective-permute-start | bytes 196616 | tf_op jit(solution)/shard_map/ppermute | solution.py:190
  159.6 3.0 %collective-permute-done.30 = f32[64,256]{1,0:T(8,128)S(1)} collective-permute-done((f32[64,256]{1,0:T(8,128)S(1)}, f32[64,256]{1,0:T(8,128)S(1)}, u32[]{:S(2)}, u32[]{:S(2)}) %collective-permute-start.30) | collective-permute-done | bytes 65568 | tf_op jit(solution)/shard_map/ppermute | solution.py:166
  164.5 4.1 %collective-permute-done.32 = f32[64,256]{1,0:T(8,128)S(1)} collective-permute-done((f32[64,256]{1,0:T(8,128)S(1)}, f32[64,256]{1,0:T(8,128)S(1)}, u32[]{:S(2)}, u32[]{:S(2)}) %collective-permute-start.32) | collective-permute-done | bytes 65568 | tf_op jit(solution)/shard_map/ppermute | solution.py:166
  171.3 3.2 %collective-permute-done.34 = f32[64,256]{1,0:T(8,128)S(1)} collective-permute-done((f32[64,256]{1,0:T(8,128)S(1)}, f32[64,256]{1,0:T(8,128)S(1)}, u32[]{:S(2)}, u32[]{:S(2)}) %collective-permute-start.34) | collective-permute-done | bytes 65568 | tf_op jit(solution)/shard_map/ppermute | solution.py:166
  176.5 4.0 %collective-permute-done.36 = f32[64,256]{1,0:T(8,128)S(1)} collective-permute-done((f32[64,256]{1,0:T(8,128)S(1)}, f32[64,256]{1,0:T(8,128)S(1)}, u32[]{:S(2)}, u32[]{:S(2)}) %collective-permute-start.36) | collective-permute-done | bytes 65568 | tf_op jit(solution)/shard_map/ppermute | solution.py:166
  180.6 1.7 collective-permute-start.37
  182.3 4.0 %collective-permute-done.37 = f32[64,256]{1,0:T(8,128)S(1)} collective-permute-done((f32[64,256]{1,0:T(8,128)S(1)}, f32[64,256]{1,0:T(8,128)S(1)}, u32[]{:S(2)}, u32[]{:S(2)}) %collective-permute-start.37) | collective-permute-done | bytes 65568 | tf_op jit(solution)/shard_map/ppermute | solution.py:190
  (144 shorter events, 46.8 us)
Async XLA Ops:
  2.3 9.4 %collective-permute-start = (bf16[16,3584]{1,0:T(8,128)(2,1)}, bf16[16,3584]{1,0:T(8,128)(2,1)}, u32[]{:S(2)}, u32[]{:S(2)}) collective-permute-start(bf16[16,3584]{1,0:T(8,128)(2,1)} %get-tuple-element.40), channel_id=1, source_target_pairs={{0,1},{1,0},{2,3},{3,2},{4,5},{5,4},{6,7},{7,6},{8,9},{9,8},{10,11... | collective-permute-start | bytes 344072 | tf_op jit(solution)/shard_map/ppermute | solution.py:113
  2.8 13.9 %collective-permute-start.1 = (bf16[16,3584]{1,0:T(8,128)(2,1)}, bf16[16,3584]{1,0:T(8,128)(2,1)}, u32[]{:S(2)}, u32[]{:S(2)}) collective-permute-start(bf16[16,3584]{1,0:T(8,128)(2,1)} %get-tuple-element.39), channel_id=1, source_target_pairs={{0,2},{1,3},{2,0},{3,1},{4,6},{5,7},{6,4},{7,5},{8,10},{9,11},{10,... | collective-permute-start | bytes 344072 | tf_op jit(solution)/shard_map/ppermute | solution.py:113
  5.4 12.7 %collective-permute-start.2 = (bf16[16,3584]{1,0:T(8,128)(2,1)}, bf16[16,3584]{1,0:T(8,128)(2,1)}, u32[]{:S(2)}, u32[]{:S(2)}) collective-permute-start(bf16[16,3584]{1,0:T(8,128)(2,1)} %get-tuple-element.38), channel_id=1, source_target_pairs={{0,3},{1,2},{2,1},{3,0},{4,7},{5,6},{6,5},{7,4},{8,11},{9,10},{10,... | collective-permute-start | bytes 344072 | tf_op jit(solution)/shard_map/ppermute | solution.py:113
  5.5 13.9 %collective-permute-start.3 = (bf16[16,3584]{1,0:T(8,128)(2,1)}, bf16[16,3584]{1,0:T(8,128)(2,1)}, u32[]{:S(2)}, u32[]{:S(2)}) collective-permute-start(bf16[16,3584]{1,0:T(8,128)(2,1)} %get-tuple-element.37), channel_id=1, source_target_pairs={{0,4},{1,5},{2,6},{3,7},{4,0},{5,1},{6,2},{7,3},{8,12},{9,13},{10,... | collective-permute-start | bytes 344072 | tf_op jit(solution)/shard_map/ppermute | solution.py:113
  8.2 16.3 %collective-permute-start.4 = (bf16[16,3584]{1,0:T(8,128)(2,1)}, bf16[16,3584]{1,0:T(8,128)(2,1)}, u32[]{:S(2)}, u32[]{:S(2)}) collective-permute-start(bf16[16,3584]{1,0:T(8,128)(2,1)} %get-tuple-element.36), channel_id=1, source_target_pairs={{0,5},{1,4},{2,7},{3,6},{4,1},{5,0},{6,3},{7,2},{8,13},{9,12},{10,... | collective-permute-start | bytes 344072 | tf_op jit(solution)/shard_map/ppermute | solution.py:113
  11.7 14.0 %collective-permute-start.5 = (bf16[16,3584]{1,0:T(8,128)(2,1)}, bf16[16,3584]{1,0:T(8,128)(2,1)S(1)}, u32[]{:S(2)}, u32[]{:S(2)}) collective-permute-start(bf16[16,3584]{1,0:T(8,128)(2,1)} %get-tuple-element.42), channel_id=1, source_target_pairs={{0,6},{1,7},{2,4},{3,5},{4,2},{5,3},{6,0},{7,1},{8,14},{9,15},{10,... | collective-permute-start | bytes 344072 | tf_op jit(solution)/shard_map/ppermute | solution.py:113
  16.6 9.5 %collective-permute-start.6 = (bf16[16,3584]{1,0:T(8,128)(2,1)S(1)}, bf16[16,3584]{1,0:T(8,128)(2,1)S(1)}, u32[]{:S(2)}, u32[]{:S(2)}) collective-permute-start(bf16[16,3584]{1,0:T(8,128)(2,1)S(1)} %copy-done.2), channel_id=1, source_target_pairs={{0,7},{1,6},{2,5},{3,4},{4,3},{5,2},{6,1},{7,0},{8,15},{9,14},{10,... | collective-permute-start | bytes 344072 | tf_op jit(solution)/shard_map/ppermute | solution.py:113
  33.6 8.0 %collective-permute-start.7 = (bf16[16,3584]{1,0:T(8,128)(2,1)S(1)}, bf16[16,3584]{1,0:T(8,128)(2,1)S(1)}, u32[]{:S(2)}, u32[]{:S(2)}) collective-permute-start(bf16[16,3584]{1,0:T(8,128)(2,1)S(1)} %bitcast.300), channel_id=1, source_target_pairs={{0,1},{1,0},{2,3},{3,2},{4,5},{5,4},{6,7},{7,6},{8,9},{9,8},{10,11... | collective-permute-start | bytes 344072 | tf_op jit(solution)/shard_map/ppermute | solution.py:134
  34.0 9.8 %collective-permute-start.8 = (bf16[16,3584]{1,0:T(8,128)(2,1)S(1)}, bf16[16,3584]{1,0:T(8,128)(2,1)S(1)}, u32[]{:S(2)}, u32[]{:S(2)}) collective-permute-start(bf16[16,3584]{1,0:T(8,128)(2,1)S(1)} %bitcast.299), channel_id=1, source_target_pairs={{0,2},{1,3},{2,0},{3,1},{4,6},{5,7},{6,4},{7,5},{8,10},{9,11},{10,... | collective-permute-start | bytes 344072 | tf_op jit(solution)/shard_map/ppermute | solution.py:134
  37.8 10.0 %collective-permute-start.9 = (bf16[16,3584]{1,0:T(8,128)(2,1)S(1)}, bf16[16,3584]{1,0:T(8,128)(2,1)S(1)}, u32[]{:S(2)}, u32[]{:S(2)}) collective-permute-start(bf16[16,3584]{1,0:T(8,128)(2,1)S(1)} %bitcast.297), channel_id=1, source_target_pairs={{0,3},{1,2},{2,1},{3,0},{4,7},{5,6},{6,5},{7,4},{8,11},{9,10},{10,... | collective-permute-start | bytes 344072 | tf_op jit(solution)/shard_map/ppermute | solution.py:134
  38.0 9.8 %collective-permute-start.10 = (bf16[16,3584]{1,0:T(8,128)(2,1)S(1)}, bf16[16,3584]{1,0:T(8,128)(2,1)S(1)}, u32[]{:S(2)}, u32[]{:S(2)}) collective-permute-start(bf16[16,3584]{1,0:T(8,128)(2,1)S(1)} %bitcast.296), channel_id=1, source_target_pairs={{0,4},{1,5},{2,6},{3,7},{4,0},{5,1},{6,2},{7,3},{8,12},{9,13},{10,... | collective-permute-start | bytes 344072 | tf_op jit(solution)/shard_map/ppermute | solution.py:134
  41.1 15.7 %collective-permute-start.11 = (bf16[16,3584]{1,0:T(8,128)(2,1)S(1)}, bf16[16,3584]{1,0:T(8,128)(2,1)S(1)}, u32[]{:S(2)}, u32[]{:S(2)}) collective-permute-start(bf16[16,3584]{1,0:T(8,128)(2,1)S(1)} %bitcast.295), channel_id=1, source_target_pairs={{0,5},{1,4},{2,7},{3,6},{4,1},{5,0},{6,3},{7,2},{8,13},{9,12},{10,... | collective-permute-start | bytes 344072 | tf_op jit(solution)/shard_map/ppermute | solution.py:134
  41.7 15.2 %collective-permute-start.12 = (bf16[16,3584]{1,0:T(8,128)(2,1)S(1)}, bf16[16,3584]{1,0:T(8,128)(2,1)S(1)}, u32[]{:S(2)}, u32[]{:S(2)}) collective-permute-start(bf16[16,3584]{1,0:T(8,128)(2,1)S(1)} %bitcast.298), channel_id=1, source_target_pairs={{0,6},{1,7},{2,4},{3,5},{4,2},{5,3},{6,0},{7,1},{8,14},{9,15},{10,... | collective-permute-start | bytes 344072 | tf_op jit(solution)/shard_map/ppermute | solution.py:134
  43.8 13.0 %collective-permute-start.13 = (bf16[16,3584]{1,0:T(8,128)(2,1)S(1)}, bf16[16,3584]{1,0:T(8,128)(2,1)S(1)}, u32[]{:S(2)}, u32[]{:S(2)}) collective-permute-start(bf16[16,3584]{1,0:T(8,128)(2,1)S(1)} %bitcast.294), channel_id=1, source_target_pairs={{0,7},{1,6},{2,5},{3,4},{4,3},{5,2},{6,1},{7,0},{8,15},{9,14},{10,... | collective-permute-start | bytes 344072 | tf_op jit(solution)/shard_map/ppermute | solution.py:134
  65.3 22.3 %collective-permute-start.15 = (bf16[128,3584]{1,0:T(8,128)(2,1)S(1)}, bf16[128,3584]{1,0:T(8,128)(2,1)S(1)}, u32[]{:S(2)}, u32[]{:S(2)}) collective-permute-start(bf16[128,3584]{1,0:T(8,128)(2,1)S(1)} %constant_dynamic-update-slice_fusion), channel_id=1, source_target_pairs={{0,8},{8,0},{16,24},{24,16},{1,9},{9,1},{17,25},{25,17},{2,10},{10... | collective-permute-start | bytes 2752520 | tf_op jit(solution)/shard_map/ppermute | solution.py:147
  66.8 30.0 %collective-permute-start.18 = (bf16[128,3584]{1,0:T(8,128)(2,1)S(1)}, bf16[128,3584]{1,0:T(8,128)(2,1)S(1)}, u32[]{:S(2)}, u32[]{:S(2)}) collective-permute-start(bf16[128,3584]{1,0:T(8,128)(2,1)S(1)} %constant_dynamic-update-slice_fusion), channel_id=1, source_target_pairs={{0,16},{8,24},{16,0},{24,8},{1,17},{9,25},{17,1},{25,9},{2,18},{10... | collective-permute-start | bytes 2752520 | tf_op jit(solution)/shard_map/ppermute | solution.py:148
  95.1 17.6 %collective-permute-start.16 = (f32[64,2048]{1,0:T(8,128)S(1)}, f32[64,2048]{1,0:T(8,128)S(1)}, u32[]{:S(2)}, u32[]{:S(2)}) collective-permute-start(f32[64,2048]{1,0:T(8,128)S(1)} %dynamic-slice_bitcast_fusion), channel_id=1, source_target_pairs={{0,1},{1,0},{2,3},{3,2},{4,5},{5,4},{6,7},{7,6},{8,9},{9,8},{10,11... | collective-permute-start | bytes 1572872 | tf_op jit(solution)/shard_map/ppermute | solution.py:173
  95.2 13.0 %collective-permute-start.20 = (bf16[64,3584]{1,0:T(8,128)(2,1)S(1)}, bf16[64,3584]{1,0:T(8,128)(2,1)S(1)}, u32[]{:S(2)}, u32[]{:S(2)}) collective-permute-start(bf16[64,3584]{1,0:T(8,128)(2,1)S(1)} %slice.114), channel_id=1, source_target_pairs={{0,16},{8,24},{16,0},{24,8},{1,17},{9,25},{17,1},{25,9},{2,18},{10... | collective-permute-start | bytes 1376264 | tf_op jit(solution)/shard_map/ppermute | solution.py:150
  96.8 12.7 %collective-permute-start.19 = (bf16[64,3584]{1,0:T(8,128)(2,1)S(1)}, bf16[64,3584]{1,0:T(8,128)(2,1)S(1)}, u32[]{:S(2)}, u32[]{:S(2)}) collective-permute-start(bf16[64,3584]{1,0:T(8,128)(2,1)S(1)} %slice.113), channel_id=1, source_target_pairs={{0,8},{8,0},{16,24},{24,16},{1,9},{9,1},{17,25},{25,17},{2,10},{10... | collective-permute-start | bytes 1376264 | tf_op jit(solution)/shard_map/ppermute | solution.py:149
  112.7 19.9 %collective-permute-start.21 = (f32[2,64,2048]{2,1,0:T(8,128)}, f32[2,64,2048]{2,1,0:T(8,128)}, u32[]{:S(2)}, u32[]{:S(2)}) collective-permute-start(f32[2,64,2048]{2,1,0:T(8,128)} %fusion.16), channel_id=1, source_target_pairs={{0,1},{1,0},{2,3},{3,2},{4,5},{5,4},{6,7},{7,6},{8,9},{9,8},{10,11... | collective-permute-start | bytes 3145736 | tf_op jit(solution)/shard_map/ppermute | solution.py:160
  113.6 17.8 %collective-permute-start.17 = (f32[64,2048]{1,0:T(8,128)}, f32[64,2048]{1,0:T(8,128)}, u32[]{:S(2)}, u32[]{:S(2)}) collective-permute-start(f32[64,2048]{1,0:T(8,128)} %fusion.25), channel_id=1, source_target_pairs={{0,2},{1,3},{2,0},{3,1},{4,6},{5,7},{6,4},{7,5},{8,10},{9,11},{10,... | collective-permute-start | bytes 1572872 | tf_op jit(solution)/shard_map/ppermute | solution.py:166
  140.2 6.5 %collective-permute-start.23 = (f32[64,256]{1,0:T(8,128)S(1)}, f32[64,256]{1,0:T(8,128)S(1)}, u32[]{:S(2)}, u32[]{:S(2)}) collective-permute-start(f32[64,256]{1,0:T(8,128)S(1)} %fusion.75), channel_id=1, source_target_pairs={{0,4},{1,5},{2,6},{3,7},{4,0},{5,1},{6,2},{7,3},{8,12},{9,13},{10,... | collective-permute-start | bytes 196616 | tf_op jit(solution)/shard_map/ppermute | solution.py:190
  143.0 9.0 %collective-permute-start.25 = (f32[64,256]{1,0:T(8,128)S(1)}, f32[64,256]{1,0:T(8,128)S(1)}, u32[]{:S(2)}, u32[]{:S(2)}) collective-permute-start(f32[64,256]{1,0:T(8,128)S(1)} %fusion.69), channel_id=1, source_target_pairs={{0,4},{1,5},{2,6},{3,7},{4,0},{5,1},{6,2},{7,3},{8,12},{9,13},{10,... | collective-permute-start | bytes 196616 | tf_op jit(solution)/shard_map/ppermute | solution.py:190
  145.2 5.2 %collective-permute-start.26 = (f32[64,256]{1,0:T(8,128)S(1)}, f32[64,256]{1,0:T(8,128)S(1)}, u32[]{:S(2)}, u32[]{:S(2)}) collective-permute-start(f32[64,256]{1,0:T(8,128)S(1)} %dynamic-slice_bitcast_fusion.7), channel_id=1, source_target_pairs={{0,2},{1,3},{2,0},{3,1},{4,6},{5,7},{6,4},{7,5},{8,10},{9,11},{10,... | collective-permute-start | bytes 196616 | tf_op jit(solution)/shard_map/ppermute | solution.py:166
  150.5 9.1 %collective-permute-start.27 = (f32[64,256]{1,0:T(8,128)S(1)}, f32[64,256]{1,0:T(8,128)S(1)}, u32[]{:S(2)}, u32[]{:S(2)}) collective-permute-start(f32[64,256]{1,0:T(8,128)S(1)} %fusion.63), channel_id=1, source_target_pairs={{0,4},{1,5},{2,6},{3,7},{4,0},{5,1},{6,2},{7,3},{8,12},{9,13},{10,... | collective-permute-start | bytes 196616 | tf_op jit(solution)/shard_map/ppermute | solution.py:190
  150.6 5.2 %collective-permute-start.28 = (f32[64,256]{1,0:T(8,128)S(1)}, f32[64,256]{1,0:T(8,128)S(1)}, u32[]{:S(2)}, u32[]{:S(2)}) collective-permute-start(f32[64,256]{1,0:T(8,128)S(1)} %dynamic-slice_bitcast_fusion.6), channel_id=1, source_target_pairs={{0,2},{1,3},{2,0},{3,1},{4,6},{5,7},{6,4},{7,5},{8,10},{9,11},{10,... | collective-permute-start | bytes 196616 | tf_op jit(solution)/shard_map/ppermute | solution.py:166
  155.9 8.6 %collective-permute-start.29 = (f32[64,256]{1,0:T(8,128)S(1)}, f32[64,256]{1,0:T(8,128)S(1)}, u32[]{:S(2)}, u32[]{:S(2)}) collective-permute-start(f32[64,256]{1,0:T(8,128)S(1)} %fusion.57), channel_id=1, source_target_pairs={{0,4},{1,5},{2,6},{3,7},{4,0},{5,1},{6,2},{7,3},{8,12},{9,13},{10,... | collective-permute-start | bytes 196616 | tf_op jit(solution)/shard_map/ppermute | solution.py:190
  162.7 8.6 %collective-permute-start.31 = (f32[64,256]{1,0:T(8,128)S(1)}, f32[64,256]{1,0:T(8,128)S(1)}, u32[]{:S(2)}, u32[]{:S(2)}) collective-permute-start(f32[64,256]{1,0:T(8,128)S(1)} %fusion.51), channel_id=1, source_target_pairs={{0,4},{1,5},{2,6},{3,7},{4,0},{5,1},{6,2},{7,3},{8,12},{9,13},{10,... | collective-permute-start | bytes 196616 | tf_op jit(solution)/shard_map/ppermute | solution.py:190
  163.6 5.0 %collective-permute-start.32 = (f32[64,256]{1,0:T(8,128)S(1)}, f32[64,256]{1,0:T(8,128)S(1)}, u32[]{:S(2)}, u32[]{:S(2)}) collective-permute-start(f32[64,256]{1,0:T(8,128)S(1)} %dynamic-slice_bitcast_fusion.4), channel_id=1, source_target_pairs={{0,2},{1,3},{2,0},{3,1},{4,6},{5,7},{6,4},{7,5},{8,10},{9,11},{10,... | collective-permute-start | bytes 196616 | tf_op jit(solution)/shard_map/ppermute | solution.py:166
  168.6 7.9 %collective-permute-start.33 = (f32[64,256]{1,0:T(8,128)S(1)}, f32[64,256]{1,0:T(8,128)S(1)}, u32[]{:S(2)}, u32[]{:S(2)}) collective-permute-start(f32[64,256]{1,0:T(8,128)S(1)} %fusion.45), channel_id=1, source_target_pairs={{0,4},{1,5},{2,6},{3,7},{4,0},{5,1},{6,2},{7,3},{8,12},{9,13},{10,... | collective-permute-start | bytes 196616 | tf_op jit(solution)/shard_map/ppermute | solution.py:190
  174.6 7.7 %collective-permute-start.35 = (f32[64,256]{1,0:T(8,128)S(1)}, f32[64,256]{1,0:T(8,128)S(1)}, u32[]{:S(2)}, u32[]{:S(2)}) collective-permute-start(f32[64,256]{1,0:T(8,128)S(1)} %fusion.39), channel_id=1, source_target_pairs={{0,4},{1,5},{2,6},{3,7},{4,0},{5,1},{6,2},{7,3},{8,12},{9,13},{10,... | collective-permute-start | bytes 196616 | tf_op jit(solution)/shard_map/ppermute | solution.py:190
  180.6 5.8 %collective-permute-start.37 = (f32[64,256]{1,0:T(8,128)S(1)}, f32[64,256]{1,0:T(8,128)S(1)}, u32[]{:S(2)}, u32[]{:S(2)}) collective-permute-start(f32[64,256]{1,0:T(8,128)S(1)} %fusion.33), channel_id=1, source_target_pairs={{0,4},{1,5},{2,6},{3,7},{4,0},{5,1},{6,2},{7,3},{8,12},{9,13},{10,... | collective-permute-start | bytes 196616 | tf_op jit(solution)/shard_map/ppermute | solution.py:190
  (15 other events, 191.3 us)

commit v20 on v16

--- a/solution.py
+++ b/solution.py
@@ -172,7 +172,15 @@
         send = lax.dynamic_index_in_dim(split, 1 - low, 0, keepdims=False)
         return keep + lax.ppermute(send, "tp", tp_pairs(1))
 
-    near = second_halving(jnp.stack([first_halving_one(block), first_halving_one(across_x)]))
+    near_summed = jnp.stack([first_halving_one(block), first_halving_one(across_x)])
+    near_width = near_summed.shape[-1] // 2
+    near = jnp.concatenate(
+        [
+            second_halving(near_summed[..., start : start + near_width])
+            for start in (0, near_width)
+        ],
+        axis=1,
+    )
     far_summed = first_halving((across_y, diagonal))
     columns = near.shape[-1]
     width = columns // TAIL_PIECES

time: 148 us -> 166 us (1.12)
  waiting for transfers between devices: 65.7 us -> 76.4 us
  other arithmetic: 3.2 us -> 8.52 us
  matrix products: 24.9 us -> 29.8 us
  starting transfers between devices: 45.6 us -> 40.8 us
  local copies, waits for them, and re-layouts: 7.85 us -> 9.54 us
    ppermute x1, waiting for transfers between devices: 11.5 us -> 18 us  [product_and_reduce(): across_x = lax.ppermute(block, 'seq', seq_pairs(1))]
    ppermute x5 -> x6, waiting for transfers between devices: 20.2 us -> 26.2 us  [second_halving(): return keep + lax.ppermute(send, 'tp', tp_pairs(2))]
    dot_general x2, matrix products: 9.78 us -> 14.7 us  [first_halving_one(): product = jnp.dot(piece, down_weight, preferred_element_type=jnp.float32)]
    ppermute x5 -> x6, starting transfers between devices: 12.3 us -> 9.34 us  [second_halving(): return keep + lax.ppermute(send, 'tp', tp_pairs(2))]
    ppermute x4, waiting for transfers between devices: 9.59 us -> 7.52 us  [product_and_reduce(): results.append(keep + lax.ppermute(send, 'tp', tp_pairs(4)))]
    add x4 -> x5, other arithmetic: 0.16 us -> 2.12 us  [second_halving(): return keep + lax.ppermute(send, 'tp', tp_pairs(2))]
  transfers between devices with their start and end apart: 30 -> 31, of which waited for: 15 -> 16; matrix products, arithmetic and copies ran while one was open for 17% -> 17% of each run, Pallas kernels for 0% -> 0%
where the time goes in v20:
time: 166 us
  waiting for transfers between devices  76.4 us (46%)
  starting transfers between devices  40.8 us (25%)
  matrix products  29.8 us (18%)
  local copies, waits for them, and re-layouts  9.54 us (6%)
  other arithmetic  8.52 us (5%)
    ppermute x6, waiting for transfers between devices, second_halving(): return keep + lax.ppermute(send, 'tp', tp_pairs(2))  26.2 us
    ppermute x1, waiting for transfers between devices, product_and_reduce(): across_x = lax.ppermute(block, 'seq', seq_pairs(1))  18 us
    dot_general x2, matrix products, first_halving_one(): product = jnp.dot(piece, down_weight, preferred_element_type=jnp.float32)  14.7 us
    ppermute x7, waiting for transfers between devices, spread_rotate_return(): block = lax.ppermute(block, 'tp', pairs(distance))  11.7 us
    ppermute x7, starting transfers between devices, spread_rotate_return(): block = lax.ppermute(block, 'tp', pairs(distance))  11.2 us
    ppermute x7, starting transfers between devices, spread_rotate_return(): send = lax.ppermute(send, 'tp', pairs(distance))  9.65 us
    ppermute x6, starting transfers between devices, second_halving(): return keep + lax.ppermute(send, 'tp', tp_pairs(2))  9.34 us
    ppermute x1, waiting for transfers between devices, product_and_reduce(): second = lax.ppermute(across_x[half:], 'seq', seq_pairs(2))  7.71 us
  transfers between devices with their start and end apart: 31, of which 16 were waited for; matrix products, arithmetic and copies ran while one was open for 17% of the time, Pallas kernels for 0%

profile of v20, /device:TPU:0, one launch (start us, length us, event | category | flops | bytes accessed | tf_op | source)
XLA Modules:
  0.0 165.6 jit_solution(632677552638698810)
XLA Ops:
  0.0 2.3 %constant_dynamic-slice_fusion = (bf16[16,3584]{1,0:T(8,128)(2,1)}, bf16[16,3584]{1,0:T(8,128)(2,1)}, bf16[16,3584]{1,0:T(8,128)(2,1)}, bf16[16,3584]{1,0:T(8,12...) fusion(bf16[128,3584]{1,0:T(8,128)(2,1)} %param.5, ...), kind=kLoop, calls=%fused_computation.130 | loop fusion | bytes 1835040 | tf_op jit(solution)/shard_map/dynamic_slice | solution.py:111
  2.7 2.6 %collective-permute-start.1 = (bf16[16,3584]{1,0:T(8,128)(2,1)}, bf16[16,3584]{1,0:T(8,128)(2,1)}, u32[]{:S(2)}, u32[]{:S(2)}) collective-permute-start(bf16[16,3584]{1,0:T(8,128)(2,1)} %get-tuple-element.27), channel_id=1, source_target_pairs={{0,2},{1,3},{2,0},{3,1},{4,6},{5,7},{6,4},{7,5},{8,10},{9,11},{10,... | collective-permute-start | bytes 344072 | tf_op jit(solution)/shard_map/ppermute | solution.py:113
  5.5 2.7 %collective-permute-start.3 = (bf16[16,3584]{1,0:T(8,128)(2,1)}, bf16[16,3584]{1,0:T(8,128)(2,1)}, u32[]{:S(2)}, u32[]{:S(2)}) collective-permute-start(bf16[16,3584]{1,0:T(8,128)(2,1)} %get-tuple-element.25), channel_id=1, source_target_pairs={{0,4},{1,5},{2,6},{3,7},{4,0},{5,1},{6,2},{7,3},{8,12},{9,13},{10,... | collective-permute-start | bytes 344072 | tf_op jit(solution)/shard_map/ppermute | solution.py:113
  10.1 1.6 mul.89
  11.7 3.6 %collective-permute-start.5 = (bf16[16,3584]{1,0:T(8,128)(2,1)}, bf16[16,3584]{1,0:T(8,128)(2,1)S(1)}, u32[]{:S(2)}, u32[]{:S(2)}) collective-permute-start(bf16[16,3584]{1,0:T(8,128)(2,1)} %get-tuple-element.30), channel_id=1, source_target_pairs={{0,6},{1,7},{2,4},{3,5},{4,2},{5,3},{6,0},{7,1},{8,14},{9,15},{10,... | collective-permute-start | bytes 344072 | tf_op jit(solution)/shard_map/ppermute | solution.py:113
  20.6 3.8 %collective-permute-done.4 = bf16[16,3584]{1,0:T(8,128)(2,1)} collective-permute-done((bf16[16,3584]{1,0:T(8,128)(2,1)}, bf16[16,3584]{1,0:T(8,128)(2,1)}, u32[]{:S(2)}, u32[]{:S(2)}) %collective-permute-start.4) | collective-permute-done | bytes 114720 | tf_op jit(solution)/shard_map/ppermute | solution.py:113
  27.8 3.5 %fusion.4 = bf16[16,32,896]{2,1,0:T(8,128)(2,1)S(1)} fusion(f32[16,32,896]{2,0,1:T(8,128)} %bitcast.214, f32[32,32]{1,0:T(8,128)S(1)} %copy-done.4), kind=kOutput, calls=%fused_computation.7 | convolution fusion | flops 177078272 | bytes 2756608 | tf_op jit(solution)/shard_map/rbm,bc->rcm/dot_general | solution.py:127
  31.9 1.7 fusion.62
  33.9 3.8 %collective-permute-start.8 = (bf16[16,3584]{1,0:T(8,128)(2,1)S(1)}, bf16[16,3584]{1,0:T(8,128)(2,1)S(1)}, u32[]{:S(2)}, u32[]{:S(2)}) collective-permute-start(bf16[16,3584]{1,0:T(8,128)(2,1)S(1)} %bitcast.227), channel_id=1, source_target_pairs={{0,2},{1,3},{2,0},{3,1},{4,6},{5,7},{6,4},{7,5},{8,10},{9,11},{10,... | collective-permute-start | bytes 344072 | tf_op jit(solution)/shard_map/ppermute | solution.py:134
  38.0 3.1 %collective-permute-start.10 = (bf16[16,3584]{1,0:T(8,128)(2,1)S(1)}, bf16[16,3584]{1,0:T(8,128)(2,1)S(1)}, u32[]{:S(2)}, u32[]{:S(2)}) collective-permute-start(bf16[16,3584]{1,0:T(8,128)(2,1)S(1)} %bitcast.224), channel_id=1, source_target_pairs={{0,4},{1,5},{2,6},{3,7},{4,0},{5,1},{6,2},{7,3},{8,12},{9,13},{10,... | collective-permute-start | bytes 344072 | tf_op jit(solution)/shard_map/ppermute | solution.py:134
  41.6 2.1 %collective-permute-start.12 = (bf16[16,3584]{1,0:T(8,128)(2,1)S(1)}, bf16[16,3584]{1,0:T(8,128)(2,1)S(1)}, u32[]{:S(2)}, u32[]{:S(2)}) collective-permute-start(bf16[16,3584]{1,0:T(8,128)(2,1)S(1)} %bitcast.226), channel_id=1, source_target_pairs={{0,6},{1,7},{2,4},{3,5},{4,2},{5,3},{6,0},{7,1},{8,14},{9,15},{10,... | collective-permute-start | bytes 344072 | tf_op jit(solution)/shard_map/ppermute | solution.py:134
  45.1 2.7 %collective-permute-done.9 = bf16[16,3584]{1,0:T(8,128)(2,1)S(1)} collective-permute-done((bf16[16,3584]{1,0:T(8,128)(2,1)S(1)}, bf16[16,3584]{1,0:T(8,128)(2,1)S(1)}, u32[]{:S(2)}, u32[]{:S(2)}) %collective-permute-start.9) | collective-permute-done | bytes 114720 | tf_op jit(solution)/shard_map/ppermute | solution.py:134
  47.8 9.0 %collective-permute-done.11 = bf16[16,3584]{1,0:T(8,128)(2,1)S(1)} collective-permute-done((bf16[16,3584]{1,0:T(8,128)(2,1)S(1)}, bf16[16,3584]{1,0:T(8,128)(2,1)S(1)}, u32[]{:S(2)}, u32[]{:S(2)}) %collective-permute-start.11) | collective-permute-done | bytes 114720 | tf_op jit(solution)/shard_map/ppermute | solution.py:134
  56.9 7.2 %fusion.63 = f32[128,2048]{1,0:T(8,128)S(1)} fusion(bf16[128,3584]{1,0:T(8,128)(2,1)S(1)} %constant_dynamic-update-slice_fusion, bf16[3584,2048]{1,0:T(8,128)(2,1)} %param.6), kind=kOutput, calls=%fused_computation.149 | convolution fusion | flops 1879048192 | bytes 16646144 | tf_op jit(solution)/shard_map/dot_general | solution.py:169
  69.5 18.0 %collective-permute-done.15 = bf16[128,3584]{1,0:T(8,128)(2,1)S(1)} collective-permute-done((bf16[128,3584]{1,0:T(8,128)(2,1)S(1)}, bf16[128,3584]{1,0:T(8,128)(2,1)S(1)}, u32[]{:S(2)}, u32[]{:S(2)}) %collective-permute-start.15) | collective-permute-done | bytes 917536 | tf_op jit(solution)/shard_map/ppermute | solution.py:147
  87.6 7.4 %fusion.64 = f32[128,2048]{1,0:T(8,128)S(1)} fusion(bf16[128,3584]{1,0:T(8,128)(2,1)S(1)} %collective-permute-done.15, bf16[3584,2048]{1,0:T(8,128)(2,1)} %param.6), kind=kOutput, calls=%fused_computation.150 | convolution fusion | flops 1879048192 | bytes 16646144 | tf_op jit(solution)/shard_map/dot_general | solution.py:169
  95.2 1.6 collective-permute-start.20
  96.8 1.6 collective-permute-start.19
  98.4 2.1 %fusion.65 = f32[128,2048]{1,0:T(8,128)S(1)} fusion(bf16[128,3584]{1,0:T(8,128)(2,1)S(1)} %collective-permute-done.18, bf16[3584,2048]{1,0:T(8,128)(2,1)S(1)} %bitcast.205), kind=kOutput, calls=%fused_computation.151 | convolution fusion | flops 1879048192 | bytes 16646144 | tf_op jit(solution)/shard_map/dot_general | solution.py:155
  100.5 7.7 %collective-permute-done.20 = bf16[64,3584]{1,0:T(8,128)(2,1)S(1)} collective-permute-done((bf16[64,3584]{1,0:T(8,128)(2,1)S(1)}, bf16[64,3584]{1,0:T(8,128)(2,1)S(1)}, u32[]{:S(2)}, u32[]{:S(2)}) %collective-permute-start.20) | collective-permute-done | bytes 458784 | tf_op jit(solution)/shard_map/ppermute | solution.py:150
  109.5 2.1 %fusion.20 = f32[128,2048]{1,0:T(8,128)S(1)} fusion(bf16[3584,2048]{1,0:T(8,128)(2,1)S(1)} %bitcast.205, bf16[64,3584]{1,0:T(8,128)(2,1)S(1)} %collective-permute-done.20, bf16[64,3584]{1,0:T(8,128)(2,1)S(1)} %collective-permute-done.19), kind=kOutput, calls=%fused_computation.31 | convolution fusion | flops 1880883200 | bytes 16646144 | tf_op jit(solution)/shard_map/dot_general | solution.py:155
  112.8 4.9 %collective-permute-start.26 = (f32[64,1024]{1,0:T(8,128)S(1)}, f32[64,1024]{1,0:T(8,128)}, u32[]{:S(2)}, u32[]{:S(2)}) collective-permute-start(f32[64,1024]{1,0:T(8,128)S(1)} %fusion.29), channel_id=1, source_target_pairs={{0,2},{1,3},{2,0},{3,1},{4,6},{5,7},{6,4},{7,5},{8,10},{9,11},{10,... | collective-permute-start | bytes 786440 | tf_op jit(solution)/shard_map/ppermute | solution.py:166
  119.3 5.7 %collective-permute-done.26 = f32[64,1024]{1,0:T(8,128)} collective-permute-done((f32[64,1024]{1,0:T(8,128)S(1)}, f32[64,1024]{1,0:T(8,128)}, u32[]{:S(2)}, u32[]{:S(2)}) %collective-permute-start.26) | collective-permute-done | bytes 262176 | tf_op jit(solution)/shard_map/ppermute | solution.py:166
  126.0 4.4 %collective-permute-done.17 = f32[64,1024]{1,0:T(8,128)} collective-permute-done((f32[64,1024]{1,0:T(8,128)}, f32[64,1024]{1,0:T(8,128)}, u32[]{:S(2)}, u32[]{:S(2)}) %collective-permute-start.17) | collective-permute-done | bytes 262176 | tf_op jit(solution)/shard_map/ppermute | solution.py:166
  133.0 1.8 %collective-permute-start.22 = (f32[64,512]{1,0:T(8,128)S(1)}, f32[64,512]{1,0:T(8,128)S(1)}, u32[]{:S(2)}, u32[]{:S(2)}) collective-permute-start(f32[64,512]{1,0:T(8,128)S(1)} %dynamic-slice_bitcast_fusion.6), channel_id=1, source_target_pairs={{0,2},{1,3},{2,0},{3,1},{4,6},{5,7},{6,4},{7,5},{8,10},{9,11},{10,... | collective-permute-start | bytes 393224 | tf_op jit(solution)/shard_map/ppermute | solution.py:166
  134.8 3.6 %collective-permute-done.22 = f32[64,512]{1,0:T(8,128)S(1)} collective-permute-done((f32[64,512]{1,0:T(8,128)S(1)}, f32[64,512]{1,0:T(8,128)S(1)}, u32[]{:S(2)}, u32[]{:S(2)}) %collective-permute-start.22) | collective-permute-done | bytes 131104 | tf_op jit(solution)/shard_map/ppermute | solution.py:166
  138.4 1.6 collective-permute-start.24
  141.3 3.7 %collective-permute-done.24 = f32[64,512]{1,0:T(8,128)S(1)} collective-permute-done((f32[64,512]{1,0:T(8,128)S(1)}, f32[64,512]{1,0:T(8,128)S(1)}, u32[]{:S(2)}, u32[]{:S(2)}) %collective-permute-start.24) | collective-permute-done | bytes 131104 | tf_op jit(solution)/shard_map/ppermute | solution.py:166
  147.7 4.0 %collective-permute-done.27 = f32[64,512]{1,0:T(8,128)S(1)} collective-permute-done((f32[64,512]{1,0:T(8,128)S(1)}, f32[64,512]{1,0:T(8,128)S(1)}, u32[]{:S(2)}, u32[]{:S(2)}) %collective-permute-start.27) | collective-permute-done | bytes 131104 | tf_op jit(solution)/shard_map/ppermute | solution.py:166
  153.5 4.8 %collective-permute-done.29 = f32[64,512]{1,0:T(8,128)S(1)} collective-permute-done((f32[64,512]{1,0:T(8,128)S(1)}, f32[64,512]{1,0:T(8,128)S(1)}, u32[]{:S(2)}, u32[]{:S(2)}) %collective-permute-start.29) | collective-permute-done | bytes 131104 | tf_op jit(solution)/shard_map/ppermute | solution.py:166
  158.5 2.5 %collective-permute-done.28 = f32[64,512]{1,0:T(8,128)S(1)} collective-permute-done((f32[64,512]{1,0:T(8,128)S(1)}, f32[64,512]{1,0:T(8,128)S(1)}, u32[]{:S(2)}, u32[]{:S(2)}) %collective-permute-start.28) | collective-permute-done | bytes 131104 | tf_op jit(solution)/shard_map/ppermute | solution.py:198
  161.0 3.7 %collective-permute-done.30 = f32[64,512]{1,0:T(8,128)S(1)} collective-permute-done((f32[64,512]{1,0:T(8,128)S(1)}, f32[64,512]{1,0:T(8,128)S(1)}, u32[]{:S(2)}, u32[]{:S(2)}) %collective-permute-start.30) | collective-permute-done | bytes 131104 | tf_op jit(solution)/shard_map/ppermute | solution.py:198
  (120 shorter events, 34.0 us)
Async XLA Ops:
  2.3 9.4 %collective-permute-start = (bf16[16,3584]{1,0:T(8,128)(2,1)}, bf16[16,3584]{1,0:T(8,128)(2,1)}, u32[]{:S(2)}, u32[]{:S(2)}) collective-permute-start(bf16[16,3584]{1,0:T(8,128)(2,1)} %get-tuple-element.28), channel_id=1, source_target_pairs={{0,1},{1,0},{2,3},{3,2},{4,5},{5,4},{6,7},{7,6},{8,9},{9,8},{10,11... | collective-permute-start | bytes 344072 | tf_op jit(solution)/shard_map/ppermute | solution.py:113
  2.7 13.9 %collective-permute-start.1 = (bf16[16,3584]{1,0:T(8,128)(2,1)}, bf16[16,3584]{1,0:T(8,128)(2,1)}, u32[]{:S(2)}, u32[]{:S(2)}) collective-permute-start(bf16[16,3584]{1,0:T(8,128)(2,1)} %get-tuple-element.27), channel_id=1, source_target_pairs={{0,2},{1,3},{2,0},{3,1},{4,6},{5,7},{6,4},{7,5},{8,10},{9,11},{10,... | collective-permute-start | bytes 344072 | tf_op jit(solution)/shard_map/ppermute | solution.py:113
  5.4 12.7 %collective-permute-start.2 = (bf16[16,3584]{1,0:T(8,128)(2,1)}, bf16[16,3584]{1,0:T(8,128)(2,1)}, u32[]{:S(2)}, u32[]{:S(2)}) collective-permute-start(bf16[16,3584]{1,0:T(8,128)(2,1)} %get-tuple-element.26), channel_id=1, source_target_pairs={{0,3},{1,2},{2,1},{3,0},{4,7},{5,6},{6,5},{7,4},{8,11},{9,10},{10,... | collective-permute-start | bytes 344072 | tf_op jit(solution)/shard_map/ppermute | solution.py:113
  5.5 13.9 %collective-permute-start.3 = (bf16[16,3584]{1,0:T(8,128)(2,1)}, bf16[16,3584]{1,0:T(8,128)(2,1)}, u32[]{:S(2)}, u32[]{:S(2)}) collective-permute-start(bf16[16,3584]{1,0:T(8,128)(2,1)} %get-tuple-element.25), channel_id=1, source_target_pairs={{0,4},{1,5},{2,6},{3,7},{4,0},{5,1},{6,2},{7,3},{8,12},{9,13},{10,... | collective-permute-start | bytes 344072 | tf_op jit(solution)/shard_map/ppermute | solution.py:113
  8.2 16.3 %collective-permute-start.4 = (bf16[16,3584]{1,0:T(8,128)(2,1)}, bf16[16,3584]{1,0:T(8,128)(2,1)}, u32[]{:S(2)}, u32[]{:S(2)}) collective-permute-start(bf16[16,3584]{1,0:T(8,128)(2,1)} %get-tuple-element.24), channel_id=1, source_target_pairs={{0,5},{1,4},{2,7},{3,6},{4,1},{5,0},{6,3},{7,2},{8,13},{9,12},{10,... | collective-permute-start | bytes 344072 | tf_op jit(solution)/shard_map/ppermute | solution.py:113
  11.7 14.0 %collective-permute-start.5 = (bf16[16,3584]{1,0:T(8,128)(2,1)}, bf16[16,3584]{1,0:T(8,128)(2,1)S(1)}, u32[]{:S(2)}, u32[]{:S(2)}) collective-permute-start(bf16[16,3584]{1,0:T(8,128)(2,1)} %get-tuple-element.30), channel_id=1, source_target_pairs={{0,6},{1,7},{2,4},{3,5},{4,2},{5,3},{6,0},{7,1},{8,14},{9,15},{10,... | collective-permute-start | bytes 344072 | tf_op jit(solution)/shard_map/ppermute | solution.py:113
  16.6 9.5 %collective-permute-start.6 = (bf16[16,3584]{1,0:T(8,128)(2,1)S(1)}, bf16[16,3584]{1,0:T(8,128)(2,1)S(1)}, u32[]{:S(2)}, u32[]{:S(2)}) collective-permute-start(bf16[16,3584]{1,0:T(8,128)(2,1)S(1)} %copy-done.3), channel_id=1, source_target_pairs={{0,7},{1,6},{2,5},{3,4},{4,3},{5,2},{6,1},{7,0},{8,15},{9,14},{10,... | collective-permute-start | bytes 344072 | tf_op jit(solution)/shard_map/ppermute | solution.py:113
  33.6 8.0 %collective-permute-start.7 = (bf16[16,3584]{1,0:T(8,128)(2,1)S(1)}, bf16[16,3584]{1,0:T(8,128)(2,1)S(1)}, u32[]{:S(2)}, u32[]{:S(2)}) collective-permute-start(bf16[16,3584]{1,0:T(8,128)(2,1)S(1)} %bitcast.228), channel_id=1, source_target_pairs={{0,1},{1,0},{2,3},{3,2},{4,5},{5,4},{6,7},{7,6},{8,9},{9,8},{10,11... | collective-permute-start | bytes 344072 | tf_op jit(solution)/shard_map/ppermute | solution.py:134
  33.9 9.8 %collective-permute-start.8 = (bf16[16,3584]{1,0:T(8,128)(2,1)S(1)}, bf16[16,3584]{1,0:T(8,128)(2,1)S(1)}, u32[]{:S(2)}, u32[]{:S(2)}) collective-permute-start(bf16[16,3584]{1,0:T(8,128)(2,1)S(1)} %bitcast.227), channel_id=1, source_target_pairs={{0,2},{1,3},{2,0},{3,1},{4,6},{5,7},{6,4},{7,5},{8,10},{9,11},{10,... | collective-permute-start | bytes 344072 | tf_op jit(solution)/shard_map/ppermute | solution.py:134
  37.8 10.0 %collective-permute-start.9 = (bf16[16,3584]{1,0:T(8,128)(2,1)S(1)}, bf16[16,3584]{1,0:T(8,128)(2,1)S(1)}, u32[]{:S(2)}, u32[]{:S(2)}) collective-permute-start(bf16[16,3584]{1,0:T(8,128)(2,1)S(1)} %bitcast.225), channel_id=1, source_target_pairs={{0,3},{1,2},{2,1},{3,0},{4,7},{5,6},{6,5},{7,4},{8,11},{9,10},{10,... | collective-permute-start | bytes 344072 | tf_op jit(solution)/shard_map/ppermute | solution.py:134
  38.0 9.8 %collective-permute-start.10 = (bf16[16,3584]{1,0:T(8,128)(2,1)S(1)}, bf16[16,3584]{1,0:T(8,128)(2,1)S(1)}, u32[]{:S(2)}, u32[]{:S(2)}) collective-permute-start(bf16[16,3584]{1,0:T(8,128)(2,1)S(1)} %bitcast.224), channel_id=1, source_target_pairs={{0,4},{1,5},{2,6},{3,7},{4,0},{5,1},{6,2},{7,3},{8,12},{9,13},{10,... | collective-permute-start | bytes 344072 | tf_op jit(solution)/shard_map/ppermute | solution.py:134
  41.1 15.7 %collective-permute-start.11 = (bf16[16,3584]{1,0:T(8,128)(2,1)S(1)}, bf16[16,3584]{1,0:T(8,128)(2,1)S(1)}, u32[]{:S(2)}, u32[]{:S(2)}) collective-permute-start(bf16[16,3584]{1,0:T(8,128)(2,1)S(1)} %bitcast.223), channel_id=1, source_target_pairs={{0,5},{1,4},{2,7},{3,6},{4,1},{5,0},{6,3},{7,2},{8,13},{9,12},{10,... | collective-permute-start | bytes 344072 | tf_op jit(solution)/shard_map/ppermute | solution.py:134
  41.6 15.2 %collective-permute-start.12 = (bf16[16,3584]{1,0:T(8,128)(2,1)S(1)}, bf16[16,3584]{1,0:T(8,128)(2,1)S(1)}, u32[]{:S(2)}, u32[]{:S(2)}) collective-permute-start(bf16[16,3584]{1,0:T(8,128)(2,1)S(1)} %bitcast.226), channel_id=1, source_target_pairs={{0,6},{1,7},{2,4},{3,5},{4,2},{5,3},{6,0},{7,1},{8,14},{9,15},{10,... | collective-permute-start | bytes 344072 | tf_op jit(solution)/shard_map/ppermute | solution.py:134
  43.8 13.1 %collective-permute-start.13 = (bf16[16,3584]{1,0:T(8,128)(2,1)S(1)}, bf16[16,3584]{1,0:T(8,128)(2,1)S(1)}, u32[]{:S(2)}, u32[]{:S(2)}) collective-permute-start(bf16[16,3584]{1,0:T(8,128)(2,1)S(1)} %bitcast.222), channel_id=1, source_target_pairs={{0,7},{1,6},{2,5},{3,4},{4,3},{5,2},{6,1},{7,0},{8,15},{9,14},{10,... | collective-permute-start | bytes 344072 | tf_op jit(solution)/shard_map/ppermute | solution.py:134
  64.2 4.1 %collective-permute-start.14 = (f32[64,2048]{1,0:T(8,128)S(1)}, f32[64,2048]{1,0:T(8,128)}, u32[]{:S(2)}, u32[]{:S(2)}) collective-permute-start(f32[64,2048]{1,0:T(8,128)S(1)} %dynamic-slice_bitcast_fusion.1), channel_id=1, source_target_pairs={{0,1},{1,0},{2,3},{3,2},{4,5},{5,4},{6,7},{7,6},{8,9},{9,8},{10,11... | collective-permute-start | bytes 1572872 | tf_op jit(solution)/shard_map/ppermute | solution.py:173
  65.2 22.3 %collective-permute-start.15 = (bf16[128,3584]{1,0:T(8,128)(2,1)S(1)}, bf16[128,3584]{1,0:T(8,128)(2,1)S(1)}, u32[]{:S(2)}, u32[]{:S(2)}) collective-permute-start(bf16[128,3584]{1,0:T(8,128)(2,1)S(1)} %constant_dynamic-update-slice_fusion), channel_id=1, source_target_pairs={{0,8},{8,0},{16,24},{24,16},{1,9},{9,1},{17,25},{25,17},{2,10},{10... | collective-permute-start | bytes 2752520 | tf_op jit(solution)/shard_map/ppermute | solution.py:147
  66.7 30.0 %collective-permute-start.18 = (bf16[128,3584]{1,0:T(8,128)(2,1)S(1)}, bf16[128,3584]{1,0:T(8,128)(2,1)S(1)}, u32[]{:S(2)}, u32[]{:S(2)}) collective-permute-start(bf16[128,3584]{1,0:T(8,128)(2,1)S(1)} %constant_dynamic-update-slice_fusion), channel_id=1, source_target_pairs={{0,16},{8,24},{16,0},{24,8},{1,17},{9,25},{17,1},{25,9},{2,18},{10... | collective-permute-start | bytes 2752520 | tf_op jit(solution)/shard_map/ppermute | solution.py:148
  68.2 30.1 %slice-start = ((s8[14680064]{0:T(1024)(128)(4,1)}), s8[4194304]{0:T(1024)(128)(4,1)S(1)}, s32[]{:S(2)}) async-start(s8[14680064]{0:T(1024)(128)(4,1)} %bitcast.204), calls=%async_computation | async-start | bytes 8388608
  95.1 17.6 %collective-permute-start.16 = (f32[64,2048]{1,0:T(8,128)S(1)}, f32[64,2048]{1,0:T(8,128)S(1)}, u32[]{:S(2)}, u32[]{:S(2)}) collective-permute-start(f32[64,2048]{1,0:T(8,128)S(1)} %dynamic-slice_bitcast_fusion), channel_id=1, source_target_pairs={{0,1},{1,0},{2,3},{3,2},{4,5},{5,4},{6,7},{7,6},{8,9},{9,8},{10,11... | collective-permute-start | bytes 1572872 | tf_op jit(solution)/shard_map/ppermute | solution.py:173
  95.2 13.0 %collective-permute-start.20 = (bf16[64,3584]{1,0:T(8,128)(2,1)S(1)}, bf16[64,3584]{1,0:T(8,128)(2,1)S(1)}, u32[]{:S(2)}, u32[]{:S(2)}) collective-permute-start(bf16[64,3584]{1,0:T(8,128)(2,1)S(1)} %slice.92), channel_id=1, source_target_pairs={{0,16},{8,24},{16,0},{24,8},{1,17},{9,25},{17,1},{25,9},{2,18},{10... | collective-permute-start | bytes 1376264 | tf_op jit(solution)/shard_map/ppermute | solution.py:150
  96.8 12.7 %collective-permute-start.19 = (bf16[64,3584]{1,0:T(8,128)(2,1)S(1)}, bf16[64,3584]{1,0:T(8,128)(2,1)S(1)}, u32[]{:S(2)}, u32[]{:S(2)}) collective-permute-start(bf16[64,3584]{1,0:T(8,128)(2,1)S(1)} %slice.91), channel_id=1, source_target_pairs={{0,8},{8,0},{16,24},{24,16},{1,9},{9,1},{17,25},{25,17},{2,10},{10... | collective-permute-start | bytes 1376264 | tf_op jit(solution)/shard_map/ppermute | solution.py:149
  112.7 18.8 %collective-permute-start.21 = (f32[2,64,2048]{2,1,0:T(8,128)}, f32[2,64,2048]{2,1,0:T(8,128)}, u32[]{:S(2)}, u32[]{:S(2)}) collective-permute-start(f32[2,64,2048]{2,1,0:T(8,128)} %fusion.16), channel_id=1, source_target_pairs={{0,1},{1,0},{2,3},{3,2},{4,5},{5,4},{6,7},{7,6},{8,9},{9,8},{10,11... | collective-permute-start | bytes 3145736 | tf_op jit(solution)/shard_map/ppermute | solution.py:160
  112.8 12.2 %collective-permute-start.26 = (f32[64,1024]{1,0:T(8,128)S(1)}, f32[64,1024]{1,0:T(8,128)}, u32[]{:S(2)}, u32[]{:S(2)}) collective-permute-start(f32[64,1024]{1,0:T(8,128)S(1)} %fusion.29), channel_id=1, source_target_pairs={{0,2},{1,3},{2,0},{3,1},{4,6},{5,7},{6,4},{7,5},{8,10},{9,11},{10,... | collective-permute-start | bytes 786440 | tf_op jit(solution)/shard_map/ppermute | solution.py:166
  119.3 11.1 %collective-permute-start.17 = (f32[64,1024]{1,0:T(8,128)}, f32[64,1024]{1,0:T(8,128)}, u32[]{:S(2)}, u32[]{:S(2)}) collective-permute-start(f32[64,1024]{1,0:T(8,128)} %dynamic-slice_bitcast_fusion.2), channel_id=1, source_target_pairs={{0,2},{1,3},{2,0},{3,1},{4,6},{5,7},{6,4},{7,5},{8,10},{9,11},{10,... | collective-permute-start | bytes 786440 | tf_op jit(solution)/shard_map/ppermute | solution.py:166
  133.0 5.4 %collective-permute-start.22 = (f32[64,512]{1,0:T(8,128)S(1)}, f32[64,512]{1,0:T(8,128)S(1)}, u32[]{:S(2)}, u32[]{:S(2)}) collective-permute-start(f32[64,512]{1,0:T(8,128)S(1)} %dynamic-slice_bitcast_fusion.6), channel_id=1, source_target_pairs={{0,2},{1,3},{2,0},{3,1},{4,6},{5,7},{6,4},{7,5},{8,10},{9,11},{10,... | collective-permute-start | bytes 393224 | tf_op jit(solution)/shard_map/ppermute | solution.py:166
  138.4 6.6 %collective-permute-start.24 = (f32[64,512]{1,0:T(8,128)S(1)}, f32[64,512]{1,0:T(8,128)S(1)}, u32[]{:S(2)}, u32[]{:S(2)}) collective-permute-start(f32[64,512]{1,0:T(8,128)S(1)} %dynamic-slice_bitcast_fusion.5), channel_id=1, source_target_pairs={{0,2},{1,3},{2,0},{3,1},{4,6},{5,7},{6,4},{7,5},{8,10},{9,11},{10,... | collective-permute-start | bytes 393224 | tf_op jit(solution)/shard_map/ppermute | solution.py:166
  140.1 7.6 %collective-permute-start.23 = (f32[64,512]{1,0:T(8,128)S(1)}, f32[64,512]{1,0:T(8,128)S(1)}, u32[]{:S(2)}, u32[]{:S(2)}) collective-permute-start(f32[64,512]{1,0:T(8,128)S(1)} %fusion.49), channel_id=1, source_target_pairs={{0,4},{1,5},{2,6},{3,7},{4,0},{5,1},{6,2},{7,3},{8,12},{9,13},{10,... | collective-permute-start | bytes 393224 | tf_op jit(solution)/shard_map/ppermute | solution.py:198
  145.0 6.6 %collective-permute-start.27 = (f32[64,512]{1,0:T(8,128)S(1)}, f32[64,512]{1,0:T(8,128)S(1)}, u32[]{:S(2)}, u32[]{:S(2)}) collective-permute-start(f32[64,512]{1,0:T(8,128)S(1)} %dynamic-slice_bitcast_fusion.4), channel_id=1, source_target_pairs={{0,2},{1,3},{2,0},{3,1},{4,6},{5,7},{6,4},{7,5},{8,10},{9,11},{10,... | collective-permute-start | bytes 393224 | tf_op jit(solution)/shard_map/ppermute | solution.py:166
  146.0 7.5 %collective-permute-start.25 = (f32[64,512]{1,0:T(8,128)S(1)}, f32[64,512]{1,0:T(8,128)S(1)}, u32[]{:S(2)}, u32[]{:S(2)}) collective-permute-start(f32[64,512]{1,0:T(8,128)S(1)} %fusion.44), channel_id=1, source_target_pairs={{0,4},{1,5},{2,6},{3,7},{4,0},{5,1},{6,2},{7,3},{8,12},{9,13},{10,... | collective-permute-start | bytes 393224 | tf_op jit(solution)/shard_map/ppermute | solution.py:198
  151.7 6.6 %collective-permute-start.29 = (f32[64,512]{1,0:T(8,128)S(1)}, f32[64,512]{1,0:T(8,128)S(1)}, u32[]{:S(2)}, u32[]{:S(2)}) collective-permute-start(f32[64,512]{1,0:T(8,128)S(1)} %dynamic-slice_bitcast_fusion.3), channel_id=1, source_target_pairs={{0,2},{1,3},{2,0},{3,1},{4,6},{5,7},{6,4},{7,5},{8,10},{9,11},{10,... | collective-permute-start | bytes 393224 | tf_op jit(solution)/shard_map/ppermute | solution.py:166
  151.8 9.2 %collective-permute-start.28 = (f32[64,512]{1,0:T(8,128)S(1)}, f32[64,512]{1,0:T(8,128)S(1)}, u32[]{:S(2)}, u32[]{:S(2)}) collective-permute-start(f32[64,512]{1,0:T(8,128)S(1)} %fusion.39), channel_id=1, source_target_pairs={{0,4},{1,5},{2,6},{3,7},{4,0},{5,1},{6,2},{7,3},{8,12},{9,13},{10,... | collective-permute-start | bytes 393224 | tf_op jit(solution)/shard_map/ppermute | solution.py:198
  158.4 6.4 %collective-permute-start.30 = (f32[64,512]{1,0:T(8,128)S(1)}, f32[64,512]{1,0:T(8,128)S(1)}, u32[]{:S(2)}, u32[]{:S(2)}) collective-permute-start(f32[64,512]{1,0:T(8,128)S(1)} %fusion.34), channel_id=1, source_target_pairs={{0,4},{1,5},{2,6},{3,7},{4,0},{5,1},{6,2},{7,3},{8,12},{9,13},{10,... | collective-permute-start | bytes 393224 | tf_op jit(solution)/shard_map/ppermute | solution.py:198
  (9 other events, 124.1 us)
